TPU v7x, 32 devices: a whole 2x2x4 slice. The times are simulated.
32 devices in a mesh: gx: 4 (over y, core), gy: 8 (over z, x).
Axes of the slice: x: 2, y: 2, z: 4, core: 2. Of those that a mesh axis runs over, the one named last changes fastest.
Arguments:
- control: float32 [3, 256, 1024], P(None, 'gy', 'gx'), may hold values from -2 to 2
- perts: float32 [16, 3, 256, 1024], P(None, None, 'gy', 'gx'), may hold values from -2.8 to 2.8
Outputs:
- basis: float32 [16, 3, 256, 1024], P(None, None, 'gy', 'gx')
- rfactor: float32 [16, 16], replicated
All inputs are finite; a program needn't handle non-finite values.
Results may differ from a plain program's by a relative error of at most 0.0003.
Values sent between devices are 32-bit elements; how exact they have to be, the bound alone decides.
No kernel may reach another device: no remote copies, remote signals or barrier semaphores. Data moves between devices by JAX's collectives and lax.ppermute only.
A program may use at most 64 MiB of HBM per device.

v0:
```python
import functools
import math

import jax
import jax.numpy as jnp
from jax import lax
from jax.experimental import pallas as pl
from jax.experimental.pallas import tpu as pltpu
from jax.sharding import PartitionSpec as P

MEMBERS = 16
STEPS = 2


mean_depth = 4.0
gravity = 1.0
coriolis_mid = 0.5
time_step = 0.1
two_pi = 2.0 * math.pi


def ring_halo(value, width, lanes):
    rows, cols = (value.shape[-2], value.shape[-1])
    across, down = (lax.axis_size("gx"), lax.axis_size("gy"))

    def shift(part, axes, dx, dy, flatten=True):
        pairs = []
        for x in range(across):
            for y in range(down):
                target = ((x + dx) % across, (y + dy) % down)
                if axes == "gx":
                    pairs.append((x, target[0])) if y == 0 else None
                elif axes == "gy":
                    pairs.append((y, target[1])) if x == 0 else None
                else:
                    pairs.append((x * down + y, target[0] * down + target[1]))
        if not flatten:
            return lax.ppermute(part, axes, pairs)
        flat = part.reshape(-1)
        return lax.ppermute(flat, axes, pairs).reshape(part.shape)

    both = ("gx", "gy")
    top, bottom = (value[..., :width, :], value[..., rows - width :, :])
    left, right = (value[..., :, :width], value[..., :, cols - width :])
    above = shift(bottom, "gy", 0, 1, flatten=False)
    below = shift(top, "gy", 0, -1, flatten=False)
    west = shift(right, "gx", 1, 0)
    east = shift(left, "gx", -1, 0)
    north_west = shift(bottom[..., cols - width :], both, 1, 1)
    north_east = shift(bottom[..., :width], both, -1, 1)
    south_west = shift(top[..., cols - width :], both, 1, -1)
    south_east = shift(top[..., :width], both, -1, -1)

    def band(centre, east_part, west_part):
        gap = jnp.zeros(centre.shape[:-1] + (lanes - cols - 2 * width,), centre.dtype)
        return jnp.concatenate([centre, east_part, gap, west_part], axis=-1)

    return jnp.concatenate(
        [band(value, east, west), band(below, south_east, south_west), band(above, north_east, north_west)],
        axis=-2,
    )


def forecast_kernel(cor_ref, x_ref, o_ref, *, steps, rows, cols):
    f = cor_ref[...]
    R, C = f.shape
    third = 1.0 / 12.0
    def dx(v):
        g = pltpu.roll(v, C - 1, 1) - pltpu.roll(v, 1, 1)
        w = pltpu.roll(v, C - 2, 1) - pltpu.roll(v, 2, 1)
        return (8.0 * g - w) * third
    def dy(v):
        g = pltpu.roll(v, R - 1, 0) - pltpu.roll(v, 1, 0)
        w = pltpu.roll(v, R - 2, 0) - pltpu.roll(v, 2, 0)
        return (8.0 * g - w) * third
    def tend(h, e, n):
        depth = 4.0 + h
        ch = -(dx(depth * e) + dy(depth * n))
        ce = -(e * dx(e) + n * dy(e)) + f * n - dx(h)
        cn = -(e * dx(n) + n * dy(n)) - f * e - dy(h)
        return ch, ce, cn
    s = (x_ref[0, 0], x_ref[0, 1], x_ref[0, 2])
    for _ in range(steps):
        first = tend(*s)
        mid = tuple(a + 0.1 * b for a, b in zip(s, first))
        second = tend(*mid)
        s = tuple(a + 0.05 * (b + c) for a, b, c in zip(s, first, second))
    for k in range(3):
        o_ref[0, k] = s[k][:rows, :cols]

def forecast(cor, padded, steps, rows, cols):
    S, F, R, C = padded.shape
    return pl.pallas_call(
        functools.partial(forecast_kernel, steps=steps, rows=rows, cols=cols),
        out_shape=jax.ShapeDtypeStruct((S, F, rows, cols), jnp.float32),
        grid=(S,),
        in_specs=[pl.BlockSpec((R, C), lambda i: (0, 0)),
                  pl.BlockSpec((1, F, R, C), lambda i: (i, 0, 0, 0))],
        out_specs=pl.BlockSpec((1, F, rows, cols), lambda i: (i, 0, 0, 0)),
    )(cor, padded)


def body(control, perts):
    tile_rows, tile_column_count = (control.shape[1], control.shape[2])
    grid_rows = tile_rows * lax.axis_size("gy")
    grid_cols = tile_column_count * lax.axis_size("gx")
    first_row = lax.axis_index("gy") * tile_rows
    margin = 4 * STEPS
    lanes = 128 * (-(-(tile_column_count + 2 * margin) // 128))
    ring_rows = tile_rows + 2 * margin
    offsets = jnp.arange(ring_rows, dtype=jnp.int32)
    offsets = jnp.where(offsets < tile_rows + margin, offsets, offsets - ring_rows)
    rows = ((first_row + offsets) % grid_rows).astype(jnp.float32)
    coriolis = coriolis_mid * (1.0 + 0.5 * jnp.sin(two_pi * rows / float(grid_rows)))
    coriolis = jnp.broadcast_to(coriolis[:, None], (ring_rows, lanes))

    states = jnp.concatenate([control[None], control[None] + perts], 0)
    padded = ring_halo(states, margin, lanes)
    current = forecast(coriolis, padded, STEPS, tile_rows, tile_column_count)
    bred = current[1:] - current[0:1]
    flat = bred.reshape(MEMBERS, -1)
    local_gram = jnp.dot(flat, flat.T, precision=lax.Precision.HIGHEST)
    gram = local_gram
    for axis in ("gx", "gy"):
        count = lax.axis_size(axis)
        if count & (count - 1):
            gram = lax.psum(gram, axis)
            continue
        stride = 1
        while stride < count:
            pairs = [(i, i ^ stride) for i in range(count)]
            gram = gram + lax.ppermute(gram, axis, pairs)
            stride *= 2
    lower = jnp.linalg.cholesky(gram)
    solved = jax.scipy.linalg.solve_triangular(lower, flat, lower=True)
    domain_length = 3 * grid_rows * grid_cols
    basis = (math.sqrt(domain_length) * solved).reshape(perts.shape)
    rfactor = lower.T / math.sqrt(domain_length)
    return (basis, rfactor)


def solution(mesh):
    in_specs = (P(None, "gy", "gx"), P(None, None, "gy", "gx"))
    out_specs = (P(None, None, "gy", "gx"), P())
    return jax.shard_map(body, mesh=mesh, in_specs=in_specs, out_specs=out_specs, check_vma=False)
```

profile of v0, /device:TPU:0, one launch (start us, length us, event | category | flops | bytes accessed | tf_op | source)
XLA Modules:
  0.0 96.0 jit_solution(16481282917316654559)
XLA Ops:
  0.6 1.6 %broadcast_add_fusion = f32[16,3,32,256]{3,2,1,0:T(8,128)S(1)} fusion(f32[16,3,32,256]{3,2,1,0:T(8,128)} %param.3, f32[3,32,256]{2,1,0:T(8,128)} %param.2), kind=kLoop, calls=%fused_computation.22 | loop fusion | flops 393216 | bytes 3244032 | tf_op jit(solution)/shard_map/add | solution.py:117
  2.3 1.0 %fusion.7 = (f32[17,3,8,256]{3,2,1,0:T(8,128)}, f32[17,3,8,256]{3,2,1,0:T(8,128)}) fusion(f32[16,3,32,256]{3,2,1,0:T(8,128)S(1)} %broadcast_add_fusion, f32[1,3,32,256]{3,2,1,0:T(8,128)S(1)} %bitcast.40), kind=kLoop, calls=%fused_computation.23 | loop fusion | flops 208896 | bytes 2506752 | tf_op jit(solution)/shard_map/concatenate | solution.py:117
  3.3 6.0 %collective-permute-start.2 = (f32[17,3,8,256]{3,2,1,0:T(8,128)}, f32[17,3,8,256]{3,2,1,0:T(8,128)}, u32[]{:S(2)}, u32[]{:S(2)}) collective-permute-start(f32[17,3,8,256]{3,2,1,0:T(8,128)} %get-tuple-element.8), channel_id=1, source_target_pairs={{0,7},{1,0},{2,1},{3,2},{4,3},{5,4},{6,5},{7,6},{8,15},{9,8},{10,9... | collective-permute-start | bytes 1253384 | tf_op jit(solution)/shard_map/ppermute | solution.py:38
  10.2 4.6 %collective-permute-start.3 = (f32[3264]{0:T(1024)}, f32[3264]{0:T(1024)}, u32[]{:S(2)}, u32[]{:S(2)}) collective-permute-start(f32[3264]{0:T(1024)} %reshape.87), channel_id=1, source_target_pairs={{0,31},{1,24},{2,25},{3,26},{4,27},{5,28},{6,29},{7,30},{8,7},{9,0... | collective-permute-start | bytes 39176 | tf_op jit(solution)/shard_map/ppermute | solution.py:40
  16.2 2.6 %collective-permute-start.6 = (f32[3264]{0:T(1024)}, f32[3264]{0:T(1024)}, u32[]{:S(2)}, u32[]{:S(2)}) collective-permute-start(f32[3264]{0:T(1024)} %reshape.91), channel_id=1, source_target_pairs={{0,25},{1,26},{2,27},{3,28},{4,29},{5,30},{6,31},{7,24},{8,1},{9,2... | collective-permute-start | bytes 39176 | tf_op jit(solution)/shard_map/ppermute | solution.py:40
  19.9 1.0 %reshape.83 = f32[13056]{0:T(1024)} reshape(f32[17,3,32,8]{3,2,1,0:T(8,128)S(1)} %get-tuple-element.6) | data formatting | bytes 104448 | tf_op jit(solution)/shard_map/reshape | solution.py:39
  21.3 3.7 %collective-permute-done.3 = f32[3264]{0:T(1024)} collective-permute-done((f32[3264]{0:T(1024)}, f32[3264]{0:T(1024)}, u32[]{:S(2)}, u32[]{:S(2)}) %collective-permute-start.3) | collective-permute-done | bytes 13088 | tf_op jit(solution)/shard_map/ppermute | solution.py:40
  25.0 1.3 %collective-permute-done.4 = f32[3264]{0:T(1024)} collective-permute-done((f32[3264]{0:T(1024)}, f32[3264]{0:T(1024)}, u32[]{:S(2)}, u32[]{:S(2)}) %collective-permute-start.4) | collective-permute-done | bytes 13088 | tf_op jit(solution)/shard_map/ppermute | solution.py:40
  26.3 1.1 %collective-permute-start = (f32[13056]{0:T(1024)}, f32[13056]{0:T(1024)S(1)}, u32[]{:S(2)}, u32[]{:S(2)}) collective-permute-start(f32[13056]{0:T(1024)} %reshape.83), channel_id=1, source_target_pairs={{0,24},{8,0},{16,8},{24,16},{1,25},{9,1},{17,9},{25,17},{2,26},{10... | collective-permute-start | bytes 156680 | tf_op jit(solution)/shard_map/ppermute | solution.py:40
  28.2 0.9 reshape.88
  29.0 1.6 %reshape.90 = f32[17,3,8,8]{3,2,1,0:T(8,128)} reshape(f32[3264]{0:T(1024)} %collective-permute-done.4) | data formatting | bytes 26112 | tf_op jit(solution)/shard_map/reshape | solution.py:40
  30.6 1.6 %reshape.92 = f32[17,3,8,8]{3,2,1,0:T(8,128)} reshape(f32[3264]{0:T(1024)} %collective-permute-done.6) | data formatting | bytes 26112 | tf_op jit(solution)/shard_map/reshape | solution.py:40
  32.2 0.8 reshape.94
  33.5 1.3 %reshape.86 = f32[17,3,32,8]{3,2,1,0:T(8,128)S(1)} reshape(f32[13056]{0:T(1024)} %collective-permute-done.1) | data formatting | bytes 104448 | tf_op jit(solution)/shard_map/reshape | solution.py:40
  34.8 5.6 %maximum_maximum_fusion.x_ref = f32[17,3,48,384]{3,2,1,0:T(8,128)} fusion(f32[17,3,8,8]{3,2,1,0:T(8,128)} %reshape.94, f32[17,3,8,112]{3,2,1,0:T(8,128)S(1)} %broadcast.125, f32[17,3,8,8]{3,2,1,0:T(8,128)} %reshape.92, f32[17,3,8,256]{3,2,1,0:T(8,128)} %collective-permute-done.5, f32[17,3,8,8]{3,2,1,0:T(8,128)} %reshape.90, f32[17,3,8,8]{3,2,1,0:T(8,128)S(1)} %reshape.88, ...), kind=kLoop, calls=%fused_computation.8 | loop fusion | flops 11280384 | bytes 6680064 | tf_op jit(solution)/shard_map/concatenate | solution.py:58
  41.1 24.0 %shard_map.41 = f32[17,3,32,256]{3,2,1,0:T(8,128)} custom-call(f32[48,384]{1,0:T(8,128)} %broadcast_in_dim.7.cor_ref, f32[17,3,48,384]{3,2,1,0:T(8,128)} %maximum_maximum_fusion.x_ref), custom_call_target="tpu_custom_call" | custom-call | tf_op jit(solution)/shard_map/pallas_call | solution.py:93
  65.1 0.9 slice_bitcast_fusion
  66.0 1.6 %slice_subtract_fusion = f32[16,3,32,256]{3,2,1,0:T(8,128)S(1)} fusion(f32[17,3,32,256]{3,2,1,0:T(8,128)} %shard_map.41, f32[3,32,256]{2,1,0:T(8,128)S(1)} %slice_bitcast_fusion), kind=kLoop, calls=%fused_computation.9 | loop fusion | flops 393216 | bytes 3244032 | tf_op jit(solution)/shard_map/sub | solution.py:120
  67.6 2.7 %fusion.2 = f32[16,16]{0,1:T(8,128)S(1)} fusion(f32[16,3,32,256]{3,2,1,0:T(8,128)S(1)} %slice_subtract_fusion), kind=kOutput, calls=%fused_computation.19 | convolution fusion | flops 75497472 | bytes 1573888 | tf_op jit(solution)/shard_map/dot_general | solution.py:122
  70.3 1.4 %collective-permute-start.8 = (f32[16,16]{0,1:T(8,128)S(1)}, f32[16,16]{0,1:T(8,128)S(1)}, u32[]{:S(2)}, u32[]{:S(2)}) collective-permute-start(f32[16,16]{0,1:T(8,128)S(1)} %fusion.2), channel_id=1, source_target_pairs={{0,8},{8,0},{16,24},{24,16},{1,9},{9,1},{17,25},{25,17},{2,10},{10... | collective-permute-start | bytes 3080 | tf_op jit(solution)/shard_map/ppermute | solution.py:132
  73.3 2.9 %collective-permute-done.9 = f32[16,16]{0,1:T(8,128)S(1)} collective-permute-done((f32[16,16]{0,1:T(8,128)S(1)}, f32[16,16]{0,1:T(8,128)S(1)}, u32[]{:S(2)}, u32[]{:S(2)}) %collective-permute-start.9) | collective-permute-done | bytes 1056 | tf_op jit(solution)/shard_map/ppermute | solution.py:132
  76.2 2.0 %collective-permute-start.10 = (f32[16,16]{0,1:T(8,128)S(1)}, f32[16,16]{0,1:T(8,128)S(1)}, u32[]{:S(2)}, u32[]{:S(2)}) collective-permute-start(f32[16,16]{0,1:T(8,128)S(1)} %add.78), channel_id=1, source_target_pairs={{0,1},{1,0},{2,3},{3,2},{4,5},{5,4},{6,7},{7,6},{8,9},{9,8},{10,11... | collective-permute-start | bytes 3080 | tf_op jit(solution)/shard_map/ppermute | solution.py:132
  78.2 1.6 %collective-permute-done.10 = f32[16,16]{0,1:T(8,128)S(1)} collective-permute-done((f32[16,16]{0,1:T(8,128)S(1)}, f32[16,16]{0,1:T(8,128)S(1)}, u32[]{:S(2)}, u32[]{:S(2)}) %collective-permute-start.10) | collective-permute-done | bytes 1056 | tf_op jit(solution)/shard_map/ppermute | solution.py:132
  79.9 1.6 %collective-permute-start.11 = (f32[16,16]{0,1:T(8,128)S(1)}, f32[16,16]{0,1:T(8,128)S(1)}, u32[]{:S(2)}, u32[]{:S(2)}) collective-permute-start(f32[16,16]{0,1:T(8,128)S(1)} %add.79), channel_id=1, source_target_pairs={{0,2},{1,3},{2,0},{3,1},{4,6},{5,7},{6,4},{7,5},{8,10},{9,11},{10,... | collective-permute-start | bytes 3080 | tf_op jit(solution)/shard_map/ppermute | solution.py:132
  81.4 2.1 %collective-permute-done.11 = f32[16,16]{0,1:T(8,128)S(1)} collective-permute-done((f32[16,16]{0,1:T(8,128)S(1)}, f32[16,16]{0,1:T(8,128)S(1)}, u32[]{:S(2)}, u32[]{:S(2)}) %collective-permute-start.11) | collective-permute-done | bytes 1056 | tf_op jit(solution)/shard_map/ppermute | solution.py:132
  83.5 2.6 %collective-permute-start.12 = (f32[16,16]{0,1:T(8,128)S(1)}, f32[16,16]{0,1:T(8,128)S(1)}, u32[]{:S(2)}, u32[]{:S(2)}) collective-permute-start(f32[16,16]{0,1:T(8,128)S(1)} %add.80), channel_id=1, source_target_pairs={{0,4},{1,5},{2,6},{3,7},{4,0},{5,1},{6,2},{7,3},{8,12},{9,13},{10,... | collective-permute-start | bytes 3080 | tf_op jit(solution)/shard_map/ppermute | solution.py:132
  86.1 0.9 copy.19
  87.0 1.0 %collective-permute-done.12 = f32[16,16]{0,1:T(8,128)S(1)} collective-permute-done((f32[16,16]{0,1:T(8,128)S(1)}, f32[16,16]{0,1:T(8,128)S(1)}, u32[]{:S(2)}, u32[]{:S(2)}) %collective-permute-start.12) | collective-permute-done | bytes 1056 | tf_op jit(solution)/shard_map/ppermute | solution.py:132
  88.2 1.5 %cholesky.16 = f32[16,16]{1,0:T(8,128)S(1)} custom-call(f32[16,16]{1,0:T(8,128)S(1)} %fusion.13), custom_call_target="Cholesky" | custom-call | tf_op jit(solution)/shard_map/jit(cholesky)/cholesky | solution.py:134
  90.9 1.2 %custom-call.7 = f32[1,16,16]{1,2,0:T(8,128)S(1)} custom-call(f32[1,16,16]{2,1,0:T(8,128)S(1)} %get-tuple-element.15), custom_call_target="InvertDiagBlocksLowerTriangular" | custom-call | tf_op jit(solution)/shard_map/jit(_solve_triangular)/triangular_solve | solution.py:135
  92.2 1.5 %convolution_multiply_fusion = f32[16,24576]{1,0:T(8,128)S(1)} fusion(f32[16,24576]{1,0:T(8,128)S(1)} %bitcast.38, f32[1,16,16]{1,2,0:T(8,128)S(1)} %custom-call.7), kind=kOutput, calls=%fused_computation | convolution fusion | flops 75890688 | bytes 3146752 | tf_op jit(solution)/shard_map/jit(_solve_triangular)/triangular_solve | solution.py:135
  93.7 1.6 %copy.20 = f32[2,8,96,256]{3,2,1,0:T(8,128)} copy(f32[2,8,96,256]{3,1,2,0:T(8,128)S(1)} %bitcast.39) | data formatting | bytes 3145728
  (38 shorter events, 9.4 us)
Async XLA Ops:
  0.6 1.7 %copy-start = (f32[3,32,256]{2,1,0:T(8,128)S(1)}, f32[3,32,256]{2,1,0:T(8,128)}, u32[]{:S(2)}) copy-start(f32[3,32,256]{2,1,0:T(8,128)} %param.2) | copy-start | bytes 294916
  3.3 31.5 %collective-permute-start.2 = (f32[17,3,8,256]{3,2,1,0:T(8,128)}, f32[17,3,8,256]{3,2,1,0:T(8,128)}, u32[]{:S(2)}, u32[]{:S(2)}) collective-permute-start(f32[17,3,8,256]{3,2,1,0:T(8,128)} %get-tuple-element.8), channel_id=1, source_target_pairs={{0,7},{1,0},{2,1},{3,2},{4,3},{5,4},{6,5},{7,6},{8,15},{9,8},{10,9... | collective-permute-start | bytes 1253384 | tf_op jit(solution)/shard_map/ppermute | solution.py:38
  9.3 25.5 %collective-permute-start.5 = (f32[17,3,8,256]{3,2,1,0:T(8,128)}, f32[17,3,8,256]{3,2,1,0:T(8,128)}, u32[]{:S(2)}, u32[]{:S(2)}) collective-permute-start(f32[17,3,8,256]{3,2,1,0:T(8,128)} %get-tuple-element.9), channel_id=1, source_target_pairs={{0,1},{1,2},{2,3},{3,4},{4,5},{5,6},{6,7},{7,0},{8,9},{9,10},{10,1... | collective-permute-start | bytes 1253384 | tf_op jit(solution)/shard_map/ppermute | solution.py:38
  10.2 14.8 %collective-permute-start.3 = (f32[3264]{0:T(1024)}, f32[3264]{0:T(1024)}, u32[]{:S(2)}, u32[]{:S(2)}) collective-permute-start(f32[3264]{0:T(1024)} %reshape.87), channel_id=1, source_target_pairs={{0,31},{1,24},{2,25},{3,26},{4,27},{5,28},{6,29},{7,30},{8,7},{9,0... | collective-permute-start | bytes 39176 | tf_op jit(solution)/shard_map/ppermute | solution.py:40
  15.5 10.8 %collective-permute-start.4 = (f32[3264]{0:T(1024)}, f32[3264]{0:T(1024)}, u32[]{:S(2)}, u32[]{:S(2)}) collective-permute-start(f32[3264]{0:T(1024)} %reshape.89), channel_id=1, source_target_pairs={{0,15},{1,8},{2,9},{3,10},{4,11},{5,12},{6,13},{7,14},{8,23},{9,16... | collective-permute-start | bytes 39176 | tf_op jit(solution)/shard_map/ppermute | solution.py:40
  16.2 11.2 %collective-permute-start.6 = (f32[3264]{0:T(1024)}, f32[3264]{0:T(1024)}, u32[]{:S(2)}, u32[]{:S(2)}) collective-permute-start(f32[3264]{0:T(1024)} %reshape.91), channel_id=1, source_target_pairs={{0,25},{1,26},{2,27},{3,28},{4,29},{5,30},{6,31},{7,24},{8,1},{9,2... | collective-permute-start | bytes 39176 | tf_op jit(solution)/shard_map/ppermute | solution.py:40
  25.0 7.2 %collective-permute-start.7 = (f32[3264]{0:T(1024)}, f32[3264]{0:T(1024)S(1)}, u32[]{:S(2)}, u32[]{:S(2)}) collective-permute-start(f32[3264]{0:T(1024)} %reshape.93), channel_id=1, source_target_pairs={{0,9},{1,10},{2,11},{3,12},{4,13},{5,14},{6,15},{7,8},{8,17},{9,18... | collective-permute-start | bytes 39176 | tf_op jit(solution)/shard_map/ppermute | solution.py:40
  26.3 6.7 %collective-permute-start = (f32[13056]{0:T(1024)}, f32[13056]{0:T(1024)S(1)}, u32[]{:S(2)}, u32[]{:S(2)}) collective-permute-start(f32[13056]{0:T(1024)} %reshape.83), channel_id=1, source_target_pairs={{0,24},{8,0},{16,8},{24,16},{1,25},{9,1},{17,9},{25,17},{2,26},{10... | collective-permute-start | bytes 156680 | tf_op jit(solution)/shard_map/ppermute | solution.py:40
  27.4 6.1 %collective-permute-start.1 = (f32[13056]{0:T(1024)S(1)}, f32[13056]{0:T(1024)}, u32[]{:S(2)}, u32[]{:S(2)}) collective-permute-start(f32[13056]{0:T(1024)S(1)} %reshape.85), channel_id=1, source_target_pairs={{0,8},{8,16},{16,24},{24,0},{1,9},{9,17},{17,25},{25,1},{2,10},{10... | collective-permute-start | bytes 156680 | tf_op jit(solution)/shard_map/ppermute | solution.py:40
  70.3 2.3 %collective-permute-start.8 = (f32[16,16]{0,1:T(8,128)S(1)}, f32[16,16]{0,1:T(8,128)S(1)}, u32[]{:S(2)}, u32[]{:S(2)}) collective-permute-start(f32[16,16]{0,1:T(8,128)S(1)} %fusion.2), channel_id=1, source_target_pairs={{0,8},{8,0},{16,24},{24,16},{1,9},{9,1},{17,25},{25,17},{2,10},{10... | collective-permute-start | bytes 3080 | tf_op jit(solution)/shard_map/ppermute | solution.py:132
  72.5 3.7 %collective-permute-start.9 = (f32[16,16]{0,1:T(8,128)S(1)}, f32[16,16]{0,1:T(8,128)S(1)}, u32[]{:S(2)}, u32[]{:S(2)}) collective-permute-start(f32[16,16]{0,1:T(8,128)S(1)} %add.77), channel_id=1, source_target_pairs={{0,16},{8,24},{16,0},{24,8},{1,17},{9,25},{17,1},{25,9},{2,18},{10... | collective-permute-start | bytes 3080 | tf_op jit(solution)/shard_map/ppermute | solution.py:132
  76.2 3.7 %collective-permute-start.10 = (f32[16,16]{0,1:T(8,128)S(1)}, f32[16,16]{0,1:T(8,128)S(1)}, u32[]{:S(2)}, u32[]{:S(2)}) collective-permute-start(f32[16,16]{0,1:T(8,128)S(1)} %add.78), channel_id=1, source_target_pairs={{0,1},{1,0},{2,3},{3,2},{4,5},{5,4},{6,7},{7,6},{8,9},{9,8},{10,11... | collective-permute-start | bytes 3080 | tf_op jit(solution)/shard_map/ppermute | solution.py:132
  79.9 3.7 %collective-permute-start.11 = (f32[16,16]{0,1:T(8,128)S(1)}, f32[16,16]{0,1:T(8,128)S(1)}, u32[]{:S(2)}, u32[]{:S(2)}) collective-permute-start(f32[16,16]{0,1:T(8,128)S(1)} %add.79), channel_id=1, source_target_pairs={{0,2},{1,3},{2,0},{3,1},{4,6},{5,7},{6,4},{7,5},{8,10},{9,11},{10,... | collective-permute-start | bytes 3080 | tf_op jit(solution)/shard_map/ppermute | solution.py:132
  83.5 4.5 %collective-permute-start.12 = (f32[16,16]{0,1:T(8,128)S(1)}, f32[16,16]{0,1:T(8,128)S(1)}, u32[]{:S(2)}, u32[]{:S(2)}) collective-permute-start(f32[16,16]{0,1:T(8,128)S(1)} %add.80), channel_id=1, source_target_pairs={{0,4},{1,5},{2,6},{3,7},{4,0},{5,1},{6,2},{7,3},{8,12},{9,13},{10,... | collective-permute-start | bytes 3080 | tf_op jit(solution)/shard_map/ppermute | solution.py:132
where the time goes:
time: 96.5 us; the launch traced here: 96 us
  Pallas kernels  24 us (25%)
  starting transfers between devices  22.7 us (24%)
  local copies, waits for them, and re-layouts  16.5 us (17%)
  other arithmetic  14.3 us (15%)
  waiting for transfers between devices  13.5 us (14%)
  matrix products  4.22 us (4%)
    pallas_call x1, Pallas kernels, forecast(): pl.pallas_call(functools.partial(forecast_kernel, steps=steps, rows=rows,...  24 us
    ppermute x5, waiting for transfers between devices, body(): gram = gram + lax.ppermute(gram, axis, pairs)  8.5 us
    ppermute x5, starting transfers between devices, body(): gram = gram + lax.ppermute(gram, axis, pairs)  8.34 us
    ppermute x6, starting transfers between devices, shift(): return lax.ppermute(flat, axes, pairs).reshape(part.shape)  8.33 us
    reshape x6, local copies, waits for them, and re-layouts, shift(): return lax.ppermute(flat, axes, pairs).reshape(part.shape)  6.55 us
    ppermute x2, starting transfers between devices, shift(): return lax.ppermute(part, axes, pairs)  6.01 us
    concatenate x1, other arithmetic, ring_halo(): jnp.concatenate([band(value, east, west), band(below, south_east, south_w...  5.58 us
    ppermute x6, waiting for transfers between devices, shift(): return lax.ppermute(flat, axes, pairs).reshape(part.shape)  5 us
  transfers between devices with their start and end apart: 13, of which 7 were waited for; matrix products, arithmetic and copies ran while one was open for 14% of the time, Pallas kernels for 0%

commit v1 on v0

--- a/solution.py
+++ b/solution.py
@@ -39,26 +39,14 @@
         flat = part.reshape(-1)
         return lax.ppermute(flat, axes, pairs).reshape(part.shape)
 
-    both = ("gx", "gy")
     top, bottom = (value[..., :width, :], value[..., rows - width :, :])
-    left, right = (value[..., :, :width], value[..., :, cols - width :])
     above = shift(bottom, "gy", 0, 1, flatten=False)
     below = shift(top, "gy", 0, -1, flatten=False)
-    west = shift(right, "gx", 1, 0)
-    east = shift(left, "gx", -1, 0)
-    north_west = shift(bottom[..., cols - width :], both, 1, 1)
-    north_east = shift(bottom[..., :width], both, -1, 1)
-    south_west = shift(top[..., cols - width :], both, 1, -1)
-    south_east = shift(top[..., :width], both, -1, -1)
-
-    def band(centre, east_part, west_part):
-        gap = jnp.zeros(centre.shape[:-1] + (lanes - cols - 2 * width,), centre.dtype)
-        return jnp.concatenate([centre, east_part, gap, west_part], axis=-1)
-
-    return jnp.concatenate(
-        [band(value, east, west), band(below, south_east, south_west), band(above, north_east, north_west)],
-        axis=-2,
-    )
+    tall = jnp.concatenate([value, below, above], axis=-2)
+    west = shift(tall[..., cols - width :], "gx", 1, 0)
+    east = shift(tall[..., :width], "gx", -1, 0)
+    gap = jnp.zeros(tall.shape[:-1] + (lanes - cols - 2 * width,), tall.dtype)
+    return jnp.concatenate([tall, east, gap, west], axis=-1)
 
 
 def forecast_kernel(cor_ref, x_ref, o_ref, *, steps, rows, cols):

time: 96.5 us -> 96.4 us (level)
  waiting for transfers between devices: 13.5 us -> 30.7 us
  starting transfers between devices: 22.7 us -> 11.8 us
  local copies, waits for them, and re-layouts: 16.5 us -> 13.4 us
  other arithmetic: 14.3 us -> 11.3 us
    ppermute x2, waiting for transfers between devices: 0.01 us -> 15.6 us  [shift(): return lax.ppermute(part, axes, pairs)]
    ppermute x6 -> x2, starting transfers between devices: 8.33 us -> 1.19 us  [shift(): return lax.ppermute(flat, axes, pairs).reshape(part.shape)]
    ppermute x5, starting transfers between devices: 8.34 us -> 4.57 us  [body(): gram = gram + lax.ppermute(gram, axis, pairs)]
    reshape x6 -> x2, local copies, waits for them, and re-layouts: 6.55 us -> 3.26 us  [shift(): return lax.ppermute(flat, axes, pairs).reshape(part.shape)]
    ppermute x5, waiting for transfers between devices: 8.5 us -> 11.7 us  [body(): gram = gram + lax.ppermute(gram, axis, pairs)]
    concatenate x4 -> x2, other arithmetic: 7.02 us -> 4 us  [the longest x1 3.76 us: ring_halo(): return jnp.concatenate([tall, east, gap, west], axis=-1)]
    ppermute x6 -> x2, waiting for transfers between devices: 5 us -> 3.45 us  [shift(): return lax.ppermute(flat, axes, pairs).reshape(part.shape)]
    slice x0 -> x1, local copies, waits for them, and re-layouts: none -> 1.43 us  [ring_halo(): east = shift(tall[..., :width], 'gx', -1, 0)]
  transfers between devices with their start and end apart: 13 -> 9, of which waited for: 7 -> 9; matrix products, arithmetic and copies ran while one was open for 14% -> 3% of each run, Pallas kernels for 0% -> 0%
where the time goes in v1:
time: 96.4 us; the launch traced here: 96.1 us
  waiting for transfers between devices  30.7 us (32%)
  Pallas kernels  24 us (25%)
  local copies, waits for them, and re-layouts  13.4 us (14%)
  starting transfers between devices  11.8 us (12%)
  other arithmetic  11.3 us (12%)
  matrix products  4.22 us (4%)
    pallas_call x1, Pallas kernels, forecast(): pl.pallas_call(functools.partial(forecast_kernel, steps=steps, rows=rows,...  24 us
    ppermute x2, waiting for transfers between devices, shift(): return lax.ppermute(part, axes, pairs)  15.6 us
    ppermute x5, waiting for transfers between devices, body(): gram = gram + lax.ppermute(gram, axis, pairs)  11.7 us
    ppermute x2, starting transfers between devices, shift(): return lax.ppermute(part, axes, pairs)  6.06 us
    ppermute x5, starting transfers between devices, body(): gram = gram + lax.ppermute(gram, axis, pairs)  4.57 us
    unnamed x7, local copies, waits for them, and re-layouts  3.95 us
    concatenate x1, other arithmetic, ring_halo(): return jnp.concatenate([tall, east, gap, west], axis=-1)  3.76 us
    ppermute x2, waiting for transfers between devices, shift(): return lax.ppermute(flat, axes, pairs).reshape(part.shape)  3.45 us
  transfers between devices with their start and end apart: 9, of which 9 were waited for; matrix products, arithmetic and copies ran while one was open for 3% of the time, Pallas kernels for 0%

profile of v1, /device:TPU:0, one launch (start us, length us, event | category | flops | bytes accessed | tf_op | source)
XLA Modules:
  0.0 96.1 jit_solution(137839329814132484)
XLA Ops:
  0.6 1.6 %broadcast_add_fusion = f32[16,3,32,256]{3,2,1,0:T(8,128)S(1)} fusion(f32[16,3,32,256]{3,2,1,0:T(8,128)} %param.3, f32[3,32,256]{2,1,0:T(8,128)} %param.2), kind=kLoop, calls=%fused_computation.7 | loop fusion | flops 393216 | bytes 3244032 | tf_op jit(solution)/shard_map/add | solution.py:105
  2.3 6.1 %collective-permute-start = (f32[17,3,8,256]{3,2,1,0:T(8,128)S(1)}, f32[17,3,8,256]{3,2,1,0:T(8,128)S(1)}, u32[]{:S(2)}, u32[]{:S(2)}) collective-permute-start(f32[17,3,8,256]{3,2,1,0:T(8,128)S(1)} %get-tuple-element.8), channel_id=1, source_target_pairs={{0,7},{1,0},{2,1},{3,2},{4,3},{5,4},{6,5},{7,6},{8,15},{9,8},{10,9... | collective-permute-start | bytes 1253384 | tf_op jit(solution)/shard_map/ppermute | solution.py:38
  8.5 15.5 %collective-permute-done = f32[17,3,8,256]{3,2,1,0:T(8,128)S(1)} collective-permute-done((f32[17,3,8,256]{3,2,1,0:T(8,128)S(1)}, f32[17,3,8,256]{3,2,1,0:T(8,128)S(1)}, u32[]{:S(2)}, u32[]{:S(2)}) %collective-permute-start) | collective-permute-done | bytes 417824 | tf_op jit(solution)/shard_map/ppermute | solution.py:38
  24.1 0.7 copy-done
  25.1 1.4 %fusion.15 = (f32[17,3,48,8]{3,2,1,0:T(8,128)}, f32[17,3,48,8]{3,2,1,0:T(8,128)S(1)}) fusion(f32[17,3,48,256]{3,2,1,0:T(8,128)S(1)} %pad_maximum_fusion.1), kind=kLoop, calls=%fused_computation.33 | loop fusion | bytes 313344 | tf_op jit(solution)/shard_map/slice | solution.py:47
  26.5 1.8 %reshape.59 = f32[19584]{0:T(1024)S(1)} reshape(f32[17,3,48,8]{3,2,1,0:T(8,128)} %get-tuple-element.6) | data formatting | bytes 156672 | tf_op jit(solution)/shard_map/reshape | solution.py:39
  28.3 1.2 %collective-permute-start.2 = (f32[19584]{0:T(1024)S(1)}, f32[19584]{0:T(1024)S(1)}, u32[]{:S(2)}, u32[]{:S(2)}) collective-permute-start(f32[19584]{0:T(1024)S(1)} %reshape.59), channel_id=1, source_target_pairs={{0,24},{8,0},{16,8},{24,16},{1,25},{9,1},{17,9},{25,17},{2,26},{10... | collective-permute-start | bytes 235016 | tf_op jit(solution)/shard_map/ppermute | solution.py:40
  29.5 1.2 %reshape.61 = f32[19584]{0:T(1024)} reshape(f32[17,3,48,8]{3,2,1,0:T(8,128)S(1)} %get-tuple-element.7) | data formatting | bytes 156672 | tf_op jit(solution)/shard_map/reshape | solution.py:39
  30.8 0.8 collective-permute-done.2
  31.6 0.7 reshape.60
  32.3 2.6 %collective-permute-done.3 = f32[19584]{0:T(1024)} collective-permute-done((f32[19584]{0:T(1024)}, f32[19584]{0:T(1024)}, u32[]{:S(2)}, u32[]{:S(2)}) %collective-permute-start.3) | collective-permute-done | bytes 78368 | tf_op jit(solution)/shard_map/ppermute | solution.py:40
  34.9 2.6 %reshape.62 = f32[17,3,48,8]{3,2,1,0:T(8,128)} reshape(f32[19584]{0:T(1024)} %collective-permute-done.3) | data formatting | bytes 156672 | tf_op jit(solution)/shard_map/reshape | solution.py:40
  37.5 3.8 %pad_maximum_fusion.x_ref = f32[17,3,48,384]{3,2,1,0:T(8,128)} fusion(f32[17,3,48,8]{3,2,1,0:T(8,128)} %reshape.62, f32[17,3,48,8]{3,2,1,0:T(8,128)S(1)} %reshape.60, f32[17,3,8,256]{3,2,1,0:T(8,128)} %copy-done, f32[17,3,8,256]{3,2,1,0:T(8,128)S(1)} %collective-permute-done, f32[16,3,32,256]{3,2,1,0:T(8,128)S(1)} %broadcast_add_fusion, ...), kind=kLoop, calls=%fused_computation.1 | loop fusion | flops 5640192 | bytes 6425088 | tf_op jit(solution)/shard_map/concatenate | solution.py:49
  41.2 0.7 broadcast_in_dim.7.cor_ref
  41.9 24.0 %shard_map.41 = f32[17,3,32,256]{3,2,1,0:T(8,128)} custom-call(f32[48,384]{1,0:T(8,128)} %broadcast_in_dim.7.cor_ref, f32[17,3,48,384]{3,2,1,0:T(8,128)} %pad_maximum_fusion.x_ref), custom_call_target="tpu_custom_call" | custom-call | tf_op jit(solution)/shard_map/pallas_call | solution.py:81
  65.9 0.9 slice_bitcast_fusion
  66.8 1.5 %slice_subtract_fusion = f32[16,3,32,256]{3,2,1,0:T(8,128)S(1)} fusion(f32[17,3,32,256]{3,2,1,0:T(8,128)} %shard_map.41, f32[3,32,256]{2,1,0:T(8,128)S(1)} %slice_bitcast_fusion), kind=kLoop, calls=%fused_computation.3 | loop fusion | flops 393216 | bytes 3244032 | tf_op jit(solution)/shard_map/sub | solution.py:108
  68.3 2.7 %fusion.2 = f32[16,16]{0,1:T(8,128)S(1)} fusion(f32[16,3,32,256]{3,2,1,0:T(8,128)S(1)} %slice_subtract_fusion), kind=kOutput, calls=%fused_computation.6 | convolution fusion | flops 75497472 | bytes 1573888 | tf_op jit(solution)/shard_map/dot_general | solution.py:110
  71.0 1.2 %collective-permute-done.4 = f32[16,16]{0,1:T(8,128)S(1)} collective-permute-done((f32[16,16]{0,1:T(8,128)S(1)}, f32[16,16]{0,1:T(8,128)S(1)}, u32[]{:S(2)}, u32[]{:S(2)}) %collective-permute-start.4) | collective-permute-done | bytes 1056 | tf_op jit(solution)/shard_map/ppermute | solution.py:120
  72.7 3.1 %collective-permute-done.5 = f32[16,16]{0,1:T(8,128)S(1)} collective-permute-done((f32[16,16]{0,1:T(8,128)S(1)}, f32[16,16]{0,1:T(8,128)S(1)}, u32[]{:S(2)}, u32[]{:S(2)}) %collective-permute-start.5) | collective-permute-done | bytes 1056 | tf_op jit(solution)/shard_map/ppermute | solution.py:120
  75.9 2.5 %collective-permute-start.6 = (f32[16,16]{0,1:T(8,128)S(1)}, f32[16,16]{0,1:T(8,128)S(1)}, u32[]{:S(2)}, u32[]{:S(2)}) collective-permute-start(f32[16,16]{0,1:T(8,128)S(1)} %add.78), channel_id=1, source_target_pairs={{0,1},{1,0},{2,3},{3,2},{4,5},{5,4},{6,7},{7,6},{8,9},{9,8},{10,11... | collective-permute-start | bytes 3080 | tf_op jit(solution)/shard_map/ppermute | solution.py:120
  78.4 1.6 %collective-permute-done.6 = f32[16,16]{0,1:T(8,128)S(1)} collective-permute-done((f32[16,16]{0,1:T(8,128)S(1)}, f32[16,16]{0,1:T(8,128)S(1)}, u32[]{:S(2)}, u32[]{:S(2)}) %collective-permute-start.6) | collective-permute-done | bytes 1056 | tf_op jit(solution)/shard_map/ppermute | solution.py:120
  80.3 3.4 %collective-permute-done.7 = f32[16,16]{0,1:T(8,128)S(1)} collective-permute-done((f32[16,16]{0,1:T(8,128)S(1)}, f32[16,16]{0,1:T(8,128)S(1)}, u32[]{:S(2)}, u32[]{:S(2)}) %collective-permute-start.7) | collective-permute-done | bytes 1056 | tf_op jit(solution)/shard_map/ppermute | solution.py:120
  83.7 1.3 %collective-permute-start.8 = (f32[16,16]{0,1:T(8,128)S(1)}, f32[16,16]{0,1:T(8,128)S(1)}, u32[]{:S(2)}, u32[]{:S(2)}) collective-permute-start(f32[16,16]{0,1:T(8,128)S(1)} %add.80), channel_id=1, source_target_pairs={{0,4},{1,5},{2,6},{3,7},{4,0},{5,1},{6,2},{7,3},{8,12},{9,13},{10,... | collective-permute-start | bytes 3080 | tf_op jit(solution)/shard_map/ppermute | solution.py:120
  85.0 0.9 copy.19
  85.9 2.3 %collective-permute-done.8 = f32[16,16]{0,1:T(8,128)S(1)} collective-permute-done((f32[16,16]{0,1:T(8,128)S(1)}, f32[16,16]{0,1:T(8,128)S(1)}, u32[]{:S(2)}, u32[]{:S(2)}) %collective-permute-start.8) | collective-permute-done | bytes 1056 | tf_op jit(solution)/shard_map/ppermute | solution.py:120
  88.3 1.5 %cholesky.16 = f32[16,16]{1,0:T(8,128)S(1)} custom-call(f32[16,16]{1,0:T(8,128)S(1)} %fusion.6), custom_call_target="Cholesky" | custom-call | tf_op jit(solution)/shard_map/jit(cholesky)/cholesky | solution.py:122
  90.4 0.7 multiply_bitcast_fusion
  91.1 1.2 %custom-call.7 = f32[1,16,16]{1,2,0:T(8,128)S(1)} custom-call(f32[1,16,16]{2,1,0:T(8,128)S(1)} %get-tuple-element.11), custom_call_target="InvertDiagBlocksLowerTriangular" | custom-call | tf_op jit(solution)/shard_map/jit(_solve_triangular)/triangular_solve | solution.py:123
  92.3 1.5 %convolution_multiply_fusion = f32[16,24576]{1,0:T(8,128)S(1)} fusion(f32[16,24576]{1,0:T(8,128)S(1)} %bitcast.30, f32[1,16,16]{1,2,0:T(8,128)S(1)} %custom-call.7), kind=kOutput, calls=%fused_computation | convolution fusion | flops 75890688 | bytes 3146752 | tf_op jit(solution)/shard_map/jit(_solve_triangular)/triangular_solve | solution.py:123
  93.8 1.6 %copy.20 = f32[2,8,96,256]{3,2,1,0:T(8,128)} copy(f32[2,8,96,256]{3,1,2,0:T(8,128)S(1)} %bitcast.31) | data formatting | bytes 3145728
  95.4 0.7 copy.15
  (23 shorter events, 2.2 us)
Async XLA Ops:
  0.6 1.6 %copy-start.1 = (f32[3,32,256]{2,1,0:T(8,128)S(1)}, f32[3,32,256]{2,1,0:T(8,128)}, u32[]{:S(2)}) copy-start(f32[3,32,256]{2,1,0:T(8,128)} %param.2) | copy-start | bytes 294916
  2.3 21.6 %collective-permute-start = (f32[17,3,8,256]{3,2,1,0:T(8,128)S(1)}, f32[17,3,8,256]{3,2,1,0:T(8,128)S(1)}, u32[]{:S(2)}, u32[]{:S(2)}) collective-permute-start(f32[17,3,8,256]{3,2,1,0:T(8,128)S(1)} %get-tuple-element.8), channel_id=1, source_target_pairs={{0,7},{1,0},{2,1},{3,2},{4,3},{5,4},{6,5},{7,6},{8,15},{9,8},{10,9... | collective-permute-start | bytes 1253384 | tf_op jit(solution)/shard_map/ppermute | solution.py:38
  8.4 15.7 %collective-permute-start.1 = (f32[17,3,8,256]{3,2,1,0:T(8,128)S(1)}, f32[17,3,8,256]{3,2,1,0:T(8,128)S(1)}, u32[]{:S(2)}, u32[]{:S(2)}) collective-permute-start(f32[17,3,8,256]{3,2,1,0:T(8,128)S(1)} %get-tuple-element.9), channel_id=1, source_target_pairs={{0,1},{1,2},{2,3},{3,4},{4,5},{5,6},{6,7},{7,0},{8,9},{9,10},{10,1... | collective-permute-start | bytes 1253384 | tf_op jit(solution)/shard_map/ppermute | solution.py:38
  24.1 0.8 copy-start
  28.3 3.2 %collective-permute-start.2 = (f32[19584]{0:T(1024)S(1)}, f32[19584]{0:T(1024)S(1)}, u32[]{:S(2)}, u32[]{:S(2)}) collective-permute-start(f32[19584]{0:T(1024)S(1)} %reshape.59), channel_id=1, source_target_pairs={{0,24},{8,0},{16,8},{24,16},{1,25},{9,1},{17,9},{25,17},{2,26},{10... | collective-permute-start | bytes 235016 | tf_op jit(solution)/shard_map/ppermute | solution.py:40
  30.7 4.2 %collective-permute-start.3 = (f32[19584]{0:T(1024)}, f32[19584]{0:T(1024)}, u32[]{:S(2)}, u32[]{:S(2)}) collective-permute-start(f32[19584]{0:T(1024)} %reshape.61), channel_id=1, source_target_pairs={{0,8},{8,16},{16,24},{24,0},{1,9},{9,17},{17,25},{25,1},{2,10},{10... | collective-permute-start | bytes 235016 | tf_op jit(solution)/shard_map/ppermute | solution.py:40
  71.0 1.2 %collective-permute-start.4 = (f32[16,16]{0,1:T(8,128)S(1)}, f32[16,16]{0,1:T(8,128)S(1)}, u32[]{:S(2)}, u32[]{:S(2)}) collective-permute-start(f32[16,16]{0,1:T(8,128)S(1)} %fusion.2), channel_id=1, source_target_pairs={{0,8},{8,0},{16,24},{24,16},{1,9},{9,1},{17,25},{25,17},{2,10},{10... | collective-permute-start | bytes 3080 | tf_op jit(solution)/shard_map/ppermute | solution.py:120
  72.2 3.7 %collective-permute-start.5 = (f32[16,16]{0,1:T(8,128)S(1)}, f32[16,16]{0,1:T(8,128)S(1)}, u32[]{:S(2)}, u32[]{:S(2)}) collective-permute-start(f32[16,16]{0,1:T(8,128)S(1)} %add.77), channel_id=1, source_target_pairs={{0,16},{8,24},{16,0},{24,8},{1,17},{9,25},{17,1},{25,9},{2,18},{10... | collective-permute-start | bytes 3080 | tf_op jit(solution)/shard_map/ppermute | solution.py:120
  75.9 4.1 %collective-permute-start.6 = (f32[16,16]{0,1:T(8,128)S(1)}, f32[16,16]{0,1:T(8,128)S(1)}, u32[]{:S(2)}, u32[]{:S(2)}) collective-permute-start(f32[16,16]{0,1:T(8,128)S(1)} %add.78), channel_id=1, source_target_pairs={{0,1},{1,0},{2,3},{3,2},{4,5},{5,4},{6,7},{7,6},{8,9},{9,8},{10,11... | collective-permute-start | bytes 3080 | tf_op jit(solution)/shard_map/ppermute | solution.py:120
  80.0 3.7 %collective-permute-start.7 = (f32[16,16]{0,1:T(8,128)S(1)}, f32[16,16]{0,1:T(8,128)S(1)}, u32[]{:S(2)}, u32[]{:S(2)}) collective-permute-start(f32[16,16]{0,1:T(8,128)S(1)} %add.79), channel_id=1, source_target_pairs={{0,2},{1,3},{2,0},{3,1},{4,6},{5,7},{6,4},{7,5},{8,10},{9,11},{10,... | collective-permute-start | bytes 3080 | tf_op jit(solution)/shard_map/ppermute | solution.py:120
  83.7 4.5 %collective-permute-start.8 = (f32[16,16]{0,1:T(8,128)S(1)}, f32[16,16]{0,1:T(8,128)S(1)}, u32[]{:S(2)}, u32[]{:S(2)}) collective-permute-start(f32[16,16]{0,1:T(8,128)S(1)} %add.80), channel_id=1, source_target_pairs={{0,4},{1,5},{2,6},{3,7},{4,0},{5,1},{6,2},{7,3},{8,12},{9,13},{10,... | collective-permute-start | bytes 3080 | tf_op jit(solution)/shard_map/ppermute | solution.py:120

commit v2 on v1

--- a/solution.py
+++ b/solution.py
@@ -19,29 +19,30 @@
 two_pi = 2.0 * math.pi
 
 
-def ring_halo(value, width, lanes):
-    rows, cols = (value.shape[-2], value.shape[-1])
+def shift(part, axes, dx, dy, flatten=True):
     across, down = (lax.axis_size("gx"), lax.axis_size("gy"))
+    pairs = []
+    for x in range(across):
+        for y in range(down):
+            target = ((x + dx) % across, (y + dy) % down)
+            if axes == "gx":
+                pairs.append((x, target[0])) if y == 0 else None
+            else:
+                pairs.append((y, target[1])) if x == 0 else None
+    if not flatten:
+        return lax.ppermute(part, axes, pairs)
+    flat = part.reshape(-1)
+    return lax.ppermute(flat, axes, pairs).reshape(part.shape)
 
-    def shift(part, axes, dx, dy, flatten=True):
-        pairs = []
-        for x in range(across):
-            for y in range(down):
-                target = ((x + dx) % across, (y + dy) % down)
-                if axes == "gx":
-                    pairs.append((x, target[0])) if y == 0 else None
-                elif axes == "gy":
-                    pairs.append((y, target[1])) if x == 0 else None
-                else:
-                    pairs.append((x * down + y, target[0] * down + target[1]))
-        if not flatten:
-            return lax.ppermute(part, axes, pairs)
-        flat = part.reshape(-1)
-        return lax.ppermute(flat, axes, pairs).reshape(part.shape)
 
+def row_halo(value, width):
+    rows = value.shape[-2]
     top, bottom = (value[..., :width, :], value[..., rows - width :, :])
-    above = shift(bottom, "gy", 0, 1, flatten=False)
-    below = shift(top, "gy", 0, -1, flatten=False)
+    return (shift(bottom, "gy", 0, 1, flatten=False), shift(top, "gy", 0, -1, flatten=False))
+
+
+def ring_halo(value, above, below, width, lanes):
+    cols = value.shape[-1]
     tall = jnp.concatenate([value, below, above], axis=-2)
     west = shift(tall[..., cols - width :], "gx", 1, 0)
     east = shift(tall[..., :width], "gx", -1, 0)
@@ -85,6 +86,9 @@
         in_specs=[pl.BlockSpec((R, C), lambda i: (0, 0)),
                   pl.BlockSpec((1, F, R, C), lambda i: (i, 0, 0, 0))],
         out_specs=pl.BlockSpec((1, F, rows, cols), lambda i: (i, 0, 0, 0)),
+        cost_estimate=pl.CostEstimate(
+            flops=S * F * R * C * 300 * steps, transcendentals=0, bytes_accessed=4 * S * F * (R * C + rows * cols)
+        ),
     )(cor, padded)
 
 
@@ -103,8 +107,16 @@
     coriolis = jnp.broadcast_to(coriolis[:, None], (ring_rows, lanes))
 
     states = jnp.concatenate([control[None], control[None] + perts], 0)
-    padded = ring_halo(states, margin, lanes)
-    current = forecast(coriolis, padded, STEPS, tile_rows, tile_column_count)
+    split = (states.shape[0] + 1) // 2
+    first_part, second_part = (states[:split], states[split:])
+    above, below = row_halo(first_part, margin)
+    above, below, second_part = lax.optimization_barrier((above, below, second_part))
+    later_above, later_below = row_halo(second_part, margin)
+    outputs = []
+    for part, up, down_ in ((first_part, above, below), (second_part, later_above, later_below)):
+        padded = ring_halo(part, up, down_, margin, lanes)
+        outputs.append(forecast(coriolis, padded, STEPS, tile_rows, tile_column_count))
+    current = jnp.concatenate(outputs, 0)
     bred = current[1:] - current[0:1]
     flat = bred.reshape(MEMBERS, -1)
     local_gram = jnp.dot(flat, flat.T, precision=lax.Precision.HIGHEST)

time: 96.4 us -> 97.1 us (level)
  starting transfers between devices: 11.8 us -> 16.5 us
  waiting for transfers between devices: 30.7 us -> 26.1 us
  local copies, waits for them, and re-layouts: 13.4 us -> 10.2 us
  other arithmetic: 11.3 us -> 13.3 us
  Pallas kernels: 24 us -> 25.6 us
    ppermute x2 -> x4, waiting for transfers between devices: 15.6 us -> 9.59 us  [shift(): return lax.ppermute(part, axes, pairs)]
    ppermute x2 -> x4, starting transfers between devices: 6.06 us -> 10.8 us  [shift(): return lax.ppermute(part, axes, pairs)]
    ppermute x5, waiting for transfers between devices: 11.7 us -> 14.9 us  [body(): gram = gram + lax.ppermute(gram, axis, pairs)]
    ppermute x5, starting transfers between devices: 4.57 us -> 2.17 us  [body(): gram = gram + lax.ppermute(gram, axis, pairs)]
    ppermute x2 -> x4, starting transfers between devices: 1.19 us -> 3.58 us  [shift(): return lax.ppermute(flat, axes, pairs).reshape(part.shape)]
    ppermute x2 -> x4, waiting for transfers between devices: 3.45 us -> 1.63 us  [shift(): return lax.ppermute(flat, axes, pairs).reshape(part.shape)]
    pallas_call x1 -> x2, Pallas kernels: 24 us -> 25.6 us  [forecast(): pl.pallas_call(functools.partial(forecast_kernel, steps=steps, rows=rows,...]
    reshape x2 -> x4, local copies, waits for them, and re-layouts: 2.97 us -> 1.78 us  [shift(): flat = part.reshape(-1)]
  transfers between devices with their start and end apart: 9 -> 13, of which waited for: 9 -> 8; matrix products, arithmetic and copies ran while one was open for 3% -> 8% of each run, Pallas kernels for 0% -> 14%
where the time goes in v2:
time: 97.1 us; the launch traced here: 96.8 us
  waiting for transfers between devices  26.1 us (27%)
  Pallas kernels  25.6 us (26%)
  starting transfers between devices  16.5 us (17%)
  other arithmetic  13.3 us (14%)
  local copies, waits for them, and re-layouts  10.2 us (11%)
  matrix products  4.21 us (4%)
    pallas_call x2, Pallas kernels, forecast(): pl.pallas_call(functools.partial(forecast_kernel, steps=steps, rows=rows,...  25.6 us
    ppermute x5, waiting for transfers between devices, body(): gram = gram + lax.ppermute(gram, axis, pairs)  14.9 us
    ppermute x4, starting transfers between devices, shift(): return lax.ppermute(part, axes, pairs)  10.8 us
    ppermute x4, waiting for transfers between devices, shift(): return lax.ppermute(part, axes, pairs)  9.59 us
    concatenate x2, other arithmetic, ring_halo(): return jnp.concatenate([tall, east, gap, west], axis=-1)  4.34 us
    ppermute x4, starting transfers between devices, shift(): return lax.ppermute(flat, axes, pairs).reshape(part.shape)  3.58 us
    unnamed x9, local copies, waits for them, and re-layouts  3.28 us
    reshape x4, local copies, waits for them, and re-layouts, shift(): return lax.ppermute(flat, axes, pairs).reshape(part.shape)  3.01 us
  transfers between devices with their start and end apart: 13, of which 8 were waited for; matrix products, arithmetic and copies ran while one was open for 8% of the time, Pallas kernels for 14%

profile of v2, /device:TPU:0, one launch (start us, length us, event | category | flops | bytes accessed | tf_op | source)
XLA Modules:
  0.0 96.8 jit_solution(9250116077417052391)
XLA Ops:
  0.6 1.6 %broadcast_add_fusion = f32[16,3,32,256]{3,2,1,0:T(8,128)S(1)} fusion(f32[16,3,32,256]{3,2,1,0:T(8,128)} %param.3, f32[3,32,256]{2,1,0:T(8,128)} %param.2), kind=kLoop, calls=%fused_computation.14 | loop fusion | flops 393216 | bytes 3244032 | tf_op jit(solution)/shard_map/add | solution.py:109
  2.2 0.8 pad_maximum_fusion.4
  3.0 6.0 %collective-permute-start.1 = (f32[9,3,8,256]{3,2,1,0:T(8,128)}, f32[9,3,8,256]{3,2,1,0:T(8,128)}, u32[]{:S(2)}, u32[]{:S(2)}) collective-permute-start(f32[9,3,8,256]{3,2,1,0:T(8,128)} %get-tuple-element.12), channel_id=1, source_target_pairs={{0,7},{1,0},{2,1},{3,2},{4,3},{5,4},{6,5},{7,6},{8,15},{9,8},{10,9... | collective-permute-start | bytes 663560 | tf_op jit(solution)/shard_map/ppermute | solution.py:33
  9.4 4.7 %collective-permute-done.1 = f32[9,3,8,256]{3,2,1,0:T(8,128)} collective-permute-done((f32[9,3,8,256]{3,2,1,0:T(8,128)}, f32[9,3,8,256]{3,2,1,0:T(8,128)}, u32[]{:S(2)}, u32[]{:S(2)}) %collective-permute-start.1) | collective-permute-done | bytes 221216 | tf_op jit(solution)/shard_map/ppermute | solution.py:33
  14.1 4.9 %collective-permute-done = f32[9,3,8,256]{3,2,1,0:T(8,128)} collective-permute-done((f32[9,3,8,256]{3,2,1,0:T(8,128)}, f32[9,3,8,256]{3,2,1,0:T(8,128)}, u32[]{:S(2)}, u32[]{:S(2)}) %collective-permute-start) | collective-permute-done | bytes 221216 | tf_op jit(solution)/shard_map/ppermute | solution.py:33
  18.9 0.7 fusion.20
  19.7 1.2 %pad_maximum_fusion.3 = f32[9,3,48,256]{3,2,1,0:T(8,128)S(1)} fusion(f32[9,3,8,256]{3,2,1,0:T(8,128)} %collective-permute-done, f32[9,3,8,256]{3,2,1,0:T(8,128)} %collective-permute-done.1, f32[9,3,32,256]{3,2,1,0:T(8,128)S(1)} %fusion.6), kind=kLoop, calls=%fused_computation.11 | loop fusion | flops 663552 | bytes 2654208 | tf_op jit(solution)/shard_map/concatenate | solution.py:46
  21.1 0.9 reshape.71
  22.4 1.7 %collective-permute-start.2 = (f32[10368]{0:T(1024)}, f32[10368]{0:T(1024)}, u32[]{:S(2)}, u32[]{:S(2)}) collective-permute-start(f32[10368]{0:T(1024)} %reshape.71), channel_id=1, source_target_pairs={{0,24},{8,0},{16,8},{24,16},{1,25},{9,1},{17,9},{25,17},{2,26},{10... | collective-permute-start | bytes 124424 | tf_op jit(solution)/shard_map/ppermute | solution.py:35
  24.4 4.5 %collective-permute-start.4 = (f32[8,3,8,256]{3,2,1,0:T(8,128)}, f32[8,3,8,256]{3,2,1,0:T(8,128)S(1)}, u32[]{:S(2)}, u32[]{:S(2)}) collective-permute-start(f32[8,3,8,256]{3,2,1,0:T(8,128)} %get-tuple-element.19), channel_id=1, source_target_pairs={{0,7},{1,0},{2,1},{3,2},{4,3},{5,4},{6,5},{7,6},{8,15},{9,8},{10,9... | collective-permute-start | bytes 589832 | tf_op jit(solution)/shard_map/ppermute | solution.py:33
  29.0 1.2 %reshape.72 = f32[9,3,48,8]{3,2,1,0:T(8,128)S(1)} reshape(f32[10368]{0:T(1024)} %collective-permute-done.2) | data formatting | bytes 82944 | tf_op jit(solution)/shard_map/reshape | solution.py:35
  30.1 1.2 %reshape.74 = f32[9,3,48,8]{3,2,1,0:T(8,128)} reshape(f32[10368]{0:T(1024)S(1)} %collective-permute-done.3) | data formatting | bytes 82944 | tf_op jit(solution)/shard_map/reshape | solution.py:35
  31.4 2.8 %pad_maximum_fusion.x_ref = f32[9,3,48,384]{3,2,1,0:T(8,128)} fusion(f32[9,3,48,8]{3,2,1,0:T(8,128)} %reshape.74, f32[9,3,48,8]{3,2,1,0:T(8,128)S(1)} %reshape.72, f32[9,3,8,256]{3,2,1,0:T(8,128)} %collective-permute-done, f32[9,3,8,256]{3,2,1,0:T(8,128)} %collective-permute-done.1, f32[9,3,32,256]{3,2,1,0:T(8,128)S(1)} %fusion.6, f32[384]{0:T(512)S(1)} %pad.10.clone), kind=kLoop, calls=%fused_computation.3 | loop fusion | flops 2488320 | bytes 3402240 | tf_op jit(solution)/shard_map/concatenate | solution.py:50
  34.2 0.7 broadcast_in_dim.18.cor_ref
  34.9 13.4 %shard_map.41 = f32[9,3,32,256]{3,2,1,0:T(8,128)} custom-call(f32[48,384]{1,0:T(8,128)} %broadcast_in_dim.18.cor_ref, f32[9,3,48,384]{3,2,1,0:T(8,128)} %pad_maximum_fusion.x_ref), custom_call_target="tpu_custom_call" | custom-call | flops 298598400 | bytes 2875392 | tf_op jit(solution)/shard_map/pallas_call | solution.py:82
  49.3 1.7 %collective-permute-start.6 = (f32[9216]{0:T(1024)S(1)}, f32[9216]{0:T(1024)S(1)}, u32[]{:S(2)}, u32[]{:S(2)}) collective-permute-start(f32[9216]{0:T(1024)S(1)} %reshape.75), channel_id=1, source_target_pairs={{0,24},{8,0},{16,8},{24,16},{1,25},{9,1},{17,9},{25,17},{2,26},{10... | collective-permute-start | bytes 110600 | tf_op jit(solution)/shard_map/ppermute | solution.py:35
  51.0 1.6 %collective-permute-done.6 = f32[9216]{0:T(1024)S(1)} collective-permute-done((f32[9216]{0:T(1024)S(1)}, f32[9216]{0:T(1024)S(1)}, u32[]{:S(2)}, u32[]{:S(2)}) %collective-permute-start.6) | collective-permute-done | bytes 36896 | tf_op jit(solution)/shard_map/ppermute | solution.py:35
  53.3 1.5 %pad_maximum_fusion.1.x_ref = f32[8,3,48,384]{3,2,1,0:T(8,128)} fusion(f32[8,3,48,8]{3,2,1,0:T(8,128)S(1)} %reshape.78, f32[8,3,48,8]{3,2,1,0:T(8,128)S(1)} %reshape.76, f32[8,3,48,256]{3,2,1,0:T(8,128)S(1)} %constant_dynamic-update-slice_fusion, f32[384]{0:T(512)S(1)} %pad.10.clone), kind=kLoop, calls=%fused_computation.4 | loop fusion | flops 1327104 | bytes 3024384 | tf_op jit(solution)/shard_map/concatenate | solution.py:50
  54.8 12.1 %shard_map.42 = f32[8,3,32,256]{3,2,1,0:T(8,128)} custom-call(f32[48,384]{1,0:T(8,128)} %broadcast_in_dim.18.cor_ref, f32[8,3,48,384]{3,2,1,0:T(8,128)} %pad_maximum_fusion.1.x_ref), custom_call_target="tpu_custom_call" | custom-call | flops 265420800 | bytes 2555904 | tf_op jit(solution)/shard_map/pallas_call | solution.py:82
  66.9 1.3 %fusion = f32[16,3,32,256]{3,2,1,0:T(8,128)S(1)} fusion(f32[8,3,32,256]{3,2,1,0:T(8,128)} %shard_map.42, f32[9,3,32,256]{3,2,1,0:T(8,128)S(1)} %copy-done, f32[3,32,256]{2,1,0:T(8,128)S(1)} %slice_bitcast_fusion), kind=kLoop, calls=%fused_computation.8 | loop fusion | flops 786432 | bytes 3342336 | tf_op jit(solution)/shard_map/sub | solution.py:120
  68.2 2.7 %fusion.3 = f32[16,16]{0,1:T(8,128)S(1)} fusion(f32[16,3,32,256]{3,2,1,0:T(8,128)S(1)} %fusion), kind=kOutput, calls=%fused_computation.12 | convolution fusion | flops 75497472 | bytes 1573888 | tf_op jit(solution)/shard_map/dot_general | solution.py:122
  70.9 1.7 %collective-permute-start.8 = (f32[16,16]{0,1:T(8,128)S(1)}, f32[16,16]{0,1:T(8,128)S(1)}, u32[]{:S(2)}, u32[]{:S(2)}) collective-permute-start(f32[16,16]{0,1:T(8,128)S(1)} %fusion.3), channel_id=1, source_target_pairs={{0,8},{8,0},{16,24},{24,16},{1,9},{9,1},{17,25},{25,17},{2,10},{10... | collective-permute-start | bytes 3080 | tf_op jit(solution)/shard_map/ppermute | solution.py:132
  72.6 0.8 collective-permute-done.8
  73.9 3.1 %collective-permute-done.9 = f32[16,16]{0,1:T(8,128)S(1)} collective-permute-done((f32[16,16]{0,1:T(8,128)S(1)}, f32[16,16]{0,1:T(8,128)S(1)}, u32[]{:S(2)}, u32[]{:S(2)}) %collective-permute-start.9) | collective-permute-done | bytes 1056 | tf_op jit(solution)/shard_map/ppermute | solution.py:132
  77.0 3.6 %collective-permute-done.10 = f32[16,16]{0,1:T(8,128)S(1)} collective-permute-done((f32[16,16]{0,1:T(8,128)S(1)}, f32[16,16]{0,1:T(8,128)S(1)}, u32[]{:S(2)}, u32[]{:S(2)}) %collective-permute-start.10) | collective-permute-done | bytes 1056 | tf_op jit(solution)/shard_map/ppermute | solution.py:132
  80.7 3.6 %collective-permute-done.11 = f32[16,16]{0,1:T(8,128)S(1)} collective-permute-done((f32[16,16]{0,1:T(8,128)S(1)}, f32[16,16]{0,1:T(8,128)S(1)}, u32[]{:S(2)}, u32[]{:S(2)}) %collective-permute-start.11) | collective-permute-done | bytes 1056 | tf_op jit(solution)/shard_map/ppermute | solution.py:132
  84.4 0.9 copy.19
  85.3 3.6 %collective-permute-done.12 = f32[16,16]{0,1:T(8,128)S(1)} collective-permute-done((f32[16,16]{0,1:T(8,128)S(1)}, f32[16,16]{0,1:T(8,128)S(1)}, u32[]{:S(2)}, u32[]{:S(2)}) %collective-permute-start.12) | collective-permute-done | bytes 1056 | tf_op jit(solution)/shard_map/ppermute | solution.py:132
  89.0 1.5 %cholesky.16 = f32[16,16]{1,0:T(8,128)S(1)} custom-call(f32[16,16]{1,0:T(8,128)S(1)} %fusion.9), custom_call_target="Cholesky" | custom-call | tf_op jit(solution)/shard_map/jit(cholesky)/cholesky | solution.py:134
  92.5 1.2 %custom-call.7 = f32[1,16,16]{1,2,0:T(8,128)S(1)} custom-call(f32[1,16,16]{2,1,0:T(8,128)S(1)} %get-tuple-element.21), custom_call_target="InvertDiagBlocksLowerTriangular" | custom-call | tf_op jit(solution)/shard_map/jit(_solve_triangular)/triangular_solve | solution.py:135
  93.7 1.5 %convolution_multiply_fusion = f32[16,24576]{1,0:T(8,128)S(1)} fusion(f32[16,24576]{1,0:T(8,128)S(1)} %bitcast.34, f32[1,16,16]{1,2,0:T(8,128)S(1)} %custom-call.7), kind=kOutput, calls=%fused_computation | convolution fusion | flops 75890688 | bytes 3146752 | tf_op jit(solution)/shard_map/jit(_solve_triangular)/triangular_solve | solution.py:135
  95.2 1.6 %copy.20 = f32[2,8,96,256]{3,2,1,0:T(8,128)} copy(f32[2,8,96,256]{3,1,2,0:T(8,128)S(1)} %bitcast.35) | data formatting | bytes 3145728
  (44 shorter events, 5.3 us)
Async XLA Ops:
  0.6 1.6 %copy-start.1 = (f32[3,32,256]{2,1,0:T(8,128)S(1)}, f32[3,32,256]{2,1,0:T(8,128)}, u32[]{:S(2)}) copy-start(f32[3,32,256]{2,1,0:T(8,128)} %param.2) | copy-start | bytes 294916
  3.0 11.0 %collective-permute-start.1 = (f32[9,3,8,256]{3,2,1,0:T(8,128)}, f32[9,3,8,256]{3,2,1,0:T(8,128)}, u32[]{:S(2)}, u32[]{:S(2)}) collective-permute-start(f32[9,3,8,256]{3,2,1,0:T(8,128)} %get-tuple-element.12), channel_id=1, source_target_pairs={{0,7},{1,0},{2,1},{3,2},{4,3},{5,4},{6,5},{7,6},{8,15},{9,8},{10,9... | collective-permute-start | bytes 663560 | tf_op jit(solution)/shard_map/ppermute | solution.py:33
  9.0 9.9 %collective-permute-start = (f32[9,3,8,256]{3,2,1,0:T(8,128)}, f32[9,3,8,256]{3,2,1,0:T(8,128)}, u32[]{:S(2)}, u32[]{:S(2)}) collective-permute-start(f32[9,3,8,256]{3,2,1,0:T(8,128)} %get-tuple-element.13), channel_id=1, source_target_pairs={{0,1},{1,2},{2,3},{3,4},{4,5},{5,6},{6,7},{7,0},{8,9},{9,10},{10,1... | collective-permute-start | bytes 663560 | tf_op jit(solution)/shard_map/ppermute | solution.py:33
  22.3 7.8 %collective-permute-start.3 = (f32[10368]{0:T(1024)S(1)}, f32[10368]{0:T(1024)S(1)}, u32[]{:S(2)}, u32[]{:S(2)}) collective-permute-start(f32[10368]{0:T(1024)S(1)} %reshape.73), channel_id=1, source_target_pairs={{0,8},{8,16},{16,24},{24,0},{1,9},{9,17},{17,25},{25,1},{2,10},{10... | collective-permute-start | bytes 124424 | tf_op jit(solution)/shard_map/ppermute | solution.py:35
  22.4 6.6 %collective-permute-start.2 = (f32[10368]{0:T(1024)}, f32[10368]{0:T(1024)}, u32[]{:S(2)}, u32[]{:S(2)}) collective-permute-start(f32[10368]{0:T(1024)} %reshape.71), channel_id=1, source_target_pairs={{0,24},{8,0},{16,8},{24,16},{1,25},{9,1},{17,9},{25,17},{2,26},{10... | collective-permute-start | bytes 124424 | tf_op jit(solution)/shard_map/ppermute | solution.py:35
  24.2 24.2 %collective-permute-start.5 = (f32[8,3,8,256]{3,2,1,0:T(8,128)S(1)}, f32[8,3,8,256]{3,2,1,0:T(8,128)S(1)}, u32[]{:S(2)}, u32[]{:S(2)}) collective-permute-start(f32[8,3,8,256]{3,2,1,0:T(8,128)S(1)} %get-tuple-element.18), channel_id=1, source_target_pairs={{0,1},{1,2},{2,3},{3,4},{4,5},{5,6},{6,7},{7,0},{8,9},{9,10},{10,1... | collective-permute-start | bytes 589832 | tf_op jit(solution)/shard_map/ppermute | solution.py:33
  24.4 23.9 %collective-permute-start.4 = (f32[8,3,8,256]{3,2,1,0:T(8,128)}, f32[8,3,8,256]{3,2,1,0:T(8,128)S(1)}, u32[]{:S(2)}, u32[]{:S(2)}) collective-permute-start(f32[8,3,8,256]{3,2,1,0:T(8,128)} %get-tuple-element.19), channel_id=1, source_target_pairs={{0,7},{1,0},{2,1},{3,2},{4,3},{5,4},{6,5},{7,6},{8,15},{9,8},{10,9... | collective-permute-start | bytes 589832 | tf_op jit(solution)/shard_map/ppermute | solution.py:33
  48.4 2.6 %copy-start = (f32[9,3,32,256]{3,2,1,0:T(8,128)S(1)}, f32[9,3,32,256]{3,2,1,0:T(8,128)}, u32[]{:S(2)}) copy-start(f32[9,3,32,256]{3,2,1,0:T(8,128)} %shard_map.41) | copy-start | bytes 2654212
  49.2 3.8 %collective-permute-start.7 = (f32[9216]{0:T(1024)S(1)}, f32[9216]{0:T(1024)S(1)}, u32[]{:S(2)}, u32[]{:S(2)}) collective-permute-start(f32[9216]{0:T(1024)S(1)} %reshape.77), channel_id=1, source_target_pairs={{0,8},{8,16},{16,24},{24,0},{1,9},{9,17},{17,25},{25,1},{2,10},{10... | collective-permute-start | bytes 110600 | tf_op jit(solution)/shard_map/ppermute | solution.py:35
  49.3 3.4 %collective-permute-start.6 = (f32[9216]{0:T(1024)S(1)}, f32[9216]{0:T(1024)S(1)}, u32[]{:S(2)}, u32[]{:S(2)}) collective-permute-start(f32[9216]{0:T(1024)S(1)} %reshape.75), channel_id=1, source_target_pairs={{0,24},{8,0},{16,8},{24,16},{1,25},{9,1},{17,9},{25,17},{2,26},{10... | collective-permute-start | bytes 110600 | tf_op jit(solution)/shard_map/ppermute | solution.py:35
  70.9 2.5 %collective-permute-start.8 = (f32[16,16]{0,1:T(8,128)S(1)}, f32[16,16]{0,1:T(8,128)S(1)}, u32[]{:S(2)}, u32[]{:S(2)}) collective-permute-start(f32[16,16]{0,1:T(8,128)S(1)} %fusion.3), channel_id=1, source_target_pairs={{0,8},{8,0},{16,24},{24,16},{1,9},{9,1},{17,25},{25,17},{2,10},{10... | collective-permute-start | bytes 3080 | tf_op jit(solution)/shard_map/ppermute | solution.py:132
  73.4 3.7 %collective-permute-start.9 = (f32[16,16]{0,1:T(8,128)S(1)}, f32[16,16]{0,1:T(8,128)S(1)}, u32[]{:S(2)}, u32[]{:S(2)}) collective-permute-start(f32[16,16]{0,1:T(8,128)S(1)} %add.77), channel_id=1, source_target_pairs={{0,16},{8,24},{16,0},{24,8},{1,17},{9,25},{17,1},{25,9},{2,18},{10... | collective-permute-start | bytes 3080 | tf_op jit(solution)/shard_map/ppermute | solution.py:132
  77.0 3.7 %collective-permute-start.10 = (f32[16,16]{0,1:T(8,128)S(1)}, f32[16,16]{0,1:T(8,128)S(1)}, u32[]{:S(2)}, u32[]{:S(2)}) collective-permute-start(f32[16,16]{0,1:T(8,128)S(1)} %add.78), channel_id=1, source_target_pairs={{0,1},{1,0},{2,3},{3,2},{4,5},{5,4},{6,7},{7,6},{8,9},{9,8},{10,11... | collective-permute-start | bytes 3080 | tf_op jit(solution)/shard_map/ppermute | solution.py:132
  80.7 3.7 %collective-permute-start.11 = (f32[16,16]{0,1:T(8,128)S(1)}, f32[16,16]{0,1:T(8,128)S(1)}, u32[]{:S(2)}, u32[]{:S(2)}) collective-permute-start(f32[16,16]{0,1:T(8,128)S(1)} %add.79), channel_id=1, source_target_pairs={{0,2},{1,3},{2,0},{3,1},{4,6},{5,7},{6,4},{7,5},{8,10},{9,11},{10,... | collective-permute-start | bytes 3080 | tf_op jit(solution)/shard_map/ppermute | solution.py:132
  84.4 4.5 %collective-permute-start.12 = (f32[16,16]{0,1:T(8,128)S(1)}, f32[16,16]{0,1:T(8,128)S(1)}, u32[]{:S(2)}, u32[]{:S(2)}) collective-permute-start(f32[16,16]{0,1:T(8,128)S(1)} %add.80), channel_id=1, source_target_pairs={{0,4},{1,5},{2,6},{3,7},{4,0},{5,1},{6,2},{7,3},{8,12},{9,13},{10,... | collective-permute-start | bytes 3080 | tf_op jit(solution)/shard_map/ppermute | solution.py:132

commit v3 on v1

--- a/solution.py
+++ b/solution.py
@@ -45,29 +45,50 @@
     tall = jnp.concatenate([value, below, above], axis=-2)
     west = shift(tall[..., cols - width :], "gx", 1, 0)
     east = shift(tall[..., :width], "gx", -1, 0)
-    gap = jnp.zeros(tall.shape[:-1] + (lanes - cols - 2 * width,), tall.dtype)
-    return jnp.concatenate([tall, east, gap, west], axis=-1)
+    return above, below, west, east
 
 
-def forecast_kernel(cor_ref, x_ref, o_ref, *, steps, rows, cols):
+def forecast_kernel(cor_ref, x_ref, up_ref, down_ref, west_ref, east_ref, o_ref, ring, east_pad, west_pad, *, steps):
+    rows, cols = (x_ref.shape[-2], x_ref.shape[-1])
+    R, C = cor_ref.shape
+    width = up_ref.shape[-2]
+    spare = C - cols
+
+    @pl.when(pl.program_id(0) == 0)
+    def _():
+        ring[...] = jnp.zeros_like(ring)
+        east_pad[...] = jnp.zeros_like(east_pad)
+        west_pad[...] = jnp.zeros_like(west_pad)
+
+    for k in range(3):
+        ring[k, :rows, :cols] = x_ref[0, k]
+        ring[k, rows : rows + width, :cols] = down_ref[0, k]
+        ring[k, rows + width :, :cols] = up_ref[0, k]
+        east_pad[:, :width] = east_ref[0, k]
+        west_pad[:, :width] = west_ref[0, k]
+        ring[k, :, cols:] = east_pad[...] + pltpu.roll(west_pad[...], spare - width, 1)
+
     f = cor_ref[...]
-    R, C = f.shape
     third = 1.0 / 12.0
+
     def dx(v):
         g = pltpu.roll(v, C - 1, 1) - pltpu.roll(v, 1, 1)
         w = pltpu.roll(v, C - 2, 1) - pltpu.roll(v, 2, 1)
         return (8.0 * g - w) * third
+
     def dy(v):
         g = pltpu.roll(v, R - 1, 0) - pltpu.roll(v, 1, 0)
         w = pltpu.roll(v, R - 2, 0) - pltpu.roll(v, 2, 0)
         return (8.0 * g - w) * third
+
     def tend(h, e, n):
         depth = 4.0 + h
         ch = -(dx(depth * e) + dy(depth * n))
         ce = -(e * dx(e) + n * dy(e)) + f * n - dx(h)
         cn = -(e * dx(n) + n * dy(n)) - f * e - dy(h)
         return ch, ce, cn
-    s = (x_ref[0, 0], x_ref[0, 1], x_ref[0, 2])
+
+    s = (ring[0], ring[1], ring[2])
     for _ in range(steps):
         first = tend(*s)
         mid = tuple(a + 0.1 * b for a, b in zip(s, first))
@@ -76,16 +97,33 @@
     for k in range(3):
         o_ref[0, k] = s[k][:rows, :cols]
 
-def forecast(cor, padded, steps, rows, cols):
-    S, F, R, C = padded.shape
+
+def forecast(cor, value, above, below, west, east, steps):
+    S, F, rows, cols = value.shape
+    R, C = cor.shape
+    width = above.shape[-2]
     return pl.pallas_call(
-        functools.partial(forecast_kernel, steps=steps, rows=rows, cols=cols),
+        functools.partial(forecast_kernel, steps=steps),
         out_shape=jax.ShapeDtypeStruct((S, F, rows, cols), jnp.float32),
         grid=(S,),
-        in_specs=[pl.BlockSpec((R, C), lambda i: (0, 0)),
-                  pl.BlockSpec((1, F, R, C), lambda i: (i, 0, 0, 0))],
+        in_specs=[
+            pl.BlockSpec((R, C), lambda i: (0, 0)),
+            pl.BlockSpec((1, F, rows, cols), lambda i: (i, 0, 0, 0)),
+            pl.BlockSpec((1, F, width, cols), lambda i: (i, 0, 0, 0)),
+            pl.BlockSpec((1, F, width, cols), lambda i: (i, 0, 0, 0)),
+            pl.BlockSpec((1, F, R, width), lambda i: (i, 0, 0, 0)),
+            pl.BlockSpec((1, F, R, width), lambda i: (i, 0, 0, 0)),
+        ],
         out_specs=pl.BlockSpec((1, F, rows, cols), lambda i: (i, 0, 0, 0)),
-    )(cor, padded)
+        scratch_shapes=[
+            pltpu.VMEM((F, R, C), jnp.float32),
+            pltpu.VMEM((R, C - cols), jnp.float32),
+            pltpu.VMEM((R, C - cols), jnp.float32),
+        ],
+        cost_estimate=pl.CostEstimate(
+            flops=S * F * R * C * 300 * steps, transcendentals=0, bytes_accessed=4 * S * F * (R * C + rows * cols)
+        ),
+    )(cor, value, above, below, west, east)
 
 
 def body(control, perts):
@@ -103,8 +141,8 @@
     coriolis = jnp.broadcast_to(coriolis[:, None], (ring_rows, lanes))
 
     states = jnp.concatenate([control[None], control[None] + perts], 0)
-    padded = ring_halo(states, margin, lanes)
-    current = forecast(coriolis, padded, STEPS, tile_rows, tile_column_count)
+    above, below, west, east = ring_halo(states, margin, lanes)
+    current = forecast(coriolis, states, above, below, west, east, STEPS)
     bred = current[1:] - current[0:1]
     flat = bred.reshape(MEMBERS, -1)
     local_gram = jnp.dot(flat, flat.T, precision=lax.Precision.HIGHEST)

time: 96.4 us -> 90.2 us (0.936)
  waiting for transfers between devices: 30.7 us -> 27.2 us
  local copies, waits for them, and re-layouts: 13.4 us -> 10.3 us
  other arithmetic: 11.3 us -> 8.83 us
  starting transfers between devices: 11.8 us -> 13.8 us
    concatenate x1 -> x2, other arithmetic: 3.76 us -> 1.39 us  [body(): states = jnp.concatenate([control[None], control[None] + perts], 0)]
    ppermute x2, waiting for transfers between devices: 3.45 us -> 1.48 us  [shift(): return lax.ppermute(flat, axes, pairs).reshape(part.shape)]
    reshape x2, local copies, waits for them, and re-layouts: 2.97 us -> 1.09 us  [shift(): flat = part.reshape(-1)]
    ppermute x5, waiting for transfers between devices: 11.7 us -> 10.1 us  [body(): gram = gram + lax.ppermute(gram, axis, pairs)]
    ppermute x5, starting transfers between devices: 4.57 us -> 5.87 us  [body(): gram = gram + lax.ppermute(gram, axis, pairs)]
    slice x1, local copies, waits for them, and re-layouts: 1.43 us -> 0.39 us  [ring_halo(): east = shift(tall[..., :width], 'gx', -1, 0)]
    unnamed x7 -> x9, local copies, waits for them, and re-layouts: 3.95 us -> 3.7 us
  transfers between devices with their start and end apart: 9 -> 9, of which waited for: 9 -> 8; matrix products, arithmetic and copies ran while one was open for 3% -> 5% of each run, Pallas kernels for 0% -> 0%
where the time goes in v3:
time: 90.2 us; the launch traced here: 90 us
  waiting for transfers between devices  27.2 us (30%)
  Pallas kernels  24.9 us (28%)
  starting transfers between devices  13.8 us (15%)
  local copies, waits for them, and re-layouts  10.3 us (11%)
  other arithmetic  8.83 us (10%)
  matrix products  4.22 us (5%)
    pallas_call x1, Pallas kernels, forecast(): pl.pallas_call(functools.partial(forecast_kernel, steps=steps), out_shape...  24.9 us
    ppermute x2, waiting for transfers between devices, shift(): return lax.ppermute(part, axes, pairs)  15.6 us
    ppermute x5, waiting for transfers between devices, body(): gram = gram + lax.ppermute(gram, axis, pairs)  10.1 us
    ppermute x2, starting transfers between devices, shift(): return lax.ppermute(part, axes, pairs)  6.12 us
    ppermute x5, starting transfers between devices, body(): gram = gram + lax.ppermute(gram, axis, pairs)  5.87 us
    unnamed x9, local copies, waits for them, and re-layouts  3.7 us
    reshape x2, local copies, waits for them, and re-layouts, shift(): return lax.ppermute(flat, axes, pairs).reshape(part.shape)  3.43 us
    dot_general x1, matrix products, body(): local_gram = jnp.dot(flat, flat.T, precision=lax.Precision.HIGHEST)  2.72 us
  transfers between devices with their start and end apart: 9, of which 8 were waited for; matrix products, arithmetic and copies ran while one was open for 5% of the time, Pallas kernels for 0%

profile of v3, /device:TPU:0, one launch (start us, length us, event | category | flops | bytes accessed | tf_op | source)
XLA Modules:
  0.0 90.0 jit_solution(17080162408297331627)
XLA Ops:
  0.6 1.6 %broadcast_add_fusion = f32[16,3,32,256]{3,2,1,0:T(8,128)S(1)} fusion(f32[16,3,32,256]{3,2,1,0:T(8,128)} %param.3, f32[3,32,256]{2,1,0:T(8,128)} %param.2), kind=kLoop, calls=%fused_computation.11 | loop fusion | flops 393216 | bytes 3244032 | tf_op jit(solution)/shard_map/add | solution.py:143
  2.3 3.0 %collective-permute-start = (f32[17,3,8,256]{3,2,1,0:T(8,128)S(1)}, f32[17,3,8,256]{3,2,1,0:T(8,128)S(1)}, u32[]{:S(2)}, u32[]{:S(2)}) collective-permute-start(f32[17,3,8,256]{3,2,1,0:T(8,128)S(1)} %get-tuple-element.9), channel_id=1, source_target_pairs={{0,1},{1,2},{2,3},{3,4},{4,5},{5,6},{6,7},{7,0},{8,9},{9,10},{10,1... | collective-permute-start | bytes 1253384 | tf_op jit(solution)/shard_map/ppermute | solution.py:38
  5.3 3.1 %collective-permute-start.1 = (f32[17,3,8,256]{3,2,1,0:T(8,128)S(1)}, f32[17,3,8,256]{3,2,1,0:T(8,128)S(1)}, u32[]{:S(2)}, u32[]{:S(2)}) collective-permute-start(f32[17,3,8,256]{3,2,1,0:T(8,128)S(1)} %get-tuple-element.8), channel_id=1, source_target_pairs={{0,7},{1,0},{2,1},{3,2},{4,3},{5,4},{6,5},{7,6},{8,15},{9,8},{10,9... | collective-permute-start | bytes 1253384 | tf_op jit(solution)/shard_map/ppermute | solution.py:38
  8.4 1.3 %pad_maximum_fusion.x_ref = f32[17,3,32,256]{3,2,1,0:T(8,128)} fusion(f32[1,3,32,256]{3,2,1,0:T(8,128)S(1)} %bitcast.33, f32[16,3,32,256]{3,2,1,0:T(8,128)S(1)} %broadcast_add_fusion), kind=kLoop, calls=%fused_computation.3 | loop fusion | flops 417792 | bytes 3342336 | tf_op jit(solution)/shard_map/concatenate | solution.py:143
  9.8 13.4 %collective-permute-done.up_ref = f32[17,3,8,256]{3,2,1,0:T(8,128)S(1)} collective-permute-done((f32[17,3,8,256]{3,2,1,0:T(8,128)S(1)}, f32[17,3,8,256]{3,2,1,0:T(8,128)S(1)}, u32[]{:S(2)}, u32[]{:S(2)}) %collective-permute-start) | collective-permute-done | bytes 417824 | tf_op jit(solution)/shard_map/ppermute | solution.py:38
  23.2 2.2 %collective-permute-done.1.down_ref = f32[17,3,8,256]{3,2,1,0:T(8,128)S(1)} collective-permute-done((f32[17,3,8,256]{3,2,1,0:T(8,128)S(1)}, f32[17,3,8,256]{3,2,1,0:T(8,128)S(1)}, u32[]{:S(2)}, u32[]{:S(2)}) %collective-permute-start.1) | collective-permute-done | bytes 417824 | tf_op jit(solution)/shard_map/ppermute | solution.py:38
  26.6 0.5 reshape.59
  27.7 1.8 %collective-permute-start.3 = (f32[19584]{0:T(1024)S(1)}, f32[19584]{0:T(1024)S(1)}, u32[]{:S(2)}, u32[]{:S(2)}) collective-permute-start(f32[19584]{0:T(1024)S(1)} %reshape.61), channel_id=1, source_target_pairs={{0,24},{8,0},{16,8},{24,16},{1,25},{9,1},{17,9},{25,17},{2,26},{10... | collective-permute-start | bytes 235016 | tf_op jit(solution)/shard_map/ppermute | solution.py:40
  29.5 1.5 %collective-permute-done.2 = f32[19584]{0:T(1024)S(1)} collective-permute-done((f32[19584]{0:T(1024)S(1)}, f32[19584]{0:T(1024)S(1)}, u32[]{:S(2)}, u32[]{:S(2)}) %collective-permute-start.2) | collective-permute-done | bytes 78368 | tf_op jit(solution)/shard_map/ppermute | solution.py:40
  31.0 1.7 %reshape.60.west_ref = f32[17,3,48,8]{3,2,1,0:T(8,128)} reshape(f32[19584]{0:T(1024)S(1)} %collective-permute-done.2) | data formatting | bytes 156672 | tf_op jit(solution)/shard_map/reshape | solution.py:40
  32.7 1.7 %reshape.62.east_ref = f32[17,3,48,8]{3,2,1,0:T(8,128)} reshape(f32[19584]{0:T(1024)S(1)} %collective-permute-done.3) | data formatting | bytes 156672 | tf_op jit(solution)/shard_map/reshape | solution.py:40
  34.5 0.7 broadcast_in_dim.5.cor_ref
  35.2 24.9 %shard_map.41 = f32[17,3,32,256]{3,2,1,0:T(8,128)} custom-call(f32[48,384]{1,0:T(8,128)} %broadcast_in_dim.5.cor_ref, f32[17,3,32,256]{3,2,1,0:T(8,128)} %pad_maximum_fusion.x_ref, f32[17,3,8,256]{3,2,1,0:T(8,128)} %copy-done, f32[17,3,8,256]{3,2,1,0:T(8,128)} %copy-done.1, f32[17,3,48,8]{3,2,1,0:T(8,128)} %reshape.60.west_ref, ...), custom_call_target="tpu_custom_call" | custom-call | flops 564019200 | bytes 5431296 | tf_op jit(solution)/shard_map/pallas_call | solution.py:105
  60.0 0.9 slice_bitcast_fusion
  60.9 1.5 %slice_subtract_fusion = f32[16,3,32,256]{3,2,1,0:T(8,128)S(1)} fusion(f32[17,3,32,256]{3,2,1,0:T(8,128)} %shard_map.41, f32[3,32,256]{2,1,0:T(8,128)S(1)} %slice_bitcast_fusion), kind=kLoop, calls=%fused_computation.5 | loop fusion | flops 393216 | bytes 3244032 | tf_op jit(solution)/shard_map/sub | solution.py:146
  62.5 2.7 %fusion.2 = f32[16,16]{0,1:T(8,128)S(1)} fusion(f32[16,3,32,256]{3,2,1,0:T(8,128)S(1)} %slice_subtract_fusion), kind=kOutput, calls=%fused_computation.10 | convolution fusion | flops 75497472 | bytes 1573888 | tf_op jit(solution)/shard_map/dot_general | solution.py:148
  65.7 0.8 collective-permute-done.4
  66.6 1.4 %collective-permute-start.5 = (f32[16,16]{0,1:T(8,128)S(1)}, f32[16,16]{0,1:T(8,128)S(1)}, u32[]{:S(2)}, u32[]{:S(2)}) collective-permute-start(f32[16,16]{0,1:T(8,128)S(1)} %add.77), channel_id=1, source_target_pairs={{0,16},{8,24},{16,0},{24,8},{1,17},{9,25},{17,1},{25,9},{2,18},{10... | collective-permute-start | bytes 3080 | tf_op jit(solution)/shard_map/ppermute | solution.py:158
  67.9 2.3 %collective-permute-done.5 = f32[16,16]{0,1:T(8,128)S(1)} collective-permute-done((f32[16,16]{0,1:T(8,128)S(1)}, f32[16,16]{0,1:T(8,128)S(1)}, u32[]{:S(2)}, u32[]{:S(2)}) %collective-permute-start.5) | collective-permute-done | bytes 1056 | tf_op jit(solution)/shard_map/ppermute | solution.py:158
  70.7 3.2 %collective-permute-done.6 = f32[16,16]{0,1:T(8,128)S(1)} collective-permute-done((f32[16,16]{0,1:T(8,128)S(1)}, f32[16,16]{0,1:T(8,128)S(1)}, u32[]{:S(2)}, u32[]{:S(2)}) %collective-permute-start.6) | collective-permute-done | bytes 1056 | tf_op jit(solution)/shard_map/ppermute | solution.py:158
  73.9 1.3 %collective-permute-start.7 = (f32[16,16]{0,1:T(8,128)S(1)}, f32[16,16]{0,1:T(8,128)S(1)}, u32[]{:S(2)}, u32[]{:S(2)}) collective-permute-start(f32[16,16]{0,1:T(8,128)S(1)} %add.79), channel_id=1, source_target_pairs={{0,2},{1,3},{2,0},{3,1},{4,6},{5,7},{6,4},{7,5},{8,10},{9,11},{10,... | collective-permute-start | bytes 3080 | tf_op jit(solution)/shard_map/ppermute | solution.py:158
  75.1 2.4 %collective-permute-done.7 = f32[16,16]{0,1:T(8,128)S(1)} collective-permute-done((f32[16,16]{0,1:T(8,128)S(1)}, f32[16,16]{0,1:T(8,128)S(1)}, u32[]{:S(2)}, u32[]{:S(2)}) %collective-permute-start.7) | collective-permute-done | bytes 1056 | tf_op jit(solution)/shard_map/ppermute | solution.py:158
  77.5 2.3 %collective-permute-start.8 = (f32[16,16]{0,1:T(8,128)S(1)}, f32[16,16]{0,1:T(8,128)S(1)}, u32[]{:S(2)}, u32[]{:S(2)}) collective-permute-start(f32[16,16]{0,1:T(8,128)S(1)} %add.80), channel_id=1, source_target_pairs={{0,4},{1,5},{2,6},{3,7},{4,0},{5,1},{6,2},{7,3},{8,12},{9,13},{10,... | collective-permute-start | bytes 3080 | tf_op jit(solution)/shard_map/ppermute | solution.py:158
  79.8 0.9 %copy.19 = f32[2,8,96,256]{3,1,2,0:T(8,128)S(1)} copy(f32[2,8,96,256]{3,2,1,0:T(8,128)S(1)} %bitcast.29) | data formatting | bytes 3145728
  80.7 1.4 %collective-permute-done.8 = f32[16,16]{0,1:T(8,128)S(1)} collective-permute-done((f32[16,16]{0,1:T(8,128)S(1)}, f32[16,16]{0,1:T(8,128)S(1)}, u32[]{:S(2)}, u32[]{:S(2)}) %collective-permute-start.8) | collective-permute-done | bytes 1056 | tf_op jit(solution)/shard_map/ppermute | solution.py:158
  82.2 1.5 %cholesky.16 = f32[16,16]{1,0:T(8,128)S(1)} custom-call(f32[16,16]{1,0:T(8,128)S(1)} %fusion.8), custom_call_target="Cholesky" | custom-call | tf_op jit(solution)/shard_map/jit(cholesky)/cholesky | solution.py:160
  83.6 0.6 compare_reduce_fusion
  84.3 0.7 multiply_bitcast_fusion
  84.9 1.2 %custom-call.7 = f32[1,16,16]{1,2,0:T(8,128)S(1)} custom-call(f32[1,16,16]{2,1,0:T(8,128)S(1)} %get-tuple-element.11), custom_call_target="InvertDiagBlocksLowerTriangular" | custom-call | tf_op jit(solution)/shard_map/jit(_solve_triangular)/triangular_solve | solution.py:161
  86.2 1.5 %convolution_multiply_fusion = f32[16,24576]{1,0:T(8,128)S(1)} fusion(f32[16,24576]{1,0:T(8,128)S(1)} %bitcast.30, f32[1,16,16]{1,2,0:T(8,128)S(1)} %custom-call.7), kind=kOutput, calls=%fused_computation | convolution fusion | flops 75890688 | bytes 3146752 | tf_op jit(solution)/shard_map/jit(_solve_triangular)/triangular_solve | solution.py:161
  87.7 1.6 %copy.20 = f32[2,8,96,256]{3,2,1,0:T(8,128)} copy(f32[2,8,96,256]{3,1,2,0:T(8,128)S(1)} %bitcast.31) | data formatting | bytes 3145728
  89.3 0.7 copy.15
  (23 shorter events, 3.0 us)
Async XLA Ops:
  0.6 1.6 %copy-start.2 = (f32[3,32,256]{2,1,0:T(8,128)S(1)}, f32[3,32,256]{2,1,0:T(8,128)}, u32[]{:S(2)}) copy-start(f32[3,32,256]{2,1,0:T(8,128)} %param.2) | copy-start | bytes 294916
  2.3 20.9 %collective-permute-start = (f32[17,3,8,256]{3,2,1,0:T(8,128)S(1)}, f32[17,3,8,256]{3,2,1,0:T(8,128)S(1)}, u32[]{:S(2)}, u32[]{:S(2)}) collective-permute-start(f32[17,3,8,256]{3,2,1,0:T(8,128)S(1)} %get-tuple-element.9), channel_id=1, source_target_pairs={{0,1},{1,2},{2,3},{3,4},{4,5},{5,6},{6,7},{7,0},{8,9},{9,10},{10,1... | collective-permute-start | bytes 1253384 | tf_op jit(solution)/shard_map/ppermute | solution.py:38
  5.3 20.1 %collective-permute-start.1 = (f32[17,3,8,256]{3,2,1,0:T(8,128)S(1)}, f32[17,3,8,256]{3,2,1,0:T(8,128)S(1)}, u32[]{:S(2)}, u32[]{:S(2)}) collective-permute-start(f32[17,3,8,256]{3,2,1,0:T(8,128)S(1)} %get-tuple-element.8), channel_id=1, source_target_pairs={{0,7},{1,0},{2,1},{3,2},{4,3},{5,4},{6,5},{7,6},{8,15},{9,8},{10,9... | collective-permute-start | bytes 1253384 | tf_op jit(solution)/shard_map/ppermute | solution.py:38
  23.2 2.5 %copy-start = (f32[17,3,8,256]{3,2,1,0:T(8,128)}, f32[17,3,8,256]{3,2,1,0:T(8,128)S(1)}, u32[]{:S(2)}) copy-start(f32[17,3,8,256]{3,2,1,0:T(8,128)S(1)} %collective-permute-done.up_ref) | copy-start | bytes 1253380
  25.4 0.8 copy-start.1
  27.1 3.9 %collective-permute-start.2 = (f32[19584]{0:T(1024)S(1)}, f32[19584]{0:T(1024)S(1)}, u32[]{:S(2)}, u32[]{:S(2)}) collective-permute-start(f32[19584]{0:T(1024)S(1)} %reshape.59), channel_id=1, source_target_pairs={{0,8},{8,16},{16,24},{24,0},{1,9},{9,17},{17,25},{25,1},{2,10},{10... | collective-permute-start | bytes 235016 | tf_op jit(solution)/shard_map/ppermute | solution.py:40
  27.7 5.0 %collective-permute-start.3 = (f32[19584]{0:T(1024)S(1)}, f32[19584]{0:T(1024)S(1)}, u32[]{:S(2)}, u32[]{:S(2)}) collective-permute-start(f32[19584]{0:T(1024)S(1)} %reshape.61), channel_id=1, source_target_pairs={{0,24},{8,0},{16,8},{24,16},{1,25},{9,1},{17,9},{25,17},{2,26},{10... | collective-permute-start | bytes 235016 | tf_op jit(solution)/shard_map/ppermute | solution.py:40
  65.2 1.4 %collective-permute-start.4 = (f32[16,16]{0,1:T(8,128)S(1)}, f32[16,16]{0,1:T(8,128)S(1)}, u32[]{:S(2)}, u32[]{:S(2)}) collective-permute-start(f32[16,16]{0,1:T(8,128)S(1)} %fusion.2), channel_id=1, source_target_pairs={{0,8},{8,0},{16,24},{24,16},{1,9},{9,1},{17,25},{25,17},{2,10},{10... | collective-permute-start | bytes 3080 | tf_op jit(solution)/shard_map/ppermute | solution.py:158
  66.6 3.7 %collective-permute-start.5 = (f32[16,16]{0,1:T(8,128)S(1)}, f32[16,16]{0,1:T(8,128)S(1)}, u32[]{:S(2)}, u32[]{:S(2)}) collective-permute-start(f32[16,16]{0,1:T(8,128)S(1)} %add.77), channel_id=1, source_target_pairs={{0,16},{8,24},{16,0},{24,8},{1,17},{9,25},{17,1},{25,9},{2,18},{10... | collective-permute-start | bytes 3080 | tf_op jit(solution)/shard_map/ppermute | solution.py:158
  70.2 3.7 %collective-permute-start.6 = (f32[16,16]{0,1:T(8,128)S(1)}, f32[16,16]{0,1:T(8,128)S(1)}, u32[]{:S(2)}, u32[]{:S(2)}) collective-permute-start(f32[16,16]{0,1:T(8,128)S(1)} %add.78), channel_id=1, source_target_pairs={{0,1},{1,0},{2,3},{3,2},{4,5},{5,4},{6,7},{7,6},{8,9},{9,8},{10,11... | collective-permute-start | bytes 3080 | tf_op jit(solution)/shard_map/ppermute | solution.py:158
  73.9 3.7 %collective-permute-start.7 = (f32[16,16]{0,1:T(8,128)S(1)}, f32[16,16]{0,1:T(8,128)S(1)}, u32[]{:S(2)}, u32[]{:S(2)}) collective-permute-start(f32[16,16]{0,1:T(8,128)S(1)} %add.79), channel_id=1, source_target_pairs={{0,2},{1,3},{2,0},{3,1},{4,6},{5,7},{6,4},{7,5},{8,10},{9,11},{10,... | collective-permute-start | bytes 3080 | tf_op jit(solution)/shard_map/ppermute | solution.py:158
  77.5 4.5 %collective-permute-start.8 = (f32[16,16]{0,1:T(8,128)S(1)}, f32[16,16]{0,1:T(8,128)S(1)}, u32[]{:S(2)}, u32[]{:S(2)}) collective-permute-start(f32[16,16]{0,1:T(8,128)S(1)} %add.80), channel_id=1, source_target_pairs={{0,4},{1,5},{2,6},{3,7},{4,0},{5,1},{6,2},{7,3},{8,12},{9,13},{10,... | collective-permute-start | bytes 3080 | tf_op jit(solution)/shard_map/ppermute | solution.py:158

commit v4 on v3

--- a/solution.py
+++ b/solution.py
@@ -48,7 +48,7 @@
     return above, below, west, east
 
 
-def forecast_kernel(cor_ref, x_ref, up_ref, down_ref, west_ref, east_ref, o_ref, ring, east_pad, west_pad, *, steps):
+def forecast_kernel(cor_ref, x_ref, up_ref, down_ref, west_ref, east_ref, o_ref, ring, east_pad, west_pad, control, *, steps):
     rows, cols = (x_ref.shape[-2], x_ref.shape[-1])
     R, C = cor_ref.shape
     width = up_ref.shape[-2]
@@ -94,8 +94,15 @@
         mid = tuple(a + 0.1 * b for a, b in zip(s, first))
         second = tend(*mid)
         s = tuple(a + 0.05 * (b + c) for a, b, c in zip(s, first, second))
-    for k in range(3):
-        o_ref[0, k] = s[k][:rows, :cols]
+    @pl.when(pl.program_id(0) == 0)
+    def _():
+        for k in range(3):
+            control[k] = s[k][:rows, :cols]
+
+    @pl.when(pl.program_id(0) > 0)
+    def _():
+        for k in range(3):
+            o_ref[0, k] = s[k][:rows, :cols] - control[k]
 
 
 def forecast(cor, value, above, below, west, east, steps):
@@ -104,7 +111,7 @@
     width = above.shape[-2]
     return pl.pallas_call(
         functools.partial(forecast_kernel, steps=steps),
-        out_shape=jax.ShapeDtypeStruct((S, F, rows, cols), jnp.float32),
+        out_shape=jax.ShapeDtypeStruct((S - 1, F, rows, cols), jnp.float32),
         grid=(S,),
         in_specs=[
             pl.BlockSpec((R, C), lambda i: (0, 0)),
@@ -114,11 +121,12 @@
             pl.BlockSpec((1, F, R, width), lambda i: (i, 0, 0, 0)),
             pl.BlockSpec((1, F, R, width), lambda i: (i, 0, 0, 0)),
         ],
-        out_specs=pl.BlockSpec((1, F, rows, cols), lambda i: (i, 0, 0, 0)),
+        out_specs=pl.BlockSpec((1, F, rows, cols), lambda i: (jnp.maximum(i - 1, 0), 0, 0, 0)),
         scratch_shapes=[
             pltpu.VMEM((F, R, C), jnp.float32),
             pltpu.VMEM((R, C - cols), jnp.float32),
             pltpu.VMEM((R, C - cols), jnp.float32),
+            pltpu.VMEM((F, rows, cols), jnp.float32),
         ],
         cost_estimate=pl.CostEstimate(
             flops=S * F * R * C * 300 * steps, transcendentals=0, bytes_accessed=4 * S * F * (R * C + rows * cols)
@@ -142,8 +150,7 @@
 
     states = jnp.concatenate([control[None], control[None] + perts], 0)
     above, below, west, east = ring_halo(states, margin, lanes)
-    current = forecast(coriolis, states, above, below, west, east, STEPS)
-    bred = current[1:] - current[0:1]
+    bred = forecast(coriolis, states, above, below, west, east, STEPS)
     flat = bred.reshape(MEMBERS, -1)
     local_gram = jnp.dot(flat, flat.T, precision=lax.Precision.HIGHEST)
     gram = local_gram

time: 90.2 us -> 90.8 us (level)
  matrix products: 4.22 us -> 6.89 us
  other arithmetic: 8.83 us -> 7.32 us
    dot_general x1, matrix products: 2.72 us -> 5.39 us  [body(): local_gram = jnp.dot(flat, flat.T, precision=lax.Precision.HIGHEST)]
    sub x1 -> x0, other arithmetic: 1.53 us -> none  [body(): bred = current[1:] - current[0:1]]
    unnamed x9 -> x11, local copies, waits for them, and re-layouts: 3.7 us -> 3.73 us
where the time goes in v4:
time: 90.8 us; the launch traced here: 90.6 us
  waiting for transfers between devices  27.2 us (30%)
  Pallas kernels  25.2 us (28%)
  starting transfers between devices  13.8 us (15%)
  local copies, waits for them, and re-layouts  9.46 us (10%)
  other arithmetic  7.32 us (8%)
  matrix products  6.89 us (8%)
    pallas_call x1, Pallas kernels, forecast(): pl.pallas_call(functools.partial(forecast_kernel, steps=steps), out_shape...  25.2 us
    ppermute x2, waiting for transfers between devices, shift(): return lax.ppermute(part, axes, pairs)  15.6 us
    ppermute x5, waiting for transfers between devices, body(): gram = gram + lax.ppermute(gram, axis, pairs)  10.1 us
    ppermute x2, starting transfers between devices, shift(): return lax.ppermute(part, axes, pairs)  6.12 us
    ppermute x5, starting transfers between devices, body(): gram = gram + lax.ppermute(gram, axis, pairs)  5.83 us
    dot_general x1, matrix products, body(): local_gram = jnp.dot(flat, flat.T, precision=lax.Precision.HIGHEST)  5.39 us
    unnamed x11, local copies, waits for them, and re-layouts  3.73 us
    reshape x2, local copies, waits for them, and re-layouts, shift(): return lax.ppermute(flat, axes, pairs).reshape(part.shape)  3.48 us
  transfers between devices with their start and end apart: 9, of which 8 were waited for; matrix products, arithmetic and copies ran while one was open for 5% of the time, Pallas kernels for 0%

profile of v4, /device:TPU:0, one launch (start us, length us, event | category | flops | bytes accessed | tf_op | source)
XLA Modules:
  0.0 90.6 jit_solution(4861034135705540978)
XLA Ops:
  0.6 1.6 %broadcast_add_fusion = f32[16,3,32,256]{3,2,1,0:T(8,128)S(1)} fusion(f32[16,3,32,256]{3,2,1,0:T(8,128)} %param.3, f32[3,32,256]{2,1,0:T(8,128)} %param.2), kind=kLoop, calls=%fused_computation.10 | loop fusion | flops 393216 | bytes 3244032 | tf_op jit(solution)/shard_map/add | solution.py:151
  2.3 3.0 %collective-permute-start = (f32[17,3,8,256]{3,2,1,0:T(8,128)S(1)}, f32[17,3,8,256]{3,2,1,0:T(8,128)S(1)}, u32[]{:S(2)}, u32[]{:S(2)}) collective-permute-start(f32[17,3,8,256]{3,2,1,0:T(8,128)S(1)} %get-tuple-element.9), channel_id=1, source_target_pairs={{0,1},{1,2},{2,3},{3,4},{4,5},{5,6},{6,7},{7,0},{8,9},{9,10},{10,1... | collective-permute-start | bytes 1253384 | tf_op jit(solution)/shard_map/ppermute | solution.py:38
  5.3 3.1 %collective-permute-start.1 = (f32[17,3,8,256]{3,2,1,0:T(8,128)S(1)}, f32[17,3,8,256]{3,2,1,0:T(8,128)S(1)}, u32[]{:S(2)}, u32[]{:S(2)}) collective-permute-start(f32[17,3,8,256]{3,2,1,0:T(8,128)S(1)} %get-tuple-element.8), channel_id=1, source_target_pairs={{0,7},{1,0},{2,1},{3,2},{4,3},{5,4},{6,5},{7,6},{8,15},{9,8},{10,9... | collective-permute-start | bytes 1253384 | tf_op jit(solution)/shard_map/ppermute | solution.py:38
  8.4 1.3 %pad_maximum_fusion.x_ref = f32[17,3,32,256]{3,2,1,0:T(8,128)} fusion(f32[1,3,32,256]{3,2,1,0:T(8,128)S(1)} %bitcast.31, f32[16,3,32,256]{3,2,1,0:T(8,128)S(1)} %broadcast_add_fusion), kind=kLoop, calls=%fused_computation.3 | loop fusion | flops 417792 | bytes 3342336 | tf_op jit(solution)/shard_map/concatenate | solution.py:151
  9.8 13.4 %collective-permute-done.up_ref = f32[17,3,8,256]{3,2,1,0:T(8,128)S(1)} collective-permute-done((f32[17,3,8,256]{3,2,1,0:T(8,128)S(1)}, f32[17,3,8,256]{3,2,1,0:T(8,128)S(1)}, u32[]{:S(2)}, u32[]{:S(2)}) %collective-permute-start) | collective-permute-done | bytes 417824 | tf_op jit(solution)/shard_map/ppermute | solution.py:38
  23.2 2.2 %collective-permute-done.1.down_ref = f32[17,3,8,256]{3,2,1,0:T(8,128)S(1)} collective-permute-done((f32[17,3,8,256]{3,2,1,0:T(8,128)S(1)}, f32[17,3,8,256]{3,2,1,0:T(8,128)S(1)}, u32[]{:S(2)}, u32[]{:S(2)}) %collective-permute-start.1) | collective-permute-done | bytes 417824 | tf_op jit(solution)/shard_map/ppermute | solution.py:38
  25.7 0.5 copy-done.2
  26.6 0.5 reshape.59
  27.2 0.5 reshape.61
  27.7 1.8 %collective-permute-start.3 = (f32[19584]{0:T(1024)S(1)}, f32[19584]{0:T(1024)S(1)}, u32[]{:S(2)}, u32[]{:S(2)}) collective-permute-start(f32[19584]{0:T(1024)S(1)} %reshape.61), channel_id=1, source_target_pairs={{0,24},{8,0},{16,8},{24,16},{1,25},{9,1},{17,9},{25,17},{2,26},{10... | collective-permute-start | bytes 235016 | tf_op jit(solution)/shard_map/ppermute | solution.py:40
  29.6 1.5 %collective-permute-done.2 = f32[19584]{0:T(1024)S(1)} collective-permute-done((f32[19584]{0:T(1024)S(1)}, f32[19584]{0:T(1024)S(1)}, u32[]{:S(2)}, u32[]{:S(2)}) %collective-permute-start.2) | collective-permute-done | bytes 78368 | tf_op jit(solution)/shard_map/ppermute | solution.py:40
  31.0 1.7 %reshape.60.west_ref = f32[17,3,48,8]{3,2,1,0:T(8,128)} reshape(f32[19584]{0:T(1024)S(1)} %collective-permute-done.2) | data formatting | bytes 156672 | tf_op jit(solution)/shard_map/reshape | solution.py:40
  32.8 1.7 %reshape.62.east_ref = f32[17,3,48,8]{3,2,1,0:T(8,128)} reshape(f32[19584]{0:T(1024)S(1)} %collective-permute-done.3) | data formatting | bytes 156672 | tf_op jit(solution)/shard_map/reshape | solution.py:40
  34.5 0.7 broadcast_in_dim.5.cor_ref
  35.2 25.2 %shard_map.41 = f32[16,3,32,256]{3,2,1,0:T(8,128)} custom-call(f32[48,384]{1,0:T(8,128)} %broadcast_in_dim.5.cor_ref, f32[17,3,32,256]{3,2,1,0:T(8,128)} %pad_maximum_fusion.x_ref, f32[17,3,8,256]{3,2,1,0:T(8,128)} %copy-done.1, f32[17,3,8,256]{3,2,1,0:T(8,128)} %copy-done.2, f32[17,3,48,8]{3,2,1,0:T(8,128)} %reshape.60.west_ref, ...), custom_call_target="tpu_custom_call" | custom-call | flops 564019200 | bytes 5431296 | tf_op jit(solution)/shard_map/pallas_call | solution.py:112
  60.5 5.4 %fusion.2 = f32[16,16]{0,1:T(8,128)S(1)} fusion(f32[16,3,32,256]{3,2,1,0:T(8,128)} %shard_map.41), kind=kOutput, calls=%fused_computation.9 | convolution fusion | flops 75497472 | bytes 1573888 | tf_op jit(solution)/shard_map/dot_general | solution.py:155
  66.4 0.8 collective-permute-done.4
  67.2 1.4 %collective-permute-start.5 = (f32[16,16]{0,1:T(8,128)S(1)}, f32[16,16]{0,1:T(8,128)S(1)}, u32[]{:S(2)}, u32[]{:S(2)}) collective-permute-start(f32[16,16]{0,1:T(8,128)S(1)} %add.77), channel_id=1, source_target_pairs={{0,16},{8,24},{16,0},{24,8},{1,17},{9,25},{17,1},{25,9},{2,18},{10... | collective-permute-start | bytes 3080 | tf_op jit(solution)/shard_map/ppermute | solution.py:165
  68.6 2.3 %collective-permute-done.5 = f32[16,16]{0,1:T(8,128)S(1)} collective-permute-done((f32[16,16]{0,1:T(8,128)S(1)}, f32[16,16]{0,1:T(8,128)S(1)}, u32[]{:S(2)}, u32[]{:S(2)}) %collective-permute-start.5) | collective-permute-done | bytes 1056 | tf_op jit(solution)/shard_map/ppermute | solution.py:165
  71.3 3.2 %collective-permute-done.6 = f32[16,16]{0,1:T(8,128)S(1)} collective-permute-done((f32[16,16]{0,1:T(8,128)S(1)}, f32[16,16]{0,1:T(8,128)S(1)}, u32[]{:S(2)}, u32[]{:S(2)}) %collective-permute-start.6) | collective-permute-done | bytes 1056 | tf_op jit(solution)/shard_map/ppermute | solution.py:165
  74.5 1.3 %collective-permute-start.7 = (f32[16,16]{0,1:T(8,128)S(1)}, f32[16,16]{0,1:T(8,128)S(1)}, u32[]{:S(2)}, u32[]{:S(2)}) collective-permute-start(f32[16,16]{0,1:T(8,128)S(1)} %add.79), channel_id=1, source_target_pairs={{0,2},{1,3},{2,0},{3,1},{4,6},{5,7},{6,4},{7,5},{8,10},{9,11},{10,... | collective-permute-start | bytes 3080 | tf_op jit(solution)/shard_map/ppermute | solution.py:165
  75.8 2.4 %collective-permute-done.7 = f32[16,16]{0,1:T(8,128)S(1)} collective-permute-done((f32[16,16]{0,1:T(8,128)S(1)}, f32[16,16]{0,1:T(8,128)S(1)}, u32[]{:S(2)}, u32[]{:S(2)}) %collective-permute-start.7) | collective-permute-done | bytes 1056 | tf_op jit(solution)/shard_map/ppermute | solution.py:165
  78.2 2.3 %collective-permute-start.8 = (f32[16,16]{0,1:T(8,128)S(1)}, f32[16,16]{0,1:T(8,128)S(1)}, u32[]{:S(2)}, u32[]{:S(2)}) collective-permute-start(f32[16,16]{0,1:T(8,128)S(1)} %add.80), channel_id=1, source_target_pairs={{0,4},{1,5},{2,6},{3,7},{4,0},{5,1},{6,2},{7,3},{8,12},{9,13},{10,... | collective-permute-start | bytes 3080 | tf_op jit(solution)/shard_map/ppermute | solution.py:165
  80.4 0.9 %copy.19 = f32[2,8,96,256]{3,1,2,0:T(8,128)S(1)} copy(f32[2,8,96,256]{3,2,1,0:T(8,128)S(1)} %bitcast.27) | data formatting | bytes 3145728
  81.4 1.4 %collective-permute-done.8 = f32[16,16]{0,1:T(8,128)S(1)} collective-permute-done((f32[16,16]{0,1:T(8,128)S(1)}, f32[16,16]{0,1:T(8,128)S(1)}, u32[]{:S(2)}, u32[]{:S(2)}) %collective-permute-start.8) | collective-permute-done | bytes 1056 | tf_op jit(solution)/shard_map/ppermute | solution.py:165
  82.8 1.5 %cholesky.16 = f32[16,16]{1,0:T(8,128)S(1)} custom-call(f32[16,16]{1,0:T(8,128)S(1)} %fusion.8), custom_call_target="Cholesky" | custom-call | tf_op jit(solution)/shard_map/jit(cholesky)/cholesky | solution.py:167
  84.3 0.6 compare_reduce_fusion
  84.9 0.7 multiply_bitcast_fusion
  85.6 1.2 %custom-call.7 = f32[1,16,16]{1,2,0:T(8,128)S(1)} custom-call(f32[1,16,16]{2,1,0:T(8,128)S(1)} %get-tuple-element.11), custom_call_target="InvertDiagBlocksLowerTriangular" | custom-call | tf_op jit(solution)/shard_map/jit(_solve_triangular)/triangular_solve | solution.py:168
  86.8 1.5 %convolution_multiply_fusion = f32[16,24576]{1,0:T(8,128)S(1)} fusion(f32[16,24576]{1,0:T(8,128)S(1)} %bitcast.28, f32[1,16,16]{1,2,0:T(8,128)S(1)} %custom-call.7), kind=kOutput, calls=%fused_computation | convolution fusion | flops 75890688 | bytes 3146752 | tf_op jit(solution)/shard_map/jit(_solve_triangular)/triangular_solve | solution.py:168
  88.3 1.6 %copy.20 = f32[2,8,96,256]{3,2,1,0:T(8,128)} copy(f32[2,8,96,256]{3,1,2,0:T(8,128)S(1)} %bitcast.29) | data formatting | bytes 3145728
  89.9 0.7 copy.15
  (23 shorter events, 1.9 us)
Async XLA Ops:
  0.6 1.6 %copy-start.3 = (f32[3,32,256]{2,1,0:T(8,128)S(1)}, f32[3,32,256]{2,1,0:T(8,128)}, u32[]{:S(2)}) copy-start(f32[3,32,256]{2,1,0:T(8,128)} %param.2) | copy-start | bytes 294916
  2.3 20.9 %collective-permute-start = (f32[17,3,8,256]{3,2,1,0:T(8,128)S(1)}, f32[17,3,8,256]{3,2,1,0:T(8,128)S(1)}, u32[]{:S(2)}, u32[]{:S(2)}) collective-permute-start(f32[17,3,8,256]{3,2,1,0:T(8,128)S(1)} %get-tuple-element.9), channel_id=1, source_target_pairs={{0,1},{1,2},{2,3},{3,4},{4,5},{5,6},{6,7},{7,0},{8,9},{9,10},{10,1... | collective-permute-start | bytes 1253384 | tf_op jit(solution)/shard_map/ppermute | solution.py:38
  5.3 20.1 %collective-permute-start.1 = (f32[17,3,8,256]{3,2,1,0:T(8,128)S(1)}, f32[17,3,8,256]{3,2,1,0:T(8,128)S(1)}, u32[]{:S(2)}, u32[]{:S(2)}) collective-permute-start(f32[17,3,8,256]{3,2,1,0:T(8,128)S(1)} %get-tuple-element.8), channel_id=1, source_target_pairs={{0,7},{1,0},{2,1},{3,2},{4,3},{5,4},{6,5},{7,6},{8,15},{9,8},{10,9... | collective-permute-start | bytes 1253384 | tf_op jit(solution)/shard_map/ppermute | solution.py:38
  23.2 2.5 %copy-start.1 = (f32[17,3,8,256]{3,2,1,0:T(8,128)}, f32[17,3,8,256]{3,2,1,0:T(8,128)S(1)}, u32[]{:S(2)}) copy-start(f32[17,3,8,256]{3,2,1,0:T(8,128)S(1)} %collective-permute-done.up_ref) | copy-start | bytes 1253380
  25.4 0.8 copy-start.2
  27.1 3.9 %collective-permute-start.2 = (f32[19584]{0:T(1024)S(1)}, f32[19584]{0:T(1024)S(1)}, u32[]{:S(2)}, u32[]{:S(2)}) collective-permute-start(f32[19584]{0:T(1024)S(1)} %reshape.59), channel_id=1, source_target_pairs={{0,8},{8,16},{16,24},{24,0},{1,9},{9,17},{17,25},{25,1},{2,10},{10... | collective-permute-start | bytes 235016 | tf_op jit(solution)/shard_map/ppermute | solution.py:40
  27.7 5.0 %collective-permute-start.3 = (f32[19584]{0:T(1024)S(1)}, f32[19584]{0:T(1024)S(1)}, u32[]{:S(2)}, u32[]{:S(2)}) collective-permute-start(f32[19584]{0:T(1024)S(1)} %reshape.61), channel_id=1, source_target_pairs={{0,24},{8,0},{16,8},{24,16},{1,25},{9,1},{17,9},{25,17},{2,26},{10... | collective-permute-start | bytes 235016 | tf_op jit(solution)/shard_map/ppermute | solution.py:40
  60.5 20.0 %copy-start = (f32[16,3,32,256]{3,2,1,0:T(8,128)S(1)}, f32[16,3,32,256]{3,2,1,0:T(8,128)}, u32[]{:S(2)}) copy-start(f32[16,3,32,256]{3,2,1,0:T(8,128)} %shard_map.41) | copy-start | bytes 4718596
  65.9 1.3 %collective-permute-start.4 = (f32[16,16]{0,1:T(8,128)S(1)}, f32[16,16]{0,1:T(8,128)S(1)}, u32[]{:S(2)}, u32[]{:S(2)}) collective-permute-start(f32[16,16]{0,1:T(8,128)S(1)} %fusion.2), channel_id=1, source_target_pairs={{0,8},{8,0},{16,24},{24,16},{1,9},{9,1},{17,25},{25,17},{2,10},{10... | collective-permute-start | bytes 3080 | tf_op jit(solution)/shard_map/ppermute | solution.py:165
  67.2 3.7 %collective-permute-start.5 = (f32[16,16]{0,1:T(8,128)S(1)}, f32[16,16]{0,1:T(8,128)S(1)}, u32[]{:S(2)}, u32[]{:S(2)}) collective-permute-start(f32[16,16]{0,1:T(8,128)S(1)} %add.77), channel_id=1, source_target_pairs={{0,16},{8,24},{16,0},{24,8},{1,17},{9,25},{17,1},{25,9},{2,18},{10... | collective-permute-start | bytes 3080 | tf_op jit(solution)/shard_map/ppermute | solution.py:165
  70.9 3.7 %collective-permute-start.6 = (f32[16,16]{0,1:T(8,128)S(1)}, f32[16,16]{0,1:T(8,128)S(1)}, u32[]{:S(2)}, u32[]{:S(2)}) collective-permute-start(f32[16,16]{0,1:T(8,128)S(1)} %add.78), channel_id=1, source_target_pairs={{0,1},{1,0},{2,3},{3,2},{4,5},{5,4},{6,7},{7,6},{8,9},{9,8},{10,11... | collective-permute-start | bytes 3080 | tf_op jit(solution)/shard_map/ppermute | solution.py:165
  74.5 3.7 %collective-permute-start.7 = (f32[16,16]{0,1:T(8,128)S(1)}, f32[16,16]{0,1:T(8,128)S(1)}, u32[]{:S(2)}, u32[]{:S(2)}) collective-permute-start(f32[16,16]{0,1:T(8,128)S(1)} %add.79), channel_id=1, source_target_pairs={{0,2},{1,3},{2,0},{3,1},{4,6},{5,7},{6,4},{7,5},{8,10},{9,11},{10,... | collective-permute-start | bytes 3080 | tf_op jit(solution)/shard_map/ppermute | solution.py:165
  78.2 4.5 %collective-permute-start.8 = (f32[16,16]{0,1:T(8,128)S(1)}, f32[16,16]{0,1:T(8,128)S(1)}, u32[]{:S(2)}, u32[]{:S(2)}) collective-permute-start(f32[16,16]{0,1:T(8,128)S(1)} %add.80), channel_id=1, source_target_pairs={{0,4},{1,5},{2,6},{3,7},{4,0},{5,1},{6,2},{7,3},{8,12},{9,13},{10,... | collective-permute-start | bytes 3080 | tf_op jit(solution)/shard_map/ppermute | solution.py:165

commit v5 on v4

--- a/solution.py
+++ b/solution.py
@@ -151,8 +151,7 @@
     states = jnp.concatenate([control[None], control[None] + perts], 0)
     above, below, west, east = ring_halo(states, margin, lanes)
     bred = forecast(coriolis, states, above, below, west, east, STEPS)
-    flat = bred.reshape(MEMBERS, -1)
-    local_gram = jnp.dot(flat, flat.T, precision=lax.Precision.HIGHEST)
+    local_gram = jnp.einsum("ifrc,jfrc->ij", bred, bred, precision=lax.Precision.HIGHEST)
     gram = local_gram
     for axis in ("gx", "gy"):
         count = lax.axis_size(axis)
@@ -165,9 +164,11 @@
             gram = gram + lax.ppermute(gram, axis, pairs)
             stride *= 2
     lower = jnp.linalg.cholesky(gram)
-    solved = jax.scipy.linalg.solve_triangular(lower, flat, lower=True)
+    members = bred.shape[0]
+    inverse = jax.scipy.linalg.solve_triangular(lower, jnp.eye(members, dtype=lower.dtype), lower=True)
     domain_length = 3 * grid_rows * grid_cols
-    basis = (math.sqrt(domain_length) * solved).reshape(perts.shape)
+    solved = jnp.einsum("ij,jfrc->ifrc", inverse, bred, precision=lax.Precision.HIGHEST)
+    basis = math.sqrt(domain_length) * solved
     rfactor = lower.T / math.sqrt(domain_length)
     return (basis, rfactor)
 

time: 90.8 us -> 92.1 us (1.014)
    dot_general x1 -> x2, matrix products: 5.39 us -> 7.57 us  [the longest x1 5.39 us: body(): jnp.einsum('ifrc,jfrc->ij', bred, bred, precision=lax.Precision.HIGHEST)]
    another operation x1, matrix products: 1.5 us -> 0.19 us  [body(): jax.scipy.linalg.solve_triangular(lower, jnp.eye(members, dtype=lower.dty...]
    unnamed x11 -> x10, local copies, waits for them, and re-layouts: 3.73 us -> 3.26 us
  transfers between devices with their start and end apart: 9 -> 9, of which waited for: 8 -> 8; matrix products, arithmetic and copies ran while one was open for 5% -> 4% of each run, Pallas kernels for 0% -> 0%
where the time goes in v5:
time: 92.1 us; the launch traced here: 91.9 us
  waiting for transfers between devices  28.1 us (31%)
  Pallas kernels  25.2 us (27%)
  starting transfers between devices  13.8 us (15%)
  local copies, waits for them, and re-layouts  8.99 us (10%)
  matrix products  7.76 us (8%)
  other arithmetic  7.32 us (8%)
    pallas_call x1, Pallas kernels, forecast(): pl.pallas_call(functools.partial(forecast_kernel, steps=steps), out_shape...  25.2 us
    ppermute x2, waiting for transfers between devices, shift(): return lax.ppermute(part, axes, pairs)  15.6 us
    ppermute x5, waiting for transfers between devices, body(): gram = gram + lax.ppermute(gram, axis, pairs)  11 us
    ppermute x2, starting transfers between devices, shift(): return lax.ppermute(part, axes, pairs)  6.12 us
    ppermute x5, starting transfers between devices, body(): gram = gram + lax.ppermute(gram, axis, pairs)  5.83 us
    dot_general x1, matrix products, body(): jnp.einsum('ifrc,jfrc->ij', bred, bred, precision=lax.Precision.HIGHEST)  5.39 us
    reshape x2, local copies, waits for them, and re-layouts, shift(): return lax.ppermute(flat, axes, pairs).reshape(part.shape)  3.48 us
    unnamed x10, local copies, waits for them, and re-layouts  3.26 us
  transfers between devices with their start and end apart: 9, of which 8 were waited for; matrix products, arithmetic and copies ran while one was open for 4% of the time, Pallas kernels for 0%

profile of v5, /device:TPU:0, one launch (start us, length us, event | category | flops | bytes accessed | tf_op | source)
XLA Modules:
  0.0 91.9 jit_solution(3269419086170529570)
XLA Ops:
  0.6 1.6 %broadcast_add_fusion = f32[16,3,32,256]{3,2,1,0:T(8,128)S(1)} fusion(f32[16,3,32,256]{3,2,1,0:T(8,128)} %param.3, f32[3,32,256]{2,1,0:T(8,128)} %param.2), kind=kLoop, calls=%fused_computation.12 | loop fusion | flops 393216 | bytes 3244032 | tf_op jit(solution)/shard_map/add | solution.py:151
  2.3 3.0 %collective-permute-start = (f32[17,3,8,256]{3,2,1,0:T(8,128)S(1)}, f32[17,3,8,256]{3,2,1,0:T(8,128)S(1)}, u32[]{:S(2)}, u32[]{:S(2)}) collective-permute-start(f32[17,3,8,256]{3,2,1,0:T(8,128)S(1)} %get-tuple-element.9), channel_id=1, source_target_pairs={{0,1},{1,2},{2,3},{3,4},{4,5},{5,6},{6,7},{7,0},{8,9},{9,10},{10,1... | collective-permute-start | bytes 1253384 | tf_op jit(solution)/shard_map/ppermute | solution.py:38
  5.3 3.1 %collective-permute-start.1 = (f32[17,3,8,256]{3,2,1,0:T(8,128)S(1)}, f32[17,3,8,256]{3,2,1,0:T(8,128)S(1)}, u32[]{:S(2)}, u32[]{:S(2)}) collective-permute-start(f32[17,3,8,256]{3,2,1,0:T(8,128)S(1)} %get-tuple-element.8), channel_id=1, source_target_pairs={{0,7},{1,0},{2,1},{3,2},{4,3},{5,4},{6,5},{7,6},{8,15},{9,8},{10,9... | collective-permute-start | bytes 1253384 | tf_op jit(solution)/shard_map/ppermute | solution.py:38
  8.4 1.3 %pad_maximum_fusion.x_ref = f32[17,3,32,256]{3,2,1,0:T(8,128)} fusion(f32[1,3,32,256]{3,2,1,0:T(8,128)S(1)} %bitcast.26, f32[16,3,32,256]{3,2,1,0:T(8,128)S(1)} %broadcast_add_fusion), kind=kLoop, calls=%fused_computation.2 | loop fusion | flops 417792 | bytes 3342336 | tf_op jit(solution)/shard_map/concatenate | solution.py:151
  9.8 13.4 %collective-permute-done.up_ref = f32[17,3,8,256]{3,2,1,0:T(8,128)S(1)} collective-permute-done((f32[17,3,8,256]{3,2,1,0:T(8,128)S(1)}, f32[17,3,8,256]{3,2,1,0:T(8,128)S(1)}, u32[]{:S(2)}, u32[]{:S(2)}) %collective-permute-start) | collective-permute-done | bytes 417824 | tf_op jit(solution)/shard_map/ppermute | solution.py:38
  23.2 2.2 %collective-permute-done.1.down_ref = f32[17,3,8,256]{3,2,1,0:T(8,128)S(1)} collective-permute-done((f32[17,3,8,256]{3,2,1,0:T(8,128)S(1)}, f32[17,3,8,256]{3,2,1,0:T(8,128)S(1)}, u32[]{:S(2)}, u32[]{:S(2)}) %collective-permute-start.1) | collective-permute-done | bytes 417824 | tf_op jit(solution)/shard_map/ppermute | solution.py:38
  25.7 0.5 copy-done.2
  26.6 0.5 reshape.53
  27.2 0.5 reshape.55
  27.7 1.8 %collective-permute-start.3 = (f32[19584]{0:T(1024)S(1)}, f32[19584]{0:T(1024)S(1)}, u32[]{:S(2)}, u32[]{:S(2)}) collective-permute-start(f32[19584]{0:T(1024)S(1)} %reshape.55), channel_id=1, source_target_pairs={{0,24},{8,0},{16,8},{24,16},{1,25},{9,1},{17,9},{25,17},{2,26},{10... | collective-permute-start | bytes 235016 | tf_op jit(solution)/shard_map/ppermute | solution.py:40
  29.6 1.5 %collective-permute-done.2 = f32[19584]{0:T(1024)S(1)} collective-permute-done((f32[19584]{0:T(1024)S(1)}, f32[19584]{0:T(1024)S(1)}, u32[]{:S(2)}, u32[]{:S(2)}) %collective-permute-start.2) | collective-permute-done | bytes 78368 | tf_op jit(solution)/shard_map/ppermute | solution.py:40
  31.0 1.7 %reshape.54.west_ref = f32[17,3,48,8]{3,2,1,0:T(8,128)} reshape(f32[19584]{0:T(1024)S(1)} %collective-permute-done.2) | data formatting | bytes 156672 | tf_op jit(solution)/shard_map/reshape | solution.py:40
  32.8 1.7 %reshape.56.east_ref = f32[17,3,48,8]{3,2,1,0:T(8,128)} reshape(f32[19584]{0:T(1024)S(1)} %collective-permute-done.3) | data formatting | bytes 156672 | tf_op jit(solution)/shard_map/reshape | solution.py:40
  34.5 0.7 broadcast_in_dim.5.cor_ref
  35.2 25.2 %shard_map.41 = f32[16,3,32,256]{3,2,1,0:T(8,128)} custom-call(f32[48,384]{1,0:T(8,128)} %broadcast_in_dim.5.cor_ref, f32[17,3,32,256]{3,2,1,0:T(8,128)} %pad_maximum_fusion.x_ref, f32[17,3,8,256]{3,2,1,0:T(8,128)} %copy-done.1, f32[17,3,8,256]{3,2,1,0:T(8,128)} %copy-done.2, f32[17,3,48,8]{3,2,1,0:T(8,128)} %reshape.54.west_ref, ...), custom_call_target="tpu_custom_call" | custom-call | flops 564019200 | bytes 5431296 | tf_op jit(solution)/shard_map/pallas_call | solution.py:112
  60.5 5.4 %fusion.3 = f32[16,16]{0,1:T(8,128)S(1)} fusion(f32[16,3,32,256]{3,2,1,0:T(8,128)} %shard_map.41), kind=kOutput, calls=%fused_computation.10 | convolution fusion | flops 75497472 | bytes 1573888 | tf_op jit(solution)/shard_map/ifrc,jfrc->ij/dot_general | solution.py:154
  65.9 0.5 collective-permute-start.4
  66.4 0.8 collective-permute-done.4
  67.2 1.4 %collective-permute-start.5 = (f32[16,16]{0,1:T(8,128)S(1)}, f32[16,16]{0,1:T(8,128)S(1)}, u32[]{:S(2)}, u32[]{:S(2)}) collective-permute-start(f32[16,16]{0,1:T(8,128)S(1)} %add.77), channel_id=1, source_target_pairs={{0,16},{8,24},{16,0},{24,8},{1,17},{9,25},{17,1},{25,9},{2,18},{10... | collective-permute-start | bytes 3080 | tf_op jit(solution)/shard_map/ppermute | solution.py:164
  68.6 2.3 %collective-permute-done.5 = f32[16,16]{0,1:T(8,128)S(1)} collective-permute-done((f32[16,16]{0,1:T(8,128)S(1)}, f32[16,16]{0,1:T(8,128)S(1)}, u32[]{:S(2)}, u32[]{:S(2)}) %collective-permute-start.5) | collective-permute-done | bytes 1056 | tf_op jit(solution)/shard_map/ppermute | solution.py:164
  71.3 3.2 %collective-permute-done.6 = f32[16,16]{0,1:T(8,128)S(1)} collective-permute-done((f32[16,16]{0,1:T(8,128)S(1)}, f32[16,16]{0,1:T(8,128)S(1)}, u32[]{:S(2)}, u32[]{:S(2)}) %collective-permute-start.6) | collective-permute-done | bytes 1056 | tf_op jit(solution)/shard_map/ppermute | solution.py:164
  74.5 1.3 %collective-permute-start.7 = (f32[16,16]{0,1:T(8,128)S(1)}, f32[16,16]{0,1:T(8,128)S(1)}, u32[]{:S(2)}, u32[]{:S(2)}) collective-permute-start(f32[16,16]{0,1:T(8,128)S(1)} %add.79), channel_id=1, source_target_pairs={{0,2},{1,3},{2,0},{3,1},{4,6},{5,7},{6,4},{7,5},{8,10},{9,11},{10,... | collective-permute-start | bytes 3080 | tf_op jit(solution)/shard_map/ppermute | solution.py:164
  75.8 2.4 %collective-permute-done.7 = f32[16,16]{0,1:T(8,128)S(1)} collective-permute-done((f32[16,16]{0,1:T(8,128)S(1)}, f32[16,16]{0,1:T(8,128)S(1)}, u32[]{:S(2)}, u32[]{:S(2)}) %collective-permute-start.7) | collective-permute-done | bytes 1056 | tf_op jit(solution)/shard_map/ppermute | solution.py:164
  78.2 2.3 %collective-permute-start.8 = (f32[16,16]{0,1:T(8,128)S(1)}, f32[16,16]{0,1:T(8,128)S(1)}, u32[]{:S(2)}, u32[]{:S(2)}) collective-permute-start(f32[16,16]{0,1:T(8,128)S(1)} %add.80), channel_id=1, source_target_pairs={{0,4},{1,5},{2,6},{3,7},{4,0},{5,1},{6,2},{7,3},{8,12},{9,13},{10,... | collective-permute-start | bytes 3080 | tf_op jit(solution)/shard_map/ppermute | solution.py:164
  80.4 2.3 %collective-permute-done.8 = f32[16,16]{0,1:T(8,128)S(1)} collective-permute-done((f32[16,16]{0,1:T(8,128)S(1)}, f32[16,16]{0,1:T(8,128)S(1)}, u32[]{:S(2)}, u32[]{:S(2)}) %collective-permute-start.8) | collective-permute-done | bytes 1056 | tf_op jit(solution)/shard_map/ppermute | solution.py:164
  82.8 1.5 %cholesky.17 = f32[16,16]{1,0:T(8,128)S(1)} custom-call(f32[16,16]{1,0:T(8,128)S(1)} %fusion.9), custom_call_target="Cholesky" | custom-call | tf_op jit(solution)/shard_map/jit(cholesky)/cholesky | solution.py:166
  84.3 0.6 compare_reduce_fusion
  84.9 0.7 multiply_bitcast_fusion
  85.6 1.2 %custom-call.7 = f32[1,16,16]{1,2,0:T(8,128)S(1)} custom-call(f32[1,16,16]{2,1,0:T(8,128)S(1)} %get-tuple-element.11), custom_call_target="InvertDiagBlocksLowerTriangular" | custom-call | tf_op jit(solution)/shard_map/jit(_solve_triangular)/triangular_solve | solution.py:168
  87.0 2.2 %convolution_multiply_fusion = f32[16,3,32,256]{3,0,2,1:T(8,128)S(1)} fusion(f32[16,16,1,1]{1,0,3,2:T(8,128)S(1)} %convolution_bitcast_fusion, f32[16,3,32,256]{3,2,1,0:T(8,128)S(1)} %copy-done), kind=kOutput, calls=%fused_computation.6 | convolution fusion | flops 75890688 | bytes 3146752 | tf_op jit(solution)/shard_map/ij,jfrc->ifrc/dot_general | solution.py:170
  89.2 2.1 %copy.18 = f32[16,3,32,256]{3,2,1,0:T(8,128)} copy(f32[16,3,32,256]{3,0,2,1:T(8,128)S(1)} %convolution_multiply_fusion) | data formatting | bytes 3145728
  91.3 0.7 copy.19
  (23 shorter events, 1.6 us)
Async XLA Ops:
  0.6 1.6 %copy-start.3 = (f32[3,32,256]{2,1,0:T(8,128)S(1)}, f32[3,32,256]{2,1,0:T(8,128)}, u32[]{:S(2)}) copy-start(f32[3,32,256]{2,1,0:T(8,128)} %param.2) | copy-start | bytes 294916
  2.3 20.9 %collective-permute-start = (f32[17,3,8,256]{3,2,1,0:T(8,128)S(1)}, f32[17,3,8,256]{3,2,1,0:T(8,128)S(1)}, u32[]{:S(2)}, u32[]{:S(2)}) collective-permute-start(f32[17,3,8,256]{3,2,1,0:T(8,128)S(1)} %get-tuple-element.9), channel_id=1, source_target_pairs={{0,1},{1,2},{2,3},{3,4},{4,5},{5,6},{6,7},{7,0},{8,9},{9,10},{10,1... | collective-permute-start | bytes 1253384 | tf_op jit(solution)/shard_map/ppermute | solution.py:38
  5.3 20.1 %collective-permute-start.1 = (f32[17,3,8,256]{3,2,1,0:T(8,128)S(1)}, f32[17,3,8,256]{3,2,1,0:T(8,128)S(1)}, u32[]{:S(2)}, u32[]{:S(2)}) collective-permute-start(f32[17,3,8,256]{3,2,1,0:T(8,128)S(1)} %get-tuple-element.8), channel_id=1, source_target_pairs={{0,7},{1,0},{2,1},{3,2},{4,3},{5,4},{6,5},{7,6},{8,15},{9,8},{10,9... | collective-permute-start | bytes 1253384 | tf_op jit(solution)/shard_map/ppermute | solution.py:38
  23.2 2.5 %copy-start.1 = (f32[17,3,8,256]{3,2,1,0:T(8,128)}, f32[17,3,8,256]{3,2,1,0:T(8,128)S(1)}, u32[]{:S(2)}) copy-start(f32[17,3,8,256]{3,2,1,0:T(8,128)S(1)} %collective-permute-done.up_ref) | copy-start | bytes 1253380
  25.4 0.8 copy-start.2
  27.1 3.9 %collective-permute-start.2 = (f32[19584]{0:T(1024)S(1)}, f32[19584]{0:T(1024)S(1)}, u32[]{:S(2)}, u32[]{:S(2)}) collective-permute-start(f32[19584]{0:T(1024)S(1)} %reshape.53), channel_id=1, source_target_pairs={{0,8},{8,16},{16,24},{24,0},{1,9},{9,17},{17,25},{25,1},{2,10},{10... | collective-permute-start | bytes 235016 | tf_op jit(solution)/shard_map/ppermute | solution.py:40
  27.7 5.0 %collective-permute-start.3 = (f32[19584]{0:T(1024)S(1)}, f32[19584]{0:T(1024)S(1)}, u32[]{:S(2)}, u32[]{:S(2)}) collective-permute-start(f32[19584]{0:T(1024)S(1)} %reshape.55), channel_id=1, source_target_pairs={{0,24},{8,0},{16,8},{24,16},{1,25},{9,1},{17,9},{25,17},{2,26},{10... | collective-permute-start | bytes 235016 | tf_op jit(solution)/shard_map/ppermute | solution.py:40
  60.5 26.5 %copy-start = (f32[16,3,32,256]{3,2,1,0:T(8,128)S(1)}, f32[16,3,32,256]{3,2,1,0:T(8,128)}, u32[]{:S(2)}) copy-start(f32[16,3,32,256]{3,2,1,0:T(8,128)} %shard_map.41) | copy-start | bytes 4718596
  65.9 1.3 %collective-permute-start.4 = (f32[16,16]{0,1:T(8,128)S(1)}, f32[16,16]{0,1:T(8,128)S(1)}, u32[]{:S(2)}, u32[]{:S(2)}) collective-permute-start(f32[16,16]{0,1:T(8,128)S(1)} %fusion.3), channel_id=1, source_target_pairs={{0,8},{8,0},{16,24},{24,16},{1,9},{9,1},{17,25},{25,17},{2,10},{10... | collective-permute-start | bytes 3080 | tf_op jit(solution)/shard_map/ppermute | solution.py:164
  67.2 3.7 %collective-permute-start.5 = (f32[16,16]{0,1:T(8,128)S(1)}, f32[16,16]{0,1:T(8,128)S(1)}, u32[]{:S(2)}, u32[]{:S(2)}) collective-permute-start(f32[16,16]{0,1:T(8,128)S(1)} %add.77), channel_id=1, source_target_pairs={{0,16},{8,24},{16,0},{24,8},{1,17},{9,25},{17,1},{25,9},{2,18},{10... | collective-permute-start | bytes 3080 | tf_op jit(solution)/shard_map/ppermute | solution.py:164
  70.9 3.7 %collective-permute-start.6 = (f32[16,16]{0,1:T(8,128)S(1)}, f32[16,16]{0,1:T(8,128)S(1)}, u32[]{:S(2)}, u32[]{:S(2)}) collective-permute-start(f32[16,16]{0,1:T(8,128)S(1)} %add.78), channel_id=1, source_target_pairs={{0,1},{1,0},{2,3},{3,2},{4,5},{5,4},{6,7},{7,6},{8,9},{9,8},{10,11... | collective-permute-start | bytes 3080 | tf_op jit(solution)/shard_map/ppermute | solution.py:164
  74.5 3.7 %collective-permute-start.7 = (f32[16,16]{0,1:T(8,128)S(1)}, f32[16,16]{0,1:T(8,128)S(1)}, u32[]{:S(2)}, u32[]{:S(2)}) collective-permute-start(f32[16,16]{0,1:T(8,128)S(1)} %add.79), channel_id=1, source_target_pairs={{0,2},{1,3},{2,0},{3,1},{4,6},{5,7},{6,4},{7,5},{8,10},{9,11},{10,... | collective-permute-start | bytes 3080 | tf_op jit(solution)/shard_map/ppermute | solution.py:164
  78.2 4.5 %collective-permute-start.8 = (f32[16,16]{0,1:T(8,128)S(1)}, f32[16,16]{0,1:T(8,128)S(1)}, u32[]{:S(2)}, u32[]{:S(2)}) collective-permute-start(f32[16,16]{0,1:T(8,128)S(1)} %add.80), channel_id=1, source_target_pairs={{0,4},{1,5},{2,6},{3,7},{4,0},{5,1},{6,2},{7,3},{8,12},{9,13},{10,... | collective-permute-start | bytes 3080 | tf_op jit(solution)/shard_map/ppermute | solution.py:164

commit v6 on v3

--- a/solution.py
+++ b/solution.py
@@ -19,33 +19,32 @@
 two_pi = 2.0 * math.pi
 
 
-def ring_halo(value, width, lanes):
-    rows, cols = (value.shape[-2], value.shape[-1])
+def row_halo(value, width):
+    rows = value.shape[-2]
+    top, bottom = (value[..., :width, :], value[..., rows - width :, :])
+    return (shift(bottom, "gy", 0, 1, flatten=False), shift(top, "gy", 0, -1, flatten=False))
+
+
+def column_halo(value, above, below, width):
+    cols = value.shape[-1]
+    tall = jnp.concatenate([value, below, above], axis=-2)
+    return (shift(tall[..., cols - width :], "gx", 1, 0), shift(tall[..., :width], "gx", -1, 0))
+
+
+def shift(part, axes, dx, dy, flatten=True):
     across, down = (lax.axis_size("gx"), lax.axis_size("gy"))
-
-    def shift(part, axes, dx, dy, flatten=True):
-        pairs = []
-        for x in range(across):
-            for y in range(down):
-                target = ((x + dx) % across, (y + dy) % down)
-                if axes == "gx":
-                    pairs.append((x, target[0])) if y == 0 else None
-                elif axes == "gy":
-                    pairs.append((y, target[1])) if x == 0 else None
-                else:
-                    pairs.append((x * down + y, target[0] * down + target[1]))
-        if not flatten:
-            return lax.ppermute(part, axes, pairs)
-        flat = part.reshape(-1)
-        return lax.ppermute(flat, axes, pairs).reshape(part.shape)
-
-    top, bottom = (value[..., :width, :], value[..., rows - width :, :])
-    above = shift(bottom, "gy", 0, 1, flatten=False)
-    below = shift(top, "gy", 0, -1, flatten=False)
-    tall = jnp.concatenate([value, below, above], axis=-2)
-    west = shift(tall[..., cols - width :], "gx", 1, 0)
-    east = shift(tall[..., :width], "gx", -1, 0)
-    return above, below, west, east
+    pairs = []
+    for x in range(across):
+        for y in range(down):
+            target = ((x + dx) % across, (y + dy) % down)
+            if axes == "gx":
+                pairs.append((x, target[0])) if y == 0 else None
+            else:
+                pairs.append((y, target[1])) if x == 0 else None
+    if not flatten:
+        return lax.ppermute(part, axes, pairs)
+    flat = part.reshape(-1)
+    return lax.ppermute(flat, axes, pairs).reshape(part.shape)
 
 
 def forecast_kernel(cor_ref, x_ref, up_ref, down_ref, west_ref, east_ref, o_ref, ring, east_pad, west_pad, *, steps):
@@ -141,8 +140,16 @@
     coriolis = jnp.broadcast_to(coriolis[:, None], (ring_rows, lanes))
 
     states = jnp.concatenate([control[None], control[None] + perts], 0)
-    above, below, west, east = ring_halo(states, margin, lanes)
-    current = forecast(coriolis, states, above, below, west, east, STEPS)
+    split = (states.shape[0] + 1) // 2
+    first_part, second_part = (states[:split], states[split:])
+    above, below = row_halo(first_part, margin)
+    above, below, second_part = lax.optimization_barrier((above, below, second_part))
+    later_above, later_below = row_halo(second_part, margin)
+    outputs = []
+    for part, up, down_ in ((first_part, above, below), (second_part, later_above, later_below)):
+        west, east = column_halo(part, up, down_, margin)
+        outputs.append(forecast(coriolis, part, up, down_, west, east, STEPS))
+    current = jnp.concatenate(outputs, 0)
     bred = current[1:] - current[0:1]
     flat = bred.reshape(MEMBERS, -1)
     local_gram = jnp.dot(flat, flat.T, precision=lax.Precision.HIGHEST)

time: 90.2 us -> 93.6 us (1.038)
  starting transfers between devices: 13.8 us -> 16.7 us
  Pallas kernels: 24.9 us -> 26.6 us
  local copies, waits for them, and re-layouts: 10.3 us -> 12 us
  other arithmetic: 8.83 us -> 7.17 us
  waiting for transfers between devices: 27.2 us -> 25.8 us
    ppermute x2 -> x4, waiting for transfers between devices: 15.6 us -> 9.33 us  [shift(): return lax.ppermute(part, axes, pairs)]
    ppermute x5, waiting for transfers between devices: 10.1 us -> 13.2 us  [body(): gram = gram + lax.ppermute(gram, axis, pairs)]
    ppermute x2 -> x4, starting transfers between devices: 6.12 us -> 8.64 us  [shift(): return lax.ppermute(part, axes, pairs)]
    ppermute x2 -> x4, starting transfers between devices: 1.83 us -> 3.84 us  [shift(): return lax.ppermute(flat, axes, pairs).reshape(part.shape)]
    ppermute x2 -> x4, waiting for transfers between devices: 1.48 us -> 3.27 us  [shift(): return lax.ppermute(flat, axes, pairs).reshape(part.shape)]
    pallas_call x1 -> x2, Pallas kernels: 24.9 us -> 26.6 us  [forecast(): pl.pallas_call(functools.partial(forecast_kernel, steps=steps), out_shape...]
    ppermute x5, starting transfers between devices: 5.87 us -> 4.22 us  [body(): gram = gram + lax.ppermute(gram, axis, pairs)]
    reshape x2 -> x4, local copies, waits for them, and re-layouts: 3.43 us -> 4.75 us  [shift(): return lax.ppermute(flat, axes, pairs).reshape(part.shape)]
  transfers between devices with their start and end apart: 9 -> 13, of which waited for: 8 -> 9; matrix products, arithmetic and copies ran while one was open for 5% -> 7% of each run, Pallas kernels for 0% -> 15%
where the time goes in v6:
time: 93.6 us; the launch traced here: 93.3 us
  Pallas kernels  26.6 us (28%)
  waiting for transfers between devices  25.8 us (28%)
  starting transfers between devices  16.7 us (18%)
  local copies, waits for them, and re-layouts  12 us (13%)
  other arithmetic  7.17 us (8%)
  matrix products  4.21 us (4%)
    pallas_call x2, Pallas kernels, forecast(): pl.pallas_call(functools.partial(forecast_kernel, steps=steps), out_shape...  26.6 us
    ppermute x5, waiting for transfers between devices, body(): gram = gram + lax.ppermute(gram, axis, pairs)  13.2 us
    ppermute x4, waiting for transfers between devices, shift(): return lax.ppermute(part, axes, pairs)  9.33 us
    ppermute x4, starting transfers between devices, shift(): return lax.ppermute(part, axes, pairs)  8.64 us
    reshape x4, local copies, waits for them, and re-layouts, shift(): return lax.ppermute(flat, axes, pairs).reshape(part.shape)  4.75 us
    ppermute x5, starting transfers between devices, body(): gram = gram + lax.ppermute(gram, axis, pairs)  4.22 us
    unnamed x21, local copies, waits for them, and re-layouts  4.02 us
    ppermute x4, starting transfers between devices, shift(): return lax.ppermute(flat, axes, pairs).reshape(part.shape)  3.84 us
  transfers between devices with their start and end apart: 13, of which 9 were waited for; matrix products, arithmetic and copies ran while one was open for 7% of the time, Pallas kernels for 15%

profile of v6, /device:TPU:0, one launch (start us, length us, event | category | flops | bytes accessed | tf_op | source)
XLA Modules:
  0.0 93.3 jit_solution(2894457676469563347)
XLA Ops:
  0.6 1.6 %broadcast_add_fusion = f32[16,3,32,256]{3,2,1,0:T(8,128)S(1)} fusion(f32[16,3,32,256]{3,2,1,0:T(8,128)} %param.3, f32[3,32,256]{2,1,0:T(8,128)} %param.2), kind=kLoop, calls=%fused_computation.12 | loop fusion | flops 393216 | bytes 3244032 | tf_op jit(solution)/shard_map/add | solution.py:142
  2.3 6.1 %collective-permute-start.1 = (f32[9,3,8,256]{3,2,1,0:T(8,128)S(1)}, f32[9,3,8,256]{3,2,1,0:T(8,128)S(1)}, u32[]{:S(2)}, u32[]{:S(2)}) collective-permute-start(f32[9,3,8,256]{3,2,1,0:T(8,128)S(1)} %get-tuple-element.12), channel_id=1, source_target_pairs={{0,7},{1,0},{2,1},{3,2},{4,3},{5,4},{6,5},{7,6},{8,15},{9,8},{10,9... | collective-permute-start | bytes 663560 | tf_op jit(solution)/shard_map/ppermute | solution.py:45
  8.6 4.4 %collective-permute-done.1.down_ref = f32[9,3,8,256]{3,2,1,0:T(8,128)S(1)} collective-permute-done((f32[9,3,8,256]{3,2,1,0:T(8,128)S(1)}, f32[9,3,8,256]{3,2,1,0:T(8,128)S(1)}, u32[]{:S(2)}, u32[]{:S(2)}) %collective-permute-start.1) | collective-permute-done | bytes 221216 | tf_op jit(solution)/shard_map/ppermute | solution.py:45
  13.0 4.9 %collective-permute-done.up_ref = f32[9,3,8,256]{3,2,1,0:T(8,128)S(1)} collective-permute-done((f32[9,3,8,256]{3,2,1,0:T(8,128)S(1)}, f32[9,3,8,256]{3,2,1,0:T(8,128)S(1)}, u32[]{:S(2)}, u32[]{:S(2)}) %collective-permute-start) | collective-permute-done | bytes 221216 | tf_op jit(solution)/shard_map/ppermute | solution.py:45
  17.9 0.7 fusion.20
  18.7 2.6 %collective-permute-start.5 = (f32[8,3,8,256]{3,2,1,0:T(8,128)}, f32[8,3,8,256]{3,2,1,0:T(8,128)S(1)}, u32[]{:S(2)}, u32[]{:S(2)}) collective-permute-start(f32[8,3,8,256]{3,2,1,0:T(8,128)} %get-tuple-element.18), channel_id=1, source_target_pairs={{0,7},{1,0},{2,1},{3,2},{4,3},{5,4},{6,5},{7,6},{8,15},{9,8},{10,9... | collective-permute-start | bytes 589832 | tf_op jit(solution)/shard_map/ppermute | solution.py:45
  22.3 1.7 %collective-permute-start.3 = (f32[10368]{0:T(1024)S(1)}, f32[10368]{0:T(1024)S(1)}, u32[]{:S(2)}, u32[]{:S(2)}) collective-permute-start(f32[10368]{0:T(1024)S(1)} %reshape.73), channel_id=1, source_target_pairs={{0,24},{8,0},{16,8},{24,16},{1,25},{9,1},{17,9},{25,17},{2,26},{10... | collective-permute-start | bytes 124424 | tf_op jit(solution)/shard_map/ppermute | solution.py:47
  24.1 1.6 %collective-permute-done.3 = f32[10368]{0:T(1024)S(1)} collective-permute-done((f32[10368]{0:T(1024)S(1)}, f32[10368]{0:T(1024)S(1)}, u32[]{:S(2)}, u32[]{:S(2)}) %collective-permute-start.3) | collective-permute-done | bytes 41504 | tf_op jit(solution)/shard_map/ppermute | solution.py:47
  25.8 1.2 %reshape.74.east_ref = f32[9,3,48,8]{3,2,1,0:T(8,128)} reshape(f32[10368]{0:T(1024)S(1)} %collective-permute-done.3) | data formatting | bytes 82944 | tf_op jit(solution)/shard_map/reshape | solution.py:47
  27.0 1.2 %reshape.72.west_ref = f32[9,3,48,8]{3,2,1,0:T(8,128)} reshape(f32[10368]{0:T(1024)S(1)} %collective-permute-done.2) | data formatting | bytes 82944 | tf_op jit(solution)/shard_map/reshape | solution.py:47
  28.2 0.7 broadcast_in_dim.5.cor_ref
  28.9 14.0 %shard_map.41 = f32[9,3,32,256]{3,2,1,0:T(8,128)} custom-call(f32[48,384]{1,0:T(8,128)} %broadcast_in_dim.5.cor_ref, f32[9,3,32,256]{3,2,1,0:T(8,128)} %copy-done.1, f32[9,3,8,256]{3,2,1,0:T(8,128)} %copy-done.5, f32[9,3,8,256]{3,2,1,0:T(8,128)} %copy-done.4, f32[9,3,48,8]{3,2,1,0:T(8,128)} %reshape.72.west_ref, f32[9,3,48,8]{3,2,1,0:T(8,128)} %reshape.74.east_ref), custom_call_target="tpu_custom_call" | custom-call | flops 298598400 | bytes 2875392 | tf_op jit(solution)/shard_map/pallas_call | solution.py:104
  43.0 0.7 copy-done.7
  44.5 2.0 %collective-permute-start.6 = (f32[9216]{0:T(1024)S(1)}, f32[9216]{0:T(1024)S(1)}, u32[]{:S(2)}, u32[]{:S(2)}) collective-permute-start(f32[9216]{0:T(1024)S(1)} %reshape.75), channel_id=1, source_target_pairs={{0,8},{8,16},{16,24},{24,0},{1,9},{9,17},{17,25},{25,1},{2,10},{10... | collective-permute-start | bytes 110600 | tf_op jit(solution)/shard_map/ppermute | solution.py:47
  46.6 1.6 %collective-permute-done.7 = f32[9216]{0:T(1024)S(1)} collective-permute-done((f32[9216]{0:T(1024)S(1)}, f32[9216]{0:T(1024)S(1)}, u32[]{:S(2)}, u32[]{:S(2)}) %collective-permute-start.7) | collective-permute-done | bytes 36896 | tf_op jit(solution)/shard_map/ppermute | solution.py:47
  48.2 1.1 %reshape.78.east_ref = f32[8,3,48,8]{3,2,1,0:T(8,128)} reshape(f32[9216]{0:T(1024)S(1)} %collective-permute-done.7) | data formatting | bytes 73728 | tf_op jit(solution)/shard_map/reshape | solution.py:47
  49.3 1.2 %reshape.76.west_ref = f32[8,3,48,8]{3,2,1,0:T(8,128)} reshape(f32[9216]{0:T(1024)S(1)} %collective-permute-done.6) | data formatting | bytes 73728 | tf_op jit(solution)/shard_map/reshape | solution.py:47
  50.5 12.6 %shard_map.42 = f32[8,3,32,256]{3,2,1,0:T(8,128)} custom-call(f32[48,384]{1,0:T(8,128)} %broadcast_in_dim.5.cor_ref, f32[8,3,32,256]{3,2,1,0:T(8,128)} %copy-done, f32[8,3,8,256]{3,2,1,0:T(8,128)} %copy-done.7, f32[8,3,8,256]{3,2,1,0:T(8,128)} %copy-done.6, f32[8,3,48,8]{3,2,1,0:T(8,128)} %reshape.76.west_ref, f32[8,3,48,8]{3,2,1,0:T(8,128)} %reshape.78.east_ref), custom_call_target="tpu_custom_call" | custom-call | flops 265420800 | bytes 2555904 | tf_op jit(solution)/shard_map/pallas_call | solution.py:104
  63.1 1.3 %fusion = f32[16,3,32,256]{3,2,1,0:T(8,128)S(1)} fusion(f32[8,3,32,256]{3,2,1,0:T(8,128)} %shard_map.42, f32[9,3,32,256]{3,2,1,0:T(8,128)S(1)} %copy-done.2, f32[3,32,256]{2,1,0:T(8,128)S(1)} %slice_bitcast_fusion), kind=kLoop, calls=%fused_computation.6 | loop fusion | flops 786432 | bytes 3342336 | tf_op jit(solution)/shard_map/sub | solution.py:153
  64.4 2.7 %fusion.3 = f32[16,16]{0,1:T(8,128)S(1)} fusion(f32[16,3,32,256]{3,2,1,0:T(8,128)S(1)} %fusion), kind=kOutput, calls=%fused_computation.10 | convolution fusion | flops 75497472 | bytes 1573888 | tf_op jit(solution)/shard_map/dot_general | solution.py:155
  67.1 2.0 %collective-permute-start.8 = (f32[16,16]{0,1:T(8,128)S(1)}, f32[16,16]{0,1:T(8,128)S(1)}, u32[]{:S(2)}, u32[]{:S(2)}) collective-permute-start(f32[16,16]{0,1:T(8,128)S(1)} %fusion.3), channel_id=1, source_target_pairs={{0,8},{8,0},{16,24},{24,16},{1,9},{9,1},{17,25},{25,17},{2,10},{10... | collective-permute-start | bytes 3080 | tf_op jit(solution)/shard_map/ppermute | solution.py:165
  69.0 0.8 collective-permute-done.8
  70.1 3.4 %collective-permute-done.9 = f32[16,16]{0,1:T(8,128)S(1)} collective-permute-done((f32[16,16]{0,1:T(8,128)S(1)}, f32[16,16]{0,1:T(8,128)S(1)}, u32[]{:S(2)}, u32[]{:S(2)}) %collective-permute-start.9) | collective-permute-done | bytes 1056 | tf_op jit(solution)/shard_map/ppermute | solution.py:165
  74.1 3.1 %collective-permute-done.10 = f32[16,16]{0,1:T(8,128)S(1)} collective-permute-done((f32[16,16]{0,1:T(8,128)S(1)}, f32[16,16]{0,1:T(8,128)S(1)}, u32[]{:S(2)}, u32[]{:S(2)}) %collective-permute-start.10) | collective-permute-done | bytes 1056 | tf_op jit(solution)/shard_map/ppermute | solution.py:165
  77.2 3.6 %collective-permute-done.11 = f32[16,16]{0,1:T(8,128)S(1)} collective-permute-done((f32[16,16]{0,1:T(8,128)S(1)}, f32[16,16]{0,1:T(8,128)S(1)}, u32[]{:S(2)}, u32[]{:S(2)}) %collective-permute-start.11) | collective-permute-done | bytes 1056 | tf_op jit(solution)/shard_map/ppermute | solution.py:165
  80.8 1.5 %collective-permute-start.12 = (f32[16,16]{0,1:T(8,128)S(1)}, f32[16,16]{0,1:T(8,128)S(1)}, u32[]{:S(2)}, u32[]{:S(2)}) collective-permute-start(f32[16,16]{0,1:T(8,128)S(1)} %add.80), channel_id=1, source_target_pairs={{0,4},{1,5},{2,6},{3,7},{4,0},{5,1},{6,2},{7,3},{8,12},{9,13},{10,... | collective-permute-start | bytes 3080 | tf_op jit(solution)/shard_map/ppermute | solution.py:165
  82.3 0.9 copy.19
  83.3 2.1 %collective-permute-done.12 = f32[16,16]{0,1:T(8,128)S(1)} collective-permute-done((f32[16,16]{0,1:T(8,128)S(1)}, f32[16,16]{0,1:T(8,128)S(1)}, u32[]{:S(2)}, u32[]{:S(2)}) %collective-permute-start.12) | collective-permute-done | bytes 1056 | tf_op jit(solution)/shard_map/ppermute | solution.py:165
  85.5 1.5 %cholesky.16 = f32[16,16]{1,0:T(8,128)S(1)} custom-call(f32[16,16]{1,0:T(8,128)S(1)} %fusion.9), custom_call_target="Cholesky" | custom-call | tf_op jit(solution)/shard_map/jit(cholesky)/cholesky | solution.py:167
  88.9 1.2 %custom-call.7 = f32[1,16,16]{1,2,0:T(8,128)S(1)} custom-call(f32[1,16,16]{2,1,0:T(8,128)S(1)} %get-tuple-element.21), custom_call_target="InvertDiagBlocksLowerTriangular" | custom-call | tf_op jit(solution)/shard_map/jit(_solve_triangular)/triangular_solve | solution.py:168
  90.2 1.5 %convolution_multiply_fusion = f32[16,24576]{1,0:T(8,128)S(1)} fusion(f32[16,24576]{1,0:T(8,128)S(1)} %bitcast.34, f32[1,16,16]{1,2,0:T(8,128)S(1)} %custom-call.7), kind=kOutput, calls=%fused_computation | convolution fusion | flops 75890688 | bytes 3146752 | tf_op jit(solution)/shard_map/jit(_solve_triangular)/triangular_solve | solution.py:168
  91.7 1.6 %copy.20 = f32[2,8,96,256]{3,2,1,0:T(8,128)} copy(f32[2,8,96,256]{3,1,2,0:T(8,128)S(1)} %bitcast.35) | data formatting | bytes 3145728
  (52 shorter events, 5.1 us)
Async XLA Ops:
  0.6 1.6 %copy-start.3 = (f32[3,32,256]{2,1,0:T(8,128)S(1)}, f32[3,32,256]{2,1,0:T(8,128)}, u32[]{:S(2)}) copy-start(f32[3,32,256]{2,1,0:T(8,128)} %param.2) | copy-start | bytes 294916
  2.3 10.7 %collective-permute-start.1 = (f32[9,3,8,256]{3,2,1,0:T(8,128)S(1)}, f32[9,3,8,256]{3,2,1,0:T(8,128)S(1)}, u32[]{:S(2)}, u32[]{:S(2)}) collective-permute-start(f32[9,3,8,256]{3,2,1,0:T(8,128)S(1)} %get-tuple-element.12), channel_id=1, source_target_pairs={{0,7},{1,0},{2,1},{3,2},{4,3},{5,4},{6,5},{7,6},{8,15},{9,8},{10,9... | collective-permute-start | bytes 663560 | tf_op jit(solution)/shard_map/ppermute | solution.py:45
  8.3 9.6 %collective-permute-start = (f32[9,3,8,256]{3,2,1,0:T(8,128)S(1)}, f32[9,3,8,256]{3,2,1,0:T(8,128)S(1)}, u32[]{:S(2)}, u32[]{:S(2)}) collective-permute-start(f32[9,3,8,256]{3,2,1,0:T(8,128)S(1)} %get-tuple-element.13), channel_id=1, source_target_pairs={{0,1},{1,2},{2,3},{3,4},{4,5},{5,6},{6,7},{7,0},{8,9},{9,10},{10,1... | collective-permute-start | bytes 663560 | tf_op jit(solution)/shard_map/ppermute | solution.py:45
  8.4 15.7 %copy-start = (f32[8,3,32,256]{3,2,1,0:T(8,128)}, f32[8,3,32,256]{3,2,1,0:T(8,128)S(1)}, u32[]{:S(2)}) copy-start(f32[8,3,32,256]{3,2,1,0:T(8,128)S(1)} %slice.66.x_ref) | copy-start | bytes 2359300
  8.6 12.8 %copy-start.1 = (f32[9,3,32,256]{3,2,1,0:T(8,128)}, f32[9,3,32,256]{3,2,1,0:T(8,128)S(1)}, u32[]{:S(2)}) copy-start(f32[9,3,32,256]{3,2,1,0:T(8,128)S(1)} %fusion.6.x_ref) | copy-start | bytes 2654212
  13.0 8.4 %copy-start.4 = (f32[9,3,8,256]{3,2,1,0:T(8,128)}, f32[9,3,8,256]{3,2,1,0:T(8,128)S(1)}, u32[]{:S(2)}) copy-start(f32[9,3,8,256]{3,2,1,0:T(8,128)S(1)} %collective-permute-done.1.down_ref) | copy-start | bytes 663556
  17.9 3.5 %copy-start.5 = (f32[9,3,8,256]{3,2,1,0:T(8,128)}, f32[9,3,8,256]{3,2,1,0:T(8,128)S(1)}, u32[]{:S(2)}) copy-start(f32[9,3,8,256]{3,2,1,0:T(8,128)S(1)} %collective-permute-done.up_ref) | copy-start | bytes 663556
  18.7 24.3 %collective-permute-start.5 = (f32[8,3,8,256]{3,2,1,0:T(8,128)}, f32[8,3,8,256]{3,2,1,0:T(8,128)S(1)}, u32[]{:S(2)}, u32[]{:S(2)}) collective-permute-start(f32[8,3,8,256]{3,2,1,0:T(8,128)} %get-tuple-element.18), channel_id=1, source_target_pairs={{0,7},{1,0},{2,1},{3,2},{4,3},{5,4},{6,5},{7,6},{8,15},{9,8},{10,9... | collective-permute-start | bytes 589832 | tf_op jit(solution)/shard_map/ppermute | solution.py:45
  21.2 21.7 %collective-permute-start.4 = (f32[8,3,8,256]{3,2,1,0:T(8,128)S(1)}, f32[8,3,8,256]{3,2,1,0:T(8,128)S(1)}, u32[]{:S(2)}, u32[]{:S(2)}) collective-permute-start(f32[8,3,8,256]{3,2,1,0:T(8,128)S(1)} %get-tuple-element.19), channel_id=1, source_target_pairs={{0,1},{1,2},{2,3},{3,4},{4,5},{5,6},{6,7},{7,0},{8,9},{9,10},{10,1... | collective-permute-start | bytes 589832 | tf_op jit(solution)/shard_map/ppermute | solution.py:45
  22.3 4.7 %collective-permute-start.2 = (f32[10368]{0:T(1024)S(1)}, f32[10368]{0:T(1024)S(1)}, u32[]{:S(2)}, u32[]{:S(2)}) collective-permute-start(f32[10368]{0:T(1024)S(1)} %reshape.71), channel_id=1, source_target_pairs={{0,8},{8,16},{16,24},{24,0},{1,9},{9,17},{17,25},{25,1},{2,10},{10... | collective-permute-start | bytes 124424 | tf_op jit(solution)/shard_map/ppermute | solution.py:47
  22.3 3.4 %collective-permute-start.3 = (f32[10368]{0:T(1024)S(1)}, f32[10368]{0:T(1024)S(1)}, u32[]{:S(2)}, u32[]{:S(2)}) collective-permute-start(f32[10368]{0:T(1024)S(1)} %reshape.73), channel_id=1, source_target_pairs={{0,24},{8,0},{16,8},{24,16},{1,25},{9,1},{17,9},{25,17},{2,26},{10... | collective-permute-start | bytes 124424 | tf_op jit(solution)/shard_map/ppermute | solution.py:47
  42.9 1.0 %copy-start.6 = (f32[8,3,8,256]{3,2,1,0:T(8,128)}, f32[8,3,8,256]{3,2,1,0:T(8,128)S(1)}, u32[]{:S(2)}) copy-start(f32[8,3,8,256]{3,2,1,0:T(8,128)S(1)} %collective-permute-done.5.down_ref) | copy-start | bytes 589828
  43.0 0.7 copy-start.7
  43.7 2.8 %copy-start.2 = (f32[9,3,32,256]{3,2,1,0:T(8,128)S(1)}, f32[9,3,32,256]{3,2,1,0:T(8,128)}, u32[]{:S(2)}) copy-start(f32[9,3,32,256]{3,2,1,0:T(8,128)} %shard_map.41) | copy-start | bytes 2654212
  44.5 4.8 %collective-permute-start.6 = (f32[9216]{0:T(1024)S(1)}, f32[9216]{0:T(1024)S(1)}, u32[]{:S(2)}, u32[]{:S(2)}) collective-permute-start(f32[9216]{0:T(1024)S(1)} %reshape.75), channel_id=1, source_target_pairs={{0,8},{8,16},{16,24},{24,0},{1,9},{9,17},{17,25},{25,1},{2,10},{10... | collective-permute-start | bytes 110600 | tf_op jit(solution)/shard_map/ppermute | solution.py:47
  46.5 1.7 %collective-permute-start.7 = (f32[9216]{0:T(1024)S(1)}, f32[9216]{0:T(1024)S(1)}, u32[]{:S(2)}, u32[]{:S(2)}) collective-permute-start(f32[9216]{0:T(1024)S(1)} %reshape.77), channel_id=1, source_target_pairs={{0,24},{8,0},{16,8},{24,16},{1,25},{9,1},{17,9},{25,17},{2,26},{10... | collective-permute-start | bytes 110600 | tf_op jit(solution)/shard_map/ppermute | solution.py:47
  67.1 2.8 %collective-permute-start.8 = (f32[16,16]{0,1:T(8,128)S(1)}, f32[16,16]{0,1:T(8,128)S(1)}, u32[]{:S(2)}, u32[]{:S(2)}) collective-permute-start(f32[16,16]{0,1:T(8,128)S(1)} %fusion.3), channel_id=1, source_target_pairs={{0,8},{8,0},{16,24},{24,16},{1,9},{9,1},{17,25},{25,17},{2,10},{10... | collective-permute-start | bytes 3080 | tf_op jit(solution)/shard_map/ppermute | solution.py:165
  69.9 3.7 %collective-permute-start.9 = (f32[16,16]{0,1:T(8,128)S(1)}, f32[16,16]{0,1:T(8,128)S(1)}, u32[]{:S(2)}, u32[]{:S(2)}) collective-permute-start(f32[16,16]{0,1:T(8,128)S(1)} %add.77), channel_id=1, source_target_pairs={{0,16},{8,24},{16,0},{24,8},{1,17},{9,25},{17,1},{25,9},{2,18},{10... | collective-permute-start | bytes 3080 | tf_op jit(solution)/shard_map/ppermute | solution.py:165
  73.5 3.7 %collective-permute-start.10 = (f32[16,16]{0,1:T(8,128)S(1)}, f32[16,16]{0,1:T(8,128)S(1)}, u32[]{:S(2)}, u32[]{:S(2)}) collective-permute-start(f32[16,16]{0,1:T(8,128)S(1)} %add.78), channel_id=1, source_target_pairs={{0,1},{1,0},{2,3},{3,2},{4,5},{5,4},{6,7},{7,6},{8,9},{9,8},{10,11... | collective-permute-start | bytes 3080 | tf_op jit(solution)/shard_map/ppermute | solution.py:165
  77.2 3.7 %collective-permute-start.11 = (f32[16,16]{0,1:T(8,128)S(1)}, f32[16,16]{0,1:T(8,128)S(1)}, u32[]{:S(2)}, u32[]{:S(2)}) collective-permute-start(f32[16,16]{0,1:T(8,128)S(1)} %add.79), channel_id=1, source_target_pairs={{0,2},{1,3},{2,0},{3,1},{4,6},{5,7},{6,4},{7,5},{8,10},{9,11},{10,... | collective-permute-start | bytes 3080 | tf_op jit(solution)/shard_map/ppermute | solution.py:165
  80.8 4.6 %collective-permute-start.12 = (f32[16,16]{0,1:T(8,128)S(1)}, f32[16,16]{0,1:T(8,128)S(1)}, u32[]{:S(2)}, u32[]{:S(2)}) collective-permute-start(f32[16,16]{0,1:T(8,128)S(1)} %add.80), channel_id=1, source_target_pairs={{0,4},{1,5},{2,6},{3,7},{4,0},{5,1},{6,2},{7,3},{8,12},{9,13},{10,... | collective-permute-start | bytes 3080 | tf_op jit(solution)/shard_map/ppermute | solution.py:165

commit v7 on v3

--- a/solution.py
+++ b/solution.py
@@ -50,7 +50,7 @@
 
 def forecast_kernel(cor_ref, x_ref, up_ref, down_ref, west_ref, east_ref, o_ref, ring, east_pad, west_pad, *, steps):
     rows, cols = (x_ref.shape[-2], x_ref.shape[-1])
-    R, C = cor_ref.shape
+    R, C = ring.shape[-2:]
     width = up_ref.shape[-2]
     spare = C - cols
 
@@ -68,24 +68,24 @@
         west_pad[:, :width] = west_ref[0, k]
         ring[k, :, cols:] = east_pad[...] + pltpu.roll(west_pad[...], spare - width, 1)
 
-    f = cor_ref[...]
-    third = 1.0 / 12.0
+    f = jnp.broadcast_to(cor_ref[...], (R, C))
+    scale = -1.0 / 12.0
 
     def dx(v):
         g = pltpu.roll(v, C - 1, 1) - pltpu.roll(v, 1, 1)
         w = pltpu.roll(v, C - 2, 1) - pltpu.roll(v, 2, 1)
-        return (8.0 * g - w) * third
+        return 8.0 * g - w
 
     def dy(v):
         g = pltpu.roll(v, R - 1, 0) - pltpu.roll(v, 1, 0)
         w = pltpu.roll(v, R - 2, 0) - pltpu.roll(v, 2, 0)
-        return (8.0 * g - w) * third
+        return 8.0 * g - w
 
     def tend(h, e, n):
         depth = 4.0 + h
-        ch = -(dx(depth * e) + dy(depth * n))
-        ce = -(e * dx(e) + n * dy(e)) + f * n - dx(h)
-        cn = -(e * dx(n) + n * dy(n)) - f * e - dy(h)
+        ch = scale * (dx(depth * e) + dy(depth * n))
+        ce = scale * (e * dx(e) + n * dy(e) + dx(h)) + f * n
+        cn = scale * (e * dx(n) + n * dy(n) + dy(h)) - f * e
         return ch, ce, cn
 
     s = (ring[0], ring[1], ring[2])
@@ -98,16 +98,16 @@
         o_ref[0, k] = s[k][:rows, :cols]
 
 
-def forecast(cor, value, above, below, west, east, steps):
+def forecast(cor, value, above, below, west, east, steps, lanes):
     S, F, rows, cols = value.shape
-    R, C = cor.shape
     width = above.shape[-2]
+    R, C = (cor.shape[0], lanes)
     return pl.pallas_call(
         functools.partial(forecast_kernel, steps=steps),
         out_shape=jax.ShapeDtypeStruct((S, F, rows, cols), jnp.float32),
         grid=(S,),
         in_specs=[
-            pl.BlockSpec((R, C), lambda i: (0, 0)),
+            pl.BlockSpec((R, 1), lambda i: (0, 0)),
             pl.BlockSpec((1, F, rows, cols), lambda i: (i, 0, 0, 0)),
             pl.BlockSpec((1, F, width, cols), lambda i: (i, 0, 0, 0)),
             pl.BlockSpec((1, F, width, cols), lambda i: (i, 0, 0, 0)),
@@ -138,11 +138,11 @@
     offsets = jnp.where(offsets < tile_rows + margin, offsets, offsets - ring_rows)
     rows = ((first_row + offsets) % grid_rows).astype(jnp.float32)
     coriolis = coriolis_mid * (1.0 + 0.5 * jnp.sin(two_pi * rows / float(grid_rows)))
-    coriolis = jnp.broadcast_to(coriolis[:, None], (ring_rows, lanes))
+    coriolis = coriolis[:, None]
 
     states = jnp.concatenate([control[None], control[None] + perts], 0)
     above, below, west, east = ring_halo(states, margin, lanes)
-    current = forecast(coriolis, states, above, below, west, east, STEPS)
+    current = forecast(coriolis, states, above, below, west, east, STEPS, lanes)
     bred = current[1:] - current[0:1]
     flat = bred.reshape(MEMBERS, -1)
     local_gram = jnp.dot(flat, flat.T, precision=lax.Precision.HIGHEST)

time: 90.2 us -> 91.7 us (1.017)
  local copies, waits for them, and re-layouts: 10.3 us -> 12.2 us
    reshape x2, local copies, waits for them, and re-layouts: 1.09 us -> 2.35 us  [shift(): flat = part.reshape(-1)]
    ppermute x2, waiting for transfers between devices: 1.48 us -> 0.22 us  [shift(): return lax.ppermute(flat, axes, pairs).reshape(part.shape)]
    slice x1, local copies, waits for them, and re-layouts: 0.39 us -> 1.43 us  [ring_halo(): east = shift(tall[..., :width], 'gx', -1, 0)]
  transfers between devices with their start and end apart: 9 -> 9, of which waited for: 8 -> 8; matrix products, arithmetic and copies ran while one was open for 5% -> 6% of each run, Pallas kernels for 0% -> 0%
where the time goes in v7:
time: 91.7 us; the launch traced here: 91.5 us
  waiting for transfers between devices  26.5 us (29%)
  Pallas kernels  24.5 us (27%)
  starting transfers between devices  13.7 us (15%)
  local copies, waits for them, and re-layouts  12.2 us (13%)
  other arithmetic  9.52 us (10%)
  matrix products  4.22 us (5%)
    pallas_call x1, Pallas kernels, forecast(): pl.pallas_call(functools.partial(forecast_kernel, steps=steps), out_shape...  24.5 us
    ppermute x2, waiting for transfers between devices, shift(): return lax.ppermute(part, axes, pairs)  16.1 us
    ppermute x5, waiting for transfers between devices, body(): gram = gram + lax.ppermute(gram, axis, pairs)  10.2 us
    ppermute x2, starting transfers between devices, shift(): return lax.ppermute(part, axes, pairs)  6.12 us
    ppermute x5, starting transfers between devices, body(): gram = gram + lax.ppermute(gram, axis, pairs)  5.76 us
    unnamed x9, local copies, waits for them, and re-layouts  3.96 us
    reshape x2, local copies, waits for them, and re-layouts, shift(): return lax.ppermute(flat, axes, pairs).reshape(part.shape)  3.43 us
    dot_general x1, matrix products, body(): local_gram = jnp.dot(flat, flat.T, precision=lax.Precision.HIGHEST)  2.72 us
  transfers between devices with their start and end apart: 9, of which 8 were waited for; matrix products, arithmetic and copies ran while one was open for 6% of the time, Pallas kernels for 0%

profile of v7, /device:TPU:0, one launch (start us, length us, event | category | flops | bytes accessed | tf_op | source)
XLA Modules:
  0.0 91.5 jit_solution(14857786041251120694)
XLA Ops:
  0.6 1.6 %broadcast_add_fusion = f32[16,3,32,256]{3,2,1,0:T(8,128)S(1)} fusion(f32[16,3,32,256]{3,2,1,0:T(8,128)} %param.3, f32[3,32,256]{2,1,0:T(8,128)} %param.2), kind=kLoop, calls=%fused_computation.11 | loop fusion | flops 393216 | bytes 3244032 | tf_op jit(solution)/shard_map/add | solution.py:143
  2.3 3.0 %collective-permute-start = (f32[17,3,8,256]{3,2,1,0:T(8,128)S(1)}, f32[17,3,8,256]{3,2,1,0:T(8,128)S(1)}, u32[]{:S(2)}, u32[]{:S(2)}) collective-permute-start(f32[17,3,8,256]{3,2,1,0:T(8,128)S(1)} %get-tuple-element.11), channel_id=1, source_target_pairs={{0,1},{1,2},{2,3},{3,4},{4,5},{5,6},{6,7},{7,0},{8,9},{9,10},{10,1... | collective-permute-start | bytes 1253384 | tf_op jit(solution)/shard_map/ppermute | solution.py:38
  5.3 3.1 %collective-permute-start.1 = (f32[17,3,8,256]{3,2,1,0:T(8,128)S(1)}, f32[17,3,8,256]{3,2,1,0:T(8,128)S(1)}, u32[]{:S(2)}, u32[]{:S(2)}) collective-permute-start(f32[17,3,8,256]{3,2,1,0:T(8,128)S(1)} %get-tuple-element.10), channel_id=1, source_target_pairs={{0,7},{1,0},{2,1},{3,2},{4,3},{5,4},{6,5},{7,6},{8,15},{9,8},{10,9... | collective-permute-start | bytes 1253384 | tf_op jit(solution)/shard_map/ppermute | solution.py:38
  8.6 0.7 add_multiply_fusion.cor_ref
  9.3 13.9 %collective-permute-done.up_ref = f32[17,3,8,256]{3,2,1,0:T(8,128)S(1)} collective-permute-done((f32[17,3,8,256]{3,2,1,0:T(8,128)S(1)}, f32[17,3,8,256]{3,2,1,0:T(8,128)S(1)}, u32[]{:S(2)}, u32[]{:S(2)}) %collective-permute-start) | collective-permute-done | bytes 417824 | tf_op jit(solution)/shard_map/ppermute | solution.py:38
  23.2 2.2 %collective-permute-done.1.down_ref = f32[17,3,8,256]{3,2,1,0:T(8,128)S(1)} collective-permute-done((f32[17,3,8,256]{3,2,1,0:T(8,128)S(1)}, f32[17,3,8,256]{3,2,1,0:T(8,128)S(1)}, u32[]{:S(2)}, u32[]{:S(2)}) %collective-permute-start.1) | collective-permute-done | bytes 417824 | tf_op jit(solution)/shard_map/ppermute | solution.py:38
  25.4 0.8 copy-done.1
  26.4 1.4 %fusion.13 = (f32[17,3,48,8]{3,2,1,0:T(8,128)S(1)}, f32[17,3,48,8]{3,2,1,0:T(8,128)}) fusion(f32[17,3,48,256]{3,2,1,0:T(8,128)S(1)} %pad_maximum_fusion.1), kind=kLoop, calls=%fused_computation.34 | loop fusion | bytes 313344 | tf_op jit(solution)/shard_map/slice | solution.py:47
  27.8 1.8 %reshape.106 = f32[19584]{0:T(1024)S(1)} reshape(f32[17,3,48,8]{3,2,1,0:T(8,128)} %get-tuple-element.9) | data formatting | bytes 156672 | tf_op jit(solution)/shard_map/reshape | solution.py:39
  30.3 1.8 %collective-permute-start.3 = (f32[19584]{0:T(1024)S(1)}, f32[19584]{0:T(1024)S(1)}, u32[]{:S(2)}, u32[]{:S(2)}) collective-permute-start(f32[19584]{0:T(1024)S(1)} %reshape.108), channel_id=1, source_target_pairs={{0,24},{8,0},{16,8},{24,16},{1,25},{9,1},{17,9},{25,17},{2,26},{10... | collective-permute-start | bytes 235016 | tf_op jit(solution)/shard_map/ppermute | solution.py:40
  32.0 1.3 %pad_maximum_fusion.x_ref = f32[17,3,32,256]{3,2,1,0:T(8,128)} fusion(f32[1,3,32,256]{3,2,1,0:T(8,128)S(1)} %bitcast.34, f32[16,3,32,256]{3,2,1,0:T(8,128)S(1)} %broadcast_add_fusion), kind=kLoop, calls=%fused_computation.3 | loop fusion | flops 417792 | bytes 3342336 | tf_op jit(solution)/shard_map/concatenate | solution.py:143
  33.6 1.7 %reshape.107.west_ref = f32[17,3,48,8]{3,2,1,0:T(8,128)} reshape(f32[19584]{0:T(1024)S(1)} %collective-permute-done.2) | data formatting | bytes 156672 | tf_op jit(solution)/shard_map/reshape | solution.py:40
  35.3 1.7 %reshape.109.east_ref = f32[17,3,48,8]{3,2,1,0:T(8,128)} reshape(f32[19584]{0:T(1024)S(1)} %collective-permute-done.3) | data formatting | bytes 156672 | tf_op jit(solution)/shard_map/reshape | solution.py:40
  37.0 24.5 %shard_map.41 = f32[17,3,32,256]{3,2,1,0:T(8,128)} custom-call(f32[48,1]{1,0:T(8,128)} %add_multiply_fusion.cor_ref, f32[17,3,32,256]{3,2,1,0:T(8,128)} %pad_maximum_fusion.x_ref, f32[17,3,8,256]{3,2,1,0:T(8,128)} %copy-done, f32[17,3,8,256]{3,2,1,0:T(8,128)} %copy-done.1, f32[17,3,48,8]{3,2,1,0:T(8,128)} %reshape.107.west_ref, ...), custom_call_target="tpu_custom_call" | custom-call | flops 564019200 | bytes 5431296 | tf_op jit(solution)/shard_map/pallas_call | solution.py:105
  61.5 0.9 slice_bitcast_fusion
  62.4 1.5 %slice_subtract_fusion = f32[16,3,32,256]{3,2,1,0:T(8,128)S(1)} fusion(f32[17,3,32,256]{3,2,1,0:T(8,128)} %shard_map.41, f32[3,32,256]{2,1,0:T(8,128)S(1)} %slice_bitcast_fusion), kind=kLoop, calls=%fused_computation.5 | loop fusion | flops 393216 | bytes 3244032 | tf_op jit(solution)/shard_map/sub | solution.py:146
  64.0 2.7 %fusion.2 = f32[16,16]{0,1:T(8,128)S(1)} fusion(f32[16,3,32,256]{3,2,1,0:T(8,128)S(1)} %slice_subtract_fusion), kind=kOutput, calls=%fused_computation.10 | convolution fusion | flops 75497472 | bytes 1573888 | tf_op jit(solution)/shard_map/dot_general | solution.py:148
  67.2 0.8 collective-permute-done.4
  68.0 1.4 %collective-permute-start.5 = (f32[16,16]{0,1:T(8,128)S(1)}, f32[16,16]{0,1:T(8,128)S(1)}, u32[]{:S(2)}, u32[]{:S(2)}) collective-permute-start(f32[16,16]{0,1:T(8,128)S(1)} %add.89), channel_id=1, source_target_pairs={{0,16},{8,24},{16,0},{24,8},{1,17},{9,25},{17,1},{25,9},{2,18},{10... | collective-permute-start | bytes 3080 | tf_op jit(solution)/shard_map/ppermute | solution.py:158
  69.4 2.3 %collective-permute-done.5 = f32[16,16]{0,1:T(8,128)S(1)} collective-permute-done((f32[16,16]{0,1:T(8,128)S(1)}, f32[16,16]{0,1:T(8,128)S(1)}, u32[]{:S(2)}, u32[]{:S(2)}) %collective-permute-start.5) | collective-permute-done | bytes 1056 | tf_op jit(solution)/shard_map/ppermute | solution.py:158
  72.0 3.3 %collective-permute-done.6 = f32[16,16]{0,1:T(8,128)S(1)} collective-permute-done((f32[16,16]{0,1:T(8,128)S(1)}, f32[16,16]{0,1:T(8,128)S(1)}, u32[]{:S(2)}, u32[]{:S(2)}) %collective-permute-start.6) | collective-permute-done | bytes 1056 | tf_op jit(solution)/shard_map/ppermute | solution.py:158
  75.4 1.3 %collective-permute-start.7 = (f32[16,16]{0,1:T(8,128)S(1)}, f32[16,16]{0,1:T(8,128)S(1)}, u32[]{:S(2)}, u32[]{:S(2)}) collective-permute-start(f32[16,16]{0,1:T(8,128)S(1)} %add.91), channel_id=1, source_target_pairs={{0,2},{1,3},{2,0},{3,1},{4,6},{5,7},{6,4},{7,5},{8,10},{9,11},{10,... | collective-permute-start | bytes 3080 | tf_op jit(solution)/shard_map/ppermute | solution.py:158
  76.6 2.4 %collective-permute-done.7 = f32[16,16]{0,1:T(8,128)S(1)} collective-permute-done((f32[16,16]{0,1:T(8,128)S(1)}, f32[16,16]{0,1:T(8,128)S(1)}, u32[]{:S(2)}, u32[]{:S(2)}) %collective-permute-start.7) | collective-permute-done | bytes 1056 | tf_op jit(solution)/shard_map/ppermute | solution.py:158
  79.0 2.3 %collective-permute-start.8 = (f32[16,16]{0,1:T(8,128)S(1)}, f32[16,16]{0,1:T(8,128)S(1)}, u32[]{:S(2)}, u32[]{:S(2)}) collective-permute-start(f32[16,16]{0,1:T(8,128)S(1)} %add.92), channel_id=1, source_target_pairs={{0,4},{1,5},{2,6},{3,7},{4,0},{5,1},{6,2},{7,3},{8,12},{9,13},{10,... | collective-permute-start | bytes 3080 | tf_op jit(solution)/shard_map/ppermute | solution.py:158
  81.3 0.9 copy.27
  82.2 1.4 %collective-permute-done.8 = f32[16,16]{0,1:T(8,128)S(1)} collective-permute-done((f32[16,16]{0,1:T(8,128)S(1)}, f32[16,16]{0,1:T(8,128)S(1)}, u32[]{:S(2)}, u32[]{:S(2)}) %collective-permute-start.8) | collective-permute-done | bytes 1056 | tf_op jit(solution)/shard_map/ppermute | solution.py:158
  83.7 1.5 %cholesky.16 = f32[16,16]{1,0:T(8,128)S(1)} custom-call(f32[16,16]{1,0:T(8,128)S(1)} %fusion.8), custom_call_target="Cholesky" | custom-call | tf_op jit(solution)/shard_map/jit(cholesky)/cholesky | solution.py:160
  85.8 0.7 multiply_bitcast_fusion
  86.4 1.2 %custom-call.7 = f32[1,16,16]{1,2,0:T(8,128)S(1)} custom-call(f32[1,16,16]{2,1,0:T(8,128)S(1)} %get-tuple-element.13), custom_call_target="InvertDiagBlocksLowerTriangular" | custom-call | tf_op jit(solution)/shard_map/jit(_solve_triangular)/triangular_solve | solution.py:161
  87.7 1.5 %convolution_multiply_fusion = f32[16,24576]{1,0:T(8,128)S(1)} fusion(f32[16,24576]{1,0:T(8,128)S(1)} %bitcast.30, f32[1,16,16]{1,2,0:T(8,128)S(1)} %custom-call.7), kind=kOutput, calls=%fused_computation | convolution fusion | flops 75890688 | bytes 3146752 | tf_op jit(solution)/shard_map/jit(_solve_triangular)/triangular_solve | solution.py:161
  89.2 1.6 %copy.28 = f32[2,8,96,256]{3,2,1,0:T(8,128)} copy(f32[2,8,96,256]{3,1,2,0:T(8,128)S(1)} %bitcast.31) | data formatting | bytes 3145728
  90.8 0.7 copy.23
  (24 shorter events, 2.9 us)
Async XLA Ops:
  0.6 1.6 %copy-start.2 = (f32[3,32,256]{2,1,0:T(8,128)S(1)}, f32[3,32,256]{2,1,0:T(8,128)}, u32[]{:S(2)}) copy-start(f32[3,32,256]{2,1,0:T(8,128)} %param.2) | copy-start | bytes 294916
  2.3 20.9 %collective-permute-start = (f32[17,3,8,256]{3,2,1,0:T(8,128)S(1)}, f32[17,3,8,256]{3,2,1,0:T(8,128)S(1)}, u32[]{:S(2)}, u32[]{:S(2)}) collective-permute-start(f32[17,3,8,256]{3,2,1,0:T(8,128)S(1)} %get-tuple-element.11), channel_id=1, source_target_pairs={{0,1},{1,2},{2,3},{3,4},{4,5},{5,6},{6,7},{7,0},{8,9},{9,10},{10,1... | collective-permute-start | bytes 1253384 | tf_op jit(solution)/shard_map/ppermute | solution.py:38
  5.3 20.1 %collective-permute-start.1 = (f32[17,3,8,256]{3,2,1,0:T(8,128)S(1)}, f32[17,3,8,256]{3,2,1,0:T(8,128)S(1)}, u32[]{:S(2)}, u32[]{:S(2)}) collective-permute-start(f32[17,3,8,256]{3,2,1,0:T(8,128)S(1)} %get-tuple-element.10), channel_id=1, source_target_pairs={{0,7},{1,0},{2,1},{3,2},{4,3},{5,4},{6,5},{7,6},{8,15},{9,8},{10,9... | collective-permute-start | bytes 1253384 | tf_op jit(solution)/shard_map/ppermute | solution.py:38
  23.2 3.2 %copy-start = (f32[17,3,8,256]{3,2,1,0:T(8,128)}, f32[17,3,8,256]{3,2,1,0:T(8,128)S(1)}, u32[]{:S(2)}) copy-start(f32[17,3,8,256]{3,2,1,0:T(8,128)S(1)} %collective-permute-done.up_ref) | copy-start | bytes 1253380
  25.4 0.8 copy-start.1
  29.7 3.9 %collective-permute-start.2 = (f32[19584]{0:T(1024)S(1)}, f32[19584]{0:T(1024)S(1)}, u32[]{:S(2)}, u32[]{:S(2)}) collective-permute-start(f32[19584]{0:T(1024)S(1)} %reshape.106), channel_id=1, source_target_pairs={{0,8},{8,16},{16,24},{24,0},{1,9},{9,17},{17,25},{25,1},{2,10},{10... | collective-permute-start | bytes 235016 | tf_op jit(solution)/shard_map/ppermute | solution.py:40
  30.3 5.0 %collective-permute-start.3 = (f32[19584]{0:T(1024)S(1)}, f32[19584]{0:T(1024)S(1)}, u32[]{:S(2)}, u32[]{:S(2)}) collective-permute-start(f32[19584]{0:T(1024)S(1)} %reshape.108), channel_id=1, source_target_pairs={{0,24},{8,0},{16,8},{24,16},{1,25},{9,1},{17,9},{25,17},{2,26},{10... | collective-permute-start | bytes 235016 | tf_op jit(solution)/shard_map/ppermute | solution.py:40
  66.7 1.4 %collective-permute-start.4 = (f32[16,16]{0,1:T(8,128)S(1)}, f32[16,16]{0,1:T(8,128)S(1)}, u32[]{:S(2)}, u32[]{:S(2)}) collective-permute-start(f32[16,16]{0,1:T(8,128)S(1)} %fusion.2), channel_id=1, source_target_pairs={{0,8},{8,0},{16,24},{24,16},{1,9},{9,1},{17,25},{25,17},{2,10},{10... | collective-permute-start | bytes 3080 | tf_op jit(solution)/shard_map/ppermute | solution.py:158
  68.0 3.7 %collective-permute-start.5 = (f32[16,16]{0,1:T(8,128)S(1)}, f32[16,16]{0,1:T(8,128)S(1)}, u32[]{:S(2)}, u32[]{:S(2)}) collective-permute-start(f32[16,16]{0,1:T(8,128)S(1)} %add.89), channel_id=1, source_target_pairs={{0,16},{8,24},{16,0},{24,8},{1,17},{9,25},{17,1},{25,9},{2,18},{10... | collective-permute-start | bytes 3080 | tf_op jit(solution)/shard_map/ppermute | solution.py:158
  71.7 3.7 %collective-permute-start.6 = (f32[16,16]{0,1:T(8,128)S(1)}, f32[16,16]{0,1:T(8,128)S(1)}, u32[]{:S(2)}, u32[]{:S(2)}) collective-permute-start(f32[16,16]{0,1:T(8,128)S(1)} %add.90), channel_id=1, source_target_pairs={{0,1},{1,0},{2,3},{3,2},{4,5},{5,4},{6,7},{7,6},{8,9},{9,8},{10,11... | collective-permute-start | bytes 3080 | tf_op jit(solution)/shard_map/ppermute | solution.py:158
  75.4 3.7 %collective-permute-start.7 = (f32[16,16]{0,1:T(8,128)S(1)}, f32[16,16]{0,1:T(8,128)S(1)}, u32[]{:S(2)}, u32[]{:S(2)}) collective-permute-start(f32[16,16]{0,1:T(8,128)S(1)} %add.91), channel_id=1, source_target_pairs={{0,2},{1,3},{2,0},{3,1},{4,6},{5,7},{6,4},{7,5},{8,10},{9,11},{10,... | collective-permute-start | bytes 3080 | tf_op jit(solution)/shard_map/ppermute | solution.py:158
  79.0 4.5 %collective-permute-start.8 = (f32[16,16]{0,1:T(8,128)S(1)}, f32[16,16]{0,1:T(8,128)S(1)}, u32[]{:S(2)}, u32[]{:S(2)}) collective-permute-start(f32[16,16]{0,1:T(8,128)S(1)} %add.92), channel_id=1, source_target_pairs={{0,4},{1,5},{2,6},{3,7},{4,0},{5,1},{6,2},{7,3},{8,12},{9,13},{10,... | collective-permute-start | bytes 3080 | tf_op jit(solution)/shard_map/ppermute | solution.py:158

commit v8 on v3

--- a/solution.py
+++ b/solution.py
@@ -43,8 +43,8 @@
     above = shift(bottom, "gy", 0, 1, flatten=False)
     below = shift(top, "gy", 0, -1, flatten=False)
     tall = jnp.concatenate([value, below, above], axis=-2)
-    west = shift(tall[..., cols - width :], "gx", 1, 0)
-    east = shift(tall[..., :width], "gx", -1, 0)
+    west = shift(jnp.swapaxes(tall[..., cols - width :], -1, -2), "gx", 1, 0, flatten=False)
+    east = shift(jnp.swapaxes(tall[..., :width], -1, -2), "gx", -1, 0, flatten=False)
     return above, below, west, east
 
 
@@ -64,8 +64,8 @@
         ring[k, :rows, :cols] = x_ref[0, k]
         ring[k, rows : rows + width, :cols] = down_ref[0, k]
         ring[k, rows + width :, :cols] = up_ref[0, k]
-        east_pad[:, :width] = east_ref[0, k]
-        west_pad[:, :width] = west_ref[0, k]
+        east_pad[:, :width] = jnp.transpose(east_ref[0, k])
+        west_pad[:, :width] = jnp.transpose(west_ref[0, k])
         ring[k, :, cols:] = east_pad[...] + pltpu.roll(west_pad[...], spare - width, 1)
 
     f = cor_ref[...]
@@ -111,8 +111,8 @@
             pl.BlockSpec((1, F, rows, cols), lambda i: (i, 0, 0, 0)),
             pl.BlockSpec((1, F, width, cols), lambda i: (i, 0, 0, 0)),
             pl.BlockSpec((1, F, width, cols), lambda i: (i, 0, 0, 0)),
-            pl.BlockSpec((1, F, R, width), lambda i: (i, 0, 0, 0)),
-            pl.BlockSpec((1, F, R, width), lambda i: (i, 0, 0, 0)),
+            pl.BlockSpec((1, F, width, R), lambda i: (i, 0, 0, 0)),
+            pl.BlockSpec((1, F, width, R), lambda i: (i, 0, 0, 0)),
         ],
         out_specs=pl.BlockSpec((1, F, rows, cols), lambda i: (i, 0, 0, 0)),
         scratch_shapes=[

time: 90.2 us -> 91.4 us (1.013)
  local copies, waits for them, and re-layouts: 10.3 us -> 6.5 us
  waiting for transfers between devices: 27.2 us -> 29.9 us
  Pallas kernels: 24.9 us -> 26.8 us
    reshape x4 -> x0, local copies, waits for them, and re-layouts: 4.52 us -> none  [the longest x2 3.43 us: shift(): return lax.ppermute(flat, axes, pairs).reshape(part.shape)]
    ppermute x2 -> x4, waiting for transfers between devices: 15.6 us -> 19.9 us  [shift(): return lax.ppermute(part, axes, pairs)]
    pallas_call x1, Pallas kernels: 24.9 us -> 26.8 us  [forecast(): pl.pallas_call(functools.partial(forecast_kernel, steps=steps), out_shape...]
    ppermute x2 -> x0, starting transfers between devices: 1.83 us -> none  [shift(): return lax.ppermute(flat, axes, pairs).reshape(part.shape)]
    ppermute x2 -> x4, starting transfers between devices: 6.12 us -> 7.91 us  [shift(): return lax.ppermute(part, axes, pairs)]
    ppermute x2 -> x0, waiting for transfers between devices: 1.48 us -> none  [shift(): return lax.ppermute(flat, axes, pairs).reshape(part.shape)]
    unnamed x9 -> x15, local copies, waits for them, and re-layouts: 3.7 us -> 4.43 us
  transfers between devices with their start and end apart: 9 -> 9, of which waited for: 8 -> 9; matrix products, arithmetic and copies ran while one was open for 5% -> 3% of each run, Pallas kernels for 0% -> 0%
where the time goes in v8:
time: 91.4 us; the launch traced here: 91.2 us
  waiting for transfers between devices  29.9 us (33%)
  Pallas kernels  26.8 us (29%)
  starting transfers between devices  14.2 us (16%)
  other arithmetic  8.84 us (10%)
  local copies, waits for them, and re-layouts  6.5 us (7%)
  matrix products  4.22 us (5%)
    pallas_call x1, Pallas kernels, forecast(): pl.pallas_call(functools.partial(forecast_kernel, steps=steps), out_shape...  26.8 us
    ppermute x4, waiting for transfers between devices, shift(): return lax.ppermute(part, axes, pairs)  19.9 us
    ppermute x5, waiting for transfers between devices, body(): gram = gram + lax.ppermute(gram, axis, pairs)  9.95 us
    ppermute x4, starting transfers between devices, shift(): return lax.ppermute(part, axes, pairs)  7.91 us
    ppermute x5, starting transfers between devices, body(): gram = gram + lax.ppermute(gram, axis, pairs)  6.26 us
    unnamed x15, local copies, waits for them, and re-layouts  4.43 us
    dot_general x1, matrix products, body(): local_gram = jnp.dot(flat, flat.T, precision=lax.Precision.HIGHEST)  2.72 us
    another operation x3, other arithmetic, body(): lower = jnp.linalg.cholesky(gram)  2.13 us
  transfers between devices with their start and end apart: 9, of which 9 were waited for; matrix products, arithmetic and copies ran while one was open for 3% of the time, Pallas kernels for 0%

profile of v8, /device:TPU:0, one launch (start us, length us, event | category | flops | bytes accessed | tf_op | source)
XLA Modules:
  0.0 91.2 jit_solution(7805346082830067282)
XLA Ops:
  0.6 1.6 %broadcast_add_fusion = f32[16,3,32,256]{3,2,1,0:T(8,128)S(1)} fusion(f32[16,3,32,256]{3,2,1,0:T(8,128)} %param.3, f32[3,32,256]{2,1,0:T(8,128)} %param.2), kind=kLoop, calls=%fused_computation.11 | loop fusion | flops 393216 | bytes 3244032 | tf_op jit(solution)/shard_map/add | solution.py:143
  2.3 3.0 %collective-permute-start = (f32[17,3,8,256]{3,2,1,0:T(8,128)S(1)}, f32[17,3,8,256]{3,2,1,0:T(8,128)S(1)}, u32[]{:S(2)}, u32[]{:S(2)}) collective-permute-start(f32[17,3,8,256]{3,2,1,0:T(8,128)S(1)} %get-tuple-element.9), channel_id=1, source_target_pairs={{0,1},{1,2},{2,3},{3,4},{4,5},{5,6},{6,7},{7,0},{8,9},{9,10},{10,1... | collective-permute-start | bytes 1253384 | tf_op jit(solution)/shard_map/ppermute | solution.py:38
  5.3 3.1 %collective-permute-start.1 = (f32[17,3,8,256]{3,2,1,0:T(8,128)S(1)}, f32[17,3,8,256]{3,2,1,0:T(8,128)S(1)}, u32[]{:S(2)}, u32[]{:S(2)}) collective-permute-start(f32[17,3,8,256]{3,2,1,0:T(8,128)S(1)} %get-tuple-element.8), channel_id=1, source_target_pairs={{0,7},{1,0},{2,1},{3,2},{4,3},{5,4},{6,5},{7,6},{8,15},{9,8},{10,9... | collective-permute-start | bytes 1253384 | tf_op jit(solution)/shard_map/ppermute | solution.py:38
  8.4 1.3 %pad_maximum_fusion.x_ref = f32[17,3,32,256]{3,2,1,0:T(8,128)} fusion(f32[1,3,32,256]{3,2,1,0:T(8,128)S(1)} %bitcast.31, f32[16,3,32,256]{3,2,1,0:T(8,128)S(1)} %broadcast_add_fusion), kind=kLoop, calls=%fused_computation.3 | loop fusion | flops 417792 | bytes 3342336 | tf_op jit(solution)/shard_map/concatenate | solution.py:143
  9.8 13.4 %collective-permute-done.up_ref = f32[17,3,8,256]{3,2,1,0:T(8,128)S(1)} collective-permute-done((f32[17,3,8,256]{3,2,1,0:T(8,128)S(1)}, f32[17,3,8,256]{3,2,1,0:T(8,128)S(1)}, u32[]{:S(2)}, u32[]{:S(2)}) %collective-permute-start) | collective-permute-done | bytes 417824 | tf_op jit(solution)/shard_map/ppermute | solution.py:38
  23.2 2.2 %collective-permute-done.1.down_ref = f32[17,3,8,256]{3,2,1,0:T(8,128)S(1)} collective-permute-done((f32[17,3,8,256]{3,2,1,0:T(8,128)S(1)}, f32[17,3,8,256]{3,2,1,0:T(8,128)S(1)}, u32[]{:S(2)}, u32[]{:S(2)}) %collective-permute-start.1) | collective-permute-done | bytes 417824 | tf_op jit(solution)/shard_map/ppermute | solution.py:38
  25.7 0.5 copy-done.1
  27.3 1.8 %collective-permute-start.3 = (f32[17,3,8,48]{3,2,1,0:T(8,128)S(1)}, f32[17,3,8,48]{3,2,1,0:T(8,128)S(1)}, u32[]{:S(2)}, u32[]{:S(2)}) collective-permute-start(f32[17,3,8,48]{3,2,1,0:T(8,128)S(1)} %bitcast.35), channel_id=1, source_target_pairs={{0,24},{8,0},{16,8},{24,16},{1,25},{9,1},{17,9},{25,17},{2,26},{10... | collective-permute-start | bytes 235016 | tf_op jit(solution)/shard_map/ppermute | solution.py:38
  29.1 3.1 %collective-permute-done.2.west_ref = f32[17,3,8,48]{3,2,1,0:T(8,128)S(1)} collective-permute-done((f32[17,3,8,48]{3,2,1,0:T(8,128)S(1)}, f32[17,3,8,48]{3,2,1,0:T(8,128)S(1)}, u32[]{:S(2)}, u32[]{:S(2)}) %collective-permute-start.2) | collective-permute-done | bytes 78368 | tf_op jit(solution)/shard_map/ppermute | solution.py:38
  32.2 1.2 %collective-permute-done.3.east_ref = f32[17,3,8,48]{3,2,1,0:T(8,128)S(1)} collective-permute-done((f32[17,3,8,48]{3,2,1,0:T(8,128)S(1)}, f32[17,3,8,48]{3,2,1,0:T(8,128)S(1)}, u32[]{:S(2)}, u32[]{:S(2)}) %collective-permute-start.3) | collective-permute-done | bytes 78368 | tf_op jit(solution)/shard_map/ppermute | solution.py:38
  33.5 0.7 broadcast_in_dim.5.cor_ref
  34.2 26.8 %shard_map.41 = f32[17,3,32,256]{3,2,1,0:T(8,128)} custom-call(f32[48,384]{1,0:T(8,128)} %broadcast_in_dim.5.cor_ref, f32[17,3,32,256]{3,2,1,0:T(8,128)} %pad_maximum_fusion.x_ref, f32[17,3,8,256]{3,2,1,0:T(8,128)} %copy-done, f32[17,3,8,256]{3,2,1,0:T(8,128)} %copy-done.1, f32[17,3,8,48]{3,2,1,0:T(8,128)} %copy-done.3, f32[17,3,8,48]{3,2,1,0:T(8,128)} %copy-done.4), custom_call_target="tpu_custom_call" | custom-call | flops 564019200 | bytes 5431296 | tf_op jit(solution)/shard_map/pallas_call | solution.py:105
  61.0 0.9 slice_bitcast_fusion
  61.9 1.5 %slice_subtract_fusion = f32[16,3,32,256]{3,2,1,0:T(8,128)S(1)} fusion(f32[17,3,32,256]{3,2,1,0:T(8,128)} %shard_map.41, f32[3,32,256]{2,1,0:T(8,128)S(1)} %slice_bitcast_fusion), kind=kLoop, calls=%fused_computation.5 | loop fusion | flops 393216 | bytes 3244032 | tf_op jit(solution)/shard_map/sub | solution.py:146
  63.4 2.7 %fusion.2 = f32[16,16]{0,1:T(8,128)S(1)} fusion(f32[16,3,32,256]{3,2,1,0:T(8,128)S(1)} %slice_subtract_fusion), kind=kOutput, calls=%fused_computation.10 | convolution fusion | flops 75497472 | bytes 1573888 | tf_op jit(solution)/shard_map/dot_general | solution.py:148
  66.1 0.8 collective-permute-start.4
  67.0 0.8 collective-permute-done.4
  67.8 1.5 %collective-permute-start.5 = (f32[16,16]{0,1:T(8,128)S(1)}, f32[16,16]{0,1:T(8,128)S(1)}, u32[]{:S(2)}, u32[]{:S(2)}) collective-permute-start(f32[16,16]{0,1:T(8,128)S(1)} %add.77), channel_id=1, source_target_pairs={{0,16},{8,24},{16,0},{24,8},{1,17},{9,25},{17,1},{25,9},{2,18},{10... | collective-permute-start | bytes 3080 | tf_op jit(solution)/shard_map/ppermute | solution.py:158
  69.3 2.1 %collective-permute-done.5 = f32[16,16]{0,1:T(8,128)S(1)} collective-permute-done((f32[16,16]{0,1:T(8,128)S(1)}, f32[16,16]{0,1:T(8,128)S(1)}, u32[]{:S(2)}, u32[]{:S(2)}) %collective-permute-start.5) | collective-permute-done | bytes 1056 | tf_op jit(solution)/shard_map/ppermute | solution.py:158
  71.8 3.3 %collective-permute-done.6 = f32[16,16]{0,1:T(8,128)S(1)} collective-permute-done((f32[16,16]{0,1:T(8,128)S(1)}, f32[16,16]{0,1:T(8,128)S(1)}, u32[]{:S(2)}, u32[]{:S(2)}) %collective-permute-start.6) | collective-permute-done | bytes 1056 | tf_op jit(solution)/shard_map/ppermute | solution.py:158
  75.1 1.3 %collective-permute-start.7 = (f32[16,16]{0,1:T(8,128)S(1)}, f32[16,16]{0,1:T(8,128)S(1)}, u32[]{:S(2)}, u32[]{:S(2)}) collective-permute-start(f32[16,16]{0,1:T(8,128)S(1)} %add.79), channel_id=1, source_target_pairs={{0,2},{1,3},{2,0},{3,1},{4,6},{5,7},{6,4},{7,5},{8,10},{9,11},{10,... | collective-permute-start | bytes 3080 | tf_op jit(solution)/shard_map/ppermute | solution.py:158
  76.4 2.4 %collective-permute-done.7 = f32[16,16]{0,1:T(8,128)S(1)} collective-permute-done((f32[16,16]{0,1:T(8,128)S(1)}, f32[16,16]{0,1:T(8,128)S(1)}, u32[]{:S(2)}, u32[]{:S(2)}) %collective-permute-start.7) | collective-permute-done | bytes 1056 | tf_op jit(solution)/shard_map/ppermute | solution.py:158
  78.7 2.3 %collective-permute-start.8 = (f32[16,16]{0,1:T(8,128)S(1)}, f32[16,16]{0,1:T(8,128)S(1)}, u32[]{:S(2)}, u32[]{:S(2)}) collective-permute-start(f32[16,16]{0,1:T(8,128)S(1)} %add.80), channel_id=1, source_target_pairs={{0,4},{1,5},{2,6},{3,7},{4,0},{5,1},{6,2},{7,3},{8,12},{9,13},{10,... | collective-permute-start | bytes 3080 | tf_op jit(solution)/shard_map/ppermute | solution.py:158
  81.0 0.9 %copy.29 = f32[2,8,96,256]{3,1,2,0:T(8,128)S(1)} copy(f32[2,8,96,256]{3,2,1,0:T(8,128)S(1)} %bitcast.27) | data formatting | bytes 3145728
  81.9 1.4 %collective-permute-done.8 = f32[16,16]{0,1:T(8,128)S(1)} collective-permute-done((f32[16,16]{0,1:T(8,128)S(1)}, f32[16,16]{0,1:T(8,128)S(1)}, u32[]{:S(2)}, u32[]{:S(2)}) %collective-permute-start.8) | collective-permute-done | bytes 1056 | tf_op jit(solution)/shard_map/ppermute | solution.py:158
  83.4 1.5 %cholesky.16 = f32[16,16]{1,0:T(8,128)S(1)} custom-call(f32[16,16]{1,0:T(8,128)S(1)} %fusion.8), custom_call_target="Cholesky" | custom-call | tf_op jit(solution)/shard_map/jit(cholesky)/cholesky | solution.py:160
  84.9 0.6 compare_reduce_fusion
  85.5 0.7 multiply_bitcast_fusion
  86.2 1.2 %custom-call.7 = f32[1,16,16]{1,2,0:T(8,128)S(1)} custom-call(f32[1,16,16]{2,1,0:T(8,128)S(1)} %get-tuple-element.11), custom_call_target="InvertDiagBlocksLowerTriangular" | custom-call | tf_op jit(solution)/shard_map/jit(_solve_triangular)/triangular_solve | solution.py:161
  87.4 1.5 %convolution_multiply_fusion = f32[16,24576]{1,0:T(8,128)S(1)} fusion(f32[16,24576]{1,0:T(8,128)S(1)} %bitcast.28, f32[1,16,16]{1,2,0:T(8,128)S(1)} %custom-call.7), kind=kOutput, calls=%fused_computation | convolution fusion | flops 75890688 | bytes 3146752 | tf_op jit(solution)/shard_map/jit(_solve_triangular)/triangular_solve | solution.py:161
  88.9 1.6 %copy.30 = f32[2,8,96,256]{3,2,1,0:T(8,128)} copy(f32[2,8,96,256]{3,1,2,0:T(8,128)S(1)} %bitcast.29) | data formatting | bytes 3145728
  90.5 0.7 copy.23
  (25 shorter events, 2.1 us)
Async XLA Ops:
  0.6 1.6 %copy-start.2 = (f32[3,32,256]{2,1,0:T(8,128)S(1)}, f32[3,32,256]{2,1,0:T(8,128)}, u32[]{:S(2)}) copy-start(f32[3,32,256]{2,1,0:T(8,128)} %param.2) | copy-start | bytes 294916
  2.3 20.9 %collective-permute-start = (f32[17,3,8,256]{3,2,1,0:T(8,128)S(1)}, f32[17,3,8,256]{3,2,1,0:T(8,128)S(1)}, u32[]{:S(2)}, u32[]{:S(2)}) collective-permute-start(f32[17,3,8,256]{3,2,1,0:T(8,128)S(1)} %get-tuple-element.9), channel_id=1, source_target_pairs={{0,1},{1,2},{2,3},{3,4},{4,5},{5,6},{6,7},{7,0},{8,9},{9,10},{10,1... | collective-permute-start | bytes 1253384 | tf_op jit(solution)/shard_map/ppermute | solution.py:38
  5.3 20.1 %collective-permute-start.1 = (f32[17,3,8,256]{3,2,1,0:T(8,128)S(1)}, f32[17,3,8,256]{3,2,1,0:T(8,128)S(1)}, u32[]{:S(2)}, u32[]{:S(2)}) collective-permute-start(f32[17,3,8,256]{3,2,1,0:T(8,128)S(1)} %get-tuple-element.8), channel_id=1, source_target_pairs={{0,7},{1,0},{2,1},{3,2},{4,3},{5,4},{6,5},{7,6},{8,15},{9,8},{10,9... | collective-permute-start | bytes 1253384 | tf_op jit(solution)/shard_map/ppermute | solution.py:38
  23.2 2.5 %copy-start = (f32[17,3,8,256]{3,2,1,0:T(8,128)}, f32[17,3,8,256]{3,2,1,0:T(8,128)S(1)}, u32[]{:S(2)}) copy-start(f32[17,3,8,256]{3,2,1,0:T(8,128)S(1)} %collective-permute-done.up_ref) | copy-start | bytes 1253380
  25.4 0.8 copy-start.1
  26.9 5.3 %collective-permute-start.2 = (f32[17,3,8,48]{3,2,1,0:T(8,128)S(1)}, f32[17,3,8,48]{3,2,1,0:T(8,128)S(1)}, u32[]{:S(2)}, u32[]{:S(2)}) collective-permute-start(f32[17,3,8,48]{3,2,1,0:T(8,128)S(1)} %bitcast.34), channel_id=1, source_target_pairs={{0,8},{8,16},{16,24},{24,0},{1,9},{9,17},{17,25},{25,1},{2,10},{10... | collective-permute-start | bytes 235016 | tf_op jit(solution)/shard_map/ppermute | solution.py:38
  27.3 6.1 %collective-permute-start.3 = (f32[17,3,8,48]{3,2,1,0:T(8,128)S(1)}, f32[17,3,8,48]{3,2,1,0:T(8,128)S(1)}, u32[]{:S(2)}, u32[]{:S(2)}) collective-permute-start(f32[17,3,8,48]{3,2,1,0:T(8,128)S(1)} %bitcast.35), channel_id=1, source_target_pairs={{0,24},{8,0},{16,8},{24,16},{1,25},{9,1},{17,9},{25,17},{2,26},{10... | collective-permute-start | bytes 235016 | tf_op jit(solution)/shard_map/ppermute | solution.py:38
  32.2 1.9 %copy-start.3 = (f32[17,3,8,48]{3,2,1,0:T(8,128)}, f32[17,3,8,48]{3,2,1,0:T(8,128)S(1)}, u32[]{:S(2)}) copy-start(f32[17,3,8,48]{3,2,1,0:T(8,128)S(1)} %collective-permute-done.2.west_ref) | copy-start | bytes 235012
  33.4 0.7 copy-start.4
  66.1 1.6 %collective-permute-start.4 = (f32[16,16]{0,1:T(8,128)S(1)}, f32[16,16]{0,1:T(8,128)S(1)}, u32[]{:S(2)}, u32[]{:S(2)}) collective-permute-start(f32[16,16]{0,1:T(8,128)S(1)} %fusion.2), channel_id=1, source_target_pairs={{0,8},{8,0},{16,24},{24,16},{1,9},{9,1},{17,25},{25,17},{2,10},{10... | collective-permute-start | bytes 3080 | tf_op jit(solution)/shard_map/ppermute | solution.py:158
  67.8 3.7 %collective-permute-start.5 = (f32[16,16]{0,1:T(8,128)S(1)}, f32[16,16]{0,1:T(8,128)S(1)}, u32[]{:S(2)}, u32[]{:S(2)}) collective-permute-start(f32[16,16]{0,1:T(8,128)S(1)} %add.77), channel_id=1, source_target_pairs={{0,16},{8,24},{16,0},{24,8},{1,17},{9,25},{17,1},{25,9},{2,18},{10... | collective-permute-start | bytes 3080 | tf_op jit(solution)/shard_map/ppermute | solution.py:158
  71.4 3.7 %collective-permute-start.6 = (f32[16,16]{0,1:T(8,128)S(1)}, f32[16,16]{0,1:T(8,128)S(1)}, u32[]{:S(2)}, u32[]{:S(2)}) collective-permute-start(f32[16,16]{0,1:T(8,128)S(1)} %add.78), channel_id=1, source_target_pairs={{0,1},{1,0},{2,3},{3,2},{4,5},{5,4},{6,7},{7,6},{8,9},{9,8},{10,11... | collective-permute-start | bytes 3080 | tf_op jit(solution)/shard_map/ppermute | solution.py:158
  75.1 3.7 %collective-permute-start.7 = (f32[16,16]{0,1:T(8,128)S(1)}, f32[16,16]{0,1:T(8,128)S(1)}, u32[]{:S(2)}, u32[]{:S(2)}) collective-permute-start(f32[16,16]{0,1:T(8,128)S(1)} %add.79), channel_id=1, source_target_pairs={{0,2},{1,3},{2,0},{3,1},{4,6},{5,7},{6,4},{7,5},{8,10},{9,11},{10,... | collective-permute-start | bytes 3080 | tf_op jit(solution)/shard_map/ppermute | solution.py:158
  78.7 4.5 %collective-permute-start.8 = (f32[16,16]{0,1:T(8,128)S(1)}, f32[16,16]{0,1:T(8,128)S(1)}, u32[]{:S(2)}, u32[]{:S(2)}) collective-permute-start(f32[16,16]{0,1:T(8,128)S(1)} %add.80), channel_id=1, source_target_pairs={{0,4},{1,5},{2,6},{3,7},{4,0},{5,1},{6,2},{7,3},{8,12},{9,13},{10,... | collective-permute-start | bytes 3080 | tf_op jit(solution)/shard_map/ppermute | solution.py:158

commit v9 on v3

--- a/solution.py
+++ b/solution.py
@@ -72,14 +72,23 @@
     third = 1.0 / 12.0
 
     def dx(v):
-        g = pltpu.roll(v, C - 1, 1) - pltpu.roll(v, 1, 1)
-        w = pltpu.roll(v, C - 2, 1) - pltpu.roll(v, 2, 1)
+        n_ = v.shape[1]
+        g = pltpu.roll(v, n_ - 1, 1) - pltpu.roll(v, 1, 1)
+        w = pltpu.roll(v, n_ - 2, 1) - pltpu.roll(v, 2, 1)
         return (8.0 * g - w) * third
 
     def dy(v):
-        g = pltpu.roll(v, R - 1, 0) - pltpu.roll(v, 1, 0)
-        w = pltpu.roll(v, R - 2, 0) - pltpu.roll(v, 2, 0)
+        n_ = v.shape[0]
+        g = pltpu.roll(v, n_ - 1, 0) - pltpu.roll(v, 1, 0)
+        w = pltpu.roll(v, n_ - 2, 0) - pltpu.roll(v, 2, 0)
         return (8.0 * g - w) * third
+
+    def shrink(v, margin, keep):
+        size = v.shape[0]
+        cut = margin - keep
+        line = lax.broadcasted_iota(jnp.int32, v.shape, 0)
+        moved = jnp.where(line < rows + keep, v, pltpu.roll(v, size - 2 * cut, 0))
+        return moved[: size - 2 * cut]
 
     def tend(h, e, n):
         depth = 4.0 + h
@@ -89,7 +98,13 @@
         return ch, ce, cn
 
     s = (ring[0], ring[1], ring[2])
-    for _ in range(steps):
+    margin = (R - rows) // 2
+    for step in range(steps):
+        keep = 4 * (steps - step)
+        if keep < margin and (rows + 2 * keep) % 8 == 0:
+            s = tuple(shrink(v, margin, keep) for v in s)
+            f = shrink(f, margin, keep)
+            margin = keep
         first = tend(*s)
         mid = tuple(a + 0.1 * b for a, b in zip(s, first))
         second = tend(*mid)

time: 90.2 us -> 89.5 us (level)
  no operation moved by 1% of the time
where the time goes in v9:
time: 89.5 us; the launch traced here: 89.3 us
  waiting for transfers between devices  27.2 us (30%)
  Pallas kernels  24.2 us (27%)
  starting transfers between devices  13.8 us (15%)
  local copies, waits for them, and re-layouts  10.3 us (12%)
  other arithmetic  8.83 us (10%)
  matrix products  4.22 us (5%)
    pallas_call x1, Pallas kernels, forecast(): pl.pallas_call(functools.partial(forecast_kernel, steps=steps), out_shape...  24.2 us
    ppermute x2, waiting for transfers between devices, shift(): return lax.ppermute(part, axes, pairs)  15.6 us
    ppermute x5, waiting for transfers between devices, body(): gram = gram + lax.ppermute(gram, axis, pairs)  10.1 us
    ppermute x2, starting transfers between devices, shift(): return lax.ppermute(part, axes, pairs)  6.12 us
    ppermute x5, starting transfers between devices, body(): gram = gram + lax.ppermute(gram, axis, pairs)  5.87 us
    unnamed x9, local copies, waits for them, and re-layouts  3.7 us
    reshape x2, local copies, waits for them, and re-layouts, shift(): return lax.ppermute(flat, axes, pairs).reshape(part.shape)  3.43 us
    dot_general x1, matrix products, body(): local_gram = jnp.dot(flat, flat.T, precision=lax.Precision.HIGHEST)  2.72 us
  transfers between devices with their start and end apart: 9, of which 8 were waited for; matrix products, arithmetic and copies ran while one was open for 5% of the time, Pallas kernels for 0%

profile of v9, /device:TPU:0, one launch (start us, length us, event | category | flops | bytes accessed | tf_op | source)
XLA Modules:
  0.0 89.3 jit_solution(15186587727132368960)
XLA Ops:
  0.6 1.6 %broadcast_add_fusion = f32[16,3,32,256]{3,2,1,0:T(8,128)S(1)} fusion(f32[16,3,32,256]{3,2,1,0:T(8,128)} %param.3, f32[3,32,256]{2,1,0:T(8,128)} %param.2), kind=kLoop, calls=%fused_computation.11 | loop fusion | flops 393216 | bytes 3244032 | tf_op jit(solution)/shard_map/add | solution.py:158
  2.3 3.0 %collective-permute-start = (f32[17,3,8,256]{3,2,1,0:T(8,128)S(1)}, f32[17,3,8,256]{3,2,1,0:T(8,128)S(1)}, u32[]{:S(2)}, u32[]{:S(2)}) collective-permute-start(f32[17,3,8,256]{3,2,1,0:T(8,128)S(1)} %get-tuple-element.9), channel_id=1, source_target_pairs={{0,1},{1,2},{2,3},{3,4},{4,5},{5,6},{6,7},{7,0},{8,9},{9,10},{10,1... | collective-permute-start | bytes 1253384 | tf_op jit(solution)/shard_map/ppermute | solution.py:38
  5.3 3.1 %collective-permute-start.1 = (f32[17,3,8,256]{3,2,1,0:T(8,128)S(1)}, f32[17,3,8,256]{3,2,1,0:T(8,128)S(1)}, u32[]{:S(2)}, u32[]{:S(2)}) collective-permute-start(f32[17,3,8,256]{3,2,1,0:T(8,128)S(1)} %get-tuple-element.8), channel_id=1, source_target_pairs={{0,7},{1,0},{2,1},{3,2},{4,3},{5,4},{6,5},{7,6},{8,15},{9,8},{10,9... | collective-permute-start | bytes 1253384 | tf_op jit(solution)/shard_map/ppermute | solution.py:38
  8.4 1.3 %pad_maximum_fusion.x_ref = f32[17,3,32,256]{3,2,1,0:T(8,128)} fusion(f32[1,3,32,256]{3,2,1,0:T(8,128)S(1)} %bitcast.33, f32[16,3,32,256]{3,2,1,0:T(8,128)S(1)} %broadcast_add_fusion), kind=kLoop, calls=%fused_computation.3 | loop fusion | flops 417792 | bytes 3342336 | tf_op jit(solution)/shard_map/concatenate | solution.py:158
  9.8 13.4 %collective-permute-done.up_ref = f32[17,3,8,256]{3,2,1,0:T(8,128)S(1)} collective-permute-done((f32[17,3,8,256]{3,2,1,0:T(8,128)S(1)}, f32[17,3,8,256]{3,2,1,0:T(8,128)S(1)}, u32[]{:S(2)}, u32[]{:S(2)}) %collective-permute-start) | collective-permute-done | bytes 417824 | tf_op jit(solution)/shard_map/ppermute | solution.py:38
  23.2 2.2 %collective-permute-done.1.down_ref = f32[17,3,8,256]{3,2,1,0:T(8,128)S(1)} collective-permute-done((f32[17,3,8,256]{3,2,1,0:T(8,128)S(1)}, f32[17,3,8,256]{3,2,1,0:T(8,128)S(1)}, u32[]{:S(2)}, u32[]{:S(2)}) %collective-permute-start.1) | collective-permute-done | bytes 417824 | tf_op jit(solution)/shard_map/ppermute | solution.py:38
  27.2 0.5 reshape.61
  27.7 1.8 %collective-permute-start.3 = (f32[19584]{0:T(1024)S(1)}, f32[19584]{0:T(1024)S(1)}, u32[]{:S(2)}, u32[]{:S(2)}) collective-permute-start(f32[19584]{0:T(1024)S(1)} %reshape.61), channel_id=1, source_target_pairs={{0,24},{8,0},{16,8},{24,16},{1,25},{9,1},{17,9},{25,17},{2,26},{10... | collective-permute-start | bytes 235016 | tf_op jit(solution)/shard_map/ppermute | solution.py:40
  29.5 1.5 %collective-permute-done.2 = f32[19584]{0:T(1024)S(1)} collective-permute-done((f32[19584]{0:T(1024)S(1)}, f32[19584]{0:T(1024)S(1)}, u32[]{:S(2)}, u32[]{:S(2)}) %collective-permute-start.2) | collective-permute-done | bytes 78368 | tf_op jit(solution)/shard_map/ppermute | solution.py:40
  31.0 1.7 %reshape.60.west_ref = f32[17,3,48,8]{3,2,1,0:T(8,128)} reshape(f32[19584]{0:T(1024)S(1)} %collective-permute-done.2) | data formatting | bytes 156672 | tf_op jit(solution)/shard_map/reshape | solution.py:40
  32.7 1.7 %reshape.62.east_ref = f32[17,3,48,8]{3,2,1,0:T(8,128)} reshape(f32[19584]{0:T(1024)S(1)} %collective-permute-done.3) | data formatting | bytes 156672 | tf_op jit(solution)/shard_map/reshape | solution.py:40
  34.5 0.7 broadcast_in_dim.5.cor_ref
  35.2 24.2 %shard_map.41 = f32[17,3,32,256]{3,2,1,0:T(8,128)} custom-call(f32[48,384]{1,0:T(8,128)} %broadcast_in_dim.5.cor_ref, f32[17,3,32,256]{3,2,1,0:T(8,128)} %pad_maximum_fusion.x_ref, f32[17,3,8,256]{3,2,1,0:T(8,128)} %copy-done, f32[17,3,8,256]{3,2,1,0:T(8,128)} %copy-done.1, f32[17,3,48,8]{3,2,1,0:T(8,128)} %reshape.60.west_ref, ...), custom_call_target="tpu_custom_call" | custom-call | flops 564019200 | bytes 5431296 | tf_op jit(solution)/shard_map/pallas_call | solution.py:120
  59.3 0.9 %slice_bitcast_fusion = f32[3,32,256]{2,1,0:T(8,128)S(1)} fusion(f32[17,3,32,256]{3,2,1,0:T(8,128)} %shard_map.41), kind=kLoop, calls=%fused_computation.14 | loop fusion | bytes 196608 | tf_op jit(solution)/shard_map/sub | solution.py:161
  60.2 1.5 %slice_subtract_fusion = f32[16,3,32,256]{3,2,1,0:T(8,128)S(1)} fusion(f32[17,3,32,256]{3,2,1,0:T(8,128)} %shard_map.41, f32[3,32,256]{2,1,0:T(8,128)S(1)} %slice_bitcast_fusion), kind=kLoop, calls=%fused_computation.5 | loop fusion | flops 393216 | bytes 3244032 | tf_op jit(solution)/shard_map/sub | solution.py:161
  61.8 2.7 %fusion.2 = f32[16,16]{0,1:T(8,128)S(1)} fusion(f32[16,3,32,256]{3,2,1,0:T(8,128)S(1)} %slice_subtract_fusion), kind=kOutput, calls=%fused_computation.10 | convolution fusion | flops 75497472 | bytes 1573888 | tf_op jit(solution)/shard_map/dot_general | solution.py:163
  65.0 0.8 collective-permute-done.4
  65.9 1.4 %collective-permute-start.5 = (f32[16,16]{0,1:T(8,128)S(1)}, f32[16,16]{0,1:T(8,128)S(1)}, u32[]{:S(2)}, u32[]{:S(2)}) collective-permute-start(f32[16,16]{0,1:T(8,128)S(1)} %add.77), channel_id=1, source_target_pairs={{0,16},{8,24},{16,0},{24,8},{1,17},{9,25},{17,1},{25,9},{2,18},{10... | collective-permute-start | bytes 3080 | tf_op jit(solution)/shard_map/ppermute | solution.py:173
  67.2 2.3 %collective-permute-done.5 = f32[16,16]{0,1:T(8,128)S(1)} collective-permute-done((f32[16,16]{0,1:T(8,128)S(1)}, f32[16,16]{0,1:T(8,128)S(1)}, u32[]{:S(2)}, u32[]{:S(2)}) %collective-permute-start.5) | collective-permute-done | bytes 1056 | tf_op jit(solution)/shard_map/ppermute | solution.py:173
  70.0 3.2 %collective-permute-done.6 = f32[16,16]{0,1:T(8,128)S(1)} collective-permute-done((f32[16,16]{0,1:T(8,128)S(1)}, f32[16,16]{0,1:T(8,128)S(1)}, u32[]{:S(2)}, u32[]{:S(2)}) %collective-permute-start.6) | collective-permute-done | bytes 1056 | tf_op jit(solution)/shard_map/ppermute | solution.py:173
  73.2 1.3 %collective-permute-start.7 = (f32[16,16]{0,1:T(8,128)S(1)}, f32[16,16]{0,1:T(8,128)S(1)}, u32[]{:S(2)}, u32[]{:S(2)}) collective-permute-start(f32[16,16]{0,1:T(8,128)S(1)} %add.79), channel_id=1, source_target_pairs={{0,2},{1,3},{2,0},{3,1},{4,6},{5,7},{6,4},{7,5},{8,10},{9,11},{10,... | collective-permute-start | bytes 3080 | tf_op jit(solution)/shard_map/ppermute | solution.py:173
  74.4 2.4 %collective-permute-done.7 = f32[16,16]{0,1:T(8,128)S(1)} collective-permute-done((f32[16,16]{0,1:T(8,128)S(1)}, f32[16,16]{0,1:T(8,128)S(1)}, u32[]{:S(2)}, u32[]{:S(2)}) %collective-permute-start.7) | collective-permute-done | bytes 1056 | tf_op jit(solution)/shard_map/ppermute | solution.py:173
  76.8 2.3 %collective-permute-start.8 = (f32[16,16]{0,1:T(8,128)S(1)}, f32[16,16]{0,1:T(8,128)S(1)}, u32[]{:S(2)}, u32[]{:S(2)}) collective-permute-start(f32[16,16]{0,1:T(8,128)S(1)} %add.80), channel_id=1, source_target_pairs={{0,4},{1,5},{2,6},{3,7},{4,0},{5,1},{6,2},{7,3},{8,12},{9,13},{10,... | collective-permute-start | bytes 3080 | tf_op jit(solution)/shard_map/ppermute | solution.py:173
  79.1 0.9 %copy.19 = f32[2,8,96,256]{3,1,2,0:T(8,128)S(1)} copy(f32[2,8,96,256]{3,2,1,0:T(8,128)S(1)} %bitcast.29) | data formatting | bytes 3145728
  80.0 1.4 %collective-permute-done.8 = f32[16,16]{0,1:T(8,128)S(1)} collective-permute-done((f32[16,16]{0,1:T(8,128)S(1)}, f32[16,16]{0,1:T(8,128)S(1)}, u32[]{:S(2)}, u32[]{:S(2)}) %collective-permute-start.8) | collective-permute-done | bytes 1056 | tf_op jit(solution)/shard_map/ppermute | solution.py:173
  81.5 1.5 %cholesky.16 = f32[16,16]{1,0:T(8,128)S(1)} custom-call(f32[16,16]{1,0:T(8,128)S(1)} %fusion.8), custom_call_target="Cholesky" | custom-call | tf_op jit(solution)/shard_map/jit(cholesky)/cholesky | solution.py:175
  82.9 0.6 compare_reduce_fusion
  83.6 0.7 multiply_bitcast_fusion
  84.2 1.2 %custom-call.7 = f32[1,16,16]{1,2,0:T(8,128)S(1)} custom-call(f32[1,16,16]{2,1,0:T(8,128)S(1)} %get-tuple-element.11), custom_call_target="InvertDiagBlocksLowerTriangular" | custom-call | tf_op jit(solution)/shard_map/jit(_solve_triangular)/triangular_solve | solution.py:176
  85.5 1.5 %convolution_multiply_fusion = f32[16,24576]{1,0:T(8,128)S(1)} fusion(f32[16,24576]{1,0:T(8,128)S(1)} %bitcast.30, f32[1,16,16]{1,2,0:T(8,128)S(1)} %custom-call.7), kind=kOutput, calls=%fused_computation | convolution fusion | flops 75890688 | bytes 3146752 | tf_op jit(solution)/shard_map/jit(_solve_triangular)/triangular_solve | solution.py:176
  87.0 1.6 %copy.20 = f32[2,8,96,256]{3,2,1,0:T(8,128)} copy(f32[2,8,96,256]{3,1,2,0:T(8,128)S(1)} %bitcast.31) | data formatting | bytes 3145728
  88.6 0.7 copy.15
  (23 shorter events, 3.0 us)
Async XLA Ops:
  0.6 1.6 %copy-start.2 = (f32[3,32,256]{2,1,0:T(8,128)S(1)}, f32[3,32,256]{2,1,0:T(8,128)}, u32[]{:S(2)}) copy-start(f32[3,32,256]{2,1,0:T(8,128)} %param.2) | copy-start | bytes 294916
  2.3 20.9 %collective-permute-start = (f32[17,3,8,256]{3,2,1,0:T(8,128)S(1)}, f32[17,3,8,256]{3,2,1,0:T(8,128)S(1)}, u32[]{:S(2)}, u32[]{:S(2)}) collective-permute-start(f32[17,3,8,256]{3,2,1,0:T(8,128)S(1)} %get-tuple-element.9), channel_id=1, source_target_pairs={{0,1},{1,2},{2,3},{3,4},{4,5},{5,6},{6,7},{7,0},{8,9},{9,10},{10,1... | collective-permute-start | bytes 1253384 | tf_op jit(solution)/shard_map/ppermute | solution.py:38
  5.3 20.1 %collective-permute-start.1 = (f32[17,3,8,256]{3,2,1,0:T(8,128)S(1)}, f32[17,3,8,256]{3,2,1,0:T(8,128)S(1)}, u32[]{:S(2)}, u32[]{:S(2)}) collective-permute-start(f32[17,3,8,256]{3,2,1,0:T(8,128)S(1)} %get-tuple-element.8), channel_id=1, source_target_pairs={{0,7},{1,0},{2,1},{3,2},{4,3},{5,4},{6,5},{7,6},{8,15},{9,8},{10,9... | collective-permute-start | bytes 1253384 | tf_op jit(solution)/shard_map/ppermute | solution.py:38
  23.2 2.5 %copy-start = (f32[17,3,8,256]{3,2,1,0:T(8,128)}, f32[17,3,8,256]{3,2,1,0:T(8,128)S(1)}, u32[]{:S(2)}) copy-start(f32[17,3,8,256]{3,2,1,0:T(8,128)S(1)} %collective-permute-done.up_ref) | copy-start | bytes 1253380
  25.4 0.8 copy-start.1
  27.1 3.9 %collective-permute-start.2 = (f32[19584]{0:T(1024)S(1)}, f32[19584]{0:T(1024)S(1)}, u32[]{:S(2)}, u32[]{:S(2)}) collective-permute-start(f32[19584]{0:T(1024)S(1)} %reshape.59), channel_id=1, source_target_pairs={{0,8},{8,16},{16,24},{24,0},{1,9},{9,17},{17,25},{25,1},{2,10},{10... | collective-permute-start | bytes 235016 | tf_op jit(solution)/shard_map/ppermute | solution.py:40
  27.7 5.0 %collective-permute-start.3 = (f32[19584]{0:T(1024)S(1)}, f32[19584]{0:T(1024)S(1)}, u32[]{:S(2)}, u32[]{:S(2)}) collective-permute-start(f32[19584]{0:T(1024)S(1)} %reshape.61), channel_id=1, source_target_pairs={{0,24},{8,0},{16,8},{24,16},{1,25},{9,1},{17,9},{25,17},{2,26},{10... | collective-permute-start | bytes 235016 | tf_op jit(solution)/shard_map/ppermute | solution.py:40
  64.5 1.4 %collective-permute-start.4 = (f32[16,16]{0,1:T(8,128)S(1)}, f32[16,16]{0,1:T(8,128)S(1)}, u32[]{:S(2)}, u32[]{:S(2)}) collective-permute-start(f32[16,16]{0,1:T(8,128)S(1)} %fusion.2), channel_id=1, source_target_pairs={{0,8},{8,0},{16,24},{24,16},{1,9},{9,1},{17,25},{25,17},{2,10},{10... | collective-permute-start | bytes 3080 | tf_op jit(solution)/shard_map/ppermute | solution.py:173
  65.9 3.7 %collective-permute-start.5 = (f32[16,16]{0,1:T(8,128)S(1)}, f32[16,16]{0,1:T(8,128)S(1)}, u32[]{:S(2)}, u32[]{:S(2)}) collective-permute-start(f32[16,16]{0,1:T(8,128)S(1)} %add.77), channel_id=1, source_target_pairs={{0,16},{8,24},{16,0},{24,8},{1,17},{9,25},{17,1},{25,9},{2,18},{10... | collective-permute-start | bytes 3080 | tf_op jit(solution)/shard_map/ppermute | solution.py:173
  69.5 3.7 %collective-permute-start.6 = (f32[16,16]{0,1:T(8,128)S(1)}, f32[16,16]{0,1:T(8,128)S(1)}, u32[]{:S(2)}, u32[]{:S(2)}) collective-permute-start(f32[16,16]{0,1:T(8,128)S(1)} %add.78), channel_id=1, source_target_pairs={{0,1},{1,0},{2,3},{3,2},{4,5},{5,4},{6,7},{7,6},{8,9},{9,8},{10,11... | collective-permute-start | bytes 3080 | tf_op jit(solution)/shard_map/ppermute | solution.py:173
  73.2 3.7 %collective-permute-start.7 = (f32[16,16]{0,1:T(8,128)S(1)}, f32[16,16]{0,1:T(8,128)S(1)}, u32[]{:S(2)}, u32[]{:S(2)}) collective-permute-start(f32[16,16]{0,1:T(8,128)S(1)} %add.79), channel_id=1, source_target_pairs={{0,2},{1,3},{2,0},{3,1},{4,6},{5,7},{6,4},{7,5},{8,10},{9,11},{10,... | collective-permute-start | bytes 3080 | tf_op jit(solution)/shard_map/ppermute | solution.py:173
  76.8 4.5 %collective-permute-start.8 = (f32[16,16]{0,1:T(8,128)S(1)}, f32[16,16]{0,1:T(8,128)S(1)}, u32[]{:S(2)}, u32[]{:S(2)}) collective-permute-start(f32[16,16]{0,1:T(8,128)S(1)} %add.80), channel_id=1, source_target_pairs={{0,4},{1,5},{2,6},{3,7},{4,0},{5,1},{6,2},{7,3},{8,12},{9,13},{10,... | collective-permute-start | bytes 3080 | tf_op jit(solution)/shard_map/ppermute | solution.py:173

commit v10 on v9

--- a/solution.py
+++ b/solution.py
@@ -60,15 +60,7 @@
         east_pad[...] = jnp.zeros_like(east_pad)
         west_pad[...] = jnp.zeros_like(west_pad)
 
-    for k in range(3):
-        ring[k, :rows, :cols] = x_ref[0, k]
-        ring[k, rows : rows + width, :cols] = down_ref[0, k]
-        ring[k, rows + width :, :cols] = up_ref[0, k]
-        east_pad[:, :width] = east_ref[0, k]
-        west_pad[:, :width] = west_ref[0, k]
-        ring[k, :, cols:] = east_pad[...] + pltpu.roll(west_pad[...], spare - width, 1)
-
-    f = cor_ref[...]
+    base = cor_ref[...]
     third = 1.0 / 12.0
 
     def dx(v):
@@ -90,27 +82,41 @@
         moved = jnp.where(line < rows + keep, v, pltpu.roll(v, size - 2 * cut, 0))
         return moved[: size - 2 * cut]
 
-    def tend(h, e, n):
+    def tend(h, e, n, f):
         depth = 4.0 + h
         ch = -(dx(depth * e) + dy(depth * n))
         ce = -(e * dx(e) + n * dy(e)) + f * n - dx(h)
         cn = -(e * dx(n) + n * dy(n)) - f * e - dy(h)
         return ch, ce, cn
 
-    s = (ring[0], ring[1], ring[2])
-    margin = (R - rows) // 2
-    for step in range(steps):
-        keep = 4 * (steps - step)
-        if keep < margin and (rows + 2 * keep) % 8 == 0:
-            s = tuple(shrink(v, margin, keep) for v in s)
-            f = shrink(f, margin, keep)
-            margin = keep
-        first = tend(*s)
-        mid = tuple(a + 0.1 * b for a, b in zip(s, first))
-        second = tend(*mid)
-        s = tuple(a + 0.05 * (b + c) for a, b, c in zip(s, first, second))
-    for k in range(3):
-        o_ref[0, k] = s[k][:rows, :cols]
+    def one(i, carry):
+        for k in range(3):
+            ring[k, :rows, :cols] = x_ref[i, k]
+            ring[k, rows : rows + width, :cols] = down_ref[i, k]
+            ring[k, rows + width :, :cols] = up_ref[i, k]
+            east_pad[:, :width] = east_ref[i, k]
+            west_pad[:, :width] = west_ref[i, k]
+            ring[k, :, cols:] = east_pad[...] + pltpu.roll(west_pad[...], spare - width, 1)
+
+        f = base
+        s = (ring[0], ring[1], ring[2])
+        margin = (R - rows) // 2
+        for step in range(steps):
+            keep = 4 * (steps - step)
+            if keep < margin and (rows + 2 * keep) % 8 == 0:
+                s = tuple(shrink(v, margin, keep) for v in s)
+                f = shrink(f, margin, keep)
+                margin = keep
+            first = tend(*s, f)
+            mid = tuple(a + 0.1 * b for a, b in zip(s, first))
+            second = tend(*mid, f)
+            s = tuple(a + 0.05 * (b + c) for a, b, c in zip(s, first, second))
+        for k in range(3):
+            o_ref[i, k] = s[k][:rows, :cols]
+
+        return carry
+
+    lax.fori_loop(0, x_ref.shape[0], one, 0)
 
 
 def forecast(cor, value, above, below, west, east, steps):
@@ -120,16 +126,16 @@
     return pl.pallas_call(
         functools.partial(forecast_kernel, steps=steps),
         out_shape=jax.ShapeDtypeStruct((S, F, rows, cols), jnp.float32),
-        grid=(S,),
+        grid=(1,),
         in_specs=[
-            pl.BlockSpec((R, C), lambda i: (0, 0)),
-            pl.BlockSpec((1, F, rows, cols), lambda i: (i, 0, 0, 0)),
-            pl.BlockSpec((1, F, width, cols), lambda i: (i, 0, 0, 0)),
-            pl.BlockSpec((1, F, width, cols), lambda i: (i, 0, 0, 0)),
-            pl.BlockSpec((1, F, R, width), lambda i: (i, 0, 0, 0)),
-            pl.BlockSpec((1, F, R, width), lambda i: (i, 0, 0, 0)),
+            pl.BlockSpec((R, C), lambda i: (0, 0), pipeline_mode=pl.Buffered(1)),
+            pl.BlockSpec((S, F, rows, cols), lambda i: (0, 0, 0, 0), pipeline_mode=pl.Buffered(1)),
+            pl.BlockSpec((S, F, width, cols), lambda i: (0, 0, 0, 0), pipeline_mode=pl.Buffered(1)),
+            pl.BlockSpec((S, F, width, cols), lambda i: (0, 0, 0, 0), pipeline_mode=pl.Buffered(1)),
+            pl.BlockSpec((S, F, R, width), lambda i: (0, 0, 0, 0), pipeline_mode=pl.Buffered(1)),
+            pl.BlockSpec((S, F, R, width), lambda i: (0, 0, 0, 0), pipeline_mode=pl.Buffered(1)),
         ],
-        out_specs=pl.BlockSpec((1, F, rows, cols), lambda i: (i, 0, 0, 0)),
+        out_specs=pl.BlockSpec((S, F, rows, cols), lambda i: (0, 0, 0, 0), pipeline_mode=pl.Buffered(1)),
         scratch_shapes=[
             pltpu.VMEM((F, R, C), jnp.float32),
             pltpu.VMEM((R, C - cols), jnp.float32),

time: 89.5 us -> 90.8 us (1.015)
  Pallas kernels: 24.2 us -> 25.5 us
    pallas_call x1, Pallas kernels: 24.2 us -> 25.5 us  [forecast(): pl.pallas_call(functools.partial(forecast_kernel, steps=steps), out_shape...]
where the time goes in v10:
time: 90.8 us; the launch traced here: 90.6 us
  waiting for transfers between devices  27.2 us (30%)
  Pallas kernels  25.5 us (28%)
  starting transfers between devices  13.8 us (15%)
  local copies, waits for them, and re-layouts  10.3 us (11%)
  other arithmetic  8.83 us (10%)
  matrix products  4.22 us (5%)
    pallas_call x1, Pallas kernels, forecast(): pl.pallas_call(functools.partial(forecast_kernel, steps=steps), out_shape...  25.5 us
    ppermute x2, waiting for transfers between devices, shift(): return lax.ppermute(part, axes, pairs)  15.6 us
    ppermute x5, waiting for transfers between devices, body(): gram = gram + lax.ppermute(gram, axis, pairs)  10.1 us
    ppermute x2, starting transfers between devices, shift(): return lax.ppermute(part, axes, pairs)  6.12 us
    ppermute x5, starting transfers between devices, body(): gram = gram + lax.ppermute(gram, axis, pairs)  5.87 us
    unnamed x9, local copies, waits for them, and re-layouts  3.7 us
    reshape x2, local copies, waits for them, and re-layouts, shift(): return lax.ppermute(flat, axes, pairs).reshape(part.shape)  3.43 us
    dot_general x1, matrix products, body(): local_gram = jnp.dot(flat, flat.T, precision=lax.Precision.HIGHEST)  2.72 us
  transfers between devices with their start and end apart: 9, of which 8 were waited for; matrix products, arithmetic and copies ran while one was open for 5% of the time, Pallas kernels for 0%

profile of v10, /device:TPU:0, one launch (start us, length us, event | category | flops | bytes accessed | tf_op | source)
XLA Modules:
  0.0 90.6 jit_solution(10912343980156330661)
XLA Ops:
  0.6 1.6 %broadcast_add_fusion = f32[16,3,32,256]{3,2,1,0:T(8,128)S(1)} fusion(f32[16,3,32,256]{3,2,1,0:T(8,128)} %param.3, f32[3,32,256]{2,1,0:T(8,128)} %param.2), kind=kLoop, calls=%fused_computation.11 | loop fusion | flops 393216 | bytes 3244032 | tf_op jit(solution)/shard_map/add | solution.py:164
  2.3 3.0 %collective-permute-start = (f32[17,3,8,256]{3,2,1,0:T(8,128)S(1)}, f32[17,3,8,256]{3,2,1,0:T(8,128)S(1)}, u32[]{:S(2)}, u32[]{:S(2)}) collective-permute-start(f32[17,3,8,256]{3,2,1,0:T(8,128)S(1)} %get-tuple-element.9), channel_id=1, source_target_pairs={{0,1},{1,2},{2,3},{3,4},{4,5},{5,6},{6,7},{7,0},{8,9},{9,10},{10,1... | collective-permute-start | bytes 1253384 | tf_op jit(solution)/shard_map/ppermute | solution.py:38
  5.3 3.1 %collective-permute-start.1 = (f32[17,3,8,256]{3,2,1,0:T(8,128)S(1)}, f32[17,3,8,256]{3,2,1,0:T(8,128)S(1)}, u32[]{:S(2)}, u32[]{:S(2)}) collective-permute-start(f32[17,3,8,256]{3,2,1,0:T(8,128)S(1)} %get-tuple-element.8), channel_id=1, source_target_pairs={{0,7},{1,0},{2,1},{3,2},{4,3},{5,4},{6,5},{7,6},{8,15},{9,8},{10,9... | collective-permute-start | bytes 1253384 | tf_op jit(solution)/shard_map/ppermute | solution.py:38
  8.4 1.3 %pad_maximum_fusion.x_ref = f32[17,3,32,256]{3,2,1,0:T(8,128)} fusion(f32[1,3,32,256]{3,2,1,0:T(8,128)S(1)} %bitcast.33, f32[16,3,32,256]{3,2,1,0:T(8,128)S(1)} %broadcast_add_fusion), kind=kLoop, calls=%fused_computation.3 | loop fusion | flops 417792 | bytes 3342336 | tf_op jit(solution)/shard_map/concatenate | solution.py:164
  9.8 13.4 %collective-permute-done.up_ref = f32[17,3,8,256]{3,2,1,0:T(8,128)S(1)} collective-permute-done((f32[17,3,8,256]{3,2,1,0:T(8,128)S(1)}, f32[17,3,8,256]{3,2,1,0:T(8,128)S(1)}, u32[]{:S(2)}, u32[]{:S(2)}) %collective-permute-start) | collective-permute-done | bytes 417824 | tf_op jit(solution)/shard_map/ppermute | solution.py:38
  23.2 2.2 %collective-permute-done.1.down_ref = f32[17,3,8,256]{3,2,1,0:T(8,128)S(1)} collective-permute-done((f32[17,3,8,256]{3,2,1,0:T(8,128)S(1)}, f32[17,3,8,256]{3,2,1,0:T(8,128)S(1)}, u32[]{:S(2)}, u32[]{:S(2)}) %collective-permute-start.1) | collective-permute-done | bytes 417824 | tf_op jit(solution)/shard_map/ppermute | solution.py:38
  26.6 0.5 reshape.59
  27.7 1.8 %collective-permute-start.3 = (f32[19584]{0:T(1024)S(1)}, f32[19584]{0:T(1024)S(1)}, u32[]{:S(2)}, u32[]{:S(2)}) collective-permute-start(f32[19584]{0:T(1024)S(1)} %reshape.61), channel_id=1, source_target_pairs={{0,24},{8,0},{16,8},{24,16},{1,25},{9,1},{17,9},{25,17},{2,26},{10... | collective-permute-start | bytes 235016 | tf_op jit(solution)/shard_map/ppermute | solution.py:40
  29.5 1.5 %collective-permute-done.2 = f32[19584]{0:T(1024)S(1)} collective-permute-done((f32[19584]{0:T(1024)S(1)}, f32[19584]{0:T(1024)S(1)}, u32[]{:S(2)}, u32[]{:S(2)}) %collective-permute-start.2) | collective-permute-done | bytes 78368 | tf_op jit(solution)/shard_map/ppermute | solution.py:40
  31.0 1.7 %reshape.60.west_ref = f32[17,3,48,8]{3,2,1,0:T(8,128)} reshape(f32[19584]{0:T(1024)S(1)} %collective-permute-done.2) | data formatting | bytes 156672 | tf_op jit(solution)/shard_map/reshape | solution.py:40
  32.7 1.7 %reshape.62.east_ref = f32[17,3,48,8]{3,2,1,0:T(8,128)} reshape(f32[19584]{0:T(1024)S(1)} %collective-permute-done.3) | data formatting | bytes 156672 | tf_op jit(solution)/shard_map/reshape | solution.py:40
  34.5 0.7 broadcast_in_dim.5.cor_ref
  35.2 25.5 %shard_map.41 = f32[17,3,32,256]{3,2,1,0:T(8,128)} custom-call(f32[48,384]{1,0:T(8,128)} %broadcast_in_dim.5.cor_ref, f32[17,3,32,256]{3,2,1,0:T(8,128)} %pad_maximum_fusion.x_ref, f32[17,3,8,256]{3,2,1,0:T(8,128)} %copy-done, f32[17,3,8,256]{3,2,1,0:T(8,128)} %copy-done.1, f32[17,3,48,8]{3,2,1,0:T(8,128)} %reshape.60.west_ref, ...), custom_call_target="tpu_custom_call" | custom-call | flops 564019200 | bytes 5431296 | tf_op jit(solution)/shard_map/pallas_call | solution.py:126
  60.6 0.9 slice_bitcast_fusion
  61.5 1.5 %slice_subtract_fusion = f32[16,3,32,256]{3,2,1,0:T(8,128)S(1)} fusion(f32[17,3,32,256]{3,2,1,0:T(8,128)} %shard_map.41, f32[3,32,256]{2,1,0:T(8,128)S(1)} %slice_bitcast_fusion), kind=kLoop, calls=%fused_computation.5 | loop fusion | flops 393216 | bytes 3244032 | tf_op jit(solution)/shard_map/sub | solution.py:167
  63.1 2.7 %fusion.2 = f32[16,16]{0,1:T(8,128)S(1)} fusion(f32[16,3,32,256]{3,2,1,0:T(8,128)S(1)} %slice_subtract_fusion), kind=kOutput, calls=%fused_computation.10 | convolution fusion | flops 75497472 | bytes 1573888 | tf_op jit(solution)/shard_map/dot_general | solution.py:169
  66.3 0.8 collective-permute-done.4
  67.2 1.4 %collective-permute-start.5 = (f32[16,16]{0,1:T(8,128)S(1)}, f32[16,16]{0,1:T(8,128)S(1)}, u32[]{:S(2)}, u32[]{:S(2)}) collective-permute-start(f32[16,16]{0,1:T(8,128)S(1)} %add.77), channel_id=1, source_target_pairs={{0,16},{8,24},{16,0},{24,8},{1,17},{9,25},{17,1},{25,9},{2,18},{10... | collective-permute-start | bytes 3080 | tf_op jit(solution)/shard_map/ppermute | solution.py:179
  68.5 2.3 %collective-permute-done.5 = f32[16,16]{0,1:T(8,128)S(1)} collective-permute-done((f32[16,16]{0,1:T(8,128)S(1)}, f32[16,16]{0,1:T(8,128)S(1)}, u32[]{:S(2)}, u32[]{:S(2)}) %collective-permute-start.5) | collective-permute-done | bytes 1056 | tf_op jit(solution)/shard_map/ppermute | solution.py:179
  71.3 3.2 %collective-permute-done.6 = f32[16,16]{0,1:T(8,128)S(1)} collective-permute-done((f32[16,16]{0,1:T(8,128)S(1)}, f32[16,16]{0,1:T(8,128)S(1)}, u32[]{:S(2)}, u32[]{:S(2)}) %collective-permute-start.6) | collective-permute-done | bytes 1056 | tf_op jit(solution)/shard_map/ppermute | solution.py:179
  74.5 1.3 %collective-permute-start.7 = (f32[16,16]{0,1:T(8,128)S(1)}, f32[16,16]{0,1:T(8,128)S(1)}, u32[]{:S(2)}, u32[]{:S(2)}) collective-permute-start(f32[16,16]{0,1:T(8,128)S(1)} %add.79), channel_id=1, source_target_pairs={{0,2},{1,3},{2,0},{3,1},{4,6},{5,7},{6,4},{7,5},{8,10},{9,11},{10,... | collective-permute-start | bytes 3080 | tf_op jit(solution)/shard_map/ppermute | solution.py:179
  75.7 2.4 %collective-permute-done.7 = f32[16,16]{0,1:T(8,128)S(1)} collective-permute-done((f32[16,16]{0,1:T(8,128)S(1)}, f32[16,16]{0,1:T(8,128)S(1)}, u32[]{:S(2)}, u32[]{:S(2)}) %collective-permute-start.7) | collective-permute-done | bytes 1056 | tf_op jit(solution)/shard_map/ppermute | solution.py:179
  78.1 2.3 %collective-permute-start.8 = (f32[16,16]{0,1:T(8,128)S(1)}, f32[16,16]{0,1:T(8,128)S(1)}, u32[]{:S(2)}, u32[]{:S(2)}) collective-permute-start(f32[16,16]{0,1:T(8,128)S(1)} %add.80), channel_id=1, source_target_pairs={{0,4},{1,5},{2,6},{3,7},{4,0},{5,1},{6,2},{7,3},{8,12},{9,13},{10,... | collective-permute-start | bytes 3080 | tf_op jit(solution)/shard_map/ppermute | solution.py:179
  80.4 0.9 %copy.19 = f32[2,8,96,256]{3,1,2,0:T(8,128)S(1)} copy(f32[2,8,96,256]{3,2,1,0:T(8,128)S(1)} %bitcast.29) | data formatting | bytes 3145728
  81.3 1.4 %collective-permute-done.8 = f32[16,16]{0,1:T(8,128)S(1)} collective-permute-done((f32[16,16]{0,1:T(8,128)S(1)}, f32[16,16]{0,1:T(8,128)S(1)}, u32[]{:S(2)}, u32[]{:S(2)}) %collective-permute-start.8) | collective-permute-done | bytes 1056 | tf_op jit(solution)/shard_map/ppermute | solution.py:179
  82.8 1.5 %cholesky.16 = f32[16,16]{1,0:T(8,128)S(1)} custom-call(f32[16,16]{1,0:T(8,128)S(1)} %fusion.8), custom_call_target="Cholesky" | custom-call | tf_op jit(solution)/shard_map/jit(cholesky)/cholesky | solution.py:181
  84.3 0.6 compare_reduce_fusion
  84.9 0.7 multiply_bitcast_fusion
  85.6 1.2 %custom-call.7 = f32[1,16,16]{1,2,0:T(8,128)S(1)} custom-call(f32[1,16,16]{2,1,0:T(8,128)S(1)} %get-tuple-element.11), custom_call_target="InvertDiagBlocksLowerTriangular" | custom-call | tf_op jit(solution)/shard_map/jit(_solve_triangular)/triangular_solve | solution.py:182
  86.8 1.5 %convolution_multiply_fusion = f32[16,24576]{1,0:T(8,128)S(1)} fusion(f32[16,24576]{1,0:T(8,128)S(1)} %bitcast.30, f32[1,16,16]{1,2,0:T(8,128)S(1)} %custom-call.7), kind=kOutput, calls=%fused_computation | convolution fusion | flops 75890688 | bytes 3146752 | tf_op jit(solution)/shard_map/jit(_solve_triangular)/triangular_solve | solution.py:182
  88.3 1.6 %copy.20 = f32[2,8,96,256]{3,2,1,0:T(8,128)} copy(f32[2,8,96,256]{3,1,2,0:T(8,128)S(1)} %bitcast.31) | data formatting | bytes 3145728
  89.9 0.7 copy.15
  (23 shorter events, 3.0 us)
Async XLA Ops:
  0.6 1.6 %copy-start.2 = (f32[3,32,256]{2,1,0:T(8,128)S(1)}, f32[3,32,256]{2,1,0:T(8,128)}, u32[]{:S(2)}) copy-start(f32[3,32,256]{2,1,0:T(8,128)} %param.2) | copy-start | bytes 294916
  2.3 20.9 %collective-permute-start = (f32[17,3,8,256]{3,2,1,0:T(8,128)S(1)}, f32[17,3,8,256]{3,2,1,0:T(8,128)S(1)}, u32[]{:S(2)}, u32[]{:S(2)}) collective-permute-start(f32[17,3,8,256]{3,2,1,0:T(8,128)S(1)} %get-tuple-element.9), channel_id=1, source_target_pairs={{0,1},{1,2},{2,3},{3,4},{4,5},{5,6},{6,7},{7,0},{8,9},{9,10},{10,1... | collective-permute-start | bytes 1253384 | tf_op jit(solution)/shard_map/ppermute | solution.py:38
  5.3 20.1 %collective-permute-start.1 = (f32[17,3,8,256]{3,2,1,0:T(8,128)S(1)}, f32[17,3,8,256]{3,2,1,0:T(8,128)S(1)}, u32[]{:S(2)}, u32[]{:S(2)}) collective-permute-start(f32[17,3,8,256]{3,2,1,0:T(8,128)S(1)} %get-tuple-element.8), channel_id=1, source_target_pairs={{0,7},{1,0},{2,1},{3,2},{4,3},{5,4},{6,5},{7,6},{8,15},{9,8},{10,9... | collective-permute-start | bytes 1253384 | tf_op jit(solution)/shard_map/ppermute | solution.py:38
  23.2 2.5 %copy-start = (f32[17,3,8,256]{3,2,1,0:T(8,128)}, f32[17,3,8,256]{3,2,1,0:T(8,128)S(1)}, u32[]{:S(2)}) copy-start(f32[17,3,8,256]{3,2,1,0:T(8,128)S(1)} %collective-permute-done.up_ref) | copy-start | bytes 1253380
  25.4 0.8 copy-start.1
  27.1 3.9 %collective-permute-start.2 = (f32[19584]{0:T(1024)S(1)}, f32[19584]{0:T(1024)S(1)}, u32[]{:S(2)}, u32[]{:S(2)}) collective-permute-start(f32[19584]{0:T(1024)S(1)} %reshape.59), channel_id=1, source_target_pairs={{0,8},{8,16},{16,24},{24,0},{1,9},{9,17},{17,25},{25,1},{2,10},{10... | collective-permute-start | bytes 235016 | tf_op jit(solution)/shard_map/ppermute | solution.py:40
  27.7 5.0 %collective-permute-start.3 = (f32[19584]{0:T(1024)S(1)}, f32[19584]{0:T(1024)S(1)}, u32[]{:S(2)}, u32[]{:S(2)}) collective-permute-start(f32[19584]{0:T(1024)S(1)} %reshape.61), channel_id=1, source_target_pairs={{0,24},{8,0},{16,8},{24,16},{1,25},{9,1},{17,9},{25,17},{2,26},{10... | collective-permute-start | bytes 235016 | tf_op jit(solution)/shard_map/ppermute | solution.py:40
  65.8 1.4 %collective-permute-start.4 = (f32[16,16]{0,1:T(8,128)S(1)}, f32[16,16]{0,1:T(8,128)S(1)}, u32[]{:S(2)}, u32[]{:S(2)}) collective-permute-start(f32[16,16]{0,1:T(8,128)S(1)} %fusion.2), channel_id=1, source_target_pairs={{0,8},{8,0},{16,24},{24,16},{1,9},{9,1},{17,25},{25,17},{2,10},{10... | collective-permute-start | bytes 3080 | tf_op jit(solution)/shard_map/ppermute | solution.py:179
  67.2 3.7 %collective-permute-start.5 = (f32[16,16]{0,1:T(8,128)S(1)}, f32[16,16]{0,1:T(8,128)S(1)}, u32[]{:S(2)}, u32[]{:S(2)}) collective-permute-start(f32[16,16]{0,1:T(8,128)S(1)} %add.77), channel_id=1, source_target_pairs={{0,16},{8,24},{16,0},{24,8},{1,17},{9,25},{17,1},{25,9},{2,18},{10... | collective-permute-start | bytes 3080 | tf_op jit(solution)/shard_map/ppermute | solution.py:179
  70.8 3.7 %collective-permute-start.6 = (f32[16,16]{0,1:T(8,128)S(1)}, f32[16,16]{0,1:T(8,128)S(1)}, u32[]{:S(2)}, u32[]{:S(2)}) collective-permute-start(f32[16,16]{0,1:T(8,128)S(1)} %add.78), channel_id=1, source_target_pairs={{0,1},{1,0},{2,3},{3,2},{4,5},{5,4},{6,7},{7,6},{8,9},{9,8},{10,11... | collective-permute-start | bytes 3080 | tf_op jit(solution)/shard_map/ppermute | solution.py:179
  74.5 3.7 %collective-permute-start.7 = (f32[16,16]{0,1:T(8,128)S(1)}, f32[16,16]{0,1:T(8,128)S(1)}, u32[]{:S(2)}, u32[]{:S(2)}) collective-permute-start(f32[16,16]{0,1:T(8,128)S(1)} %add.79), channel_id=1, source_target_pairs={{0,2},{1,3},{2,0},{3,1},{4,6},{5,7},{6,4},{7,5},{8,10},{9,11},{10,... | collective-permute-start | bytes 3080 | tf_op jit(solution)/shard_map/ppermute | solution.py:179
  78.1 4.5 %collective-permute-start.8 = (f32[16,16]{0,1:T(8,128)S(1)}, f32[16,16]{0,1:T(8,128)S(1)}, u32[]{:S(2)}, u32[]{:S(2)}) collective-permute-start(f32[16,16]{0,1:T(8,128)S(1)} %add.80), channel_id=1, source_target_pairs={{0,4},{1,5},{2,6},{3,7},{4,0},{5,1},{6,2},{7,3},{8,12},{9,13},{10,... | collective-permute-start | bytes 3080 | tf_op jit(solution)/shard_map/ppermute | solution.py:179

commit v11 on v3

--- a/solution.py
+++ b/solution.py
@@ -42,13 +42,13 @@
     top, bottom = (value[..., :width, :], value[..., rows - width :, :])
     above = shift(bottom, "gy", 0, 1, flatten=False)
     below = shift(top, "gy", 0, -1, flatten=False)
-    tall = jnp.concatenate([value, below, above], axis=-2)
+    tall = jnp.concatenate([above, value, below], axis=-2)
     west = shift(tall[..., cols - width :], "gx", 1, 0)
     east = shift(tall[..., :width], "gx", -1, 0)
     return above, below, west, east
 
 
-def forecast_kernel(cor_ref, x_ref, up_ref, down_ref, west_ref, east_ref, o_ref, ring, east_pad, west_pad, *, steps):
+def forecast_kernel(cor_ref, x_ref, up_ref, down_ref, west_ref, east_ref, o_ref, ring, east_pad, west_pad, shifted, *, steps):
     rows, cols = (x_ref.shape[-2], x_ref.shape[-1])
     R, C = cor_ref.shape
     width = up_ref.shape[-2]
@@ -59,11 +59,12 @@
         ring[...] = jnp.zeros_like(ring)
         east_pad[...] = jnp.zeros_like(east_pad)
         west_pad[...] = jnp.zeros_like(west_pad)
+        shifted[...] = jnp.zeros_like(shifted)
 
     for k in range(3):
-        ring[k, :rows, :cols] = x_ref[0, k]
-        ring[k, rows : rows + width, :cols] = down_ref[0, k]
-        ring[k, rows + width :, :cols] = up_ref[0, k]
+        ring[k, :width, :cols] = up_ref[0, k]
+        ring[k, width : width + rows, :cols] = x_ref[0, k]
+        ring[k, width + rows :, :cols] = down_ref[0, k]
         east_pad[:, :width] = east_ref[0, k]
         west_pad[:, :width] = west_ref[0, k]
         ring[k, :, cols:] = east_pad[...] + pltpu.roll(west_pad[...], spare - width, 1)
@@ -77,8 +78,9 @@
         return (8.0 * g - w) * third
 
     def dy(v):
-        g = pltpu.roll(v, R - 1, 0) - pltpu.roll(v, 1, 0)
-        w = pltpu.roll(v, R - 2, 0) - pltpu.roll(v, 2, 0)
+        shifted[8 : 8 + R, :] = v
+        g = shifted[pl.ds(9, R), :] - shifted[pl.ds(7, R), :]
+        w = shifted[pl.ds(10, R), :] - shifted[pl.ds(6, R), :]
         return (8.0 * g - w) * third
 
     def tend(h, e, n):
@@ -95,7 +97,7 @@
         second = tend(*mid)
         s = tuple(a + 0.05 * (b + c) for a, b, c in zip(s, first, second))
     for k in range(3):
-        o_ref[0, k] = s[k][:rows, :cols]
+        o_ref[0, k] = s[k][width : width + rows, :cols]
 
 
 def forecast(cor, value, above, below, west, east, steps):
@@ -119,6 +121,7 @@
             pltpu.VMEM((F, R, C), jnp.float32),
             pltpu.VMEM((R, C - cols), jnp.float32),
             pltpu.VMEM((R, C - cols), jnp.float32),
+            pltpu.VMEM((R + 16, C), jnp.float32),
         ],
         cost_estimate=pl.CostEstimate(
             flops=S * F * R * C * 300 * steps, transcendentals=0, bytes_accessed=4 * S * F * (R * C + rows * cols)
@@ -134,8 +137,7 @@
     margin = 4 * STEPS
     lanes = 128 * (-(-(tile_column_count + 2 * margin) // 128))
     ring_rows = tile_rows + 2 * margin
-    offsets = jnp.arange(ring_rows, dtype=jnp.int32)
-    offsets = jnp.where(offsets < tile_rows + margin, offsets, offsets - ring_rows)
+    offsets = jnp.arange(ring_rows, dtype=jnp.int32) - margin
     rows = ((first_row + offsets) % grid_rows).astype(jnp.float32)
     coriolis = coriolis_mid * (1.0 + 0.5 * jnp.sin(two_pi * rows / float(grid_rows)))
     coriolis = jnp.broadcast_to(coriolis[:, None], (ring_rows, lanes))

time: 90.2 us -> 90.9 us (level)
  no operation moved by 1% of the time
where the time goes in v11:
time: 90.9 us; the launch traced here: 90.6 us
  waiting for transfers between devices  27.2 us (30%)
  Pallas kernels  25.6 us (28%)
  starting transfers between devices  13.8 us (15%)
  local copies, waits for them, and re-layouts  10.3 us (11%)
  other arithmetic  8.83 us (10%)
  matrix products  4.22 us (5%)
    pallas_call x1, Pallas kernels, forecast(): pl.pallas_call(functools.partial(forecast_kernel, steps=steps), out_shape...  25.6 us
    ppermute x2, waiting for transfers between devices, shift(): return lax.ppermute(part, axes, pairs)  15.6 us
    ppermute x5, waiting for transfers between devices, body(): gram = gram + lax.ppermute(gram, axis, pairs)  10.1 us
    ppermute x2, starting transfers between devices, shift(): return lax.ppermute(part, axes, pairs)  6.12 us
    ppermute x5, starting transfers between devices, body(): gram = gram + lax.ppermute(gram, axis, pairs)  5.88 us
    unnamed x9, local copies, waits for them, and re-layouts  3.7 us
    reshape x2, local copies, waits for them, and re-layouts, shift(): return lax.ppermute(flat, axes, pairs).reshape(part.shape)  3.43 us
    dot_general x1, matrix products, body(): local_gram = jnp.dot(flat, flat.T, precision=lax.Precision.HIGHEST)  2.72 us
  transfers between devices with their start and end apart: 9, of which 8 were waited for; matrix products, arithmetic and copies ran while one was open for 5% of the time, Pallas kernels for 0%

profile of v11, /device:TPU:0, one launch (start us, length us, event | category | flops | bytes accessed | tf_op | source)
XLA Modules:
  0.0 90.6 jit_solution(16034630878198299007)
XLA Ops:
  0.6 1.6 %broadcast_add_fusion = f32[16,3,32,256]{3,2,1,0:T(8,128)S(1)} fusion(f32[16,3,32,256]{3,2,1,0:T(8,128)} %param.3, f32[3,32,256]{2,1,0:T(8,128)} %param.2), kind=kLoop, calls=%fused_computation.11 | loop fusion | flops 393216 | bytes 3244032 | tf_op jit(solution)/shard_map/add | solution.py:145
  2.3 3.0 %collective-permute-start = (f32[17,3,8,256]{3,2,1,0:T(8,128)S(1)}, f32[17,3,8,256]{3,2,1,0:T(8,128)S(1)}, u32[]{:S(2)}, u32[]{:S(2)}) collective-permute-start(f32[17,3,8,256]{3,2,1,0:T(8,128)S(1)} %get-tuple-element.9), channel_id=1, source_target_pairs={{0,1},{1,2},{2,3},{3,4},{4,5},{5,6},{6,7},{7,0},{8,9},{9,10},{10,1... | collective-permute-start | bytes 1253384 | tf_op jit(solution)/shard_map/ppermute | solution.py:38
  5.3 3.1 %collective-permute-start.1 = (f32[17,3,8,256]{3,2,1,0:T(8,128)S(1)}, f32[17,3,8,256]{3,2,1,0:T(8,128)S(1)}, u32[]{:S(2)}, u32[]{:S(2)}) collective-permute-start(f32[17,3,8,256]{3,2,1,0:T(8,128)S(1)} %get-tuple-element.8), channel_id=1, source_target_pairs={{0,7},{1,0},{2,1},{3,2},{4,3},{5,4},{6,5},{7,6},{8,15},{9,8},{10,9... | collective-permute-start | bytes 1253384 | tf_op jit(solution)/shard_map/ppermute | solution.py:38
  8.4 1.3 %pad_maximum_fusion.x_ref = f32[17,3,32,256]{3,2,1,0:T(8,128)} fusion(f32[1,3,32,256]{3,2,1,0:T(8,128)S(1)} %bitcast.33, f32[16,3,32,256]{3,2,1,0:T(8,128)S(1)} %broadcast_add_fusion), kind=kLoop, calls=%fused_computation.3 | loop fusion | flops 417792 | bytes 3342336 | tf_op jit(solution)/shard_map/concatenate | solution.py:145
  9.8 13.4 %collective-permute-done.up_ref = f32[17,3,8,256]{3,2,1,0:T(8,128)S(1)} collective-permute-done((f32[17,3,8,256]{3,2,1,0:T(8,128)S(1)}, f32[17,3,8,256]{3,2,1,0:T(8,128)S(1)}, u32[]{:S(2)}, u32[]{:S(2)}) %collective-permute-start) | collective-permute-done | bytes 417824 | tf_op jit(solution)/shard_map/ppermute | solution.py:38
  23.2 2.2 %collective-permute-done.1.down_ref = f32[17,3,8,256]{3,2,1,0:T(8,128)S(1)} collective-permute-done((f32[17,3,8,256]{3,2,1,0:T(8,128)S(1)}, f32[17,3,8,256]{3,2,1,0:T(8,128)S(1)}, u32[]{:S(2)}, u32[]{:S(2)}) %collective-permute-start.1) | collective-permute-done | bytes 417824 | tf_op jit(solution)/shard_map/ppermute | solution.py:38
  26.6 0.5 reshape.55
  27.7 1.8 %collective-permute-start.3 = (f32[19584]{0:T(1024)S(1)}, f32[19584]{0:T(1024)S(1)}, u32[]{:S(2)}, u32[]{:S(2)}) collective-permute-start(f32[19584]{0:T(1024)S(1)} %reshape.57), channel_id=1, source_target_pairs={{0,24},{8,0},{16,8},{24,16},{1,25},{9,1},{17,9},{25,17},{2,26},{10... | collective-permute-start | bytes 235016 | tf_op jit(solution)/shard_map/ppermute | solution.py:40
  29.5 1.5 %collective-permute-done.2 = f32[19584]{0:T(1024)S(1)} collective-permute-done((f32[19584]{0:T(1024)S(1)}, f32[19584]{0:T(1024)S(1)}, u32[]{:S(2)}, u32[]{:S(2)}) %collective-permute-start.2) | collective-permute-done | bytes 78368 | tf_op jit(solution)/shard_map/ppermute | solution.py:40
  31.0 1.7 %reshape.56.west_ref = f32[17,3,48,8]{3,2,1,0:T(8,128)} reshape(f32[19584]{0:T(1024)S(1)} %collective-permute-done.2) | data formatting | bytes 156672 | tf_op jit(solution)/shard_map/reshape | solution.py:40
  32.7 1.7 %reshape.58.east_ref = f32[17,3,48,8]{3,2,1,0:T(8,128)} reshape(f32[19584]{0:T(1024)S(1)} %collective-permute-done.3) | data formatting | bytes 156672 | tf_op jit(solution)/shard_map/reshape | solution.py:40
  34.4 0.7 broadcast_in_dim.5.cor_ref
  35.1 25.6 %shard_map.41 = f32[17,3,32,256]{3,2,1,0:T(8,128)} custom-call(f32[48,384]{1,0:T(8,128)} %broadcast_in_dim.5.cor_ref, f32[17,3,32,256]{3,2,1,0:T(8,128)} %pad_maximum_fusion.x_ref, f32[17,3,8,256]{3,2,1,0:T(8,128)} %copy-done, f32[17,3,8,256]{3,2,1,0:T(8,128)} %copy-done.1, f32[17,3,48,8]{3,2,1,0:T(8,128)} %reshape.56.west_ref, ...), custom_call_target="tpu_custom_call" | custom-call | flops 564019200 | bytes 5431296 | tf_op jit(solution)/shard_map/pallas_call | solution.py:107
  60.7 0.9 slice_bitcast_fusion
  61.6 1.5 %slice_subtract_fusion = f32[16,3,32,256]{3,2,1,0:T(8,128)S(1)} fusion(f32[17,3,32,256]{3,2,1,0:T(8,128)} %shard_map.41, f32[3,32,256]{2,1,0:T(8,128)S(1)} %slice_bitcast_fusion), kind=kLoop, calls=%fused_computation.5 | loop fusion | flops 393216 | bytes 3244032 | tf_op jit(solution)/shard_map/sub | solution.py:148
  63.2 2.7 %fusion.2 = f32[16,16]{0,1:T(8,128)S(1)} fusion(f32[16,3,32,256]{3,2,1,0:T(8,128)S(1)} %slice_subtract_fusion), kind=kOutput, calls=%fused_computation.10 | convolution fusion | flops 75497472 | bytes 1573888 | tf_op jit(solution)/shard_map/dot_general | solution.py:150
  66.4 0.8 collective-permute-done.4
  67.2 1.4 %collective-permute-start.5 = (f32[16,16]{0,1:T(8,128)S(1)}, f32[16,16]{0,1:T(8,128)S(1)}, u32[]{:S(2)}, u32[]{:S(2)}) collective-permute-start(f32[16,16]{0,1:T(8,128)S(1)} %add.77), channel_id=1, source_target_pairs={{0,16},{8,24},{16,0},{24,8},{1,17},{9,25},{17,1},{25,9},{2,18},{10... | collective-permute-start | bytes 3080 | tf_op jit(solution)/shard_map/ppermute | solution.py:160
  68.6 2.3 %collective-permute-done.5 = f32[16,16]{0,1:T(8,128)S(1)} collective-permute-done((f32[16,16]{0,1:T(8,128)S(1)}, f32[16,16]{0,1:T(8,128)S(1)}, u32[]{:S(2)}, u32[]{:S(2)}) %collective-permute-start.5) | collective-permute-done | bytes 1056 | tf_op jit(solution)/shard_map/ppermute | solution.py:160
  71.4 3.2 %collective-permute-done.6 = f32[16,16]{0,1:T(8,128)S(1)} collective-permute-done((f32[16,16]{0,1:T(8,128)S(1)}, f32[16,16]{0,1:T(8,128)S(1)}, u32[]{:S(2)}, u32[]{:S(2)}) %collective-permute-start.6) | collective-permute-done | bytes 1056 | tf_op jit(solution)/shard_map/ppermute | solution.py:160
  74.6 1.3 %collective-permute-start.7 = (f32[16,16]{0,1:T(8,128)S(1)}, f32[16,16]{0,1:T(8,128)S(1)}, u32[]{:S(2)}, u32[]{:S(2)}) collective-permute-start(f32[16,16]{0,1:T(8,128)S(1)} %add.79), channel_id=1, source_target_pairs={{0,2},{1,3},{2,0},{3,1},{4,6},{5,7},{6,4},{7,5},{8,10},{9,11},{10,... | collective-permute-start | bytes 3080 | tf_op jit(solution)/shard_map/ppermute | solution.py:160
  75.8 2.4 %collective-permute-done.7 = f32[16,16]{0,1:T(8,128)S(1)} collective-permute-done((f32[16,16]{0,1:T(8,128)S(1)}, f32[16,16]{0,1:T(8,128)S(1)}, u32[]{:S(2)}, u32[]{:S(2)}) %collective-permute-start.7) | collective-permute-done | bytes 1056 | tf_op jit(solution)/shard_map/ppermute | solution.py:160
  78.2 2.3 %collective-permute-start.8 = (f32[16,16]{0,1:T(8,128)S(1)}, f32[16,16]{0,1:T(8,128)S(1)}, u32[]{:S(2)}, u32[]{:S(2)}) collective-permute-start(f32[16,16]{0,1:T(8,128)S(1)} %add.80), channel_id=1, source_target_pairs={{0,4},{1,5},{2,6},{3,7},{4,0},{5,1},{6,2},{7,3},{8,12},{9,13},{10,... | collective-permute-start | bytes 3080 | tf_op jit(solution)/shard_map/ppermute | solution.py:160
  80.5 0.9 %copy.19 = f32[2,8,96,256]{3,1,2,0:T(8,128)S(1)} copy(f32[2,8,96,256]{3,2,1,0:T(8,128)S(1)} %bitcast.29) | data formatting | bytes 3145728
  81.4 1.4 %collective-permute-done.8 = f32[16,16]{0,1:T(8,128)S(1)} collective-permute-done((f32[16,16]{0,1:T(8,128)S(1)}, f32[16,16]{0,1:T(8,128)S(1)}, u32[]{:S(2)}, u32[]{:S(2)}) %collective-permute-start.8) | collective-permute-done | bytes 1056 | tf_op jit(solution)/shard_map/ppermute | solution.py:160
  82.8 1.5 %cholesky.16 = f32[16,16]{1,0:T(8,128)S(1)} custom-call(f32[16,16]{1,0:T(8,128)S(1)} %fusion.8), custom_call_target="Cholesky" | custom-call | tf_op jit(solution)/shard_map/jit(cholesky)/cholesky | solution.py:162
  84.3 0.6 compare_reduce_fusion
  85.0 0.7 multiply_bitcast_fusion
  85.6 1.2 %custom-call.7 = f32[1,16,16]{1,2,0:T(8,128)S(1)} custom-call(f32[1,16,16]{2,1,0:T(8,128)S(1)} %get-tuple-element.11), custom_call_target="InvertDiagBlocksLowerTriangular" | custom-call | tf_op jit(solution)/shard_map/jit(_solve_triangular)/triangular_solve | solution.py:163
  86.9 1.5 %convolution_multiply_fusion = f32[16,24576]{1,0:T(8,128)S(1)} fusion(f32[16,24576]{1,0:T(8,128)S(1)} %bitcast.30, f32[1,16,16]{1,2,0:T(8,128)S(1)} %custom-call.7), kind=kOutput, calls=%fused_computation | convolution fusion | flops 75890688 | bytes 3146752 | tf_op jit(solution)/shard_map/jit(_solve_triangular)/triangular_solve | solution.py:163
  88.4 1.6 %copy.20 = f32[2,8,96,256]{3,2,1,0:T(8,128)} copy(f32[2,8,96,256]{3,1,2,0:T(8,128)S(1)} %bitcast.31) | data formatting | bytes 3145728
  90.0 0.7 copy.15
  (23 shorter events, 3.0 us)
Async XLA Ops:
  0.6 1.6 %copy-start.2 = (f32[3,32,256]{2,1,0:T(8,128)S(1)}, f32[3,32,256]{2,1,0:T(8,128)}, u32[]{:S(2)}) copy-start(f32[3,32,256]{2,1,0:T(8,128)} %param.2) | copy-start | bytes 294916
  2.3 20.9 %collective-permute-start = (f32[17,3,8,256]{3,2,1,0:T(8,128)S(1)}, f32[17,3,8,256]{3,2,1,0:T(8,128)S(1)}, u32[]{:S(2)}, u32[]{:S(2)}) collective-permute-start(f32[17,3,8,256]{3,2,1,0:T(8,128)S(1)} %get-tuple-element.9), channel_id=1, source_target_pairs={{0,1},{1,2},{2,3},{3,4},{4,5},{5,6},{6,7},{7,0},{8,9},{9,10},{10,1... | collective-permute-start | bytes 1253384 | tf_op jit(solution)/shard_map/ppermute | solution.py:38
  5.3 20.1 %collective-permute-start.1 = (f32[17,3,8,256]{3,2,1,0:T(8,128)S(1)}, f32[17,3,8,256]{3,2,1,0:T(8,128)S(1)}, u32[]{:S(2)}, u32[]{:S(2)}) collective-permute-start(f32[17,3,8,256]{3,2,1,0:T(8,128)S(1)} %get-tuple-element.8), channel_id=1, source_target_pairs={{0,7},{1,0},{2,1},{3,2},{4,3},{5,4},{6,5},{7,6},{8,15},{9,8},{10,9... | collective-permute-start | bytes 1253384 | tf_op jit(solution)/shard_map/ppermute | solution.py:38
  23.2 2.5 %copy-start = (f32[17,3,8,256]{3,2,1,0:T(8,128)}, f32[17,3,8,256]{3,2,1,0:T(8,128)S(1)}, u32[]{:S(2)}) copy-start(f32[17,3,8,256]{3,2,1,0:T(8,128)S(1)} %collective-permute-done.up_ref) | copy-start | bytes 1253380
  25.4 0.8 copy-start.1
  27.1 3.9 %collective-permute-start.2 = (f32[19584]{0:T(1024)S(1)}, f32[19584]{0:T(1024)S(1)}, u32[]{:S(2)}, u32[]{:S(2)}) collective-permute-start(f32[19584]{0:T(1024)S(1)} %reshape.55), channel_id=1, source_target_pairs={{0,8},{8,16},{16,24},{24,0},{1,9},{9,17},{17,25},{25,1},{2,10},{10... | collective-permute-start | bytes 235016 | tf_op jit(solution)/shard_map/ppermute | solution.py:40
  27.7 5.0 %collective-permute-start.3 = (f32[19584]{0:T(1024)S(1)}, f32[19584]{0:T(1024)S(1)}, u32[]{:S(2)}, u32[]{:S(2)}) collective-permute-start(f32[19584]{0:T(1024)S(1)} %reshape.57), channel_id=1, source_target_pairs={{0,24},{8,0},{16,8},{24,16},{1,25},{9,1},{17,9},{25,17},{2,26},{10... | collective-permute-start | bytes 235016 | tf_op jit(solution)/shard_map/ppermute | solution.py:40
  65.9 1.4 %collective-permute-start.4 = (f32[16,16]{0,1:T(8,128)S(1)}, f32[16,16]{0,1:T(8,128)S(1)}, u32[]{:S(2)}, u32[]{:S(2)}) collective-permute-start(f32[16,16]{0,1:T(8,128)S(1)} %fusion.2), channel_id=1, source_target_pairs={{0,8},{8,0},{16,24},{24,16},{1,9},{9,1},{17,25},{25,17},{2,10},{10... | collective-permute-start | bytes 3080 | tf_op jit(solution)/shard_map/ppermute | solution.py:160
  67.2 3.7 %collective-permute-start.5 = (f32[16,16]{0,1:T(8,128)S(1)}, f32[16,16]{0,1:T(8,128)S(1)}, u32[]{:S(2)}, u32[]{:S(2)}) collective-permute-start(f32[16,16]{0,1:T(8,128)S(1)} %add.77), channel_id=1, source_target_pairs={{0,16},{8,24},{16,0},{24,8},{1,17},{9,25},{17,1},{25,9},{2,18},{10... | collective-permute-start | bytes 3080 | tf_op jit(solution)/shard_map/ppermute | solution.py:160
  70.9 3.7 %collective-permute-start.6 = (f32[16,16]{0,1:T(8,128)S(1)}, f32[16,16]{0,1:T(8,128)S(1)}, u32[]{:S(2)}, u32[]{:S(2)}) collective-permute-start(f32[16,16]{0,1:T(8,128)S(1)} %add.78), channel_id=1, source_target_pairs={{0,1},{1,0},{2,3},{3,2},{4,5},{5,4},{6,7},{7,6},{8,9},{9,8},{10,11... | collective-permute-start | bytes 3080 | tf_op jit(solution)/shard_map/ppermute | solution.py:160
  74.6 3.7 %collective-permute-start.7 = (f32[16,16]{0,1:T(8,128)S(1)}, f32[16,16]{0,1:T(8,128)S(1)}, u32[]{:S(2)}, u32[]{:S(2)}) collective-permute-start(f32[16,16]{0,1:T(8,128)S(1)} %add.79), channel_id=1, source_target_pairs={{0,2},{1,3},{2,0},{3,1},{4,6},{5,7},{6,4},{7,5},{8,10},{9,11},{10,... | collective-permute-start | bytes 3080 | tf_op jit(solution)/shard_map/ppermute | solution.py:160
  78.2 4.5 %collective-permute-start.8 = (f32[16,16]{0,1:T(8,128)S(1)}, f32[16,16]{0,1:T(8,128)S(1)}, u32[]{:S(2)}, u32[]{:S(2)}) collective-permute-start(f32[16,16]{0,1:T(8,128)S(1)} %add.80), channel_id=1, source_target_pairs={{0,4},{1,5},{2,6},{3,7},{4,0},{5,1},{6,2},{7,3},{8,12},{9,13},{10,... | collective-permute-start | bytes 3080 | tf_op jit(solution)/shard_map/ppermute | solution.py:160

commit v12 on v9

--- a/solution.py
+++ b/solution.py
@@ -48,8 +48,9 @@
     return above, below, west, east
 
 
-def forecast_kernel(cor_ref, x_ref, up_ref, down_ref, west_ref, east_ref, o_ref, ring, east_pad, west_pad, *, steps):
-    rows, cols = (x_ref.shape[-2], x_ref.shape[-1])
+def forecast_kernel(cor_ref, c_ref, p_ref, up_ref, down_ref, west_ref, east_ref, o_ref, ring, east_pad, west_pad, *, steps):
+    rows, cols = (c_ref.shape[-2], c_ref.shape[-1])
+    state = pl.program_id(0)
     R, C = cor_ref.shape
     width = up_ref.shape[-2]
     spare = C - cols
@@ -60,8 +61,17 @@
         east_pad[...] = jnp.zeros_like(east_pad)
         west_pad[...] = jnp.zeros_like(west_pad)
 
+    @pl.when(state == 0)
+    def _():
+        for k in range(3):
+            ring[k, :rows, :cols] = c_ref[k]
+
+    @pl.when(state > 0)
+    def _():
+        for k in range(3):
+            ring[k, :rows, :cols] = c_ref[k] + p_ref[0, k]
+
     for k in range(3):
-        ring[k, :rows, :cols] = x_ref[0, k]
         ring[k, rows : rows + width, :cols] = down_ref[0, k]
         ring[k, rows + width :, :cols] = up_ref[0, k]
         east_pad[:, :width] = east_ref[0, k]
@@ -113,8 +123,9 @@
         o_ref[0, k] = s[k][:rows, :cols]
 
 
-def forecast(cor, value, above, below, west, east, steps):
-    S, F, rows, cols = value.shape
+def forecast(cor, control, perts, above, below, west, east, steps):
+    F, rows, cols = control.shape
+    S = perts.shape[0] + 1
     R, C = cor.shape
     width = above.shape[-2]
     return pl.pallas_call(
@@ -123,7 +134,8 @@
         grid=(S,),
         in_specs=[
             pl.BlockSpec((R, C), lambda i: (0, 0)),
-            pl.BlockSpec((1, F, rows, cols), lambda i: (i, 0, 0, 0)),
+            pl.BlockSpec((F, rows, cols), lambda i: (0, 0, 0)),
+            pl.BlockSpec((1, F, rows, cols), lambda i: (jnp.maximum(i - 1, 0), 0, 0, 0)),
             pl.BlockSpec((1, F, width, cols), lambda i: (i, 0, 0, 0)),
             pl.BlockSpec((1, F, width, cols), lambda i: (i, 0, 0, 0)),
             pl.BlockSpec((1, F, R, width), lambda i: (i, 0, 0, 0)),
@@ -138,7 +150,7 @@
         cost_estimate=pl.CostEstimate(
             flops=S * F * R * C * 300 * steps, transcendentals=0, bytes_accessed=4 * S * F * (R * C + rows * cols)
         ),
-    )(cor, value, above, below, west, east)
+    )(cor, control, perts, above, below, west, east)
 
 
 def body(control, perts):
@@ -157,7 +169,7 @@
 
     states = jnp.concatenate([control[None], control[None] + perts], 0)
     above, below, west, east = ring_halo(states, margin, lanes)
-    current = forecast(coriolis, states, above, below, west, east, STEPS)
+    current = forecast(coriolis, control, perts, above, below, west, east, STEPS)
     bred = current[1:] - current[0:1]
     flat = bred.reshape(MEMBERS, -1)
     local_gram = jnp.dot(flat, flat.T, precision=lax.Precision.HIGHEST)

time: 89.5 us -> 89.8 us (level)
  other arithmetic: 8.83 us -> 7.52 us
  waiting for transfers between devices: 27.2 us -> 28.5 us
    ppermute x2, waiting for transfers between devices: 15.6 us -> 16.9 us  [shift(): return lax.ppermute(part, axes, pairs)]
    concatenate x2 -> x1, other arithmetic: 1.39 us -> 0.07 us  [body(): states = jnp.concatenate([control[None], control[None] + perts], 0)]
  transfers between devices with their start and end apart: 9 -> 9, of which waited for: 8 -> 8; matrix products, arithmetic and copies ran while one was open for 5% -> 4% of each run, Pallas kernels for 0% -> 0%
where the time goes in v12:
time: 89.8 us; the launch traced here: 89.5 us
  waiting for transfers between devices  28.5 us (32%)
  Pallas kernels  24.5 us (27%)
  starting transfers between devices  13.8 us (15%)
  local copies, waits for them, and re-layouts  10.3 us (11%)
  other arithmetic  7.52 us (8%)
  matrix products  4.22 us (5%)
    pallas_call x1, Pallas kernels, forecast(): pl.pallas_call(functools.partial(forecast_kernel, steps=steps), out_shape...  24.5 us
    ppermute x2, waiting for transfers between devices, shift(): return lax.ppermute(part, axes, pairs)  16.9 us
    ppermute x5, waiting for transfers between devices, body(): gram = gram + lax.ppermute(gram, axis, pairs)  10.1 us
    ppermute x2, starting transfers between devices, shift(): return lax.ppermute(part, axes, pairs)  6.12 us
    ppermute x5, starting transfers between devices, body(): gram = gram + lax.ppermute(gram, axis, pairs)  5.84 us
    unnamed x9, local copies, waits for them, and re-layouts  3.7 us
    reshape x2, local copies, waits for them, and re-layouts, shift(): return lax.ppermute(flat, axes, pairs).reshape(part.shape)  3.44 us
    dot_general x1, matrix products, body(): local_gram = jnp.dot(flat, flat.T, precision=lax.Precision.HIGHEST)  2.72 us
  transfers between devices with their start and end apart: 9, of which 8 were waited for; matrix products, arithmetic and copies ran while one was open for 4% of the time, Pallas kernels for 0%

profile of v12, /device:TPU:0, one launch (start us, length us, event | category | flops | bytes accessed | tf_op | source)
XLA Modules:
  0.0 89.5 jit_solution(16455019180952572886)
XLA Ops:
  0.6 1.6 %broadcast_add_fusion = f32[16,3,32,256]{3,2,1,0:T(8,128)S(1)} fusion(f32[16,3,32,256]{3,2,1,0:T(8,128)} %p_ref.1, f32[3,32,256]{2,1,0:T(8,128)} %c_ref.1), kind=kLoop, calls=%fused_computation.6 | loop fusion | flops 393216 | bytes 3244032 | tf_op jit(solution)/shard_map/add | solution.py:170
  2.3 3.0 %collective-permute-start = (f32[17,3,8,256]{3,2,1,0:T(8,128)S(1)}, f32[17,3,8,256]{3,2,1,0:T(8,128)S(1)}, u32[]{:S(2)}, u32[]{:S(2)}) collective-permute-start(f32[17,3,8,256]{3,2,1,0:T(8,128)S(1)} %get-tuple-element.9), channel_id=1, source_target_pairs={{0,1},{1,2},{2,3},{3,4},{4,5},{5,6},{6,7},{7,0},{8,9},{9,10},{10,1... | collective-permute-start | bytes 1253384 | tf_op jit(solution)/shard_map/ppermute | solution.py:38
  5.3 3.1 %collective-permute-start.1 = (f32[17,3,8,256]{3,2,1,0:T(8,128)S(1)}, f32[17,3,8,256]{3,2,1,0:T(8,128)S(1)}, u32[]{:S(2)}, u32[]{:S(2)}) collective-permute-start(f32[17,3,8,256]{3,2,1,0:T(8,128)S(1)} %get-tuple-element.8), channel_id=1, source_target_pairs={{0,7},{1,0},{2,1},{3,2},{4,3},{5,4},{6,5},{7,6},{8,15},{9,8},{10,9... | collective-permute-start | bytes 1253384 | tf_op jit(solution)/shard_map/ppermute | solution.py:38
  8.4 14.7 %collective-permute-done.up_ref = f32[17,3,8,256]{3,2,1,0:T(8,128)S(1)} collective-permute-done((f32[17,3,8,256]{3,2,1,0:T(8,128)S(1)}, f32[17,3,8,256]{3,2,1,0:T(8,128)S(1)}, u32[]{:S(2)}, u32[]{:S(2)}) %collective-permute-start) | collective-permute-done | bytes 417824 | tf_op jit(solution)/shard_map/ppermute | solution.py:38
  23.2 2.2 %collective-permute-done.1.down_ref = f32[17,3,8,256]{3,2,1,0:T(8,128)S(1)} collective-permute-done((f32[17,3,8,256]{3,2,1,0:T(8,128)S(1)}, f32[17,3,8,256]{3,2,1,0:T(8,128)S(1)}, u32[]{:S(2)}, u32[]{:S(2)}) %collective-permute-start.1) | collective-permute-done | bytes 417824 | tf_op jit(solution)/shard_map/ppermute | solution.py:38
  26.6 0.5 reshape.59
  27.2 0.5 reshape.61
  27.7 1.8 %collective-permute-start.3 = (f32[19584]{0:T(1024)S(1)}, f32[19584]{0:T(1024)S(1)}, u32[]{:S(2)}, u32[]{:S(2)}) collective-permute-start(f32[19584]{0:T(1024)S(1)} %reshape.61), channel_id=1, source_target_pairs={{0,24},{8,0},{16,8},{24,16},{1,25},{9,1},{17,9},{25,17},{2,26},{10... | collective-permute-start | bytes 235016 | tf_op jit(solution)/shard_map/ppermute | solution.py:40
  29.5 1.5 %collective-permute-done.2 = f32[19584]{0:T(1024)S(1)} collective-permute-done((f32[19584]{0:T(1024)S(1)}, f32[19584]{0:T(1024)S(1)}, u32[]{:S(2)}, u32[]{:S(2)}) %collective-permute-start.2) | collective-permute-done | bytes 78368 | tf_op jit(solution)/shard_map/ppermute | solution.py:40
  31.0 1.7 %reshape.60.west_ref = f32[17,3,48,8]{3,2,1,0:T(8,128)} reshape(f32[19584]{0:T(1024)S(1)} %collective-permute-done.2) | data formatting | bytes 156672 | tf_op jit(solution)/shard_map/reshape | solution.py:40
  32.7 1.7 %reshape.62.east_ref = f32[17,3,48,8]{3,2,1,0:T(8,128)} reshape(f32[19584]{0:T(1024)S(1)} %collective-permute-done.3) | data formatting | bytes 156672 | tf_op jit(solution)/shard_map/reshape | solution.py:40
  34.5 0.7 broadcast_in_dim.5.cor_ref
  35.1 24.5 %shard_map.41 = f32[17,3,32,256]{3,2,1,0:T(8,128)} custom-call(f32[48,384]{1,0:T(8,128)} %broadcast_in_dim.5.cor_ref, f32[3,32,256]{2,1,0:T(8,128)} %c_ref.1, f32[16,3,32,256]{3,2,1,0:T(8,128)} %p_ref.1, f32[17,3,8,256]{3,2,1,0:T(8,128)} %copy-done, f32[17,3,8,256]{3,2,1,0:T(8,128)} %copy-done.1, f32[17,3,48,8]{3,2,1,0:T(8,128)} %reshape.60.west_ref, ...), custom_call_target="tpu_custom_call" | custom-call | flops 564019200 | bytes 5431296 | tf_op jit(solution)/shard_map/pallas_call | solution.py:131
  59.6 0.9 %slice_bitcast_fusion = f32[3,32,256]{2,1,0:T(8,128)S(1)} fusion(f32[17,3,32,256]{3,2,1,0:T(8,128)} %shard_map.41), kind=kLoop, calls=%fused_computation.9 | loop fusion | bytes 196608 | tf_op jit(solution)/shard_map/sub | solution.py:173
  60.5 1.5 %slice_subtract_fusion = f32[16,3,32,256]{3,2,1,0:T(8,128)S(1)} fusion(f32[17,3,32,256]{3,2,1,0:T(8,128)} %shard_map.41, f32[3,32,256]{2,1,0:T(8,128)S(1)} %slice_bitcast_fusion), kind=kLoop, calls=%fused_computation.2 | loop fusion | flops 393216 | bytes 3244032 | tf_op jit(solution)/shard_map/sub | solution.py:173
  62.0 2.7 %fusion.2 = f32[16,16]{0,1:T(8,128)S(1)} fusion(f32[16,3,32,256]{3,2,1,0:T(8,128)S(1)} %slice_subtract_fusion), kind=kOutput, calls=%fused_computation.5 | convolution fusion | flops 75497472 | bytes 1573888 | tf_op jit(solution)/shard_map/dot_general | solution.py:175
  65.3 0.8 collective-permute-done.4
  66.1 1.4 %collective-permute-start.5 = (f32[16,16]{0,1:T(8,128)S(1)}, f32[16,16]{0,1:T(8,128)S(1)}, u32[]{:S(2)}, u32[]{:S(2)}) collective-permute-start(f32[16,16]{0,1:T(8,128)S(1)} %add.77), channel_id=1, source_target_pairs={{0,16},{8,24},{16,0},{24,8},{1,17},{9,25},{17,1},{25,9},{2,18},{10... | collective-permute-start | bytes 3080 | tf_op jit(solution)/shard_map/ppermute | solution.py:185
  67.5 2.3 %collective-permute-done.5 = f32[16,16]{0,1:T(8,128)S(1)} collective-permute-done((f32[16,16]{0,1:T(8,128)S(1)}, f32[16,16]{0,1:T(8,128)S(1)}, u32[]{:S(2)}, u32[]{:S(2)}) %collective-permute-start.5) | collective-permute-done | bytes 1056 | tf_op jit(solution)/shard_map/ppermute | solution.py:185
  70.2 3.2 %collective-permute-done.6 = f32[16,16]{0,1:T(8,128)S(1)} collective-permute-done((f32[16,16]{0,1:T(8,128)S(1)}, f32[16,16]{0,1:T(8,128)S(1)}, u32[]{:S(2)}, u32[]{:S(2)}) %collective-permute-start.6) | collective-permute-done | bytes 1056 | tf_op jit(solution)/shard_map/ppermute | solution.py:185
  73.4 1.3 %collective-permute-start.7 = (f32[16,16]{0,1:T(8,128)S(1)}, f32[16,16]{0,1:T(8,128)S(1)}, u32[]{:S(2)}, u32[]{:S(2)}) collective-permute-start(f32[16,16]{0,1:T(8,128)S(1)} %add.79), channel_id=1, source_target_pairs={{0,2},{1,3},{2,0},{3,1},{4,6},{5,7},{6,4},{7,5},{8,10},{9,11},{10,... | collective-permute-start | bytes 3080 | tf_op jit(solution)/shard_map/ppermute | solution.py:185
  74.7 2.4 %collective-permute-done.7 = f32[16,16]{0,1:T(8,128)S(1)} collective-permute-done((f32[16,16]{0,1:T(8,128)S(1)}, f32[16,16]{0,1:T(8,128)S(1)}, u32[]{:S(2)}, u32[]{:S(2)}) %collective-permute-start.7) | collective-permute-done | bytes 1056 | tf_op jit(solution)/shard_map/ppermute | solution.py:185
  77.1 2.3 %collective-permute-start.8 = (f32[16,16]{0,1:T(8,128)S(1)}, f32[16,16]{0,1:T(8,128)S(1)}, u32[]{:S(2)}, u32[]{:S(2)}) collective-permute-start(f32[16,16]{0,1:T(8,128)S(1)} %add.80), channel_id=1, source_target_pairs={{0,4},{1,5},{2,6},{3,7},{4,0},{5,1},{6,2},{7,3},{8,12},{9,13},{10,... | collective-permute-start | bytes 3080 | tf_op jit(solution)/shard_map/ppermute | solution.py:185
  79.4 0.9 %copy.19 = f32[2,8,96,256]{3,1,2,0:T(8,128)S(1)} copy(f32[2,8,96,256]{3,2,1,0:T(8,128)S(1)} %bitcast.29) | data formatting | bytes 3145728
  80.3 1.4 %collective-permute-done.8 = f32[16,16]{0,1:T(8,128)S(1)} collective-permute-done((f32[16,16]{0,1:T(8,128)S(1)}, f32[16,16]{0,1:T(8,128)S(1)}, u32[]{:S(2)}, u32[]{:S(2)}) %collective-permute-start.8) | collective-permute-done | bytes 1056 | tf_op jit(solution)/shard_map/ppermute | solution.py:185
  81.7 1.5 %cholesky.16 = f32[16,16]{1,0:T(8,128)S(1)} custom-call(f32[16,16]{1,0:T(8,128)S(1)} %fusion.6), custom_call_target="Cholesky" | custom-call | tf_op jit(solution)/shard_map/jit(cholesky)/cholesky | solution.py:187
  83.2 0.6 compare_reduce_fusion
  83.9 0.7 multiply_bitcast_fusion
  84.5 1.2 %custom-call.7 = f32[1,16,16]{1,2,0:T(8,128)S(1)} custom-call(f32[1,16,16]{2,1,0:T(8,128)S(1)} %get-tuple-element.11), custom_call_target="InvertDiagBlocksLowerTriangular" | custom-call | tf_op jit(solution)/shard_map/jit(_solve_triangular)/triangular_solve | solution.py:188
  85.7 1.5 %convolution_multiply_fusion = f32[16,24576]{1,0:T(8,128)S(1)} fusion(f32[16,24576]{1,0:T(8,128)S(1)} %bitcast.30, f32[1,16,16]{1,2,0:T(8,128)S(1)} %custom-call.7), kind=kOutput, calls=%fused_computation | convolution fusion | flops 75890688 | bytes 3146752 | tf_op jit(solution)/shard_map/jit(_solve_triangular)/triangular_solve | solution.py:188
  87.2 1.6 %copy.20 = f32[2,8,96,256]{3,2,1,0:T(8,128)} copy(f32[2,8,96,256]{3,1,2,0:T(8,128)S(1)} %bitcast.31) | data formatting | bytes 3145728
  88.9 0.7 copy.15
  (22 shorter events, 2.4 us)
Async XLA Ops:
  0.6 1.6 %copy-start.2 = (f32[3,32,256]{2,1,0:T(8,128)S(1)}, f32[3,32,256]{2,1,0:T(8,128)}, u32[]{:S(2)}) copy-start(f32[3,32,256]{2,1,0:T(8,128)} %c_ref.1) | copy-start | bytes 294916
  2.3 20.9 %collective-permute-start = (f32[17,3,8,256]{3,2,1,0:T(8,128)S(1)}, f32[17,3,8,256]{3,2,1,0:T(8,128)S(1)}, u32[]{:S(2)}, u32[]{:S(2)}) collective-permute-start(f32[17,3,8,256]{3,2,1,0:T(8,128)S(1)} %get-tuple-element.9), channel_id=1, source_target_pairs={{0,1},{1,2},{2,3},{3,4},{4,5},{5,6},{6,7},{7,0},{8,9},{9,10},{10,1... | collective-permute-start | bytes 1253384 | tf_op jit(solution)/shard_map/ppermute | solution.py:38
  5.3 20.1 %collective-permute-start.1 = (f32[17,3,8,256]{3,2,1,0:T(8,128)S(1)}, f32[17,3,8,256]{3,2,1,0:T(8,128)S(1)}, u32[]{:S(2)}, u32[]{:S(2)}) collective-permute-start(f32[17,3,8,256]{3,2,1,0:T(8,128)S(1)} %get-tuple-element.8), channel_id=1, source_target_pairs={{0,7},{1,0},{2,1},{3,2},{4,3},{5,4},{6,5},{7,6},{8,15},{9,8},{10,9... | collective-permute-start | bytes 1253384 | tf_op jit(solution)/shard_map/ppermute | solution.py:38
  23.2 2.5 %copy-start = (f32[17,3,8,256]{3,2,1,0:T(8,128)}, f32[17,3,8,256]{3,2,1,0:T(8,128)S(1)}, u32[]{:S(2)}) copy-start(f32[17,3,8,256]{3,2,1,0:T(8,128)S(1)} %collective-permute-done.up_ref) | copy-start | bytes 1253380
  25.4 0.8 copy-start.1
  27.1 3.9 %collective-permute-start.2 = (f32[19584]{0:T(1024)S(1)}, f32[19584]{0:T(1024)S(1)}, u32[]{:S(2)}, u32[]{:S(2)}) collective-permute-start(f32[19584]{0:T(1024)S(1)} %reshape.59), channel_id=1, source_target_pairs={{0,8},{8,16},{16,24},{24,0},{1,9},{9,17},{17,25},{25,1},{2,10},{10... | collective-permute-start | bytes 235016 | tf_op jit(solution)/shard_map/ppermute | solution.py:40
  27.7 5.0 %collective-permute-start.3 = (f32[19584]{0:T(1024)S(1)}, f32[19584]{0:T(1024)S(1)}, u32[]{:S(2)}, u32[]{:S(2)}) collective-permute-start(f32[19584]{0:T(1024)S(1)} %reshape.61), channel_id=1, source_target_pairs={{0,24},{8,0},{16,8},{24,16},{1,25},{9,1},{17,9},{25,17},{2,26},{10... | collective-permute-start | bytes 235016 | tf_op jit(solution)/shard_map/ppermute | solution.py:40
  64.8 1.4 %collective-permute-start.4 = (f32[16,16]{0,1:T(8,128)S(1)}, f32[16,16]{0,1:T(8,128)S(1)}, u32[]{:S(2)}, u32[]{:S(2)}) collective-permute-start(f32[16,16]{0,1:T(8,128)S(1)} %fusion.2), channel_id=1, source_target_pairs={{0,8},{8,0},{16,24},{24,16},{1,9},{9,1},{17,25},{25,17},{2,10},{10... | collective-permute-start | bytes 3080 | tf_op jit(solution)/shard_map/ppermute | solution.py:185
  66.1 3.7 %collective-permute-start.5 = (f32[16,16]{0,1:T(8,128)S(1)}, f32[16,16]{0,1:T(8,128)S(1)}, u32[]{:S(2)}, u32[]{:S(2)}) collective-permute-start(f32[16,16]{0,1:T(8,128)S(1)} %add.77), channel_id=1, source_target_pairs={{0,16},{8,24},{16,0},{24,8},{1,17},{9,25},{17,1},{25,9},{2,18},{10... | collective-permute-start | bytes 3080 | tf_op jit(solution)/shard_map/ppermute | solution.py:185
  69.8 3.7 %collective-permute-start.6 = (f32[16,16]{0,1:T(8,128)S(1)}, f32[16,16]{0,1:T(8,128)S(1)}, u32[]{:S(2)}, u32[]{:S(2)}) collective-permute-start(f32[16,16]{0,1:T(8,128)S(1)} %add.78), channel_id=1, source_target_pairs={{0,1},{1,0},{2,3},{3,2},{4,5},{5,4},{6,7},{7,6},{8,9},{9,8},{10,11... | collective-permute-start | bytes 3080 | tf_op jit(solution)/shard_map/ppermute | solution.py:185
  73.4 3.7 %collective-permute-start.7 = (f32[16,16]{0,1:T(8,128)S(1)}, f32[16,16]{0,1:T(8,128)S(1)}, u32[]{:S(2)}, u32[]{:S(2)}) collective-permute-start(f32[16,16]{0,1:T(8,128)S(1)} %add.79), channel_id=1, source_target_pairs={{0,2},{1,3},{2,0},{3,1},{4,6},{5,7},{6,4},{7,5},{8,10},{9,11},{10,... | collective-permute-start | bytes 3080 | tf_op jit(solution)/shard_map/ppermute | solution.py:185
  77.1 4.5 %collective-permute-start.8 = (f32[16,16]{0,1:T(8,128)S(1)}, f32[16,16]{0,1:T(8,128)S(1)}, u32[]{:S(2)}, u32[]{:S(2)}) collective-permute-start(f32[16,16]{0,1:T(8,128)S(1)} %add.80), channel_id=1, source_target_pairs={{0,4},{1,5},{2,6},{3,7},{4,0},{5,1},{6,2},{7,3},{8,12},{9,13},{10,... | collective-permute-start | bytes 3080 | tf_op jit(solution)/shard_map/ppermute | solution.py:185

commit v13 on v12

--- a/solution.py
+++ b/solution.py
@@ -19,32 +19,39 @@
 two_pi = 2.0 * math.pi
 
 
-def ring_halo(value, width, lanes):
-    rows, cols = (value.shape[-2], value.shape[-1])
+def shift(part, axes, dx, dy, flatten=True):
     across, down = (lax.axis_size("gx"), lax.axis_size("gy"))
-
-    def shift(part, axes, dx, dy, flatten=True):
-        pairs = []
-        for x in range(across):
-            for y in range(down):
-                target = ((x + dx) % across, (y + dy) % down)
-                if axes == "gx":
-                    pairs.append((x, target[0])) if y == 0 else None
-                elif axes == "gy":
-                    pairs.append((y, target[1])) if x == 0 else None
-                else:
-                    pairs.append((x * down + y, target[0] * down + target[1]))
-        if not flatten:
-            return lax.ppermute(part, axes, pairs)
-        flat = part.reshape(-1)
-        return lax.ppermute(flat, axes, pairs).reshape(part.shape)
-
-    top, bottom = (value[..., :width, :], value[..., rows - width :, :])
+    pairs = []
+    for x in range(across):
+        for y in range(down):
+            target = ((x + dx) % across, (y + dy) % down)
+            if axes == "gx":
+                pairs.append((x, target[0])) if y == 0 else None
+            else:
+                pairs.append((y, target[1])) if x == 0 else None
+    if not flatten:
+        return lax.ppermute(part, axes, pairs)
+    flat = part.reshape(-1)
+    return lax.ppermute(flat, axes, pairs).reshape(part.shape)
+
+
+def ring_halo(control, perts, width):
+    rows, cols = (control.shape[-2], control.shape[-1])
+
+    def part(index):
+        base = control[None][index]
+        return jnp.concatenate([base, base + perts[index]], 0)
+
+    top = part((Ellipsis, slice(0, width), slice(None)))
+    bottom = part((Ellipsis, slice(rows - width, rows), slice(None)))
+    left = part((Ellipsis, slice(None), slice(0, width)))
+    right = part((Ellipsis, slice(None), slice(cols - width, cols)))
     above = shift(bottom, "gy", 0, 1, flatten=False)
     below = shift(top, "gy", 0, -1, flatten=False)
-    tall = jnp.concatenate([value, below, above], axis=-2)
-    west = shift(tall[..., cols - width :], "gx", 1, 0)
-    east = shift(tall[..., :width], "gx", -1, 0)
+    west_source = jnp.concatenate([right, below[..., cols - width :], above[..., cols - width :]], axis=-2)
+    east_source = jnp.concatenate([left, below[..., :width], above[..., :width]], axis=-2)
+    west = shift(west_source, "gx", 1, 0)
+    east = shift(east_source, "gx", -1, 0)
     return above, below, west, east
 
 
@@ -167,8 +174,7 @@
     coriolis = coriolis_mid * (1.0 + 0.5 * jnp.sin(two_pi * rows / float(grid_rows)))
     coriolis = jnp.broadcast_to(coriolis[:, None], (ring_rows, lanes))
 
-    states = jnp.concatenate([control[None], control[None] + perts], 0)
-    above, below, west, east = ring_halo(states, margin, lanes)
+    above, below, west, east = ring_halo(control, perts, margin)
     current = forecast(coriolis, control, perts, above, below, west, east, STEPS)
     bred = current[1:] - current[0:1]
     flat = bred.reshape(MEMBERS, -1)

time: 89.8 us -> 93.2 us (1.038)
  local copies, waits for them, and re-layouts: 10.3 us -> 12.9 us
    ppermute x2, waiting for transfers between devices: 16.9 us -> 15.4 us  [shift(): return lax.ppermute(part, axes, pairs)]
    slice x1 -> x11, local copies, waits for them, and re-layouts: 0.39 us -> 1.96 us  [the longest x4 0.99 us: part(): base = control[None][index]]
    ppermute x5, starting transfers between devices: 5.84 us -> 6.8 us  [body(): gram = gram + lax.ppermute(gram, axis, pairs)]
    unnamed x9 -> x13, local copies, waits for them, and re-layouts: 3.7 us -> 3.74 us
  transfers between devices with their start and end apart: 9 -> 9, of which waited for: 8 -> 8; matrix products, arithmetic and copies ran while one was open for 4% -> 6% of each run, Pallas kernels for 0% -> 0%
where the time goes in v13:
time: 93.2 us; the launch traced here: 92.9 us
  waiting for transfers between devices  27.7 us (30%)
  Pallas kernels  24.4 us (26%)
  starting transfers between devices  14.7 us (16%)
  local copies, waits for them, and re-layouts  12.9 us (14%)
  other arithmetic  8.12 us (9%)
  matrix products  4.21 us (5%)
    pallas_call x1, Pallas kernels, forecast(): pl.pallas_call(functools.partial(forecast_kernel, steps=steps), out_shape...  24.4 us
    ppermute x2, waiting for transfers between devices, shift(): return lax.ppermute(part, axes, pairs)  15.4 us
    ppermute x5, waiting for transfers between devices, body(): gram = gram + lax.ppermute(gram, axis, pairs)  10.3 us
    ppermute x5, starting transfers between devices, body(): gram = gram + lax.ppermute(gram, axis, pairs)  6.8 us
    ppermute x2, starting transfers between devices, shift(): return lax.ppermute(part, axes, pairs)  6.06 us
    unnamed x13, local copies, waits for them, and re-layouts  3.74 us
    reshape x2, local copies, waits for them, and re-layouts, shift(): return lax.ppermute(flat, axes, pairs).reshape(part.shape)  3.45 us
    dot_general x1, matrix products, body(): local_gram = jnp.dot(flat, flat.T, precision=lax.Precision.HIGHEST)  2.72 us
  transfers between devices with their start and end apart: 9, of which 8 were waited for; matrix products, arithmetic and copies ran while one was open for 6% of the time, Pallas kernels for 0%

profile of v13, /device:TPU:0, one launch (start us, length us, event | category | flops | bytes accessed | tf_op | source)
XLA Modules:
  0.0 92.9 jit_solution(2806530675305621459)
XLA Ops:
  0.6 0.8 fusion.19
  1.4 1.3 %slice_add_fusion = (f32[16,3,8,256]{3,2,1,0:T(8,128)S(1)}, f32[16,3,8,256]{3,2,1,0:T(8,128)S(1)}) fusion(f32[16,3,32,256]{3,2,1,0:T(8,128)} %p_ref.1, f32[3,8,256]{2,1,0:T(8,128)S(1)} %get-tuple-element.24, f32[3,8,256]{2,1,0:T(8,128)S(1)} %get-tuple-element.23), kind=kLoop, calls=%fused_computation.7 | loop fusion | flops 196608 | bytes 1622016 | tf_op jit(solution)/shard_map/add | solution.py:43
  2.7 0.8 pad_maximum_fusion
  3.5 3.0 %collective-permute-start = (f32[17,3,8,256]{3,2,1,0:T(8,128)}, f32[17,3,8,256]{3,2,1,0:T(8,128)S(1)}, u32[]{:S(2)}, u32[]{:S(2)}) collective-permute-start(f32[17,3,8,256]{3,2,1,0:T(8,128)} %pad_maximum_fusion), channel_id=1, source_target_pairs={{0,1},{1,2},{2,3},{3,4},{4,5},{5,6},{6,7},{7,0},{8,9},{9,10},{10,1... | collective-permute-start | bytes 1253384 | tf_op jit(solution)/shard_map/ppermute | solution.py:33
  6.5 3.1 %collective-permute-start.1 = (f32[17,3,8,256]{3,2,1,0:T(8,128)S(1)}, f32[17,3,8,256]{3,2,1,0:T(8,128)S(1)}, u32[]{:S(2)}, u32[]{:S(2)}) collective-permute-start(f32[17,3,8,256]{3,2,1,0:T(8,128)S(1)} %pad_maximum_fusion.1), channel_id=1, source_target_pairs={{0,7},{1,0},{2,1},{3,2},{4,3},{5,4},{6,5},{7,6},{8,15},{9,8},{10,9... | collective-permute-start | bytes 1253384 | tf_op jit(solution)/shard_map/ppermute | solution.py:33
  10.9 13.8 %collective-permute-done.up_ref = f32[17,3,8,256]{3,2,1,0:T(8,128)S(1)} collective-permute-done((f32[17,3,8,256]{3,2,1,0:T(8,128)}, f32[17,3,8,256]{3,2,1,0:T(8,128)S(1)}, u32[]{:S(2)}, u32[]{:S(2)}) %collective-permute-start) | collective-permute-done | bytes 417824 | tf_op jit(solution)/shard_map/ppermute | solution.py:33
  25.0 1.6 %collective-permute-done.1.down_ref = f32[17,3,8,256]{3,2,1,0:T(8,128)S(1)} collective-permute-done((f32[17,3,8,256]{3,2,1,0:T(8,128)S(1)}, f32[17,3,8,256]{3,2,1,0:T(8,128)S(1)}, u32[]{:S(2)}, u32[]{:S(2)}) %collective-permute-start.1) | collective-permute-done | bytes 417824 | tf_op jit(solution)/shard_map/ppermute | solution.py:33
  29.4 1.8 %collective-permute-start.3 = (f32[19584]{0:T(1024)S(1)}, f32[19584]{0:T(1024)S(1)}, u32[]{:S(2)}, u32[]{:S(2)}) collective-permute-start(f32[19584]{0:T(1024)S(1)} %reshape.60), channel_id=1, source_target_pairs={{0,24},{8,0},{16,8},{24,16},{1,25},{9,1},{17,9},{25,17},{2,26},{10... | collective-permute-start | bytes 235016 | tf_op jit(solution)/shard_map/ppermute | solution.py:35
  31.2 2.0 %collective-permute-done.3 = f32[19584]{0:T(1024)S(1)} collective-permute-done((f32[19584]{0:T(1024)S(1)}, f32[19584]{0:T(1024)S(1)}, u32[]{:S(2)}, u32[]{:S(2)}) %collective-permute-start.3) | collective-permute-done | bytes 78368 | tf_op jit(solution)/shard_map/ppermute | solution.py:35
  33.2 1.7 %reshape.61.east_ref = f32[17,3,48,8]{3,2,1,0:T(8,128)} reshape(f32[19584]{0:T(1024)S(1)} %collective-permute-done.3) | data formatting | bytes 156672 | tf_op jit(solution)/shard_map/reshape | solution.py:35
  34.9 1.7 %reshape.59.west_ref = f32[17,3,48,8]{3,2,1,0:T(8,128)} reshape(f32[19584]{0:T(1024)S(1)} %collective-permute-done.2) | data formatting | bytes 156672 | tf_op jit(solution)/shard_map/reshape | solution.py:35
  36.6 0.7 broadcast_in_dim.5.cor_ref
  37.4 24.4 %shard_map.41 = f32[17,3,32,256]{3,2,1,0:T(8,128)} custom-call(f32[48,384]{1,0:T(8,128)} %broadcast_in_dim.5.cor_ref, f32[3,32,256]{2,1,0:T(8,128)} %c_ref.1, f32[16,3,32,256]{3,2,1,0:T(8,128)} %p_ref.1, f32[17,3,8,256]{3,2,1,0:T(8,128)} %copy-done.1, f32[17,3,8,256]{3,2,1,0:T(8,128)} %copy-done.2, f32[17,3,48,8]{3,2,1,0:T(8,128)} %reshape.59.west_ref, ...), custom_call_target="tpu_custom_call" | custom-call | flops 564019200 | bytes 5431296 | tf_op jit(solution)/shard_map/pallas_call | solution.py:138
  61.8 0.9 slice_bitcast_fusion
  62.7 1.5 %slice_subtract_fusion = f32[16,3,32,256]{3,2,1,0:T(8,128)S(1)} fusion(f32[17,3,32,256]{3,2,1,0:T(8,128)} %shard_map.41, f32[3,32,256]{2,1,0:T(8,128)S(1)} %slice_bitcast_fusion), kind=kLoop, calls=%fused_computation.1 | loop fusion | flops 393216 | bytes 3244032 | tf_op jit(solution)/shard_map/sub | solution.py:179
  64.2 2.7 %fusion.2 = f32[16,16]{0,1:T(8,128)S(1)} fusion(f32[16,3,32,256]{3,2,1,0:T(8,128)S(1)} %slice_subtract_fusion), kind=kOutput, calls=%fused_computation.4 | convolution fusion | flops 75497472 | bytes 1573888 | tf_op jit(solution)/shard_map/dot_general | solution.py:181
  67.0 1.7 %collective-permute-start.4 = (f32[16,16]{0,1:T(8,128)S(1)}, f32[16,16]{0,1:T(8,128)S(1)}, u32[]{:S(2)}, u32[]{:S(2)}) collective-permute-start(f32[16,16]{0,1:T(8,128)S(1)} %fusion.2), channel_id=1, source_target_pairs={{0,8},{8,0},{16,24},{24,16},{1,9},{9,1},{17,25},{25,17},{2,10},{10... | collective-permute-start | bytes 3080 | tf_op jit(solution)/shard_map/ppermute | solution.py:191
  68.7 0.8 collective-permute-done.4
  70.0 3.1 %collective-permute-done.5 = f32[16,16]{0,1:T(8,128)S(1)} collective-permute-done((f32[16,16]{0,1:T(8,128)S(1)}, f32[16,16]{0,1:T(8,128)S(1)}, u32[]{:S(2)}, u32[]{:S(2)}) %collective-permute-start.5) | collective-permute-done | bytes 1056 | tf_op jit(solution)/shard_map/ppermute | solution.py:191
  73.2 0.8 collective-permute-start.6
  74.0 2.9 %collective-permute-done.6 = f32[16,16]{0,1:T(8,128)S(1)} collective-permute-done((f32[16,16]{0,1:T(8,128)S(1)}, f32[16,16]{0,1:T(8,128)S(1)}, u32[]{:S(2)}, u32[]{:S(2)}) %collective-permute-start.6) | collective-permute-done | bytes 1056 | tf_op jit(solution)/shard_map/ppermute | solution.py:191
  76.8 1.4 %collective-permute-start.7 = (f32[16,16]{0,1:T(8,128)S(1)}, f32[16,16]{0,1:T(8,128)S(1)}, u32[]{:S(2)}, u32[]{:S(2)}) collective-permute-start(f32[16,16]{0,1:T(8,128)S(1)} %add.121), channel_id=1, source_target_pairs={{0,2},{1,3},{2,0},{3,1},{4,6},{5,7},{6,4},{7,5},{8,10},{9,11},{10,... | collective-permute-start | bytes 3080 | tf_op jit(solution)/shard_map/ppermute | solution.py:191
  78.2 2.3 %collective-permute-done.7 = f32[16,16]{0,1:T(8,128)S(1)} collective-permute-done((f32[16,16]{0,1:T(8,128)S(1)}, f32[16,16]{0,1:T(8,128)S(1)}, u32[]{:S(2)}, u32[]{:S(2)}) %collective-permute-start.7) | collective-permute-done | bytes 1056 | tf_op jit(solution)/shard_map/ppermute | solution.py:191
  80.5 2.4 %collective-permute-start.8 = (f32[16,16]{0,1:T(8,128)S(1)}, f32[16,16]{0,1:T(8,128)S(1)}, u32[]{:S(2)}, u32[]{:S(2)}) collective-permute-start(f32[16,16]{0,1:T(8,128)S(1)} %add.122), channel_id=1, source_target_pairs={{0,4},{1,5},{2,6},{3,7},{4,0},{5,1},{6,2},{7,3},{8,12},{9,13},{10,... | collective-permute-start | bytes 3080 | tf_op jit(solution)/shard_map/ppermute | solution.py:191
  82.9 0.9 copy.57
  83.8 1.2 %collective-permute-done.8 = f32[16,16]{0,1:T(8,128)S(1)} collective-permute-done((f32[16,16]{0,1:T(8,128)S(1)}, f32[16,16]{0,1:T(8,128)S(1)}, u32[]{:S(2)}, u32[]{:S(2)}) %collective-permute-start.8) | collective-permute-done | bytes 1056 | tf_op jit(solution)/shard_map/ppermute | solution.py:191
  85.1 1.5 %cholesky.16 = f32[16,16]{1,0:T(8,128)S(1)} custom-call(f32[16,16]{1,0:T(8,128)S(1)} %fusion.6), custom_call_target="Cholesky" | custom-call | tf_op jit(solution)/shard_map/jit(cholesky)/cholesky | solution.py:193
  87.2 0.7 multiply_bitcast_fusion
  87.9 0.7 copy.51
  88.6 1.2 %custom-call.7 = f32[1,16,16]{1,2,0:T(8,128)S(1)} custom-call(f32[1,16,16]{2,1,0:T(8,128)S(1)} %get-tuple-element.27), custom_call_target="InvertDiagBlocksLowerTriangular" | custom-call | tf_op jit(solution)/shard_map/jit(_solve_triangular)/triangular_solve | solution.py:194
  89.8 1.5 %convolution_multiply_fusion = f32[16,24576]{1,0:T(8,128)S(1)} fusion(f32[16,24576]{1,0:T(8,128)S(1)} %bitcast.38, f32[1,16,16]{1,2,0:T(8,128)S(1)} %custom-call.7), kind=kOutput, calls=%fused_computation | convolution fusion | flops 75890688 | bytes 3146752 | tf_op jit(solution)/shard_map/jit(_solve_triangular)/triangular_solve | solution.py:194
  91.3 1.6 %copy.58 = f32[2,8,96,256]{3,2,1,0:T(8,128)} copy(f32[2,8,96,256]{3,1,2,0:T(8,128)S(1)} %bitcast.39) | data formatting | bytes 3145728
  (44 shorter events, 5.6 us)
Async XLA Ops:
  1.4 8.2 %copy-start.3 = (f32[3,32,256]{2,1,0:T(8,128)S(1)}, f32[3,32,256]{2,1,0:T(8,128)}, u32[]{:S(2)}) copy-start(f32[3,32,256]{2,1,0:T(8,128)} %c_ref.1) | copy-start | bytes 294916
  1.4 8.3 %copy-start = (f32[16,3,32,256]{3,2,1,0:T(8,128)S(1)}, f32[16,3,32,256]{3,2,1,0:T(8,128)}, u32[]{:S(2)}) copy-start(f32[16,3,32,256]{3,2,1,0:T(8,128)} %p_ref.1) | copy-start | bytes 4718596
  3.5 21.1 %collective-permute-start = (f32[17,3,8,256]{3,2,1,0:T(8,128)}, f32[17,3,8,256]{3,2,1,0:T(8,128)S(1)}, u32[]{:S(2)}, u32[]{:S(2)}) collective-permute-start(f32[17,3,8,256]{3,2,1,0:T(8,128)} %pad_maximum_fusion), channel_id=1, source_target_pairs={{0,1},{1,2},{2,3},{3,4},{4,5},{5,6},{6,7},{7,0},{8,9},{9,10},{10,1... | collective-permute-start | bytes 1253384 | tf_op jit(solution)/shard_map/ppermute | solution.py:33
  6.5 20.1 %collective-permute-start.1 = (f32[17,3,8,256]{3,2,1,0:T(8,128)S(1)}, f32[17,3,8,256]{3,2,1,0:T(8,128)S(1)}, u32[]{:S(2)}, u32[]{:S(2)}) collective-permute-start(f32[17,3,8,256]{3,2,1,0:T(8,128)S(1)} %pad_maximum_fusion.1), channel_id=1, source_target_pairs={{0,7},{1,0},{2,1},{3,2},{4,3},{5,4},{6,5},{7,6},{8,15},{9,8},{10,9... | collective-permute-start | bytes 1253384 | tf_op jit(solution)/shard_map/ppermute | solution.py:33
  24.6 2.3 %copy-start.1 = (f32[17,3,8,256]{3,2,1,0:T(8,128)}, f32[17,3,8,256]{3,2,1,0:T(8,128)S(1)}, u32[]{:S(2)}) copy-start(f32[17,3,8,256]{3,2,1,0:T(8,128)S(1)} %collective-permute-done.up_ref) | copy-start | bytes 1253380
  26.6 1.0 %copy-start.2 = (f32[17,3,8,256]{3,2,1,0:T(8,128)}, f32[17,3,8,256]{3,2,1,0:T(8,128)S(1)}, u32[]{:S(2)}) copy-start(f32[17,3,8,256]{3,2,1,0:T(8,128)S(1)} %collective-permute-done.1.down_ref) | copy-start | bytes 1253380
  28.1 6.8 %collective-permute-start.2 = (f32[19584]{0:T(1024)S(1)}, f32[19584]{0:T(1024)S(1)}, u32[]{:S(2)}, u32[]{:S(2)}) collective-permute-start(f32[19584]{0:T(1024)S(1)} %reshape.58), channel_id=1, source_target_pairs={{0,8},{8,16},{16,24},{24,0},{1,9},{9,17},{17,25},{25,1},{2,10},{10... | collective-permute-start | bytes 235016 | tf_op jit(solution)/shard_map/ppermute | solution.py:35
  29.4 3.8 %collective-permute-start.3 = (f32[19584]{0:T(1024)S(1)}, f32[19584]{0:T(1024)S(1)}, u32[]{:S(2)}, u32[]{:S(2)}) collective-permute-start(f32[19584]{0:T(1024)S(1)} %reshape.60), channel_id=1, source_target_pairs={{0,24},{8,0},{16,8},{24,16},{1,25},{9,1},{17,9},{25,17},{2,26},{10... | collective-permute-start | bytes 235016 | tf_op jit(solution)/shard_map/ppermute | solution.py:35
  67.0 2.5 %collective-permute-start.4 = (f32[16,16]{0,1:T(8,128)S(1)}, f32[16,16]{0,1:T(8,128)S(1)}, u32[]{:S(2)}, u32[]{:S(2)}) collective-permute-start(f32[16,16]{0,1:T(8,128)S(1)} %fusion.2), channel_id=1, source_target_pairs={{0,8},{8,0},{16,24},{24,16},{1,9},{9,1},{17,25},{25,17},{2,10},{10... | collective-permute-start | bytes 3080 | tf_op jit(solution)/shard_map/ppermute | solution.py:191
  69.5 3.7 %collective-permute-start.5 = (f32[16,16]{0,1:T(8,128)S(1)}, f32[16,16]{0,1:T(8,128)S(1)}, u32[]{:S(2)}, u32[]{:S(2)}) collective-permute-start(f32[16,16]{0,1:T(8,128)S(1)} %add.119), channel_id=1, source_target_pairs={{0,16},{8,24},{16,0},{24,8},{1,17},{9,25},{17,1},{25,9},{2,18},{10... | collective-permute-start | bytes 3080 | tf_op jit(solution)/shard_map/ppermute | solution.py:191
  73.2 3.7 %collective-permute-start.6 = (f32[16,16]{0,1:T(8,128)S(1)}, f32[16,16]{0,1:T(8,128)S(1)}, u32[]{:S(2)}, u32[]{:S(2)}) collective-permute-start(f32[16,16]{0,1:T(8,128)S(1)} %add.120), channel_id=1, source_target_pairs={{0,1},{1,0},{2,3},{3,2},{4,5},{5,4},{6,7},{7,6},{8,9},{9,8},{10,11... | collective-permute-start | bytes 3080 | tf_op jit(solution)/shard_map/ppermute | solution.py:191
  76.8 3.7 %collective-permute-start.7 = (f32[16,16]{0,1:T(8,128)S(1)}, f32[16,16]{0,1:T(8,128)S(1)}, u32[]{:S(2)}, u32[]{:S(2)}) collective-permute-start(f32[16,16]{0,1:T(8,128)S(1)} %add.121), channel_id=1, source_target_pairs={{0,2},{1,3},{2,0},{3,1},{4,6},{5,7},{6,4},{7,5},{8,10},{9,11},{10,... | collective-permute-start | bytes 3080 | tf_op jit(solution)/shard_map/ppermute | solution.py:191
  80.5 4.5 %collective-permute-start.8 = (f32[16,16]{0,1:T(8,128)S(1)}, f32[16,16]{0,1:T(8,128)S(1)}, u32[]{:S(2)}, u32[]{:S(2)}) collective-permute-start(f32[16,16]{0,1:T(8,128)S(1)} %add.122), channel_id=1, source_target_pairs={{0,4},{1,5},{2,6},{3,7},{4,0},{5,1},{6,2},{7,3},{8,12},{9,13},{10,... | collective-permute-start | bytes 3080 | tf_op jit(solution)/shard_map/ppermute | solution.py:191

commit v14 on v9

--- a/solution.py
+++ b/solution.py
@@ -160,7 +160,7 @@
     current = forecast(coriolis, states, above, below, west, east, STEPS)
     bred = current[1:] - current[0:1]
     flat = bred.reshape(MEMBERS, -1)
-    local_gram = jnp.dot(flat, flat.T, precision=lax.Precision.HIGHEST)
+    local_gram = jnp.dot(flat, flat.T, precision=lax.Precision.HIGH)
     gram = local_gram
     for axis in ("gx", "gy"):
         count = lax.axis_size(axis)

time: 89.5 us -> 88.8 us (level)
  no operation moved by 1% of the time
where the time goes in v14:
time: 88.8 us; the launch traced here: 88.5 us
  waiting for transfers between devices  27.2 us (31%)
  Pallas kernels  24.2 us (27%)
  starting transfers between devices  13.8 us (16%)
  local copies, waits for them, and re-layouts  10.3 us (12%)
  other arithmetic  8.83 us (10%)
  matrix products  3.5 us (4%)
    pallas_call x1, Pallas kernels, forecast(): pl.pallas_call(functools.partial(forecast_kernel, steps=steps), out_shape...  24.2 us
    ppermute x2, waiting for transfers between devices, shift(): return lax.ppermute(part, axes, pairs)  15.6 us
    ppermute x5, waiting for transfers between devices, body(): gram = gram + lax.ppermute(gram, axis, pairs)  10.1 us
    ppermute x2, starting transfers between devices, shift(): return lax.ppermute(part, axes, pairs)  6.12 us
    ppermute x5, starting transfers between devices, body(): gram = gram + lax.ppermute(gram, axis, pairs)  5.86 us
    unnamed x9, local copies, waits for them, and re-layouts  3.7 us
    reshape x2, local copies, waits for them, and re-layouts, shift(): return lax.ppermute(flat, axes, pairs).reshape(part.shape)  3.43 us
    another operation x3, other arithmetic, body(): lower = jnp.linalg.cholesky(gram)  2.13 us
  transfers between devices with their start and end apart: 9, of which 8 were waited for; matrix products, arithmetic and copies ran while one was open for 5% of the time, Pallas kernels for 0%

profile of v14, /device:TPU:0, one launch (start us, length us, event | category | flops | bytes accessed | tf_op | source)
XLA Modules:
  0.0 88.5 jit_solution(10663937421408104686)
XLA Ops:
  0.6 1.6 %broadcast_add_fusion = f32[16,3,32,256]{3,2,1,0:T(8,128)S(1)} fusion(f32[16,3,32,256]{3,2,1,0:T(8,128)} %param.3, f32[3,32,256]{2,1,0:T(8,128)} %param.2), kind=kLoop, calls=%fused_computation.11 | loop fusion | flops 393216 | bytes 3244032 | tf_op jit(solution)/shard_map/add | solution.py:158
  2.3 3.0 %collective-permute-start = (f32[17,3,8,256]{3,2,1,0:T(8,128)S(1)}, f32[17,3,8,256]{3,2,1,0:T(8,128)S(1)}, u32[]{:S(2)}, u32[]{:S(2)}) collective-permute-start(f32[17,3,8,256]{3,2,1,0:T(8,128)S(1)} %get-tuple-element.9), channel_id=1, source_target_pairs={{0,1},{1,2},{2,3},{3,4},{4,5},{5,6},{6,7},{7,0},{8,9},{9,10},{10,1... | collective-permute-start | bytes 1253384 | tf_op jit(solution)/shard_map/ppermute | solution.py:38
  5.3 3.1 %collective-permute-start.1 = (f32[17,3,8,256]{3,2,1,0:T(8,128)S(1)}, f32[17,3,8,256]{3,2,1,0:T(8,128)S(1)}, u32[]{:S(2)}, u32[]{:S(2)}) collective-permute-start(f32[17,3,8,256]{3,2,1,0:T(8,128)S(1)} %get-tuple-element.8), channel_id=1, source_target_pairs={{0,7},{1,0},{2,1},{3,2},{4,3},{5,4},{6,5},{7,6},{8,15},{9,8},{10,9... | collective-permute-start | bytes 1253384 | tf_op jit(solution)/shard_map/ppermute | solution.py:38
  8.4 1.3 %pad_maximum_fusion.x_ref = f32[17,3,32,256]{3,2,1,0:T(8,128)} fusion(f32[1,3,32,256]{3,2,1,0:T(8,128)S(1)} %bitcast.33, f32[16,3,32,256]{3,2,1,0:T(8,128)S(1)} %broadcast_add_fusion), kind=kLoop, calls=%fused_computation.3 | loop fusion | flops 417792 | bytes 3342336 | tf_op jit(solution)/shard_map/concatenate | solution.py:158
  9.8 13.4 %collective-permute-done.up_ref = f32[17,3,8,256]{3,2,1,0:T(8,128)S(1)} collective-permute-done((f32[17,3,8,256]{3,2,1,0:T(8,128)S(1)}, f32[17,3,8,256]{3,2,1,0:T(8,128)S(1)}, u32[]{:S(2)}, u32[]{:S(2)}) %collective-permute-start) | collective-permute-done | bytes 417824 | tf_op jit(solution)/shard_map/ppermute | solution.py:38
  23.2 2.2 %collective-permute-done.1.down_ref = f32[17,3,8,256]{3,2,1,0:T(8,128)S(1)} collective-permute-done((f32[17,3,8,256]{3,2,1,0:T(8,128)S(1)}, f32[17,3,8,256]{3,2,1,0:T(8,128)S(1)}, u32[]{:S(2)}, u32[]{:S(2)}) %collective-permute-start.1) | collective-permute-done | bytes 417824 | tf_op jit(solution)/shard_map/ppermute | solution.py:38
  26.6 0.5 reshape.59
  27.7 1.8 %collective-permute-start.3 = (f32[19584]{0:T(1024)S(1)}, f32[19584]{0:T(1024)S(1)}, u32[]{:S(2)}, u32[]{:S(2)}) collective-permute-start(f32[19584]{0:T(1024)S(1)} %reshape.61), channel_id=1, source_target_pairs={{0,24},{8,0},{16,8},{24,16},{1,25},{9,1},{17,9},{25,17},{2,26},{10... | collective-permute-start | bytes 235016 | tf_op jit(solution)/shard_map/ppermute | solution.py:40
  29.5 1.5 %collective-permute-done.2 = f32[19584]{0:T(1024)S(1)} collective-permute-done((f32[19584]{0:T(1024)S(1)}, f32[19584]{0:T(1024)S(1)}, u32[]{:S(2)}, u32[]{:S(2)}) %collective-permute-start.2) | collective-permute-done | bytes 78368 | tf_op jit(solution)/shard_map/ppermute | solution.py:40
  31.0 1.7 %reshape.60.west_ref = f32[17,3,48,8]{3,2,1,0:T(8,128)} reshape(f32[19584]{0:T(1024)S(1)} %collective-permute-done.2) | data formatting | bytes 156672 | tf_op jit(solution)/shard_map/reshape | solution.py:40
  32.7 1.7 %reshape.62.east_ref = f32[17,3,48,8]{3,2,1,0:T(8,128)} reshape(f32[19584]{0:T(1024)S(1)} %collective-permute-done.3) | data formatting | bytes 156672 | tf_op jit(solution)/shard_map/reshape | solution.py:40
  34.5 0.7 broadcast_in_dim.5.cor_ref
  35.2 24.2 %shard_map.41 = f32[17,3,32,256]{3,2,1,0:T(8,128)} custom-call(f32[48,384]{1,0:T(8,128)} %broadcast_in_dim.5.cor_ref, f32[17,3,32,256]{3,2,1,0:T(8,128)} %pad_maximum_fusion.x_ref, f32[17,3,8,256]{3,2,1,0:T(8,128)} %copy-done, f32[17,3,8,256]{3,2,1,0:T(8,128)} %copy-done.1, f32[17,3,48,8]{3,2,1,0:T(8,128)} %reshape.60.west_ref, ...), custom_call_target="tpu_custom_call" | custom-call | flops 564019200 | bytes 5431296 | tf_op jit(solution)/shard_map/pallas_call | solution.py:120
  59.3 0.9 %slice_bitcast_fusion = f32[3,32,256]{2,1,0:T(8,128)S(1)} fusion(f32[17,3,32,256]{3,2,1,0:T(8,128)} %shard_map.41), kind=kLoop, calls=%fused_computation.14 | loop fusion | bytes 196608 | tf_op jit(solution)/shard_map/sub | solution.py:161
  60.2 1.5 %slice_subtract_fusion = f32[16,3,32,256]{3,2,1,0:T(8,128)S(1)} fusion(f32[17,3,32,256]{3,2,1,0:T(8,128)} %shard_map.41, f32[3,32,256]{2,1,0:T(8,128)S(1)} %slice_bitcast_fusion), kind=kLoop, calls=%fused_computation.5 | loop fusion | flops 393216 | bytes 3244032 | tf_op jit(solution)/shard_map/sub | solution.py:161
  61.8 2.0 %fusion.2 = f32[16,16]{0,1:T(8,128)S(1)} fusion(f32[16,3,32,256]{3,2,1,0:T(8,128)S(1)} %slice_subtract_fusion), kind=kOutput, calls=%fused_computation.10 | convolution fusion | flops 37748736 | bytes 1573888 | tf_op jit(solution)/shard_map/dot_general | solution.py:163
  64.3 0.8 collective-permute-done.4
  65.1 1.4 %collective-permute-start.5 = (f32[16,16]{0,1:T(8,128)S(1)}, f32[16,16]{0,1:T(8,128)S(1)}, u32[]{:S(2)}, u32[]{:S(2)}) collective-permute-start(f32[16,16]{0,1:T(8,128)S(1)} %add.77), channel_id=1, source_target_pairs={{0,16},{8,24},{16,0},{24,8},{1,17},{9,25},{17,1},{25,9},{2,18},{10... | collective-permute-start | bytes 3080 | tf_op jit(solution)/shard_map/ppermute | solution.py:173
  66.5 2.3 %collective-permute-done.5 = f32[16,16]{0,1:T(8,128)S(1)} collective-permute-done((f32[16,16]{0,1:T(8,128)S(1)}, f32[16,16]{0,1:T(8,128)S(1)}, u32[]{:S(2)}, u32[]{:S(2)}) %collective-permute-start.5) | collective-permute-done | bytes 1056 | tf_op jit(solution)/shard_map/ppermute | solution.py:173
  69.2 3.2 %collective-permute-done.6 = f32[16,16]{0,1:T(8,128)S(1)} collective-permute-done((f32[16,16]{0,1:T(8,128)S(1)}, f32[16,16]{0,1:T(8,128)S(1)}, u32[]{:S(2)}, u32[]{:S(2)}) %collective-permute-start.6) | collective-permute-done | bytes 1056 | tf_op jit(solution)/shard_map/ppermute | solution.py:173
  72.4 1.3 %collective-permute-start.7 = (f32[16,16]{0,1:T(8,128)S(1)}, f32[16,16]{0,1:T(8,128)S(1)}, u32[]{:S(2)}, u32[]{:S(2)}) collective-permute-start(f32[16,16]{0,1:T(8,128)S(1)} %add.79), channel_id=1, source_target_pairs={{0,2},{1,3},{2,0},{3,1},{4,6},{5,7},{6,4},{7,5},{8,10},{9,11},{10,... | collective-permute-start | bytes 3080 | tf_op jit(solution)/shard_map/ppermute | solution.py:173
  73.7 2.4 %collective-permute-done.7 = f32[16,16]{0,1:T(8,128)S(1)} collective-permute-done((f32[16,16]{0,1:T(8,128)S(1)}, f32[16,16]{0,1:T(8,128)S(1)}, u32[]{:S(2)}, u32[]{:S(2)}) %collective-permute-start.7) | collective-permute-done | bytes 1056 | tf_op jit(solution)/shard_map/ppermute | solution.py:173
  76.1 2.3 %collective-permute-start.8 = (f32[16,16]{0,1:T(8,128)S(1)}, f32[16,16]{0,1:T(8,128)S(1)}, u32[]{:S(2)}, u32[]{:S(2)}) collective-permute-start(f32[16,16]{0,1:T(8,128)S(1)} %add.80), channel_id=1, source_target_pairs={{0,4},{1,5},{2,6},{3,7},{4,0},{5,1},{6,2},{7,3},{8,12},{9,13},{10,... | collective-permute-start | bytes 3080 | tf_op jit(solution)/shard_map/ppermute | solution.py:173
  78.4 0.9 %copy.19 = f32[2,8,96,256]{3,1,2,0:T(8,128)S(1)} copy(f32[2,8,96,256]{3,2,1,0:T(8,128)S(1)} %bitcast.29) | data formatting | bytes 3145728
  79.3 1.4 %collective-permute-done.8 = f32[16,16]{0,1:T(8,128)S(1)} collective-permute-done((f32[16,16]{0,1:T(8,128)S(1)}, f32[16,16]{0,1:T(8,128)S(1)}, u32[]{:S(2)}, u32[]{:S(2)}) %collective-permute-start.8) | collective-permute-done | bytes 1056 | tf_op jit(solution)/shard_map/ppermute | solution.py:173
  80.7 1.5 %cholesky.16 = f32[16,16]{1,0:T(8,128)S(1)} custom-call(f32[16,16]{1,0:T(8,128)S(1)} %fusion.8), custom_call_target="Cholesky" | custom-call | tf_op jit(solution)/shard_map/jit(cholesky)/cholesky | solution.py:175
  82.2 0.6 compare_reduce_fusion
  82.9 0.7 multiply_bitcast_fusion
  83.5 1.2 %custom-call.7 = f32[1,16,16]{1,2,0:T(8,128)S(1)} custom-call(f32[1,16,16]{2,1,0:T(8,128)S(1)} %get-tuple-element.11), custom_call_target="InvertDiagBlocksLowerTriangular" | custom-call | tf_op jit(solution)/shard_map/jit(_solve_triangular)/triangular_solve | solution.py:176
  84.8 1.5 %convolution_multiply_fusion = f32[16,24576]{1,0:T(8,128)S(1)} fusion(f32[16,24576]{1,0:T(8,128)S(1)} %bitcast.30, f32[1,16,16]{1,2,0:T(8,128)S(1)} %custom-call.7), kind=kOutput, calls=%fused_computation | convolution fusion | flops 75890688 | bytes 3146752 | tf_op jit(solution)/shard_map/jit(_solve_triangular)/triangular_solve | solution.py:176
  86.3 1.6 %copy.20 = f32[2,8,96,256]{3,2,1,0:T(8,128)} copy(f32[2,8,96,256]{3,1,2,0:T(8,128)S(1)} %bitcast.31) | data formatting | bytes 3145728
  87.9 0.7 copy.15
  (23 shorter events, 3.0 us)
Async XLA Ops:
  0.6 1.6 %copy-start.2 = (f32[3,32,256]{2,1,0:T(8,128)S(1)}, f32[3,32,256]{2,1,0:T(8,128)}, u32[]{:S(2)}) copy-start(f32[3,32,256]{2,1,0:T(8,128)} %param.2) | copy-start | bytes 294916
  2.3 20.9 %collective-permute-start = (f32[17,3,8,256]{3,2,1,0:T(8,128)S(1)}, f32[17,3,8,256]{3,2,1,0:T(8,128)S(1)}, u32[]{:S(2)}, u32[]{:S(2)}) collective-permute-start(f32[17,3,8,256]{3,2,1,0:T(8,128)S(1)} %get-tuple-element.9), channel_id=1, source_target_pairs={{0,1},{1,2},{2,3},{3,4},{4,5},{5,6},{6,7},{7,0},{8,9},{9,10},{10,1... | collective-permute-start | bytes 1253384 | tf_op jit(solution)/shard_map/ppermute | solution.py:38
  5.3 20.1 %collective-permute-start.1 = (f32[17,3,8,256]{3,2,1,0:T(8,128)S(1)}, f32[17,3,8,256]{3,2,1,0:T(8,128)S(1)}, u32[]{:S(2)}, u32[]{:S(2)}) collective-permute-start(f32[17,3,8,256]{3,2,1,0:T(8,128)S(1)} %get-tuple-element.8), channel_id=1, source_target_pairs={{0,7},{1,0},{2,1},{3,2},{4,3},{5,4},{6,5},{7,6},{8,15},{9,8},{10,9... | collective-permute-start | bytes 1253384 | tf_op jit(solution)/shard_map/ppermute | solution.py:38
  23.2 2.5 %copy-start = (f32[17,3,8,256]{3,2,1,0:T(8,128)}, f32[17,3,8,256]{3,2,1,0:T(8,128)S(1)}, u32[]{:S(2)}) copy-start(f32[17,3,8,256]{3,2,1,0:T(8,128)S(1)} %collective-permute-done.up_ref) | copy-start | bytes 1253380
  25.4 0.8 copy-start.1
  27.1 3.9 %collective-permute-start.2 = (f32[19584]{0:T(1024)S(1)}, f32[19584]{0:T(1024)S(1)}, u32[]{:S(2)}, u32[]{:S(2)}) collective-permute-start(f32[19584]{0:T(1024)S(1)} %reshape.59), channel_id=1, source_target_pairs={{0,8},{8,16},{16,24},{24,0},{1,9},{9,17},{17,25},{25,1},{2,10},{10... | collective-permute-start | bytes 235016 | tf_op jit(solution)/shard_map/ppermute | solution.py:40
  27.7 5.0 %collective-permute-start.3 = (f32[19584]{0:T(1024)S(1)}, f32[19584]{0:T(1024)S(1)}, u32[]{:S(2)}, u32[]{:S(2)}) collective-permute-start(f32[19584]{0:T(1024)S(1)} %reshape.61), channel_id=1, source_target_pairs={{0,24},{8,0},{16,8},{24,16},{1,25},{9,1},{17,9},{25,17},{2,26},{10... | collective-permute-start | bytes 235016 | tf_op jit(solution)/shard_map/ppermute | solution.py:40
  63.8 1.4 %collective-permute-start.4 = (f32[16,16]{0,1:T(8,128)S(1)}, f32[16,16]{0,1:T(8,128)S(1)}, u32[]{:S(2)}, u32[]{:S(2)}) collective-permute-start(f32[16,16]{0,1:T(8,128)S(1)} %fusion.2), channel_id=1, source_target_pairs={{0,8},{8,0},{16,24},{24,16},{1,9},{9,1},{17,25},{25,17},{2,10},{10... | collective-permute-start | bytes 3080 | tf_op jit(solution)/shard_map/ppermute | solution.py:173
  65.1 3.7 %collective-permute-start.5 = (f32[16,16]{0,1:T(8,128)S(1)}, f32[16,16]{0,1:T(8,128)S(1)}, u32[]{:S(2)}, u32[]{:S(2)}) collective-permute-start(f32[16,16]{0,1:T(8,128)S(1)} %add.77), channel_id=1, source_target_pairs={{0,16},{8,24},{16,0},{24,8},{1,17},{9,25},{17,1},{25,9},{2,18},{10... | collective-permute-start | bytes 3080 | tf_op jit(solution)/shard_map/ppermute | solution.py:173
  68.8 3.7 %collective-permute-start.6 = (f32[16,16]{0,1:T(8,128)S(1)}, f32[16,16]{0,1:T(8,128)S(1)}, u32[]{:S(2)}, u32[]{:S(2)}) collective-permute-start(f32[16,16]{0,1:T(8,128)S(1)} %add.78), channel_id=1, source_target_pairs={{0,1},{1,0},{2,3},{3,2},{4,5},{5,4},{6,7},{7,6},{8,9},{9,8},{10,11... | collective-permute-start | bytes 3080 | tf_op jit(solution)/shard_map/ppermute | solution.py:173
  72.4 3.7 %collective-permute-start.7 = (f32[16,16]{0,1:T(8,128)S(1)}, f32[16,16]{0,1:T(8,128)S(1)}, u32[]{:S(2)}, u32[]{:S(2)}) collective-permute-start(f32[16,16]{0,1:T(8,128)S(1)} %add.79), channel_id=1, source_target_pairs={{0,2},{1,3},{2,0},{3,1},{4,6},{5,7},{6,4},{7,5},{8,10},{9,11},{10,... | collective-permute-start | bytes 3080 | tf_op jit(solution)/shard_map/ppermute | solution.py:173
  76.1 4.5 %collective-permute-start.8 = (f32[16,16]{0,1:T(8,128)S(1)}, f32[16,16]{0,1:T(8,128)S(1)}, u32[]{:S(2)}, u32[]{:S(2)}) collective-permute-start(f32[16,16]{0,1:T(8,128)S(1)} %add.80), channel_id=1, source_target_pairs={{0,4},{1,5},{2,6},{3,7},{4,0},{5,1},{6,2},{7,3},{8,12},{9,13},{10,... | collective-permute-start | bytes 3080 | tf_op jit(solution)/shard_map/ppermute | solution.py:173

commit v15 on v14

--- a/solution.py
+++ b/solution.py
@@ -173,7 +173,8 @@
             gram = gram + lax.ppermute(gram, axis, pairs)
             stride *= 2
     lower = jnp.linalg.cholesky(gram)
-    solved = jax.scipy.linalg.solve_triangular(lower, flat, lower=True)
+    inverse = jax.scipy.linalg.solve_triangular(lower, jnp.eye(flat.shape[0], dtype=flat.dtype), lower=True)
+    solved = jnp.dot(inverse, flat, precision=lax.Precision.HIGH)
     domain_length = 3 * grid_rows * grid_cols
     basis = (math.sqrt(domain_length) * solved).reshape(perts.shape)
     rfactor = lower.T / math.sqrt(domain_length)

time: 88.8 us -> 88.3 us (level)
    another operation x1, matrix products: 1.5 us -> 0.19 us  [body(): jax.scipy.linalg.solve_triangular(lower, jnp.eye(flat.shape[0], dtype=fla...]
where the time goes in v15:
time: 88.3 us; the launch traced here: 88 us
  waiting for transfers between devices  27.2 us (31%)
  Pallas kernels  24.2 us (27%)
  starting transfers between devices  13.8 us (16%)
  local copies, waits for them, and re-layouts  10.3 us (12%)
  other arithmetic  8.83 us (10%)
  matrix products  2.97 us (3%)
    pallas_call x1, Pallas kernels, forecast(): pl.pallas_call(functools.partial(forecast_kernel, steps=steps), out_shape...  24.2 us
    ppermute x2, waiting for transfers between devices, shift(): return lax.ppermute(part, axes, pairs)  15.6 us
    ppermute x5, waiting for transfers between devices, body(): gram = gram + lax.ppermute(gram, axis, pairs)  10.1 us
    ppermute x2, starting transfers between devices, shift(): return lax.ppermute(part, axes, pairs)  6.12 us
    ppermute x5, starting transfers between devices, body(): gram = gram + lax.ppermute(gram, axis, pairs)  5.86 us
    unnamed x9, local copies, waits for them, and re-layouts  3.7 us
    reshape x2, local copies, waits for them, and re-layouts, shift(): return lax.ppermute(flat, axes, pairs).reshape(part.shape)  3.43 us
    another operation x3, other arithmetic, body(): lower = jnp.linalg.cholesky(gram)  2.13 us
  transfers between devices with their start and end apart: 9, of which 8 were waited for; matrix products, arithmetic and copies ran while one was open for 5% of the time, Pallas kernels for 0%

profile of v15, /device:TPU:0, one launch (start us, length us, event | category | flops | bytes accessed | tf_op | source)
XLA Modules:
  0.0 88.0 jit_solution(3696106867388674565)
XLA Ops:
  0.6 1.6 %broadcast_add_fusion = f32[16,3,32,256]{3,2,1,0:T(8,128)S(1)} fusion(f32[16,3,32,256]{3,2,1,0:T(8,128)} %param.3, f32[3,32,256]{2,1,0:T(8,128)} %param.2), kind=kLoop, calls=%fused_computation.11 | loop fusion | flops 393216 | bytes 3244032 | tf_op jit(solution)/shard_map/add | solution.py:158
  2.3 3.0 %collective-permute-start = (f32[17,3,8,256]{3,2,1,0:T(8,128)S(1)}, f32[17,3,8,256]{3,2,1,0:T(8,128)S(1)}, u32[]{:S(2)}, u32[]{:S(2)}) collective-permute-start(f32[17,3,8,256]{3,2,1,0:T(8,128)S(1)} %get-tuple-element.9), channel_id=1, source_target_pairs={{0,1},{1,2},{2,3},{3,4},{4,5},{5,6},{6,7},{7,0},{8,9},{9,10},{10,1... | collective-permute-start | bytes 1253384 | tf_op jit(solution)/shard_map/ppermute | solution.py:38
  5.3 3.1 %collective-permute-start.1 = (f32[17,3,8,256]{3,2,1,0:T(8,128)S(1)}, f32[17,3,8,256]{3,2,1,0:T(8,128)S(1)}, u32[]{:S(2)}, u32[]{:S(2)}) collective-permute-start(f32[17,3,8,256]{3,2,1,0:T(8,128)S(1)} %get-tuple-element.8), channel_id=1, source_target_pairs={{0,7},{1,0},{2,1},{3,2},{4,3},{5,4},{6,5},{7,6},{8,15},{9,8},{10,9... | collective-permute-start | bytes 1253384 | tf_op jit(solution)/shard_map/ppermute | solution.py:38
  8.4 1.3 %pad_maximum_fusion.x_ref = f32[17,3,32,256]{3,2,1,0:T(8,128)} fusion(f32[1,3,32,256]{3,2,1,0:T(8,128)S(1)} %bitcast.34, f32[16,3,32,256]{3,2,1,0:T(8,128)S(1)} %broadcast_add_fusion), kind=kLoop, calls=%fused_computation.3 | loop fusion | flops 417792 | bytes 3342336 | tf_op jit(solution)/shard_map/concatenate | solution.py:158
  9.8 13.4 %collective-permute-done.up_ref = f32[17,3,8,256]{3,2,1,0:T(8,128)S(1)} collective-permute-done((f32[17,3,8,256]{3,2,1,0:T(8,128)S(1)}, f32[17,3,8,256]{3,2,1,0:T(8,128)S(1)}, u32[]{:S(2)}, u32[]{:S(2)}) %collective-permute-start) | collective-permute-done | bytes 417824 | tf_op jit(solution)/shard_map/ppermute | solution.py:38
  23.2 2.2 %collective-permute-done.1.down_ref = f32[17,3,8,256]{3,2,1,0:T(8,128)S(1)} collective-permute-done((f32[17,3,8,256]{3,2,1,0:T(8,128)S(1)}, f32[17,3,8,256]{3,2,1,0:T(8,128)S(1)}, u32[]{:S(2)}, u32[]{:S(2)}) %collective-permute-start.1) | collective-permute-done | bytes 417824 | tf_op jit(solution)/shard_map/ppermute | solution.py:38
  26.6 0.5 reshape.59
  27.7 1.8 %collective-permute-start.3 = (f32[19584]{0:T(1024)S(1)}, f32[19584]{0:T(1024)S(1)}, u32[]{:S(2)}, u32[]{:S(2)}) collective-permute-start(f32[19584]{0:T(1024)S(1)} %reshape.61), channel_id=1, source_target_pairs={{0,24},{8,0},{16,8},{24,16},{1,25},{9,1},{17,9},{25,17},{2,26},{10... | collective-permute-start | bytes 235016 | tf_op jit(solution)/shard_map/ppermute | solution.py:40
  29.5 1.5 %collective-permute-done.2 = f32[19584]{0:T(1024)S(1)} collective-permute-done((f32[19584]{0:T(1024)S(1)}, f32[19584]{0:T(1024)S(1)}, u32[]{:S(2)}, u32[]{:S(2)}) %collective-permute-start.2) | collective-permute-done | bytes 78368 | tf_op jit(solution)/shard_map/ppermute | solution.py:40
  31.0 1.7 %reshape.60.west_ref = f32[17,3,48,8]{3,2,1,0:T(8,128)} reshape(f32[19584]{0:T(1024)S(1)} %collective-permute-done.2) | data formatting | bytes 156672 | tf_op jit(solution)/shard_map/reshape | solution.py:40
  32.7 1.7 %reshape.62.east_ref = f32[17,3,48,8]{3,2,1,0:T(8,128)} reshape(f32[19584]{0:T(1024)S(1)} %collective-permute-done.3) | data formatting | bytes 156672 | tf_op jit(solution)/shard_map/reshape | solution.py:40
  34.5 0.7 broadcast_in_dim.5.cor_ref
  35.2 24.2 %shard_map.41 = f32[17,3,32,256]{3,2,1,0:T(8,128)} custom-call(f32[48,384]{1,0:T(8,128)} %broadcast_in_dim.5.cor_ref, f32[17,3,32,256]{3,2,1,0:T(8,128)} %pad_maximum_fusion.x_ref, f32[17,3,8,256]{3,2,1,0:T(8,128)} %copy-done, f32[17,3,8,256]{3,2,1,0:T(8,128)} %copy-done.1, f32[17,3,48,8]{3,2,1,0:T(8,128)} %reshape.60.west_ref, ...), custom_call_target="tpu_custom_call" | custom-call | flops 564019200 | bytes 5431296 | tf_op jit(solution)/shard_map/pallas_call | solution.py:120
  59.3 0.9 %slice_bitcast_fusion = f32[3,32,256]{2,1,0:T(8,128)S(1)} fusion(f32[17,3,32,256]{3,2,1,0:T(8,128)} %shard_map.41), kind=kLoop, calls=%fused_computation.14 | loop fusion | bytes 196608 | tf_op jit(solution)/shard_map/sub | solution.py:161
  60.2 1.5 %slice_subtract_fusion = f32[16,3,32,256]{3,2,1,0:T(8,128)S(1)} fusion(f32[17,3,32,256]{3,2,1,0:T(8,128)} %shard_map.41, f32[3,32,256]{2,1,0:T(8,128)S(1)} %slice_bitcast_fusion), kind=kLoop, calls=%fused_computation.5 | loop fusion | flops 393216 | bytes 3244032 | tf_op jit(solution)/shard_map/sub | solution.py:161
  61.8 2.0 %fusion.2 = f32[16,16]{0,1:T(8,128)S(1)} fusion(f32[16,3,32,256]{3,2,1,0:T(8,128)S(1)} %slice_subtract_fusion), kind=kOutput, calls=%fused_computation.10 | convolution fusion | flops 37748736 | bytes 1573888 | tf_op jit(solution)/shard_map/dot_general | solution.py:163
  64.3 0.8 collective-permute-done.4
  65.1 1.4 %collective-permute-start.5 = (f32[16,16]{0,1:T(8,128)S(1)}, f32[16,16]{0,1:T(8,128)S(1)}, u32[]{:S(2)}, u32[]{:S(2)}) collective-permute-start(f32[16,16]{0,1:T(8,128)S(1)} %add.77), channel_id=1, source_target_pairs={{0,16},{8,24},{16,0},{24,8},{1,17},{9,25},{17,1},{25,9},{2,18},{10... | collective-permute-start | bytes 3080 | tf_op jit(solution)/shard_map/ppermute | solution.py:173
  66.5 2.3 %collective-permute-done.5 = f32[16,16]{0,1:T(8,128)S(1)} collective-permute-done((f32[16,16]{0,1:T(8,128)S(1)}, f32[16,16]{0,1:T(8,128)S(1)}, u32[]{:S(2)}, u32[]{:S(2)}) %collective-permute-start.5) | collective-permute-done | bytes 1056 | tf_op jit(solution)/shard_map/ppermute | solution.py:173
  69.2 3.2 %collective-permute-done.6 = f32[16,16]{0,1:T(8,128)S(1)} collective-permute-done((f32[16,16]{0,1:T(8,128)S(1)}, f32[16,16]{0,1:T(8,128)S(1)}, u32[]{:S(2)}, u32[]{:S(2)}) %collective-permute-start.6) | collective-permute-done | bytes 1056 | tf_op jit(solution)/shard_map/ppermute | solution.py:173
  72.4 1.3 %collective-permute-start.7 = (f32[16,16]{0,1:T(8,128)S(1)}, f32[16,16]{0,1:T(8,128)S(1)}, u32[]{:S(2)}, u32[]{:S(2)}) collective-permute-start(f32[16,16]{0,1:T(8,128)S(1)} %add.79), channel_id=1, source_target_pairs={{0,2},{1,3},{2,0},{3,1},{4,6},{5,7},{6,4},{7,5},{8,10},{9,11},{10,... | collective-permute-start | bytes 3080 | tf_op jit(solution)/shard_map/ppermute | solution.py:173
  73.7 2.4 %collective-permute-done.7 = f32[16,16]{0,1:T(8,128)S(1)} collective-permute-done((f32[16,16]{0,1:T(8,128)S(1)}, f32[16,16]{0,1:T(8,128)S(1)}, u32[]{:S(2)}, u32[]{:S(2)}) %collective-permute-start.7) | collective-permute-done | bytes 1056 | tf_op jit(solution)/shard_map/ppermute | solution.py:173
  76.1 2.3 %collective-permute-start.8 = (f32[16,16]{0,1:T(8,128)S(1)}, f32[16,16]{0,1:T(8,128)S(1)}, u32[]{:S(2)}, u32[]{:S(2)}) collective-permute-start(f32[16,16]{0,1:T(8,128)S(1)} %add.80), channel_id=1, source_target_pairs={{0,4},{1,5},{2,6},{3,7},{4,0},{5,1},{6,2},{7,3},{8,12},{9,13},{10,... | collective-permute-start | bytes 3080 | tf_op jit(solution)/shard_map/ppermute | solution.py:173
  78.4 0.9 %copy.19 = f32[2,8,96,256]{3,1,2,0:T(8,128)S(1)} copy(f32[2,8,96,256]{3,2,1,0:T(8,128)S(1)} %bitcast.30) | data formatting | bytes 3145728
  79.3 1.4 %collective-permute-done.8 = f32[16,16]{0,1:T(8,128)S(1)} collective-permute-done((f32[16,16]{0,1:T(8,128)S(1)}, f32[16,16]{0,1:T(8,128)S(1)}, u32[]{:S(2)}, u32[]{:S(2)}) %collective-permute-start.8) | collective-permute-done | bytes 1056 | tf_op jit(solution)/shard_map/ppermute | solution.py:173
  80.7 1.5 %cholesky.17 = f32[16,16]{1,0:T(8,128)S(1)} custom-call(f32[16,16]{1,0:T(8,128)S(1)} %fusion.9), custom_call_target="Cholesky" | custom-call | tf_op jit(solution)/shard_map/jit(cholesky)/cholesky | solution.py:175
  82.2 0.6 compare_reduce_fusion
  82.9 0.7 multiply_bitcast_fusion
  83.5 1.2 %custom-call.7 = f32[1,16,16]{1,2,0:T(8,128)S(1)} custom-call(f32[1,16,16]{2,1,0:T(8,128)S(1)} %get-tuple-element.11), custom_call_target="InvertDiagBlocksLowerTriangular" | custom-call | tf_op jit(solution)/shard_map/jit(_solve_triangular)/triangular_solve | solution.py:176
  84.9 0.8 convolution_multiply_fusion
  85.7 1.6 %copy.20 = f32[2,8,96,256]{3,2,1,0:T(8,128)} copy(f32[2,8,96,256]{3,1,2,0:T(8,128)S(1)} %bitcast.32) | data formatting | bytes 3145728
  87.3 0.7 copy.15
  (24 shorter events, 3.2 us)
Async XLA Ops:
  0.6 1.6 %copy-start.2 = (f32[3,32,256]{2,1,0:T(8,128)S(1)}, f32[3,32,256]{2,1,0:T(8,128)}, u32[]{:S(2)}) copy-start(f32[3,32,256]{2,1,0:T(8,128)} %param.2) | copy-start | bytes 294916
  2.3 20.9 %collective-permute-start = (f32[17,3,8,256]{3,2,1,0:T(8,128)S(1)}, f32[17,3,8,256]{3,2,1,0:T(8,128)S(1)}, u32[]{:S(2)}, u32[]{:S(2)}) collective-permute-start(f32[17,3,8,256]{3,2,1,0:T(8,128)S(1)} %get-tuple-element.9), channel_id=1, source_target_pairs={{0,1},{1,2},{2,3},{3,4},{4,5},{5,6},{6,7},{7,0},{8,9},{9,10},{10,1... | collective-permute-start | bytes 1253384 | tf_op jit(solution)/shard_map/ppermute | solution.py:38
  5.3 20.1 %collective-permute-start.1 = (f32[17,3,8,256]{3,2,1,0:T(8,128)S(1)}, f32[17,3,8,256]{3,2,1,0:T(8,128)S(1)}, u32[]{:S(2)}, u32[]{:S(2)}) collective-permute-start(f32[17,3,8,256]{3,2,1,0:T(8,128)S(1)} %get-tuple-element.8), channel_id=1, source_target_pairs={{0,7},{1,0},{2,1},{3,2},{4,3},{5,4},{6,5},{7,6},{8,15},{9,8},{10,9... | collective-permute-start | bytes 1253384 | tf_op jit(solution)/shard_map/ppermute | solution.py:38
  23.2 2.5 %copy-start = (f32[17,3,8,256]{3,2,1,0:T(8,128)}, f32[17,3,8,256]{3,2,1,0:T(8,128)S(1)}, u32[]{:S(2)}) copy-start(f32[17,3,8,256]{3,2,1,0:T(8,128)S(1)} %collective-permute-done.up_ref) | copy-start | bytes 1253380
  25.4 0.8 copy-start.1
  27.1 3.9 %collective-permute-start.2 = (f32[19584]{0:T(1024)S(1)}, f32[19584]{0:T(1024)S(1)}, u32[]{:S(2)}, u32[]{:S(2)}) collective-permute-start(f32[19584]{0:T(1024)S(1)} %reshape.59), channel_id=1, source_target_pairs={{0,8},{8,16},{16,24},{24,0},{1,9},{9,17},{17,25},{25,1},{2,10},{10... | collective-permute-start | bytes 235016 | tf_op jit(solution)/shard_map/ppermute | solution.py:40
  27.7 5.0 %collective-permute-start.3 = (f32[19584]{0:T(1024)S(1)}, f32[19584]{0:T(1024)S(1)}, u32[]{:S(2)}, u32[]{:S(2)}) collective-permute-start(f32[19584]{0:T(1024)S(1)} %reshape.61), channel_id=1, source_target_pairs={{0,24},{8,0},{16,8},{24,16},{1,25},{9,1},{17,9},{25,17},{2,26},{10... | collective-permute-start | bytes 235016 | tf_op jit(solution)/shard_map/ppermute | solution.py:40
  63.8 1.4 %collective-permute-start.4 = (f32[16,16]{0,1:T(8,128)S(1)}, f32[16,16]{0,1:T(8,128)S(1)}, u32[]{:S(2)}, u32[]{:S(2)}) collective-permute-start(f32[16,16]{0,1:T(8,128)S(1)} %fusion.2), channel_id=1, source_target_pairs={{0,8},{8,0},{16,24},{24,16},{1,9},{9,1},{17,25},{25,17},{2,10},{10... | collective-permute-start | bytes 3080 | tf_op jit(solution)/shard_map/ppermute | solution.py:173
  65.1 3.7 %collective-permute-start.5 = (f32[16,16]{0,1:T(8,128)S(1)}, f32[16,16]{0,1:T(8,128)S(1)}, u32[]{:S(2)}, u32[]{:S(2)}) collective-permute-start(f32[16,16]{0,1:T(8,128)S(1)} %add.77), channel_id=1, source_target_pairs={{0,16},{8,24},{16,0},{24,8},{1,17},{9,25},{17,1},{25,9},{2,18},{10... | collective-permute-start | bytes 3080 | tf_op jit(solution)/shard_map/ppermute | solution.py:173
  68.8 3.7 %collective-permute-start.6 = (f32[16,16]{0,1:T(8,128)S(1)}, f32[16,16]{0,1:T(8,128)S(1)}, u32[]{:S(2)}, u32[]{:S(2)}) collective-permute-start(f32[16,16]{0,1:T(8,128)S(1)} %add.78), channel_id=1, source_target_pairs={{0,1},{1,0},{2,3},{3,2},{4,5},{5,4},{6,7},{7,6},{8,9},{9,8},{10,11... | collective-permute-start | bytes 3080 | tf_op jit(solution)/shard_map/ppermute | solution.py:173
  72.4 3.7 %collective-permute-start.7 = (f32[16,16]{0,1:T(8,128)S(1)}, f32[16,16]{0,1:T(8,128)S(1)}, u32[]{:S(2)}, u32[]{:S(2)}) collective-permute-start(f32[16,16]{0,1:T(8,128)S(1)} %add.79), channel_id=1, source_target_pairs={{0,2},{1,3},{2,0},{3,1},{4,6},{5,7},{6,4},{7,5},{8,10},{9,11},{10,... | collective-permute-start | bytes 3080 | tf_op jit(solution)/shard_map/ppermute | solution.py:173
  76.1 4.5 %collective-permute-start.8 = (f32[16,16]{0,1:T(8,128)S(1)}, f32[16,16]{0,1:T(8,128)S(1)}, u32[]{:S(2)}, u32[]{:S(2)}) collective-permute-start(f32[16,16]{0,1:T(8,128)S(1)} %add.80), channel_id=1, source_target_pairs={{0,4},{1,5},{2,6},{3,7},{4,0},{5,1},{6,2},{7,3},{8,12},{9,13},{10,... | collective-permute-start | bytes 3080 | tf_op jit(solution)/shard_map/ppermute | solution.py:173

commit v16 on v14

--- a/solution.py
+++ b/solution.py
@@ -172,11 +172,11 @@
             pairs = [(i, i ^ stride) for i in range(count)]
             gram = gram + lax.ppermute(gram, axis, pairs)
             stride *= 2
-    lower = jnp.linalg.cholesky(gram)
-    solved = jax.scipy.linalg.solve_triangular(lower, flat, lower=True)
     domain_length = 3 * grid_rows * grid_cols
-    basis = (math.sqrt(domain_length) * solved).reshape(perts.shape)
-    rfactor = lower.T / math.sqrt(domain_length)
+    lower = jnp.linalg.cholesky(gram * (1.0 / domain_length))
+    inverse = jax.scipy.linalg.solve_triangular(lower, jnp.eye(flat.shape[0], dtype=flat.dtype), lower=True)
+    basis = jnp.dot(inverse, flat, precision=lax.Precision.HIGH).reshape(perts.shape)
+    rfactor = lower.T
     return (basis, rfactor)
 
 

time: 88.8 us -> 89.5 us (level)
    dot_general x0 -> x1, matrix products: none -> 1.52 us  [body(): jnp.dot(inverse, flat, precision=lax.Precision.HIGH).reshape(perts.shape)]
    another operation x1, matrix products: 1.5 us -> 0.19 us  [body(): jax.scipy.linalg.solve_triangular(lower, jnp.eye(flat.shape[0], dtype=fla...]
    unnamed x9 -> x10, local copies, waits for them, and re-layouts: 3.7 us -> 3.23 us
  transfers between devices with their start and end apart: 9 -> 9, of which waited for: 8 -> 8; matrix products, arithmetic and copies ran while one was open for 5% -> 4% of each run, Pallas kernels for 0% -> 0%
where the time goes in v16:
time: 89.5 us; the launch traced here: 89.2 us
  waiting for transfers between devices  27.9 us (31%)
  Pallas kernels  24.2 us (27%)
  starting transfers between devices  13.8 us (15%)
  local copies, waits for them, and re-layouts  9.83 us (11%)
  other arithmetic  8.97 us (10%)
  matrix products  3.71 us (4%)
    pallas_call x1, Pallas kernels, forecast(): pl.pallas_call(functools.partial(forecast_kernel, steps=steps), out_shape...  24.2 us
    ppermute x2, waiting for transfers between devices, shift(): return lax.ppermute(part, axes, pairs)  15.6 us
    ppermute x5, waiting for transfers between devices, body(): gram = gram + lax.ppermute(gram, axis, pairs)  10.9 us
    ppermute x2, starting transfers between devices, shift(): return lax.ppermute(part, axes, pairs)  6.12 us
    ppermute x5, starting transfers between devices, body(): gram = gram + lax.ppermute(gram, axis, pairs)  5.86 us
    reshape x2, local copies, waits for them, and re-layouts, shift(): return lax.ppermute(flat, axes, pairs).reshape(part.shape)  3.44 us
    unnamed x10, local copies, waits for them, and re-layouts  3.23 us
    another operation x3, other arithmetic, body(): lower = jnp.linalg.cholesky(gram * (1.0 / domain_length))  2.13 us
  transfers between devices with their start and end apart: 9, of which 8 were waited for; matrix products, arithmetic and copies ran while one was open for 4% of the time, Pallas kernels for 0%

profile of v16, /device:TPU:0, one launch (start us, length us, event | category | flops | bytes accessed | tf_op | source)
XLA Modules:
  0.0 89.2 jit_solution(6871366756471604589)
XLA Ops:
  0.6 1.6 %broadcast_add_fusion = f32[16,3,32,256]{3,2,1,0:T(8,128)S(1)} fusion(f32[16,3,32,256]{3,2,1,0:T(8,128)} %param.3, f32[3,32,256]{2,1,0:T(8,128)} %param.2), kind=kLoop, calls=%fused_computation.13 | loop fusion | flops 393216 | bytes 3244032 | tf_op jit(solution)/shard_map/add | solution.py:158
  2.3 3.0 %collective-permute-start = (f32[17,3,8,256]{3,2,1,0:T(8,128)S(1)}, f32[17,3,8,256]{3,2,1,0:T(8,128)S(1)}, u32[]{:S(2)}, u32[]{:S(2)}) collective-permute-start(f32[17,3,8,256]{3,2,1,0:T(8,128)S(1)} %get-tuple-element.9), channel_id=1, source_target_pairs={{0,1},{1,2},{2,3},{3,4},{4,5},{5,6},{6,7},{7,0},{8,9},{9,10},{10,1... | collective-permute-start | bytes 1253384 | tf_op jit(solution)/shard_map/ppermute | solution.py:38
  5.3 3.1 %collective-permute-start.1 = (f32[17,3,8,256]{3,2,1,0:T(8,128)S(1)}, f32[17,3,8,256]{3,2,1,0:T(8,128)S(1)}, u32[]{:S(2)}, u32[]{:S(2)}) collective-permute-start(f32[17,3,8,256]{3,2,1,0:T(8,128)S(1)} %get-tuple-element.8), channel_id=1, source_target_pairs={{0,7},{1,0},{2,1},{3,2},{4,3},{5,4},{6,5},{7,6},{8,15},{9,8},{10,9... | collective-permute-start | bytes 1253384 | tf_op jit(solution)/shard_map/ppermute | solution.py:38
  8.4 1.3 %pad_maximum_fusion.x_ref = f32[17,3,32,256]{3,2,1,0:T(8,128)} fusion(f32[1,3,32,256]{3,2,1,0:T(8,128)S(1)} %bitcast.40, f32[16,3,32,256]{3,2,1,0:T(8,128)S(1)} %broadcast_add_fusion), kind=kLoop, calls=%fused_computation.2 | loop fusion | flops 417792 | bytes 3342336 | tf_op jit(solution)/shard_map/concatenate | solution.py:158
  9.8 13.4 %collective-permute-done.up_ref = f32[17,3,8,256]{3,2,1,0:T(8,128)S(1)} collective-permute-done((f32[17,3,8,256]{3,2,1,0:T(8,128)S(1)}, f32[17,3,8,256]{3,2,1,0:T(8,128)S(1)}, u32[]{:S(2)}, u32[]{:S(2)}) %collective-permute-start) | collective-permute-done | bytes 417824 | tf_op jit(solution)/shard_map/ppermute | solution.py:38
  23.2 2.2 %collective-permute-done.1.down_ref = f32[17,3,8,256]{3,2,1,0:T(8,128)S(1)} collective-permute-done((f32[17,3,8,256]{3,2,1,0:T(8,128)S(1)}, f32[17,3,8,256]{3,2,1,0:T(8,128)S(1)}, u32[]{:S(2)}, u32[]{:S(2)}) %collective-permute-start.1) | collective-permute-done | bytes 417824 | tf_op jit(solution)/shard_map/ppermute | solution.py:38
  26.6 0.5 reshape.58
  27.2 0.5 reshape.60
  27.7 1.8 %collective-permute-start.3 = (f32[19584]{0:T(1024)S(1)}, f32[19584]{0:T(1024)S(1)}, u32[]{:S(2)}, u32[]{:S(2)}) collective-permute-start(f32[19584]{0:T(1024)S(1)} %reshape.60), channel_id=1, source_target_pairs={{0,24},{8,0},{16,8},{24,16},{1,25},{9,1},{17,9},{25,17},{2,26},{10... | collective-permute-start | bytes 235016 | tf_op jit(solution)/shard_map/ppermute | solution.py:40
  29.5 1.5 %collective-permute-done.2 = f32[19584]{0:T(1024)S(1)} collective-permute-done((f32[19584]{0:T(1024)S(1)}, f32[19584]{0:T(1024)S(1)}, u32[]{:S(2)}, u32[]{:S(2)}) %collective-permute-start.2) | collective-permute-done | bytes 78368 | tf_op jit(solution)/shard_map/ppermute | solution.py:40
  31.0 1.7 %reshape.59.west_ref = f32[17,3,48,8]{3,2,1,0:T(8,128)} reshape(f32[19584]{0:T(1024)S(1)} %collective-permute-done.2) | data formatting | bytes 156672 | tf_op jit(solution)/shard_map/reshape | solution.py:40
  32.7 1.7 %reshape.61.east_ref = f32[17,3,48,8]{3,2,1,0:T(8,128)} reshape(f32[19584]{0:T(1024)S(1)} %collective-permute-done.3) | data formatting | bytes 156672 | tf_op jit(solution)/shard_map/reshape | solution.py:40
  34.5 0.7 broadcast_in_dim.5.cor_ref
  35.2 24.2 %shard_map.41 = f32[17,3,32,256]{3,2,1,0:T(8,128)} custom-call(f32[48,384]{1,0:T(8,128)} %broadcast_in_dim.5.cor_ref, f32[17,3,32,256]{3,2,1,0:T(8,128)} %pad_maximum_fusion.x_ref, f32[17,3,8,256]{3,2,1,0:T(8,128)} %copy-done.1, f32[17,3,8,256]{3,2,1,0:T(8,128)} %copy-done.2, f32[17,3,48,8]{3,2,1,0:T(8,128)} %reshape.59.west_ref, ...), custom_call_target="tpu_custom_call" | custom-call | flops 564019200 | bytes 5431296 | tf_op jit(solution)/shard_map/pallas_call | solution.py:120
  59.4 0.9 %slice_bitcast_fusion = f32[3,32,256]{2,1,0:T(8,128)S(1)} fusion(f32[17,3,32,256]{3,2,1,0:T(8,128)} %shard_map.41), kind=kLoop, calls=%fused_computation.16 | loop fusion | bytes 196608 | tf_op jit(solution)/shard_map/sub | solution.py:161
  60.3 1.5 %slice_subtract_fusion = f32[16,3,32,256]{3,2,1,0:T(8,128)S(1)} fusion(f32[17,3,32,256]{3,2,1,0:T(8,128)} %shard_map.41, f32[3,32,256]{2,1,0:T(8,128)S(1)} %slice_bitcast_fusion), kind=kLoop, calls=%fused_computation.4 | loop fusion | flops 393216 | bytes 3244032 | tf_op jit(solution)/shard_map/sub | solution.py:161
  61.8 2.0 %fusion.4 = f32[16,16]{0,1:T(8,128)S(1)} fusion(f32[16,3,32,256]{3,2,1,0:T(8,128)S(1)} %slice_subtract_fusion), kind=kOutput, calls=%fused_computation.11 | convolution fusion | flops 37748736 | bytes 1573888 | tf_op jit(solution)/shard_map/dot_general | solution.py:163
  64.3 0.8 collective-permute-done.4
  65.2 1.4 %collective-permute-start.5 = (f32[16,16]{0,1:T(8,128)S(1)}, f32[16,16]{0,1:T(8,128)S(1)}, u32[]{:S(2)}, u32[]{:S(2)}) collective-permute-start(f32[16,16]{0,1:T(8,128)S(1)} %add.77), channel_id=1, source_target_pairs={{0,16},{8,24},{16,0},{24,8},{1,17},{9,25},{17,1},{25,9},{2,18},{10... | collective-permute-start | bytes 3080 | tf_op jit(solution)/shard_map/ppermute | solution.py:173
  66.5 2.3 %collective-permute-done.5 = f32[16,16]{0,1:T(8,128)S(1)} collective-permute-done((f32[16,16]{0,1:T(8,128)S(1)}, f32[16,16]{0,1:T(8,128)S(1)}, u32[]{:S(2)}, u32[]{:S(2)}) %collective-permute-start.5) | collective-permute-done | bytes 1056 | tf_op jit(solution)/shard_map/ppermute | solution.py:173
  69.3 3.2 %collective-permute-done.6 = f32[16,16]{0,1:T(8,128)S(1)} collective-permute-done((f32[16,16]{0,1:T(8,128)S(1)}, f32[16,16]{0,1:T(8,128)S(1)}, u32[]{:S(2)}, u32[]{:S(2)}) %collective-permute-start.6) | collective-permute-done | bytes 1056 | tf_op jit(solution)/shard_map/ppermute | solution.py:173
  72.5 1.3 %collective-permute-start.7 = (f32[16,16]{0,1:T(8,128)S(1)}, f32[16,16]{0,1:T(8,128)S(1)}, u32[]{:S(2)}, u32[]{:S(2)}) collective-permute-start(f32[16,16]{0,1:T(8,128)S(1)} %add.79), channel_id=1, source_target_pairs={{0,2},{1,3},{2,0},{3,1},{4,6},{5,7},{6,4},{7,5},{8,10},{9,11},{10,... | collective-permute-start | bytes 3080 | tf_op jit(solution)/shard_map/ppermute | solution.py:173
  73.7 2.4 %collective-permute-done.7 = f32[16,16]{0,1:T(8,128)S(1)} collective-permute-done((f32[16,16]{0,1:T(8,128)S(1)}, f32[16,16]{0,1:T(8,128)S(1)}, u32[]{:S(2)}, u32[]{:S(2)}) %collective-permute-start.7) | collective-permute-done | bytes 1056 | tf_op jit(solution)/shard_map/ppermute | solution.py:173
  76.1 2.3 %collective-permute-start.8 = (f32[16,16]{0,1:T(8,128)S(1)}, f32[16,16]{0,1:T(8,128)S(1)}, u32[]{:S(2)}, u32[]{:S(2)}) collective-permute-start(f32[16,16]{0,1:T(8,128)S(1)} %add.80), channel_id=1, source_target_pairs={{0,4},{1,5},{2,6},{3,7},{4,0},{5,1},{6,2},{7,3},{8,12},{9,13},{10,... | collective-permute-start | bytes 3080 | tf_op jit(solution)/shard_map/ppermute | solution.py:173
  78.5 2.1 %collective-permute-done.8 = f32[16,16]{0,1:T(8,128)S(1)} collective-permute-done((f32[16,16]{0,1:T(8,128)S(1)}, f32[16,16]{0,1:T(8,128)S(1)}, u32[]{:S(2)}, u32[]{:S(2)}) %collective-permute-start.8) | collective-permute-done | bytes 1056 | tf_op jit(solution)/shard_map/ppermute | solution.py:173
  80.8 1.5 %cholesky.17 = f32[16,16]{1,0:T(8,128)S(1)} custom-call(f32[16,16]{1,0:T(8,128)S(1)} %fusion.10), custom_call_target="Cholesky" | custom-call | tf_op jit(solution)/shard_map/jit(cholesky)/cholesky | solution.py:176
  82.3 0.6 compare_reduce_fusion
  82.9 0.6 fusion.11
  83.6 1.2 %custom-call.7 = f32[1,16,16]{1,2,0:T(8,128)S(1)} custom-call(f32[1,16,16]{2,1,0:T(8,128)S(1)} %get-tuple-element.11), custom_call_target="InvertDiagBlocksLowerTriangular" | custom-call | tf_op jit(solution)/shard_map/jit(_solve_triangular)/triangular_solve | solution.py:177
  85.0 1.5 %fusion = f32[16,3,32,256]{3,0,2,1:T(8,128)S(1)} fusion(f32[16,16,1,1]{1,0,3,2:T(8,128)S(1)} %convolution_bitcast_fusion, f32[3,32,256,16]{2,1,0,3:T(8,128)S(1)} %fusion.22), kind=kOutput, calls=%fused_computation.5 | convolution fusion | flops 37748736 | bytes 3146752 | tf_op jit(solution)/shard_map/dot_general | solution.py:178
  86.5 2.1 %copy.17 = f32[16,3,32,256]{3,2,1,0:T(8,128)} copy(f32[16,3,32,256]{3,0,2,1:T(8,128)S(1)} %fusion) | data formatting | bytes 3145728
  88.6 0.7 copy.18
  (26 shorter events, 2.7 us)
Async XLA Ops:
  0.6 1.6 %copy-start.3 = (f32[3,32,256]{2,1,0:T(8,128)S(1)}, f32[3,32,256]{2,1,0:T(8,128)}, u32[]{:S(2)}) copy-start(f32[3,32,256]{2,1,0:T(8,128)} %param.2) | copy-start | bytes 294916
  2.3 20.9 %collective-permute-start = (f32[17,3,8,256]{3,2,1,0:T(8,128)S(1)}, f32[17,3,8,256]{3,2,1,0:T(8,128)S(1)}, u32[]{:S(2)}, u32[]{:S(2)}) collective-permute-start(f32[17,3,8,256]{3,2,1,0:T(8,128)S(1)} %get-tuple-element.9), channel_id=1, source_target_pairs={{0,1},{1,2},{2,3},{3,4},{4,5},{5,6},{6,7},{7,0},{8,9},{9,10},{10,1... | collective-permute-start | bytes 1253384 | tf_op jit(solution)/shard_map/ppermute | solution.py:38
  5.3 20.1 %collective-permute-start.1 = (f32[17,3,8,256]{3,2,1,0:T(8,128)S(1)}, f32[17,3,8,256]{3,2,1,0:T(8,128)S(1)}, u32[]{:S(2)}, u32[]{:S(2)}) collective-permute-start(f32[17,3,8,256]{3,2,1,0:T(8,128)S(1)} %get-tuple-element.8), channel_id=1, source_target_pairs={{0,7},{1,0},{2,1},{3,2},{4,3},{5,4},{6,5},{7,6},{8,15},{9,8},{10,9... | collective-permute-start | bytes 1253384 | tf_op jit(solution)/shard_map/ppermute | solution.py:38
  23.2 2.5 %copy-start.1 = (f32[17,3,8,256]{3,2,1,0:T(8,128)}, f32[17,3,8,256]{3,2,1,0:T(8,128)S(1)}, u32[]{:S(2)}) copy-start(f32[17,3,8,256]{3,2,1,0:T(8,128)S(1)} %collective-permute-done.up_ref) | copy-start | bytes 1253380
  25.4 0.8 copy-start.2
  27.1 3.9 %collective-permute-start.2 = (f32[19584]{0:T(1024)S(1)}, f32[19584]{0:T(1024)S(1)}, u32[]{:S(2)}, u32[]{:S(2)}) collective-permute-start(f32[19584]{0:T(1024)S(1)} %reshape.58), channel_id=1, source_target_pairs={{0,8},{8,16},{16,24},{24,0},{1,9},{9,17},{17,25},{25,1},{2,10},{10... | collective-permute-start | bytes 235016 | tf_op jit(solution)/shard_map/ppermute | solution.py:40
  27.7 5.0 %collective-permute-start.3 = (f32[19584]{0:T(1024)S(1)}, f32[19584]{0:T(1024)S(1)}, u32[]{:S(2)}, u32[]{:S(2)}) collective-permute-start(f32[19584]{0:T(1024)S(1)} %reshape.60), channel_id=1, source_target_pairs={{0,24},{8,0},{16,8},{24,16},{1,25},{9,1},{17,9},{25,17},{2,26},{10... | collective-permute-start | bytes 235016 | tf_op jit(solution)/shard_map/ppermute | solution.py:40
  61.8 16.6 %copy-start = (f32[17,3,32,256]{3,2,1,0:T(8,128)S(1)}, f32[17,3,32,256]{3,2,1,0:T(8,128)}, u32[]{:S(2)}) copy-start(f32[17,3,32,256]{3,2,1,0:T(8,128)} %shard_map.41) | copy-start | bytes 5013508
  63.8 1.4 %collective-permute-start.4 = (f32[16,16]{0,1:T(8,128)S(1)}, f32[16,16]{0,1:T(8,128)S(1)}, u32[]{:S(2)}, u32[]{:S(2)}) collective-permute-start(f32[16,16]{0,1:T(8,128)S(1)} %fusion.4), channel_id=1, source_target_pairs={{0,8},{8,0},{16,24},{24,16},{1,9},{9,1},{17,25},{25,17},{2,10},{10... | collective-permute-start | bytes 3080 | tf_op jit(solution)/shard_map/ppermute | solution.py:173
  65.2 3.7 %collective-permute-start.5 = (f32[16,16]{0,1:T(8,128)S(1)}, f32[16,16]{0,1:T(8,128)S(1)}, u32[]{:S(2)}, u32[]{:S(2)}) collective-permute-start(f32[16,16]{0,1:T(8,128)S(1)} %add.77), channel_id=1, source_target_pairs={{0,16},{8,24},{16,0},{24,8},{1,17},{9,25},{17,1},{25,9},{2,18},{10... | collective-permute-start | bytes 3080 | tf_op jit(solution)/shard_map/ppermute | solution.py:173
  68.8 3.7 %collective-permute-start.6 = (f32[16,16]{0,1:T(8,128)S(1)}, f32[16,16]{0,1:T(8,128)S(1)}, u32[]{:S(2)}, u32[]{:S(2)}) collective-permute-start(f32[16,16]{0,1:T(8,128)S(1)} %add.78), channel_id=1, source_target_pairs={{0,1},{1,0},{2,3},{3,2},{4,5},{5,4},{6,7},{7,6},{8,9},{9,8},{10,11... | collective-permute-start | bytes 3080 | tf_op jit(solution)/shard_map/ppermute | solution.py:173
  72.5 3.7 %collective-permute-start.7 = (f32[16,16]{0,1:T(8,128)S(1)}, f32[16,16]{0,1:T(8,128)S(1)}, u32[]{:S(2)}, u32[]{:S(2)}) collective-permute-start(f32[16,16]{0,1:T(8,128)S(1)} %add.79), channel_id=1, source_target_pairs={{0,2},{1,3},{2,0},{3,1},{4,6},{5,7},{6,4},{7,5},{8,10},{9,11},{10,... | collective-permute-start | bytes 3080 | tf_op jit(solution)/shard_map/ppermute | solution.py:173
  76.1 4.5 %collective-permute-start.8 = (f32[16,16]{0,1:T(8,128)S(1)}, f32[16,16]{0,1:T(8,128)S(1)}, u32[]{:S(2)}, u32[]{:S(2)}) collective-permute-start(f32[16,16]{0,1:T(8,128)S(1)} %add.80), channel_id=1, source_target_pairs={{0,4},{1,5},{2,6},{3,7},{4,0},{5,1},{6,2},{7,3},{8,12},{9,13},{10,... | collective-permute-start | bytes 3080 | tf_op jit(solution)/shard_map/ppermute | solution.py:173
